TPU v7x, 32 devices: a whole 2x2x4 slice. The times are simulated.
32 devices in a mesh: grp: 2 (over y), row: 4 (over z), col: 4 (over x, core).
Axes of the slice: x: 2, y: 2, z: 4, core: 2. Of those that a mesh axis runs over, the one named last changes fastest.
Arguments:
- tokens: bfloat16 [256, 10240], P(('grp', 'col'), 'row'), parts along dimension 0, may hold values from -6 to 6
- gate_up: bfloat16 [2, 10240, 26624], P(None, 'row', 'col'), may hold values from -0.0625 to 0.0625
Outputs:
- hidden: bfloat16 [256, 26624], P(('grp', 'row'), 'col'), parts along dimension 0
There are 2 independent parts, one for each index of `grp`. A program takes and returns all parts, laid end to end along the dimension named above; an argument that names none is the same for every part. Nothing has to cross between parts.
All inputs are finite; a program needn't handle non-finite values.
Results may differ from a plain program's by a relative error of at most 0.015.
Values may be sent and summed in bfloat16 or wider, within the bound.
No kernel may reach another device: no remote copies, remote signals or barrier semaphores. Data moves between devices by JAX's collectives and lax.ppermute only.
A program may use at most 192 MiB of HBM per device.

v0:
```python
import jax
import jax.numpy as jnp
from jax import lax
from jax.sharding import PartitionSpec as P


def on_device(tokens, gate_up):
    gathered = lax.all_gather(tokens, "col", axis=0, tiled=True)
    mine = lax.psum_scatter(
        jnp.einsum("td,gdf->tgf", gathered, gate_up, preferred_element_type=jnp.float32).astype(
            jnp.bfloat16
        ),
        "row",
        scatter_dimension=0,
        tiled=True,
    ).astype(jnp.float32)
    return (jax.nn.silu(mine[:, 0]) * mine[:, 1]).astype(jnp.bfloat16)


def solution(mesh):
    placed = (P(("grp", "col"), "row"), P(None, "row", "col"))
    return jax.shard_map(
        on_device, mesh=mesh, in_specs=placed, out_specs=P(("grp", "row"), "col"), check_vma=False
    )
```

profile of v0, /device:TPU:0, one launch (start us, length us, event | category | flops | bytes accessed | tf_op | source)
XLA Modules:
  0.0 116.4 jit_solution(15428799561953705559)
XLA Ops:
  6.5 0.0 reduce-scatter.2.cloned.1.call-start
  6.5 9.6 %all_gather.3 = bf16[128,2560]{1,0:T(8,128)(2,1)S(1)} all-gather(bf16[32,2560]{1,0:T(8,128)(2,1)} %param.2), channel_id=1, replica_groups=mesh['grp'=2,'row'=4,'col'=4] {'col'}, dimensions={0}, use_global_device_ids=true | all-gather | bytes 819200 | tf_op jit(solution)/shard_map/all_gather | solution.py:8
  16.1 25.7 %convolution_convert_fusion = bf16[128,2,6656]{2,0,1:T(8,128)(2,1)} fusion(bf16[2,2560,6656]{2,1,0:T(8,128)(2,1)} %param.3, bf16[128,2560]{1,0:T(8,128)(2,1)S(1)} %all_gather.3), kind=kOutput, calls=%fused_computation | convolution fusion | flops 8725856256 | bytes 72220672 | tf_op jit(solution)/shard_map/td,gdf->tgf/dot_general | solution.py:10
  41.8 0.0 reduce-scatter.2.cloned.1.call-update
  41.8 65.5 %reduce-scatter.2.cloned.1.call-done = bf16[32,2,6656]{2,0,1:T(8,128)(2,1)} async-done(((bf16[128,2,6656]{2,0,1:T(8,128)(2,1)}), bf16[32,2,6656]{2,0,1:T(8,128)(2,1)}) %reduce-scatter.2.cloned.1.call-update) | async-done | bytes 851984 | tf_op jit(solution)/shard_map/reduce_scatter | solution.py:9
  107.3 1.3 %convert_element_type.10 = f32[32,2,6656]{2,0,1:T(8,128)S(1)} convert(bf16[32,2,6656]{2,0,1:T(8,128)(2,1)} %reduce-scatter.2.cloned.1.call-done) | non-fusion elementwise | flops 425984 | bytes 2555904 | tf_op jit(solution)/shard_map/convert_element_type | solution.py:16
  108.6 1.0 fusion.1
Async XLA Ops:
  6.5 100.8 %reduce-scatter.2.cloned.1.call-start = ((), (), s32[]{:S(2)}) async-start(), calls=%async_computation.1 | async-start | bytes 4259840 | tf_op jit(solution)/shard_map/reduce_scatter | solution.py:9
Sparse Core Ops, SparseCore 0:
  42.0 65.2 reduce-scatter.1
where the time goes:
time: 117 us; the launch traced here: 116 us
  waiting for transfers between devices  65.5 us (56%)
  matrix products  25.7 us (22%)
  between operations  13.4 us (11%)
  blocking collectives  9.56 us (8%)
  other arithmetic  2.25 us (2%)
    reduce_scatter x1, waiting for transfers between devices, on_device(): lax.psum_scatter(jnp.einsum('td,gdf->tgf', gathered, gate_up, preferred_e...  65.5 us
    dot_general x1, matrix products, on_device(): jnp.einsum('td,gdf->tgf', gathered, gate_up, preferred_element_type=jnp.f...  25.7 us
    all_gather x1, blocking collectives, on_device(): gathered = lax.all_gather(tokens, 'col', axis=0, tiled=True)  9.56 us
  transfers between devices with their start and end apart: 1, of which 1 were waited for; matrix products, arithmetic and copies ran while one was open for 0% of the time, Pallas kernels for 0%

commit v1 on v0

v1 whole, which is shorter than its diff:
```python
import jax
import jax.numpy as jnp
from jax import lax
from jax.sharding import PartitionSpec as P

CHUNKS = 4


def gather_cols(tokens, m):
    c = lax.axis_index("col")
    rows = tokens.shape[0]
    buf = jnp.zeros((m, rows, tokens.shape[1]), tokens.dtype)
    buf = lax.dynamic_update_index_in_dim(buf, tokens, c, 0)
    for s in range(1, m):
        got = lax.ppermute(tokens, "col", [(i, (i + s) % m) for i in range(m)])
        buf = lax.dynamic_update_index_in_dim(buf, got, (c - s + m) % m, 0)
    return buf.reshape(m * rows, tokens.shape[1])


def line_reduce(part, n, p):
    def block(d):
        return lax.dynamic_index_in_dim(part, jnp.clip(d, 0, n - 1), 0, keepdims=False)

    def add(a, b):
        return (a.astype(jnp.float32) + b.astype(jnp.float32)).astype(jnp.bfloat16)

    with jax.named_scope("up"):
        origin = [lax.ppermute(part[n - r], "row", [(0, 1)]) for r in range(1, n)]
        plus = origin[0]
        for r in range(2, n):
            sent = lax.ppermute(add(block(p + n - r), plus), "row", [(q, q + 1) for q in range(1, r)])
            plus = origin[r - 1] + sent
    with jax.named_scope("down"):
        origin = [lax.ppermute(part[r - 1], "row", [(n - 1, n - 2)]) for r in range(1, n)]
        minus = origin[0]
        for r in range(2, n):
            sent = lax.ppermute(add(block(p - n + r), minus), "row", [(q, q - 1) for q in range(n - r, n - 1)])
            minus = origin[r - 1] + sent
    return plus, minus


def on_device(tokens, gate_up, n, m):
    p = lax.axis_index("row")
    gathered = gather_cols(tokens, m)
    t = gathered.shape[0]
    tb = t // n
    f = gate_up.shape[2]
    units = f // 128
    k = min(CHUNKS, units)
    edges = [128 * (units * i // k) for i in range(k + 1)]
    edges[-1] = f
    outs = []
    for i in range(k):
        w = gate_up[:, :, edges[i] : edges[i + 1]]
        part = jnp.einsum("td,gdf->tgf", gathered, w, preferred_element_type=jnp.float32).astype(jnp.bfloat16)
        part = part.reshape(n, tb, 2, edges[i + 1] - edges[i])
        own = lax.dynamic_index_in_dim(part, p, 0, keepdims=False).astype(jnp.float32)
        if n > 1:
            plus, minus = line_reduce(part, n, p)
            own = own + plus.astype(jnp.float32) + minus.astype(jnp.float32)
        outs.append((jax.nn.silu(own[:, 0]) * own[:, 1]).astype(jnp.bfloat16))
    return jnp.concatenate(outs, axis=1)


def solution(mesh):
    n = mesh.shape["row"]
    m = mesh.shape["col"]
    placed = (P(("grp", "col"), "row"), P(None, "row", "col"))

    def body(tokens, gate_up):
        return on_device(tokens, gate_up, n, m)

    return jax.shard_map(
        body, mesh=mesh, in_specs=placed, out_specs=P(("grp", "row"), "col"), check_vma=False
    )
```

time: 117 us -> 150 us (1.28)
  starting transfers between devices: 0.01 us -> 74.6 us
  waiting for transfers between devices: 65.5 us -> 36.9 us
  between operations: 13.4 us -> 0.8 us
  blocking collectives: 9.56 us -> 0 us
  matrix products: 25.7 us -> 33.1 us
    ppermute x0 -> x43, starting transfers between devices: none -> 74.6 us  [the longest x12 48.9 us: line_reduce(): origin = [lax.ppermute(part[n - r], 'row', [(0, 1)]) for r in range(1, n)]]
    reduce_scatter x1 -> x0, waiting for transfers between devices: 65.5 us -> none  [on_device(): lax.psum_scatter(jnp.einsum('td,gdf->tgf', gathered, gate_up, preferred_e...]
    ppermute x0 -> x43, waiting for transfers between devices: none -> 36.9 us  [the longest x12 20.4 us: line_reduce(): origin = [lax.ppermute(part[n - r], 'row', [(0, 1)]) for r in range(1, n)]]
    all_gather x1 -> x0, blocking collectives: 9.56 us -> none  [on_device(): gathered = lax.all_gather(tokens, 'col', axis=0, tiled=True)]
    dot_general x1 -> x4, matrix products: 25.7 us -> 33.1 us  [on_device(): jnp.einsum('td,gdf->tgf', gathered, w, preferred_element_type=jnp.float32)]
  transfers between devices with their start and end apart: 1 -> 43, of which waited for: 1 -> 13; matrix products, arithmetic and copies ran while one was open for 0% -> 19% of each run, Pallas kernels for 0% -> 0%
where the time goes in v1:
time: 150 us; the launch traced here: 149 us
  starting transfers between devices  74.6 us (50%)
  waiting for transfers between devices  36.9 us (25%)
  matrix products  33.1 us (22%)
  other arithmetic  2.7 us (2%)
    ppermute x12, starting transfers between devices, line_reduce(): origin = [lax.ppermute(part[n - r], 'row', [(0, 1)]) for r in range(1, n)]  48.9 us
    dot_general x4, matrix products, on_device(): jnp.einsum('td,gdf->tgf', gathered, w, preferred_element_type=jnp.float32)  33.1 us
    ppermute x12, waiting for transfers between devices, line_reduce(): origin = [lax.ppermute(part[n - r], 'row', [(0, 1)]) for r in range(1, n)]  20.4 us
    ppermute x8, waiting for transfers between devices, line_reduce(): lax.ppermute(add(block(p - n + r), minus), 'row', [(q, q - 1) for q in ra...  11.2 us
    ppermute x12, starting transfers between devices, line_reduce(): lax.ppermute(part[r - 1], 'row', [(n - 1, n - 2)])  8.07 us
    ppermute x8, starting transfers between devices, line_reduce(): lax.ppermute(add(block(p - n + r), minus), 'row', [(q, q - 1) for q in ra...  7.84 us
    ppermute x8, starting transfers between devices, line_reduce(): lax.ppermute(add(block(p + n - r), plus), 'row', [(q, q + 1) for q in ran...  5.39 us
    ppermute x3, waiting for transfers between devices, gather_cols(): got = lax.ppermute(tokens, 'col', [(i, (i + s) % m) for i in range(m)])  5.28 us
  transfers between devices with their start and end apart: 43, of which 13 were waited for; matrix products, arithmetic and copies ran while one was open for 19% of the time, Pallas kernels for 0%

profile of v1, /device:TPU:0, one launch (start us, length us, event | category | flops | bytes accessed | tf_op | source)
XLA Modules:
  0.0 149.5 jit_solution(17717062554312602619)
XLA Ops:
  0.5 2.5 %collective-permute-start.1 = (bf16[32,2560]{1,0:T(8,128)(2,1)}, bf16[32,2560]{1,0:T(8,128)(2,1)S(1)}, u32[]{:S(2)}, u32[]{:S(2)}) collective-permute-start(bf16[32,2560]{1,0:T(8,128)(2,1)} %param.2), channel_id=1, source_target_pairs={{0,2},{1,3},{2,0},{3,1},{4,6},{5,7},{6,4},{7,5},{8,10},{9,11},{10,... | collective-permute-start | bytes 491528 | tf_op jit(solution)/shard_map/ppermute | solution.py:15
  3.0 1.5 collective-permute-start.2
  6.5 1.7 %collective-permute-done.1 = bf16[32,2560]{1,0:T(8,128)(2,1)S(1)} collective-permute-done((bf16[32,2560]{1,0:T(8,128)(2,1)}, bf16[32,2560]{1,0:T(8,128)(2,1)S(1)}, u32[]{:S(2)}, u32[]{:S(2)}) %collective-permute-start.1) | collective-permute-done | bytes 163872 | tf_op jit(solution)/shard_map/ppermute | solution.py:15
  8.2 2.6 %collective-permute-done.2 = bf16[32,2560]{1,0:T(8,128)(2,1)S(1)} collective-permute-done((bf16[32,2560]{1,0:T(8,128)(2,1)}, bf16[32,2560]{1,0:T(8,128)(2,1)S(1)}, u32[]{:S(2)}, u32[]{:S(2)}) %collective-permute-start.2) | collective-permute-done | bytes 163872 | tf_op jit(solution)/shard_map/ppermute | solution.py:15
  10.8 8.2 %fusion.8 = bf16[128,2,1664]{2,0,1:T(8,128)(2,1)S(1)} fusion(bf16[128,2560,1]{1,0,2:T(8,128)(2,1)S(1)} %bitcast.171, bf16[2,2560,6656]{2,1,0:T(8,128)(2,1)} %param.3), kind=kOutput, calls=%fused_computation.8 | convolution fusion | flops 2181464064 | bytes 18546688 | tf_op jit(solution)/shard_map/td,gdf->tgf/dot_general | solution.py:55
  19.8 3.5 %collective-permute-start.3 = (bf16[32,2,1664]{2,0,1:T(8,128)(2,1)S(1)}, bf16[32,2,1664]{2,0,1:T(8,128)(2,1)S(1)}, u32[]{:S(2)}, u32[]{:S(2)}) collective-permute-start(bf16[32,2,1664]{2,0,1:T(8,128)(2,1)S(1)} %get-tuple-element.12), channel_id=1, source_target_pairs={{0,4},{1,5},{2,6},{3,7},{16,20},{17,21},{18,22},{19,23}} | collective-permute-start | bytes 638984 | tf_op jit(solution)/shard_map/up/ppermute | solution.py:28
  23.3 8.3 %fusion.11 = bf16[128,2,1664]{2,0,1:T(8,128)(2,1)S(1)} fusion(bf16[128,2560,1]{1,0,2:T(8,128)(2,1)S(1)} %bitcast.172, bf16[2,2560,6656]{2,1,0:T(8,128)(2,1)} %param.3), kind=kOutput, calls=%fused_computation.9 | convolution fusion | flops 2181464064 | bytes 18546688 | tf_op jit(solution)/shard_map/td,gdf->tgf/dot_general | solution.py:55
  31.7 8.3 %fusion.14 = bf16[128,2,1664]{2,0,1:T(8,128)(2,1)S(1)} fusion(bf16[128,2560,1]{1,0,2:T(8,128)(2,1)S(1)} %bitcast.173, bf16[2,2560,6656]{2,1,0:T(8,128)(2,1)} %param.3), kind=kOutput, calls=%fused_computation.10 | convolution fusion | flops 2181464064 | bytes 18546688 | tf_op jit(solution)/shard_map/td,gdf->tgf/dot_general | solution.py:55
  40.0 8.2 %fusion.17 = bf16[128,2,1664]{2,0,1:T(8,128)(2,1)S(1)} fusion(bf16[128,2560,1]{1,0,2:T(8,128)(2,1)S(1)} %bitcast.174, bf16[2,2560,6656]{2,1,0:T(8,128)(2,1)} %param.3), kind=kOutput, calls=%fused_computation.11 | convolution fusion | flops 2181464064 | bytes 18546688 | tf_op jit(solution)/shard_map/td,gdf->tgf/dot_general | solution.py:55
  48.9 1.3 collective-permute-start.5
  50.3 1.3 collective-permute-start.4
  51.8 1.3 collective-permute-start.15
  53.1 2.7 %collective-permute-done.5 = bf16[32,2,1664]{2,0,1:T(8,128)(2,1)S(1)} collective-permute-done((bf16[32,2,1664]{2,0,1:T(8,128)(2,1)S(1)}, bf16[32,2,1664]{2,0,1:T(8,128)(2,1)S(1)}, u32[]{:S(2)}, u32[]{:S(2)}) %collective-permute-start.5) | collective-permute-done | bytes 213024 | tf_op jit(solution)/shard_map/up/ppermute | solution.py:28
  56.7 8.1 %collective-permute-done.15 = bf16[32,2,1664]{2,0,1:T(8,128)(2,1)S(1)} collective-permute-done((bf16[32,2,1664]{2,0,1:T(8,128)(2,1)S(1)}, bf16[32,2,1664]{2,0,1:T(8,128)(2,1)S(1)}, u32[]{:S(2)}, u32[]{:S(2)}) %collective-permute-start.15) | collective-permute-done | bytes 213024 | tf_op jit(solution)/shard_map/up/ppermute | solution.py:28
  64.7 4.4 %collective-permute-start.25 = (bf16[32,2,1664]{2,0,1:T(8,128)(2,1)S(1)}, bf16[32,2,1664]{2,0,1:T(8,128)(2,1)S(1)}, u32[]{:S(2)}, u32[]{:S(2)}) collective-permute-start(bf16[32,2,1664]{2,0,1:T(8,128)(2,1)S(1)} %get-tuple-element.25), channel_id=1, source_target_pairs={{0,4},{1,5},{2,6},{3,7},{16,20},{17,21},{18,22},{19,23}} | collective-permute-start | bytes 638984 | tf_op jit(solution)/shard_map/up/ppermute | solution.py:28
  69.9 3.7 %collective-permute-done.25 = bf16[32,2,1664]{2,0,1:T(8,128)(2,1)S(1)} collective-permute-done((bf16[32,2,1664]{2,0,1:T(8,128)(2,1)S(1)}, bf16[32,2,1664]{2,0,1:T(8,128)(2,1)S(1)}, u32[]{:S(2)}, u32[]{:S(2)}) %collective-permute-start.25) | collective-permute-done | bytes 213024 | tf_op jit(solution)/shard_map/up/ppermute | solution.py:28
  73.6 4.4 %collective-permute-start.35 = (bf16[32,2,1664]{2,0,1:T(8,128)(2,1)S(1)}, bf16[32,2,1664]{2,0,1:T(8,128)(2,1)S(1)}, u32[]{:S(2)}, u32[]{:S(2)}) collective-permute-start(bf16[32,2,1664]{2,0,1:T(8,128)(2,1)S(1)} %get-tuple-element.33), channel_id=1, source_target_pairs={{0,4},{1,5},{2,6},{3,7},{16,20},{17,21},{18,22},{19,23}} | collective-permute-start | bytes 638984 | tf_op jit(solution)/shard_map/up/ppermute | solution.py:28
  78.8 2.8 %collective-permute-done.35 = bf16[32,2,1664]{2,0,1:T(8,128)(2,1)S(1)} collective-permute-done((bf16[32,2,1664]{2,0,1:T(8,128)(2,1)S(1)}, bf16[32,2,1664]{2,0,1:T(8,128)(2,1)S(1)}, u32[]{:S(2)}, u32[]{:S(2)}) %collective-permute-start.35) | collective-permute-done | bytes 213024 | tf_op jit(solution)/shard_map/up/ppermute | solution.py:28
  83.1 9.1 %collective-permute-start.14 = (bf16[32,2,1664]{2,0,1:T(8,128)(2,1)S(1)}, bf16[32,2,1664]{2,0,1:T(8,128)(2,1)S(1)}, u32[]{:S(2)}, u32[]{:S(2)}) collective-permute-start(bf16[32,2,1664]{2,0,1:T(8,128)(2,1)S(1)} %get-tuple-element.19), channel_id=1, source_target_pairs={{0,4},{1,5},{2,6},{3,7},{16,20},{17,21},{18,22},{19,23}} | collective-permute-start | bytes 638984 | tf_op jit(solution)/shard_map/up/ppermute | solution.py:28
  95.4 4.4 %collective-permute-start.24 = (bf16[32,2,1664]{2,0,1:T(8,128)(2,1)S(1)}, bf16[32,2,1664]{2,0,1:T(8,128)(2,1)S(1)}, u32[]{:S(2)}, u32[]{:S(2)}) collective-permute-start(bf16[32,2,1664]{2,0,1:T(8,128)(2,1)S(1)} %get-tuple-element.27), channel_id=1, source_target_pairs={{0,4},{1,5},{2,6},{3,7},{16,20},{17,21},{18,22},{19,23}} | collective-permute-start | bytes 638984 | tf_op jit(solution)/shard_map/up/ppermute | solution.py:28
  102.1 1.1 collective-permute-done.24
  103.1 4.4 %collective-permute-start.34 = (bf16[32,2,1664]{2,0,1:T(8,128)(2,1)S(1)}, bf16[32,2,1664]{2,0,1:T(8,128)(2,1)S(1)}, u32[]{:S(2)}, u32[]{:S(2)}) collective-permute-start(bf16[32,2,1664]{2,0,1:T(8,128)(2,1)S(1)} %get-tuple-element.35), channel_id=1, source_target_pairs={{0,4},{1,5},{2,6},{3,7},{16,20},{17,21},{18,22},{19,23}} | collective-permute-start | bytes 638984 | tf_op jit(solution)/shard_map/up/ppermute | solution.py:28
  109.8 1.1 collective-permute-done.34
  111.5 4.4 %collective-permute-start.13 = (bf16[32,2,1664]{2,0,1:T(8,128)(2,1)S(1)}, bf16[32,2,1664]{2,0,1:T(8,128)(2,1)S(1)}, u32[]{:S(2)}, u32[]{:S(2)}) collective-permute-start(bf16[32,2,1664]{2,0,1:T(8,128)(2,1)S(1)} %get-tuple-element.20), channel_id=1, source_target_pairs={{0,4},{1,5},{2,6},{3,7},{16,20},{17,21},{18,22},{19,23}} | collective-permute-start | bytes 638984 | tf_op jit(solution)/shard_map/up/ppermute | solution.py:28
  116.0 1.3 collective-permute-start.12
  118.8 5.9 %collective-permute-start.23 = (bf16[32,2,1664]{2,0,1:T(8,128)(2,1)S(1)}, bf16[32,2,1664]{2,0,1:T(8,128)(2,1)S(1)}, u32[]{:S(2)}, u32[]{:S(2)}) collective-permute-start(bf16[32,2,1664]{2,0,1:T(8,128)(2,1)S(1)} %get-tuple-element.28), channel_id=1, source_target_pairs={{0,4},{1,5},{2,6},{3,7},{16,20},{17,21},{18,22},{19,23}} | collective-permute-start | bytes 638984 | tf_op jit(solution)/shard_map/up/ppermute | solution.py:28
  125.4 1.3 collective-permute-start.22
  127.6 4.6 %collective-permute-start.33 = (bf16[32,2,1664]{2,0,1:T(8,128)(2,1)S(1)}, bf16[32,2,1664]{2,0,1:T(8,128)(2,1)S(1)}, u32[]{:S(2)}, u32[]{:S(2)}) collective-permute-start(bf16[32,2,1664]{2,0,1:T(8,128)(2,1)S(1)} %get-tuple-element.36), channel_id=1, source_target_pairs={{0,4},{1,5},{2,6},{3,7},{16,20},{17,21},{18,22},{19,23}} | collective-permute-start | bytes 638984 | tf_op jit(solution)/shard_map/up/ppermute | solution.py:28
  133.2 1.3 collective-permute-start.32
  136.1 1.3 collective-permute-start.42
  137.4 4.0 %collective-permute-done.32 = bf16[32,2,1664]{2,0,1:T(8,128)(2,1)S(1)} collective-permute-done((bf16[32,2,1664]{2,0,1:T(8,128)(2,1)S(1)}, bf16[32,2,1664]{2,0,1:T(8,128)(2,1)S(1)}, u32[]{:S(2)}, u32[]{:S(2)}) %collective-permute-start.32) | collective-permute-done | bytes 213024 | tf_op jit(solution)/shard_map/down/ppermute | solution.py:37
  141.6 6.9 %collective-permute-done.42 = bf16[32,2,1664]{2,0,1:T(8,128)(2,1)S(1)} collective-permute-done((bf16[32,2,1664]{2,0,1:T(8,128)(2,1)S(1)}, bf16[32,2,1664]{2,0,1:T(8,128)(2,1)S(1)}, u32[]{:S(2)}, u32[]{:S(2)}) %collective-permute-start.42) | collective-permute-done | bytes 213024 | tf_op jit(solution)/shard_map/down/ppermute | solution.py:37
  (84 shorter events, 22.9 us)
Async XLA Ops:
  0.5 7.7 %collective-permute-start.1 = (bf16[32,2560]{1,0:T(8,128)(2,1)}, bf16[32,2560]{1,0:T(8,128)(2,1)S(1)}, u32[]{:S(2)}, u32[]{:S(2)}) collective-permute-start(bf16[32,2560]{1,0:T(8,128)(2,1)} %param.2), channel_id=1, source_target_pairs={{0,2},{1,3},{2,0},{3,1},{4,6},{5,7},{6,4},{7,5},{8,10},{9,11},{10,... | collective-permute-start | bytes 491528 | tf_op jit(solution)/shard_map/ppermute | solution.py:15
  3.0 7.8 %collective-permute-start.2 = (bf16[32,2560]{1,0:T(8,128)(2,1)}, bf16[32,2560]{1,0:T(8,128)(2,1)S(1)}, u32[]{:S(2)}, u32[]{:S(2)}) collective-permute-start(bf16[32,2560]{1,0:T(8,128)(2,1)} %param.2), channel_id=1, source_target_pairs={{0,3},{1,0},{2,1},{3,2},{4,7},{5,4},{6,5},{7,6},{8,11},{9,8},{10,9... | collective-permute-start | bytes 491528 | tf_op jit(solution)/shard_map/ppermute | solution.py:15
  19.1 73.1 %collective-permute-start.9 = (bf16[32,2,1664]{2,0,1:T(8,128)(2,1)S(1)}, bf16[32,2,1664]{2,0,1:T(8,128)(2,1)S(1)}, u32[]{:S(2)}, u32[]{:S(2)}) collective-permute-start(bf16[32,2,1664]{2,0,1:T(8,128)(2,1)S(1)} %get-tuple-element.12), channel_id=1, source_target_pairs={{12,8},{13,9},{14,10},{15,11},{28,24},{29,25},{30,26},{31,27}} | collective-permute-start | bytes 638984 | tf_op jit(solution)/shard_map/down/ppermute | solution.py:34
  19.8 98.3 %collective-permute-start.3 = (bf16[32,2,1664]{2,0,1:T(8,128)(2,1)S(1)}, bf16[32,2,1664]{2,0,1:T(8,128)(2,1)S(1)}, u32[]{:S(2)}, u32[]{:S(2)}) collective-permute-start(bf16[32,2,1664]{2,0,1:T(8,128)(2,1)S(1)} %get-tuple-element.12), channel_id=1, source_target_pairs={{0,4},{1,5},{2,6},{3,7},{16,20},{17,21},{18,22},{19,23}} | collective-permute-start | bytes 638984 | tf_op jit(solution)/shard_map/up/ppermute | solution.py:28
  50.3 32.9 %collective-permute-start.4 = (bf16[32,2,1664]{2,0,1:T(8,128)(2,1)S(1)}, bf16[32,2,1664]{2,0,1:T(8,128)(2,1)S(1)}, u32[]{:S(2)}, u32[]{:S(2)}) collective-permute-start(bf16[32,2,1664]{2,0,1:T(8,128)(2,1)S(1)} %get-tuple-element.11), channel_id=1, source_target_pairs={{0,4},{1,5},{2,6},{3,7},{16,20},{17,21},{18,22},{19,23}} | collective-permute-start | bytes 638984 | tf_op jit(solution)/shard_map/up/ppermute | solution.py:28
  51.8 12.9 %collective-permute-start.15 = (bf16[32,2,1664]{2,0,1:T(8,128)(2,1)S(1)}, bf16[32,2,1664]{2,0,1:T(8,128)(2,1)S(1)}, u32[]{:S(2)}, u32[]{:S(2)}) collective-permute-start(bf16[32,2,1664]{2,0,1:T(8,128)(2,1)S(1)} %get-tuple-element.17), channel_id=1, source_target_pairs={{0,4},{1,5},{2,6},{3,7},{16,20},{17,21},{18,22},{19,23}} | collective-permute-start | bytes 638984 | tf_op jit(solution)/shard_map/up/ppermute | solution.py:28
  55.9 13.3 %collective-permute-start.20 = (bf16[32,2,1664]{2,0,1:T(8,128)(2,1)S(1)}, bf16[32,2,1664]{2,0,1:T(8,128)(2,1)S(1)}, u32[]{:S(2)}, u32[]{:S(2)}) collective-permute-start(bf16[32,2,1664]{2,0,1:T(8,128)(2,1)S(1)} %get-tuple-element.18), channel_id=1, source_target_pairs={{12,8},{13,9},{14,10},{15,11},{28,24},{29,25},{30,26},{31,27}} | collective-permute-start | bytes 638984 | tf_op jit(solution)/shard_map/down/ppermute | solution.py:34
  64.7 8.9 %collective-permute-start.25 = (bf16[32,2,1664]{2,0,1:T(8,128)(2,1)S(1)}, bf16[32,2,1664]{2,0,1:T(8,128)(2,1)S(1)}, u32[]{:S(2)}, u32[]{:S(2)}) collective-permute-start(bf16[32,2,1664]{2,0,1:T(8,128)(2,1)S(1)} %get-tuple-element.25), channel_id=1, source_target_pairs={{0,4},{1,5},{2,6},{3,7},{16,20},{17,21},{18,22},{19,23}} | collective-permute-start | bytes 638984 | tf_op jit(solution)/shard_map/up/ppermute | solution.py:28
  69.1 8.9 %collective-permute-start.30 = (bf16[32,2,1664]{2,0,1:T(8,128)(2,1)S(1)}, bf16[32,2,1664]{2,0,1:T(8,128)(2,1)S(1)}, u32[]{:S(2)}, u32[]{:S(2)}) collective-permute-start(bf16[32,2,1664]{2,0,1:T(8,128)(2,1)S(1)} %get-tuple-element.26), channel_id=1, source_target_pairs={{12,8},{13,9},{14,10},{15,11},{28,24},{29,25},{30,26},{31,27}} | collective-permute-start | bytes 638984 | tf_op jit(solution)/shard_map/down/ppermute | solution.py:34
  73.6 8.0 %collective-permute-start.35 = (bf16[32,2,1664]{2,0,1:T(8,128)(2,1)S(1)}, bf16[32,2,1664]{2,0,1:T(8,128)(2,1)S(1)}, u32[]{:S(2)}, u32[]{:S(2)}) collective-permute-start(bf16[32,2,1664]{2,0,1:T(8,128)(2,1)S(1)} %get-tuple-element.33), channel_id=1, source_target_pairs={{0,4},{1,5},{2,6},{3,7},{16,20},{17,21},{18,22},{19,23}} | collective-permute-start | bytes 638984 | tf_op jit(solution)/shard_map/up/ppermute | solution.py:28
  81.7 11.3 %collective-permute-start.11 = (bf16[32,2,1664]{2,0,1:T(8,128)(2,1)S(1)}, bf16[32,2,1664]{2,0,1:T(8,128)(2,1)S(1)}, u32[]{:S(2)}, u32[]{:S(2)}) collective-permute-start(bf16[32,2,1664]{2,0,1:T(8,128)(2,1)S(1)} %get-tuple-element.8), channel_id=1, source_target_pairs={{8,4},{9,5},{10,6},{11,7},{24,20},{25,21},{26,22},{27,23}} | collective-permute-start | bytes 638984 | tf_op jit(solution)/shard_map/down/ppermute | solution.py:37
  82.3 11.3 %collective-permute-start.6 = (bf16[32,2,1664]{2,0,1:T(8,128)(2,1)S(1)}, bf16[32,2,1664]{2,0,1:T(8,128)(2,1)S(1)}, u32[]{:S(2)}, u32[]{:S(2)}) collective-permute-start(bf16[32,2,1664]{2,0,1:T(8,128)(2,1)S(1)} %get-tuple-element.7), channel_id=1, source_target_pairs={{4,8},{5,9},{6,10},{7,11},{20,24},{21,25},{22,26},{23,27}} | collective-permute-start | bytes 638984 | tf_op jit(solution)/shard_map/up/ppermute | solution.py:31
  83.1 12.3 %collective-permute-start.14 = (bf16[32,2,1664]{2,0,1:T(8,128)(2,1)S(1)}, bf16[32,2,1664]{2,0,1:T(8,128)(2,1)S(1)}, u32[]{:S(2)}, u32[]{:S(2)}) collective-permute-start(bf16[32,2,1664]{2,0,1:T(8,128)(2,1)S(1)} %get-tuple-element.19), channel_id=1, source_target_pairs={{0,4},{1,5},{2,6},{3,7},{16,20},{17,21},{18,22},{19,23}} | collective-permute-start | bytes 638984 | tf_op jit(solution)/shard_map/up/ppermute | solution.py:28
  92.3 7.5 %collective-permute-start.19 = (bf16[32,2,1664]{2,0,1:T(8,128)(2,1)S(1)}, bf16[32,2,1664]{2,0,1:T(8,128)(2,1)S(1)}, u32[]{:S(2)}, u32[]{:S(2)}) collective-permute-start(bf16[32,2,1664]{2,0,1:T(8,128)(2,1)S(1)} %get-tuple-element.20), channel_id=1, source_target_pairs={{12,8},{13,9},{14,10},{15,11},{28,24},{29,25},{30,26},{31,27}} | collective-permute-start | bytes 638984 | tf_op jit(solution)/shard_map/down/ppermute | solution.py:34
  95.4 7.7 %collective-permute-start.24 = (bf16[32,2,1664]{2,0,1:T(8,128)(2,1)S(1)}, bf16[32,2,1664]{2,0,1:T(8,128)(2,1)S(1)}, u32[]{:S(2)}, u32[]{:S(2)}) collective-permute-start(bf16[32,2,1664]{2,0,1:T(8,128)(2,1)S(1)} %get-tuple-element.27), channel_id=1, source_target_pairs={{0,4},{1,5},{2,6},{3,7},{16,20},{17,21},{18,22},{19,23}} | collective-permute-start | bytes 638984 | tf_op jit(solution)/shard_map/up/ppermute | solution.py:28
  99.8 7.7 %collective-permute-start.29 = (bf16[32,2,1664]{2,0,1:T(8,128)(2,1)S(1)}, bf16[32,2,1664]{2,0,1:T(8,128)(2,1)S(1)}, u32[]{:S(2)}, u32[]{:S(2)}) collective-permute-start(bf16[32,2,1664]{2,0,1:T(8,128)(2,1)S(1)} %get-tuple-element.28), channel_id=1, source_target_pairs={{12,8},{13,9},{14,10},{15,11},{28,24},{29,25},{30,26},{31,27}} | collective-permute-start | bytes 638984 | tf_op jit(solution)/shard_map/down/ppermute | solution.py:34
  100.5 7.7 %collective-permute-start.26 = (bf16[32,2,1664]{2,0,1:T(8,128)(2,1)S(1)}, bf16[32,2,1664]{2,0,1:T(8,128)(2,1)S(1)}, u32[]{:S(2)}, u32[]{:S(2)}) collective-permute-start(bf16[32,2,1664]{2,0,1:T(8,128)(2,1)S(1)} %get-tuple-element.23), channel_id=1, source_target_pairs={{4,8},{5,9},{6,10},{7,11},{20,24},{21,25},{22,26},{23,27}} | collective-permute-start | bytes 638984 | tf_op jit(solution)/shard_map/up/ppermute | solution.py:31
  101.2 7.7 %collective-permute-start.31 = (bf16[32,2,1664]{2,0,1:T(8,128)(2,1)S(1)}, bf16[32,2,1664]{2,0,1:T(8,128)(2,1)S(1)}, u32[]{:S(2)}, u32[]{:S(2)}) collective-permute-start(bf16[32,2,1664]{2,0,1:T(8,128)(2,1)S(1)} %get-tuple-element.24), channel_id=1, source_target_pairs={{8,4},{9,5},{10,6},{11,7},{24,20},{25,21},{26,22},{27,23}} | collective-permute-start | bytes 638984 | tf_op jit(solution)/shard_map/down/ppermute | solution.py:37
  103.1 7.7 %collective-permute-start.34 = (bf16[32,2,1664]{2,0,1:T(8,128)(2,1)S(1)}, bf16[32,2,1664]{2,0,1:T(8,128)(2,1)S(1)}, u32[]{:S(2)}, u32[]{:S(2)}) collective-permute-start(bf16[32,2,1664]{2,0,1:T(8,128)(2,1)S(1)} %get-tuple-element.35), channel_id=1, source_target_pairs={{0,4},{1,5},{2,6},{3,7},{16,20},{17,21},{18,22},{19,23}} | collective-permute-start | bytes 638984 | tf_op jit(solution)/shard_map/up/ppermute | solution.py:28
  108.2 7.7 %collective-permute-start.36 = (bf16[32,2,1664]{2,0,1:T(8,128)(2,1)S(1)}, bf16[32,2,1664]{2,0,1:T(8,128)(2,1)S(1)}, u32[]{:S(2)}, u32[]{:S(2)}) collective-permute-start(bf16[32,2,1664]{2,0,1:T(8,128)(2,1)S(1)} %get-tuple-element.31), channel_id=1, source_target_pairs={{4,8},{5,9},{6,10},{7,11},{20,24},{21,25},{22,26},{23,27}} | collective-permute-start | bytes 638984 | tf_op jit(solution)/shard_map/up/ppermute | solution.py:31
  108.9 8.3 %collective-permute-start.41 = (bf16[32,2,1664]{2,0,1:T(8,128)(2,1)S(1)}, bf16[32,2,1664]{2,0,1:T(8,128)(2,1)S(1)}, u32[]{:S(2)}, u32[]{:S(2)}) collective-permute-start(bf16[32,2,1664]{2,0,1:T(8,128)(2,1)S(1)} %get-tuple-element.32), channel_id=1, source_target_pairs={{8,4},{9,5},{10,6},{11,7},{24,20},{25,21},{26,22},{27,23}} | collective-permute-start | bytes 638984 | tf_op jit(solution)/shard_map/down/ppermute | solution.py:37
  110.9 8.0 %collective-permute-start.8 = (bf16[32,2,1664]{2,0,1:T(8,128)(2,1)S(1)}, bf16[32,2,1664]{2,0,1:T(8,128)(2,1)S(1)}, u32[]{:S(2)}, u32[]{:S(2)}) collective-permute-start(bf16[32,2,1664]{2,0,1:T(8,128)(2,1)S(1)} %get-tuple-element.11), channel_id=1, source_target_pairs={{12,8},{13,9},{14,10},{15,11},{28,24},{29,25},{30,26},{31,27}} | collective-permute-start | bytes 638984 | tf_op jit(solution)/shard_map/down/ppermute | solution.py:34
  111.5 15.4 %collective-permute-start.13 = (bf16[32,2,1664]{2,0,1:T(8,128)(2,1)S(1)}, bf16[32,2,1664]{2,0,1:T(8,128)(2,1)S(1)}, u32[]{:S(2)}, u32[]{:S(2)}) collective-permute-start(bf16[32,2,1664]{2,0,1:T(8,128)(2,1)S(1)} %get-tuple-element.20), channel_id=1, source_target_pairs={{0,4},{1,5},{2,6},{3,7},{16,20},{17,21},{18,22},{19,23}} | collective-permute-start | bytes 638984 | tf_op jit(solution)/shard_map/up/ppermute | solution.py:28
  116.0 8.8 %collective-permute-start.12 = (bf16[32,2,1664]{2,0,1:T(8,128)(2,1)S(1)}, bf16[32,2,1664]{2,0,1:T(8,128)(2,1)S(1)}, u32[]{:S(2)}, u32[]{:S(2)}) collective-permute-start(bf16[32,2,1664]{2,0,1:T(8,128)(2,1)S(1)} %get-tuple-element.6), channel_id=1, source_target_pairs={{4,0},{8,4},{5,1},{9,5},{6,2},{10,6},{7,3},{11,7},{20,16},{24,20},... | collective-permute-start | bytes 638984 | tf_op jit(solution)/shard_map/down/ppermute | solution.py:37
  117.3 8.1 %collective-permute-start.7 = (bf16[32,2,1664]{2,0,1:T(8,128)(2,1)S(1)}, bf16[32,2,1664]{2,0,1:T(8,128)(2,1)S(1)}, u32[]{:S(2)}, u32[]{:S(2)}) collective-permute-start(bf16[32,2,1664]{2,0,1:T(8,128)(2,1)S(1)} %get-tuple-element.5), channel_id=1, source_target_pairs={{4,8},{8,12},{5,9},{9,13},{6,10},{10,14},{7,11},{11,15},{20,24},{2... | collective-permute-start | bytes 638984 | tf_op jit(solution)/shard_map/up/ppermute | solution.py:31
  118.1 9.5 %collective-permute-start.18 = (bf16[32,2,1664]{2,0,1:T(8,128)(2,1)S(1)}, bf16[32,2,1664]{2,0,1:T(8,128)(2,1)S(1)}, u32[]{:S(2)}, u32[]{:S(2)}) collective-permute-start(bf16[32,2,1664]{2,0,1:T(8,128)(2,1)S(1)} %get-tuple-element.19), channel_id=1, source_target_pairs={{12,8},{13,9},{14,10},{15,11},{28,24},{29,25},{30,26},{31,27}} | collective-permute-start | bytes 638984 | tf_op jit(solution)/shard_map/down/ppermute | solution.py:34
  118.8 15.8 %collective-permute-start.23 = (bf16[32,2,1664]{2,0,1:T(8,128)(2,1)S(1)}, bf16[32,2,1664]{2,0,1:T(8,128)(2,1)S(1)}, u32[]{:S(2)}, u32[]{:S(2)}) collective-permute-start(bf16[32,2,1664]{2,0,1:T(8,128)(2,1)S(1)} %get-tuple-element.28), channel_id=1, source_target_pairs={{0,4},{1,5},{2,6},{3,7},{16,20},{17,21},{18,22},{19,23}} | collective-permute-start | bytes 638984 | tf_op jit(solution)/shard_map/up/ppermute | solution.py:28
  125.4 7.7 %collective-permute-start.22 = (bf16[32,2,1664]{2,0,1:T(8,128)(2,1)S(1)}, bf16[32,2,1664]{2,0,1:T(8,128)(2,1)S(1)}, u32[]{:S(2)}, u32[]{:S(2)}) collective-permute-start(bf16[32,2,1664]{2,0,1:T(8,128)(2,1)S(1)} %get-tuple-element.14), channel_id=1, source_target_pairs={{4,0},{8,4},{5,1},{9,5},{6,2},{10,6},{7,3},{11,7},{20,16},{24,20},... | collective-permute-start | bytes 638984 | tf_op jit(solution)/shard_map/down/ppermute | solution.py:37
  126.9 8.4 %collective-permute-start.28 = (bf16[32,2,1664]{2,0,1:T(8,128)(2,1)S(1)}, bf16[32,2,1664]{2,0,1:T(8,128)(2,1)S(1)}, u32[]{:S(2)}, u32[]{:S(2)}) collective-permute-start(bf16[32,2,1664]{2,0,1:T(8,128)(2,1)S(1)} %get-tuple-element.27), channel_id=1, source_target_pairs={{12,8},{13,9},{14,10},{15,11},{28,24},{29,25},{30,26},{31,27}} | collective-permute-start | bytes 638984 | tf_op jit(solution)/shard_map/down/ppermute | solution.py:34
  127.6 13.9 %collective-permute-start.33 = (bf16[32,2,1664]{2,0,1:T(8,128)(2,1)S(1)}, bf16[32,2,1664]{2,0,1:T(8,128)(2,1)S(1)}, u32[]{:S(2)}, u32[]{:S(2)}) collective-permute-start(bf16[32,2,1664]{2,0,1:T(8,128)(2,1)S(1)} %get-tuple-element.36), channel_id=1, source_target_pairs={{0,4},{1,5},{2,6},{3,7},{16,20},{17,21},{18,22},{19,23}} | collective-permute-start | bytes 638984 | tf_op jit(solution)/shard_map/up/ppermute | solution.py:28
  133.2 8.2 %collective-permute-start.32 = (bf16[32,2,1664]{2,0,1:T(8,128)(2,1)S(1)}, bf16[32,2,1664]{2,0,1:T(8,128)(2,1)S(1)}, u32[]{:S(2)}, u32[]{:S(2)}) collective-permute-start(bf16[32,2,1664]{2,0,1:T(8,128)(2,1)S(1)} %get-tuple-element.22), channel_id=1, source_target_pairs={{4,0},{8,4},{5,1},{9,5},{6,2},{10,6},{7,3},{11,7},{20,16},{24,20},... | collective-permute-start | bytes 638984 | tf_op jit(solution)/shard_map/down/ppermute | solution.py:37
  136.1 12.4 %collective-permute-start.42 = (bf16[32,2,1664]{2,0,1:T(8,128)(2,1)S(1)}, bf16[32,2,1664]{2,0,1:T(8,128)(2,1)S(1)}, u32[]{:S(2)}, u32[]{:S(2)}) collective-permute-start(bf16[32,2,1664]{2,0,1:T(8,128)(2,1)S(1)} %get-tuple-element.30), channel_id=1, source_target_pairs={{4,0},{8,4},{5,1},{9,5},{6,2},{10,6},{7,3},{11,7},{20,16},{24,20},... | collective-permute-start | bytes 638984 | tf_op jit(solution)/shard_map/down/ppermute | solution.py:37
  (11 other events, 64.8 us)

commit v2 on v1

--- a/solution.py
+++ b/solution.py
@@ -41,7 +41,7 @@
 
 def on_device(tokens, gate_up, n, m):
     p = lax.axis_index("row")
-    gathered = gather_cols(tokens, m)
+    gathered = lax.all_gather(tokens, "col", axis=0, tiled=True)
     t = gathered.shape[0]
     tb = t // n
     f = gate_up.shape[2]
@@ -53,11 +53,7 @@
     for i in range(k):
         w = gate_up[:, :, edges[i] : edges[i + 1]]
         part = jnp.einsum("td,gdf->tgf", gathered, w, preferred_element_type=jnp.float32).astype(jnp.bfloat16)
-        part = part.reshape(n, tb, 2, edges[i + 1] - edges[i])
-        own = lax.dynamic_index_in_dim(part, p, 0, keepdims=False).astype(jnp.float32)
-        if n > 1:
-            plus, minus = line_reduce(part, n, p)
-            own = own + plus.astype(jnp.float32) + minus.astype(jnp.float32)
+        own = lax.psum_scatter(part, "row", scatter_dimension=0, tiled=True).astype(jnp.float32)
         outs.append((jax.nn.silu(own[:, 0]) * own[:, 1]).astype(jnp.bfloat16))
     return jnp.concatenate(outs, axis=1)
 

time: 150 us -> 136 us (0.907)
  starting transfers between devices: 74.6 us -> 0.13 us
  waiting for transfers between devices: 36.9 us -> 71.3 us
  between operations: 0.8 us -> 13.2 us
  blocking collectives: 0 us -> 9.56 us
  matrix products: 33.1 us -> 36.9 us
  other arithmetic: 2.7 us -> 4.9 us
    ppermute x43 -> x0, starting transfers between devices: 74.6 us -> none  [the longest x12 48.9 us: line_reduce(): origin = [lax.ppermute(part[n - r], 'row', [(0, 1)]) for r in range(1, n)]]
    reduce_scatter x0 -> x4, waiting for transfers between devices: none -> 71.2 us  [on_device(): lax.psum_scatter(part, 'row', scatter_dimension=0, tiled=True)]
    ppermute x43 -> x0, waiting for transfers between devices: 36.9 us -> none  [the longest x12 20.4 us: line_reduce(): origin = [lax.ppermute(part[n - r], 'row', [(0, 1)]) for r in range(1, n)]]
    all_gather x0 -> x1, blocking collectives: none -> 9.56 us  [on_device(): gathered = lax.all_gather(tokens, 'col', axis=0, tiled=True)]
    dot_general x4, matrix products: 33.1 us -> 36.9 us  [on_device(): jnp.einsum('td,gdf->tgf', gathered, w, preferred_element_type=jnp.float32)]
    convert_element_type x8 -> x4, other arithmetic: 1.13 us -> 3.85 us  [on_device(): lax.psum_scatter(part, 'row', scatter_dimension=0, tiled=True)]
  transfers between devices with their start and end apart: 43 -> 4, of which waited for: 13 -> 3; matrix products, arithmetic and copies ran while one was open for 19% -> 23% of each run, Pallas kernels for 0% -> 0%
where the time goes in v2:
time: 136 us
  waiting for transfers between devices  71.3 us (52%)
  matrix products  36.9 us (27%)
  between operations  13.2 us (10%)
  blocking collectives  9.56 us (7%)
  other arithmetic  4.9 us (4%)
    reduce_scatter x4, waiting for transfers between devices, on_device(): lax.psum_scatter(part, 'row', scatter_dimension=0, tiled=True)  71.2 us
    dot_general x4, matrix products, on_device(): jnp.einsum('td,gdf->tgf', gathered, w, preferred_element_type=jnp.float32)  36.9 us
    all_gather x1, blocking collectives, on_device(): gathered = lax.all_gather(tokens, 'col', axis=0, tiled=True)  9.56 us
    convert_element_type x4, other arithmetic, on_device(): lax.psum_scatter(part, 'row', scatter_dimension=0, tiled=True)  3.85 us
  transfers between devices with their start and end apart: 4, of which 3 were waited for; matrix products, arithmetic and copies ran while one was open for 23% of the time, Pallas kernels for 0%

profile of v2, /device:TPU:0, one launch (start us, length us, event | category | flops | bytes accessed | tf_op | source)
XLA Modules:
  0.0 135.9 jit_solution(6800542610575264821)
XLA Ops:
  6.5 0.0 reduce-scatter.7.cloned.1.call-start
  6.5 9.6 %all_gather.3 = bf16[128,2560]{1,0:T(8,128)(2,1)S(1)} all-gather(bf16[32,2560]{1,0:T(8,128)(2,1)} %param.2), channel_id=1, replica_groups=mesh['grp'=2,'row'=4,'col'=4] {'col'}, dimensions={0}, use_global_device_ids=true | all-gather | bytes 819200 | tf_op jit(solution)/shard_map/all_gather | solution.py:44
  16.1 9.2 %fusion.11 = bf16[128,2,1664]{2,0,1:T(8,128)(2,1)} fusion(bf16[2,2560,6656]{2,1,0:T(8,128)(2,1)} %param.3, bf16[128,2560]{1,0:T(8,128)(2,1)S(1)} %all_gather.3), kind=kOutput, calls=%fused_computation.9 | convolution fusion | flops 2181464064 | bytes 18546688 | tf_op jit(solution)/shard_map/td,gdf->tgf/dot_general | solution.py:55
  25.3 0.0 reduce-scatter.7.cloned.1.call-update
  25.4 0.0 reduce-scatter.9.cloned.1.call-start
  25.4 9.2 %fusion.14 = bf16[128,2,1664]{2,0,1:T(8,128)(2,1)} fusion(bf16[2,2560,6656]{2,1,0:T(8,128)(2,1)} %param.3, bf16[128,2560]{1,0:T(8,128)(2,1)S(1)} %all_gather.3), kind=kOutput, calls=%fused_computation.10 | convolution fusion | flops 2181464064 | bytes 18546688 | tf_op jit(solution)/shard_map/td,gdf->tgf/dot_general | solution.py:55
  34.6 0.0 reduce-scatter.9.cloned.1.call-update
  34.7 0.0 reduce-scatter.5.cloned.1.call-start
  34.7 9.2 %fusion.8 = bf16[128,2,1664]{2,0,1:T(8,128)(2,1)} fusion(bf16[2,2560,6656]{2,1,0:T(8,128)(2,1)} %param.3, bf16[128,2560]{1,0:T(8,128)(2,1)S(1)} %all_gather.3), kind=kOutput, calls=%fused_computation.8 | convolution fusion | flops 2181464064 | bytes 18546688 | tf_op jit(solution)/shard_map/td,gdf->tgf/dot_general | solution.py:55
  43.9 0.0 reduce-scatter.5.cloned.1.call-update
  43.9 0.0 reduce-scatter.11.cloned.1.call-start
  44.0 9.2 %fusion.17 = bf16[128,2,1664]{2,0,1:T(8,128)(2,1)} fusion(bf16[2,2560,6656]{2,1,0:T(8,128)(2,1)} %param.3, bf16[128,2560]{1,0:T(8,128)(2,1)S(1)} %all_gather.3), kind=kOutput, calls=%fused_computation.11 | convolution fusion | flops 2181464064 | bytes 18546688 | tf_op jit(solution)/shard_map/td,gdf->tgf/dot_general | solution.py:55
  53.2 0.0 reduce-scatter.11.cloned.1.call-update
  53.2 0.0 reduce-scatter.7.cloned.1.call-done
  53.2 1.0 convert_element_type.40
  54.2 22.1 %reduce-scatter.9.cloned.1.call-done = bf16[32,2,1664]{2,0,1:T(8,128)(2,1)} async-done(((bf16[128,2,1664]{2,0,1:T(8,128)(2,1)}), bf16[32,2,1664]{2,0,1:T(8,128)(2,1)}) %reduce-scatter.9.cloned.1.call-update) | async-done | bytes 213008 | tf_op jit(solution)/shard_map/reduce_scatter | solution.py:56
  76.3 1.0 convert_element_type.43
  77.2 24.8 %reduce-scatter.5.cloned.1.call-done = bf16[32,2,1664]{2,0,1:T(8,128)(2,1)} async-done(((bf16[128,2,1664]{2,0,1:T(8,128)(2,1)}), bf16[32,2,1664]{2,0,1:T(8,128)(2,1)}) %reduce-scatter.5.cloned.1.call-update) | async-done | bytes 213008 | tf_op jit(solution)/shard_map/reduce_scatter | solution.py:56
  102.0 1.0 convert_element_type.37
  103.0 0.1 fusion.29
  103.0 0.1 fusion.27
  103.1 0.1 fusion.31
  103.2 24.4 %reduce-scatter.11.cloned.1.call-done = bf16[32,2,1664]{2,0,1:T(8,128)(2,1)} async-done(((bf16[128,2,1664]{2,0,1:T(8,128)(2,1)}), bf16[32,2,1664]{2,0,1:T(8,128)(2,1)}) %reduce-scatter.11.cloned.1.call-update) | async-done | bytes 213008 | tf_op jit(solution)/shard_map/reduce_scatter | solution.py:56
  127.6 1.0 convert_element_type.46
  128.6 0.1 fusion.25
  128.6 0.8 pad_maximum_fusion
Async XLA Ops:
  6.5 46.7 %reduce-scatter.7.cloned.1.call-start = ((), (), s32[]{:S(2)}) async-start(), calls=%async_computation.5 | async-start | bytes 1064960 | tf_op jit(solution)/shard_map/reduce_scatter | solution.py:56
  25.4 50.9 %reduce-scatter.9.cloned.1.call-start = ((), (), s32[]{:S(2)}) async-start(), calls=%async_computation.6 | async-start | bytes 1064960 | tf_op jit(solution)/shard_map/reduce_scatter | solution.py:56
  34.7 67.3 %reduce-scatter.5.cloned.1.call-start = ((), (), s32[]{:S(2)}) async-start(), calls=%async_computation.4 | async-start | bytes 1064960 | tf_op jit(solution)/shard_map/reduce_scatter | solution.py:56
  43.9 83.7 %reduce-scatter.11.cloned.1.call-start = ((), (), s32[]{:S(2)}) async-start(), calls=%async_computation.7 | async-start | bytes 1064960 | tf_op jit(solution)/shard_map/reduce_scatter | solution.py:56
Sparse Core Ops, SparseCore 0:
  25.5 25.0 reduce-scatter.6
  52.9 23.3 reduce-scatter.8
  78.6 23.3 reduce-scatter.4
  104.2 23.3 reduce-scatter.10

commit v3 on v1

--- a/solution.py
+++ b/solution.py
@@ -3,7 +3,7 @@
 from jax import lax
 from jax.sharding import PartitionSpec as P
 
-CHUNKS = 4
+CHUNKS = 1
 
 
 def gather_cols(tokens, m):

time: 150 us -> 118 us (0.79)
  the two profiles are of different devices: /device:TPU:0 before, /device:TPU:14 now
where the time goes in v3:
time: 118 us
  waiting for transfers between devices  57.1 us (48%)
  matrix products  24.1 us (20%)
  starting transfers between devices  22.4 us (19%)
  other arithmetic  10.2 us (9%)
  local copies, waits for them, and re-layouts  3.67 us (3%)
    ppermute x3, waiting for transfers between devices, line_reduce(): origin = [lax.ppermute(part[n - r], 'row', [(0, 1)]) for r in range(1, n)]  24.3 us
    dot_general x1, matrix products, on_device(): jnp.einsum('td,gdf->tgf', gathered, w, preferred_element_type=jnp.float32)  24.1 us
    ppermute x2, waiting for transfers between devices, line_reduce(): lax.ppermute(add(block(p + n - r), plus), 'row', [(q, q + 1) for q in ran...  15.9 us
    ppermute x2, waiting for transfers between devices, line_reduce(): lax.ppermute(add(block(p - n + r), minus), 'row', [(q, q - 1) for q in ra...  10.1 us
    ppermute x2, starting transfers between devices, line_reduce(): lax.ppermute(add(block(p + n - r), plus), 'row', [(q, q + 1) for q in ran...  8.39 us
    ppermute x3, waiting for transfers between devices, gather_cols(): got = lax.ppermute(tokens, 'col', [(i, (i + s) % m) for i in range(m)])  6.88 us
    convert_element_type x2, other arithmetic, add(): return (a.astype(jnp.float32) + b.astype(jnp.float32)).astype(jnp.bfloat16)  6.84 us
    ppermute x3, starting transfers between devices, line_reduce(): lax.ppermute(part[r - 1], 'row', [(n - 1, n - 2)])  4.74 us
  transfers between devices with their start and end apart: 13, of which 9 were waited for; matrix products, arithmetic and copies ran while one was open for 7% of the time, Pallas kernels for 0%

profile of v3, /device:TPU:14, one launch (start us, length us, event | category | flops | bytes accessed | tf_op | source)
XLA Modules:
  0.0 117.7 jit_solution(7370619415255110934)
XLA Ops:
  0.0 0.0 collective-permute-start
  0.0 1.7 %collective-permute-start.2 = (bf16[32,2560]{1,0:T(8,128)(2,1)}, bf16[32,2560]{1,0:T(8,128)(2,1)S(1)}, u32[]{:S(2)}, u32[]{:S(2)}) collective-permute-start(bf16[32,2560]{1,0:T(8,128)(2,1)} %param.2), channel_id=1, source_target_pairs={{0,3},{1,0},{2,1},{3,2},{4,7},{5,4},{6,5},{7,6},{8,11},{9,8},{10,9... | collective-permute-start | bytes 491528 | tf_op jit(solution)/shard_map/ppermute | solution.py:15
  1.7 0.5 collective-permute-start.1
  2.3 1.0 bitcast_dynamic-update-slice_fusion.3
  3.3 2.5 %collective-permute-done = bf16[32,2560]{1,0:T(8,128)(2,1)S(1)} collective-permute-done((bf16[32,2560]{1,0:T(8,128)(2,1)}, bf16[32,2560]{1,0:T(8,128)(2,1)S(1)}, u32[]{:S(2)}, u32[]{:S(2)}) %collective-permute-start) | collective-permute-done | bytes 163872 | tf_op jit(solution)/shard_map/ppermute | solution.py:15
  5.9 4.3 %collective-permute-done.1 = bf16[32,2560]{1,0:T(8,128)(2,1)S(1)} collective-permute-done((bf16[32,2560]{1,0:T(8,128)(2,1)}, bf16[32,2560]{1,0:T(8,128)(2,1)S(1)}, u32[]{:S(2)}, u32[]{:S(2)}) %collective-permute-start.1) | collective-permute-done | bytes 163872 | tf_op jit(solution)/shard_map/ppermute | solution.py:15
  10.3 0.8 copy-done
  11.1 24.1 %convolution_convert_fusion = bf16[128,2,6656]{2,0,1:T(8,128)(2,1)S(1)} fusion(bf16[128,2560,1]{1,0,2:T(8,128)(2,1)} %bitcast.52, bf16[2,2560,6656]{2,1,0:T(8,128)(2,1)} %param.3), kind=kOutput, calls=%fused_computation | convolution fusion | flops 8725856256 | bytes 72220672 | tf_op jit(solution)/shard_map/td,gdf->tgf/dot_general | solution.py:55
  35.2 1.8 %fusion.7 = (bf16[32,2,6656]{2,0,1:T(8,128)(2,1)}, bf16[32,2,6656]{2,0,1:T(8,128)(2,1)}, bf16[32,2,6656]{2,0,1:T(8,128)(2,1)}, bf16[32,2,6656]{2,0,1:T(8,128)(2,1)}) fusion(bf16[128,2,6656]{2,0,1:T(8,128)(2,1)S(1)} %convolution_convert_fusion), kind=kLoop, calls=%fused_computation.19 | loop fusion | bytes 6815744 | tf_op jit(solution)/shard_map/up/slice | solution.py:28
  37.0 1.3 %collective-permute-start.5 = (bf16[32,2,6656]{2,0,1:T(8,128)(2,1)}, bf16[32,2,6656]{2,0,1:T(8,128)(2,1)}, u32[]{:S(2)}, u32[]{:S(2)}) collective-permute-start(bf16[32,2,6656]{2,0,1:T(8,128)(2,1)} %get-tuple-element.9), channel_id=1, source_target_pairs={{0,4},{1,5},{2,6},{3,7},{16,20},{17,21},{18,22},{19,23}} | collective-permute-start | bytes 2555912 | tf_op jit(solution)/shard_map/up/ppermute | solution.py:28
  38.3 1.6 %collective-permute-start.10 = (bf16[32,2,6656]{2,0,1:T(8,128)(2,1)}, bf16[32,2,6656]{2,0,1:T(8,128)(2,1)}, u32[]{:S(2)}, u32[]{:S(2)}) collective-permute-start(bf16[32,2,6656]{2,0,1:T(8,128)(2,1)} %get-tuple-element.10), channel_id=1, source_target_pairs={{12,8},{13,9},{14,10},{15,11},{28,24},{29,25},{30,26},{31,27}} | collective-permute-start | bytes 2555912 | tf_op jit(solution)/shard_map/down/ppermute | solution.py:34
  39.9 1.3 %collective-permute-start.4 = (bf16[32,2,6656]{2,0,1:T(8,128)(2,1)}, bf16[32,2,6656]{2,0,1:T(8,128)(2,1)}, u32[]{:S(2)}, u32[]{:S(2)}) collective-permute-start(bf16[32,2,6656]{2,0,1:T(8,128)(2,1)} %get-tuple-element.11), channel_id=1, source_target_pairs={{0,4},{1,5},{2,6},{3,7},{16,20},{17,21},{18,22},{19,23}} | collective-permute-start | bytes 2555912 | tf_op jit(solution)/shard_map/up/ppermute | solution.py:28
  41.1 1.6 %collective-permute-start.9 = (bf16[32,2,6656]{2,0,1:T(8,128)(2,1)}, bf16[32,2,6656]{2,0,1:T(8,128)(2,1)}, u32[]{:S(2)}, u32[]{:S(2)}) collective-permute-start(bf16[32,2,6656]{2,0,1:T(8,128)(2,1)} %get-tuple-element.12), channel_id=1, source_target_pairs={{12,8},{13,9},{14,10},{15,11},{28,24},{29,25},{30,26},{31,27}} | collective-permute-start | bytes 2555912 | tf_op jit(solution)/shard_map/down/ppermute | solution.py:34
  42.7 18.3 %collective-permute-done.5 = bf16[32,2,6656]{2,0,1:T(8,128)(2,1)} collective-permute-done((bf16[32,2,6656]{2,0,1:T(8,128)(2,1)}, bf16[32,2,6656]{2,0,1:T(8,128)(2,1)}, u32[]{:S(2)}, u32[]{:S(2)}) %collective-permute-start.5) | collective-permute-done | bytes 852000 | tf_op jit(solution)/shard_map/up/ppermute | solution.py:28
  61.0 0.0 collective-permute-done.10
  61.0 3.1 %fusion.2 = (bf16[32,2,6656]{2,0,1:T(8,128)(2,1)}, bf16[32,2,6656]{2,0,1:T(8,128)(2,1)}) fusion(bf16[32,2,6656]{2,0,1:T(8,128)(2,1)} %collective-permute-done.5, bf16[4,32,2,6656]{3,1,0,2:T(8,128)(2,1)S(1)} %bitcast.49, s32[]{:T(128)S(6)} %min.14, bf16[32,2,6656]{2,0,1:T(8,128)(2,1)} %collective-permute-done.10, s32[]{:T(128)S(6)} %min.16), kind=kLoop, calls=%fused_computation.6 | loop fusion | flops 3407872 | bytes 5111816 | tf_op jit(solution)/shard_map/up/convert_element_type | solution.py:25
  64.1 6.0 %collective-permute-start.6 = (bf16[32,2,6656]{2,0,1:T(8,128)(2,1)}, bf16[32,2,6656]{2,0,1:T(8,128)(2,1)}, u32[]{:S(2)}, u32[]{:S(2)}) collective-permute-start(bf16[32,2,6656]{2,0,1:T(8,128)(2,1)} %get-tuple-element.7), channel_id=1, source_target_pairs={{4,8},{5,9},{6,10},{7,11},{20,24},{21,25},{22,26},{23,27}} | collective-permute-start | bytes 2555912 | tf_op jit(solution)/shard_map/up/ppermute | solution.py:31
  70.1 1.3 %collective-permute-start.11 = (bf16[32,2,6656]{2,0,1:T(8,128)(2,1)}, bf16[32,2,6656]{2,0,1:T(8,128)(2,1)}, u32[]{:S(2)}, u32[]{:S(2)}) collective-permute-start(bf16[32,2,6656]{2,0,1:T(8,128)(2,1)} %get-tuple-element.8), channel_id=1, source_target_pairs={{8,4},{9,5},{10,6},{11,7},{24,20},{25,21},{26,22},{27,23}} | collective-permute-start | bytes 2555912 | tf_op jit(solution)/shard_map/down/ppermute | solution.py:37
  71.4 1.6 %collective-permute-start.8 = (bf16[32,2,6656]{2,0,1:T(8,128)(2,1)}, bf16[32,2,6656]{2,0,1:T(8,128)(2,1)}, u32[]{:S(2)}, u32[]{:S(2)}) collective-permute-start(bf16[32,2,6656]{2,0,1:T(8,128)(2,1)} %get-tuple-element.11), channel_id=1, source_target_pairs={{12,8},{13,9},{14,10},{15,11},{28,24},{29,25},{30,26},{31,27}} | collective-permute-start | bytes 2555912 | tf_op jit(solution)/shard_map/down/ppermute | solution.py:34
  73.0 4.6 %collective-permute-done.4 = bf16[32,2,6656]{2,0,1:T(8,128)(2,1)} collective-permute-done((bf16[32,2,6656]{2,0,1:T(8,128)(2,1)}, bf16[32,2,6656]{2,0,1:T(8,128)(2,1)}, u32[]{:S(2)}, u32[]{:S(2)}) %collective-permute-start.4) | collective-permute-done | bytes 852000 | tf_op jit(solution)/shard_map/up/ppermute | solution.py:28
  77.6 1.3 %collective-permute-start.3 = (bf16[32,2,6656]{2,0,1:T(8,128)(2,1)}, bf16[32,2,6656]{2,0,1:T(8,128)(2,1)}, u32[]{:S(2)}, u32[]{:S(2)}) collective-permute-start(bf16[32,2,6656]{2,0,1:T(8,128)(2,1)} %get-tuple-element.12), channel_id=1, source_target_pairs={{0,4},{1,5},{2,6},{3,7},{16,20},{17,21},{18,22},{19,23}} | collective-permute-start | bytes 2555912 | tf_op jit(solution)/shard_map/up/ppermute | solution.py:28
  78.9 0.0 collective-permute-done.9
  78.9 5.7 %collective-permute-done.6 = bf16[32,2,6656]{2,0,1:T(8,128)(2,1)} collective-permute-done((bf16[32,2,6656]{2,0,1:T(8,128)(2,1)}, bf16[32,2,6656]{2,0,1:T(8,128)(2,1)}, u32[]{:S(2)}, u32[]{:S(2)}) %collective-permute-start.6) | collective-permute-done | bytes 852000 | tf_op jit(solution)/shard_map/up/ppermute | solution.py:31
  84.6 5.1 %collective-permute-done.11 = bf16[32,2,6656]{2,0,1:T(8,128)(2,1)} collective-permute-done((bf16[32,2,6656]{2,0,1:T(8,128)(2,1)}, bf16[32,2,6656]{2,0,1:T(8,128)(2,1)}, u32[]{:S(2)}, u32[]{:S(2)}) %collective-permute-start.11) | collective-permute-done | bytes 852000 | tf_op jit(solution)/shard_map/down/ppermute | solution.py:37
  89.6 3.8 %fusion.3 = (bf16[32,2,6656]{2,0,1:T(8,128)(2,1)}, bf16[32,2,6656]{2,0,1:T(8,128)(2,1)}) fusion(bf16[32,2,6656]{2,0,1:T(8,128)(2,1)} %collective-permute-done.4, bf16[32,2,6656]{2,0,1:T(8,128)(2,1)} %collective-permute-done.6, bf16[4,32,2,6656]{3,1,0,2:T(8,128)(2,1)S(1)} %bitcast.50, s32[]{:T(128)S(6)} %min.13, ...), kind=kLoop, calls=%fused_computation.8 | loop fusion | flops 4259840 | bytes 6815752 | tf_op jit(solution)/shard_map/up/convert_element_type | solution.py:25
  93.4 2.3 %collective-permute-start.7 = (bf16[32,2,6656]{2,0,1:T(8,128)(2,1)}, bf16[32,2,6656]{2,0,1:T(8,128)(2,1)}, u32[]{:S(2)}, u32[]{:S(2)}) collective-permute-start(bf16[32,2,6656]{2,0,1:T(8,128)(2,1)} %get-tuple-element.5), channel_id=1, source_target_pairs={{4,8},{8,12},{5,9},{9,13},{6,10},{10,14},{7,11},{11,15},{20,24},{2... | collective-permute-start | bytes 2555912 | tf_op jit(solution)/shard_map/up/ppermute | solution.py:31
  95.7 1.9 %collective-permute-start.12 = (bf16[32,2,6656]{2,0,1:T(8,128)(2,1)}, bf16[32,2,6656]{2,0,1:T(8,128)(2,1)}, u32[]{:S(2)}, u32[]{:S(2)}) collective-permute-start(bf16[32,2,6656]{2,0,1:T(8,128)(2,1)} %get-tuple-element.6), channel_id=1, source_target_pairs={{4,0},{8,4},{5,1},{9,5},{6,2},{10,6},{7,3},{11,7},{20,16},{24,20},... | collective-permute-start | bytes 2555912 | tf_op jit(solution)/shard_map/down/ppermute | solution.py:37
  97.7 1.4 %collective-permute-done.3 = bf16[32,2,6656]{2,0,1:T(8,128)(2,1)} collective-permute-done((bf16[32,2,6656]{2,0,1:T(8,128)(2,1)}, bf16[32,2,6656]{2,0,1:T(8,128)(2,1)}, u32[]{:S(2)}, u32[]{:S(2)}) %collective-permute-start.3) | collective-permute-done | bytes 852000 | tf_op jit(solution)/shard_map/up/ppermute | solution.py:28
  99.1 10.2 %collective-permute-done.7 = bf16[32,2,6656]{2,0,1:T(8,128)(2,1)} collective-permute-done((bf16[32,2,6656]{2,0,1:T(8,128)(2,1)}, bf16[32,2,6656]{2,0,1:T(8,128)(2,1)}, u32[]{:S(2)}, u32[]{:S(2)}) %collective-permute-start.7) | collective-permute-done | bytes 852000 | tf_op jit(solution)/shard_map/up/ppermute | solution.py:31
  109.2 5.0 %collective-permute-done.12 = bf16[32,2,6656]{2,0,1:T(8,128)(2,1)} collective-permute-done((bf16[32,2,6656]{2,0,1:T(8,128)(2,1)}, bf16[32,2,6656]{2,0,1:T(8,128)(2,1)}, u32[]{:S(2)}, u32[]{:S(2)}) %collective-permute-start.12) | collective-permute-done | bytes 852000 | tf_op jit(solution)/shard_map/down/ppermute | solution.py:37
  114.2 2.4 %fusion.4 = f32[32,2,6656]{2,0,1:T(8,128)S(1)} fusion(bf16[32,2,6656]{2,0,1:T(8,128)(2,1)} %collective-permute-done.8, bf16[32,2,6656]{2,0,1:T(8,128)(2,1)} %collective-permute-done.12, bf16[32,2,6656]{2,0,1:T(8,128)(2,1)} %collective-permute-done.3, bf16[32,2,6656]{2,0,1:T(8,128)(2,1)} %collective-permute-done.7, bf16[4,32,2,6656]{3,1,0,2:T(8,128)(2,1)S(1)} %bitcast.51, ...), kind=kLoop, calls=%fused_computation.10 | loop fusion | flops 2981888 | bytes 5963780 | tf_op jit(solution)/shard_map/add | solution.py:60
  116.7 1.0 fusion.6
  (7 shorter events, 0.1 us)
Async XLA Ops:
  0.0 5.9 %collective-permute-start = (bf16[32,2560]{1,0:T(8,128)(2,1)}, bf16[32,2560]{1,0:T(8,128)(2,1)S(1)}, u32[]{:S(2)}, u32[]{:S(2)}) collective-permute-start(bf16[32,2560]{1,0:T(8,128)(2,1)} %param.2), channel_id=1, source_target_pairs={{0,1},{1,2},{2,3},{3,0},{4,5},{5,6},{6,7},{7,4},{8,9},{9,10},{10,1... | collective-permute-start | bytes 491528 | tf_op jit(solution)/shard_map/ppermute | solution.py:15
  0.0 10.2 %collective-permute-start.2 = (bf16[32,2560]{1,0:T(8,128)(2,1)}, bf16[32,2560]{1,0:T(8,128)(2,1)S(1)}, u32[]{:S(2)}, u32[]{:S(2)}) collective-permute-start(bf16[32,2560]{1,0:T(8,128)(2,1)} %param.2), channel_id=1, source_target_pairs={{0,3},{1,0},{2,1},{3,2},{4,7},{5,4},{6,5},{7,6},{8,11},{9,8},{10,9... | collective-permute-start | bytes 491528 | tf_op jit(solution)/shard_map/ppermute | solution.py:15
  1.7 8.5 %collective-permute-start.1 = (bf16[32,2560]{1,0:T(8,128)(2,1)}, bf16[32,2560]{1,0:T(8,128)(2,1)S(1)}, u32[]{:S(2)}, u32[]{:S(2)}) collective-permute-start(bf16[32,2560]{1,0:T(8,128)(2,1)} %param.2), channel_id=1, source_target_pairs={{0,2},{1,3},{2,0},{3,1},{4,6},{5,7},{6,4},{7,5},{8,10},{9,11},{10,... | collective-permute-start | bytes 491528 | tf_op jit(solution)/shard_map/ppermute | solution.py:15
  10.3 0.8 copy-start
  37.0 24.0 %collective-permute-start.5 = (bf16[32,2,6656]{2,0,1:T(8,128)(2,1)}, bf16[32,2,6656]{2,0,1:T(8,128)(2,1)}, u32[]{:S(2)}, u32[]{:S(2)}) collective-permute-start(bf16[32,2,6656]{2,0,1:T(8,128)(2,1)} %get-tuple-element.9), channel_id=1, source_target_pairs={{0,4},{1,5},{2,6},{3,7},{16,20},{17,21},{18,22},{19,23}} | collective-permute-start | bytes 2555912 | tf_op jit(solution)/shard_map/up/ppermute | solution.py:28
  38.3 22.7 %collective-permute-start.10 = (bf16[32,2,6656]{2,0,1:T(8,128)(2,1)}, bf16[32,2,6656]{2,0,1:T(8,128)(2,1)}, u32[]{:S(2)}, u32[]{:S(2)}) collective-permute-start(bf16[32,2,6656]{2,0,1:T(8,128)(2,1)} %get-tuple-element.10), channel_id=1, source_target_pairs={{12,8},{13,9},{14,10},{15,11},{28,24},{29,25},{30,26},{31,27}} | collective-permute-start | bytes 2555912 | tf_op jit(solution)/shard_map/down/ppermute | solution.py:34
  39.9 37.7 %collective-permute-start.4 = (bf16[32,2,6656]{2,0,1:T(8,128)(2,1)}, bf16[32,2,6656]{2,0,1:T(8,128)(2,1)}, u32[]{:S(2)}, u32[]{:S(2)}) collective-permute-start(bf16[32,2,6656]{2,0,1:T(8,128)(2,1)} %get-tuple-element.11), channel_id=1, source_target_pairs={{0,4},{1,5},{2,6},{3,7},{16,20},{17,21},{18,22},{19,23}} | collective-permute-start | bytes 2555912 | tf_op jit(solution)/shard_map/up/ppermute | solution.py:28
  41.1 37.7 %collective-permute-start.9 = (bf16[32,2,6656]{2,0,1:T(8,128)(2,1)}, bf16[32,2,6656]{2,0,1:T(8,128)(2,1)}, u32[]{:S(2)}, u32[]{:S(2)}) collective-permute-start(bf16[32,2,6656]{2,0,1:T(8,128)(2,1)} %get-tuple-element.12), channel_id=1, source_target_pairs={{12,8},{13,9},{14,10},{15,11},{28,24},{29,25},{30,26},{31,27}} | collective-permute-start | bytes 2555912 | tf_op jit(solution)/shard_map/down/ppermute | solution.py:34
  64.1 20.5 %collective-permute-start.6 = (bf16[32,2,6656]{2,0,1:T(8,128)(2,1)}, bf16[32,2,6656]{2,0,1:T(8,128)(2,1)}, u32[]{:S(2)}, u32[]{:S(2)}) collective-permute-start(bf16[32,2,6656]{2,0,1:T(8,128)(2,1)} %get-tuple-element.7), channel_id=1, source_target_pairs={{4,8},{5,9},{6,10},{7,11},{20,24},{21,25},{22,26},{23,27}} | collective-permute-start | bytes 2555912 | tf_op jit(solution)/shard_map/up/ppermute | solution.py:31
  70.1 19.5 %collective-permute-start.11 = (bf16[32,2,6656]{2,0,1:T(8,128)(2,1)}, bf16[32,2,6656]{2,0,1:T(8,128)(2,1)}, u32[]{:S(2)}, u32[]{:S(2)}) collective-permute-start(bf16[32,2,6656]{2,0,1:T(8,128)(2,1)} %get-tuple-element.8), channel_id=1, source_target_pairs={{8,4},{9,5},{10,6},{11,7},{24,20},{25,21},{26,22},{27,23}} | collective-permute-start | bytes 2555912 | tf_op jit(solution)/shard_map/down/ppermute | solution.py:37
  71.4 26.3 %collective-permute-start.8 = (bf16[32,2,6656]{2,0,1:T(8,128)(2,1)}, bf16[32,2,6656]{2,0,1:T(8,128)(2,1)}, u32[]{:S(2)}, u32[]{:S(2)}) collective-permute-start(bf16[32,2,6656]{2,0,1:T(8,128)(2,1)} %get-tuple-element.11), channel_id=1, source_target_pairs={{12,8},{13,9},{14,10},{15,11},{28,24},{29,25},{30,26},{31,27}} | collective-permute-start | bytes 2555912 | tf_op jit(solution)/shard_map/down/ppermute | solution.py:34
  77.6 21.5 %collective-permute-start.3 = (bf16[32,2,6656]{2,0,1:T(8,128)(2,1)}, bf16[32,2,6656]{2,0,1:T(8,128)(2,1)}, u32[]{:S(2)}, u32[]{:S(2)}) collective-permute-start(bf16[32,2,6656]{2,0,1:T(8,128)(2,1)} %get-tuple-element.12), channel_id=1, source_target_pairs={{0,4},{1,5},{2,6},{3,7},{16,20},{17,21},{18,22},{19,23}} | collective-permute-start | bytes 2555912 | tf_op jit(solution)/shard_map/up/ppermute | solution.py:28
  93.4 15.8 %collective-permute-start.7 = (bf16[32,2,6656]{2,0,1:T(8,128)(2,1)}, bf16[32,2,6656]{2,0,1:T(8,128)(2,1)}, u32[]{:S(2)}, u32[]{:S(2)}) collective-permute-start(bf16[32,2,6656]{2,0,1:T(8,128)(2,1)} %get-tuple-element.5), channel_id=1, source_target_pairs={{4,8},{8,12},{5,9},{9,13},{6,10},{10,14},{7,11},{11,15},{20,24},{2... | collective-permute-start | bytes 2555912 | tf_op jit(solution)/shard_map/up/ppermute | solution.py:31
  95.7 18.5 %collective-permute-start.12 = (bf16[32,2,6656]{2,0,1:T(8,128)(2,1)}, bf16[32,2,6656]{2,0,1:T(8,128)(2,1)}, u32[]{:S(2)}, u32[]{:S(2)}) collective-permute-start(bf16[32,2,6656]{2,0,1:T(8,128)(2,1)} %get-tuple-element.6), channel_id=1, source_target_pairs={{4,0},{8,4},{5,1},{9,5},{6,2},{10,6},{7,3},{11,7},{20,16},{24,20},... | collective-permute-start | bytes 2555912 | tf_op jit(solution)/shard_map/down/ppermute | solution.py:37

commit v4 on v3

--- a/solution.py
+++ b/solution.py
@@ -3,7 +3,7 @@
 from jax import lax
 from jax.sharding import PartitionSpec as P
 
-CHUNKS = 1
+CHUNKS = 2
 
 
 def gather_cols(tokens, m):
@@ -26,6 +26,7 @@
 
     with jax.named_scope("up"):
         origin = [lax.ppermute(part[n - r], "row", [(0, 1)]) for r in range(1, n)]
+        first = origin[0]
         plus = origin[0]
         for r in range(2, n):
             sent = lax.ppermute(add(block(p + n - r), plus), "row", [(q, q + 1) for q in range(1, r)])
@@ -36,7 +37,7 @@
         for r in range(2, n):
             sent = lax.ppermute(add(block(p - n + r), minus), "row", [(q, q - 1) for q in range(n - r, n - 1)])
             minus = origin[r - 1] + sent
-    return plus, minus
+    return plus, minus, (first, origin[0])
 
 
 def on_device(tokens, gate_up, n, m):
@@ -50,13 +51,15 @@
     edges = [128 * (units * i // k) for i in range(k + 1)]
     edges[-1] = f
     outs = []
+    held = gathered
     for i in range(k):
         w = gate_up[:, :, edges[i] : edges[i + 1]]
-        part = jnp.einsum("td,gdf->tgf", gathered, w, preferred_element_type=jnp.float32).astype(jnp.bfloat16)
+        part = jnp.einsum("td,gdf->tgf", held, w, preferred_element_type=jnp.float32).astype(jnp.bfloat16)
         part = part.reshape(n, tb, 2, edges[i + 1] - edges[i])
         own = lax.dynamic_index_in_dim(part, p, 0, keepdims=False).astype(jnp.float32)
         if n > 1:
-            plus, minus = line_reduce(part, n, p)
+            plus, minus, first = line_reduce(part, n, p)
+            held = lax.optimization_barrier((gathered, first))[0]
             own = own + plus.astype(jnp.float32) + minus.astype(jnp.float32)
         outs.append((jax.nn.silu(own[:, 0]) * own[:, 1]).astype(jnp.bfloat16))
     return jnp.concatenate(outs, axis=1)

time: 118 us -> 110 us (0.932)
  the two profiles are of different devices: /device:TPU:14 before, /device:TPU:0 now
where the time goes in v4:
time: 110 us; the launch traced here: 109 us
  starting transfers between devices  49 us (45%)
  matrix products  26.9 us (24%)
  waiting for transfers between devices  24.9 us (23%)
  other arithmetic  4.77 us (4%)
  local copies, waits for them, and re-layouts  2.97 us (3%)
    ppermute x6, starting transfers between devices, line_reduce(): origin = [lax.ppermute(part[n - r], 'row', [(0, 1)]) for r in range(1, n)]  32.8 us
    dot_general x2, matrix products, on_device(): jnp.einsum('td,gdf->tgf', held, w, preferred_element_type=jnp.float32)  26.9 us
    ppermute x6, waiting for transfers between devices, line_reduce(): origin = [lax.ppermute(part[n - r], 'row', [(0, 1)]) for r in range(1, n)]  11.5 us
    ppermute x4, waiting for transfers between devices, line_reduce(): lax.ppermute(add(block(p - n + r), minus), 'row', [(q, q - 1) for q in ra...  8.04 us
    ppermute x3, waiting for transfers between devices, gather_cols(): got = lax.ppermute(tokens, 'col', [(i, (i + s) % m) for i in range(m)])  5.37 us
    ppermute x6, starting transfers between devices, line_reduce(): lax.ppermute(part[r - 1], 'row', [(n - 1, n - 2)])  4.86 us
    ppermute x3, starting transfers between devices, gather_cols(): got = lax.ppermute(tokens, 'col', [(i, (i + s) % m) for i in range(m)])  4.71 us
    ppermute x4, starting transfers between devices, line_reduce(): lax.ppermute(add(block(p - n + r), minus), 'row', [(q, q - 1) for q in ra...  3.96 us
  transfers between devices with their start and end apart: 23, of which 6 were waited for; matrix products, arithmetic and copies ran while one was open for 17% of the time, Pallas kernels for 0%

profile of v4, /device:TPU:0, one launch (start us, length us, event | category | flops | bytes accessed | tf_op | source)
XLA Modules:
  0.0 109.0 jit_solution(1008385775548677388)
XLA Ops:
  0.5 1.9 %collective-permute-start.2 = (bf16[32,2560]{1,0:T(8,128)(2,1)}, bf16[32,2560]{1,0:T(8,128)(2,1)S(1)}, u32[]{:S(2)}, u32[]{:S(2)}) collective-permute-start(bf16[32,2560]{1,0:T(8,128)(2,1)} %param.2), channel_id=1, source_target_pairs={{0,3},{1,0},{2,1},{3,2},{4,7},{5,4},{6,5},{7,6},{8,11},{9,8},{10,9... | collective-permute-start | bytes 491528 | tf_op jit(solution)/shard_map/ppermute | solution.py:15
  2.4 2.3 %collective-permute-start.1 = (bf16[32,2560]{1,0:T(8,128)(2,1)}, bf16[32,2560]{1,0:T(8,128)(2,1)S(1)}, u32[]{:S(2)}, u32[]{:S(2)}) collective-permute-start(bf16[32,2560]{1,0:T(8,128)(2,1)} %param.2), channel_id=1, source_target_pairs={{0,2},{1,3},{2,0},{3,1},{4,6},{5,7},{6,4},{7,5},{8,10},{9,11},{10,... | collective-permute-start | bytes 491528 | tf_op jit(solution)/shard_map/ppermute | solution.py:15
  4.8 1.0 bitcast_dynamic-update-slice_fusion.3
  5.8 5.4 %collective-permute-done.1 = bf16[32,2560]{1,0:T(8,128)(2,1)S(1)} collective-permute-done((bf16[32,2560]{1,0:T(8,128)(2,1)}, bf16[32,2560]{1,0:T(8,128)(2,1)S(1)}, u32[]{:S(2)}, u32[]{:S(2)}) %collective-permute-start.1) | collective-permute-done | bytes 163872 | tf_op jit(solution)/shard_map/ppermute | solution.py:15
  11.2 13.4 %fusion.4 = bf16[128,2,3328]{2,0,1:T(8,128)(2,1)S(1)} fusion(bf16[128,2560,1]{1,0,2:T(8,128)(2,1)S(1)} %bitcast.93, bf16[2,2560,6656]{2,1,0:T(8,128)(2,1)} %param.3), kind=kOutput, calls=%fused_computation.4 | convolution fusion | flops 4362928128 | bytes 36438016 | tf_op jit(solution)/shard_map/td,gdf->tgf/dot_general | solution.py:57
  24.6 1.0 fusion.25
  26.3 4.0 %collective-permute-start.5 = (bf16[32,2,3328]{2,0,1:T(8,128)(2,1)S(1)}, bf16[32,2,3328]{2,0,1:T(8,128)(2,1)S(1)}, u32[]{:S(2)}, u32[]{:S(2)}) collective-permute-start(bf16[32,2,3328]{2,0,1:T(8,128)(2,1)S(1)} %get-tuple-element.13), channel_id=1, source_target_pairs={{0,4},{1,5},{2,6},{3,7},{16,20},{17,21},{18,22},{19,23}} | collective-permute-start | bytes 1277960 | tf_op jit(solution)/shard_map/up/ppermute | solution.py:28
  30.4 1.4 %collective-permute-start.9 = (bf16[32,2,3328]{2,0,1:T(8,128)(2,1)}, bf16[32,2,3328]{2,0,1:T(8,128)(2,1)}, u32[]{:S(2)}, u32[]{:S(2)}) collective-permute-start(bf16[32,2,3328]{2,0,1:T(8,128)(2,1)} %get-tuple-element.11), channel_id=1, source_target_pairs={{12,8},{13,9},{14,10},{15,11},{28,24},{29,25},{30,26},{31,27}} | collective-permute-start | bytes 1277960 | tf_op jit(solution)/shard_map/down/ppermute | solution.py:35
  31.8 2.1 %collective-permute-start.3 = (bf16[32,2,3328]{2,0,1:T(8,128)(2,1)}, bf16[32,2,3328]{2,0,1:T(8,128)(2,1)}, u32[]{:S(2)}, u32[]{:S(2)}) collective-permute-start(bf16[32,2,3328]{2,0,1:T(8,128)(2,1)} %get-tuple-element.11), channel_id=1, source_target_pairs={{0,4},{1,5},{2,6},{3,7},{16,20},{17,21},{18,22},{19,23}} | collective-permute-start | bytes 1277960 | tf_op jit(solution)/shard_map/up/ppermute | solution.py:28
  33.9 2.0 %collective-permute-start.4 = (bf16[32,2,3328]{2,0,1:T(8,128)(2,1)}, bf16[32,2,3328]{2,0,1:T(8,128)(2,1)}, u32[]{:S(2)}, u32[]{:S(2)}) collective-permute-start(bf16[32,2,3328]{2,0,1:T(8,128)(2,1)} %get-tuple-element.14), channel_id=1, source_target_pairs={{0,4},{1,5},{2,6},{3,7},{16,20},{17,21},{18,22},{19,23}} | collective-permute-start | bytes 1277960 | tf_op jit(solution)/shard_map/up/ppermute | solution.py:28
  35.9 4.6 %collective-permute-done.5 = bf16[32,2,3328]{2,0,1:T(8,128)(2,1)S(1)} collective-permute-done((bf16[32,2,3328]{2,0,1:T(8,128)(2,1)S(1)}, bf16[32,2,3328]{2,0,1:T(8,128)(2,1)S(1)}, u32[]{:S(2)}, u32[]{:S(2)}) %collective-permute-start.5) | collective-permute-done | bytes 426016 | tf_op jit(solution)/shard_map/up/ppermute | solution.py:28
  40.5 0.8 copy-done.3
  41.3 13.6 %fusion.7 = bf16[128,2,3328]{2,0,1:T(8,128)(2,1)S(1)} fusion(bf16[2,2560,6656]{2,1,0:T(8,128)(2,1)} %param.3, bf16[128,2560]{1,0:T(8,128)(2,1)} %bitcast.94), kind=kOutput, calls=%fused_computation.5 | convolution fusion | flops 4362928128 | bytes 36438016 | tf_op jit(solution)/shard_map/td,gdf->tgf/dot_general | solution.py:57
  55.0 4.5 %collective-permute-start.15 = (bf16[32,2,3328]{2,0,1:T(8,128)(2,1)S(1)}, bf16[32,2,3328]{2,0,1:T(8,128)(2,1)S(1)}, u32[]{:S(2)}, u32[]{:S(2)}) collective-permute-start(bf16[32,2,3328]{2,0,1:T(8,128)(2,1)S(1)} %get-tuple-element.19), channel_id=1, source_target_pairs={{0,4},{1,5},{2,6},{3,7},{16,20},{17,21},{18,22},{19,23}} | collective-permute-start | bytes 1277960 | tf_op jit(solution)/shard_map/up/ppermute | solution.py:28
  59.6 0.7 collective-permute-start.20
  60.5 4.8 %collective-permute-done.15 = bf16[32,2,3328]{2,0,1:T(8,128)(2,1)S(1)} collective-permute-done((bf16[32,2,3328]{2,0,1:T(8,128)(2,1)S(1)}, bf16[32,2,3328]{2,0,1:T(8,128)(2,1)S(1)}, u32[]{:S(2)}, u32[]{:S(2)}) %collective-permute-start.15) | collective-permute-done | bytes 426016 | tf_op jit(solution)/shard_map/up/ppermute | solution.py:28
  66.0 0.7 collective-permute-start.11
  67.0 5.6 %collective-permute-start.14 = (bf16[32,2,3328]{2,0,1:T(8,128)(2,1)S(1)}, bf16[32,2,3328]{2,0,1:T(8,128)(2,1)S(1)}, u32[]{:S(2)}, u32[]{:S(2)}) collective-permute-start(bf16[32,2,3328]{2,0,1:T(8,128)(2,1)S(1)} %get-tuple-element.21), channel_id=1, source_target_pairs={{0,4},{1,5},{2,6},{3,7},{16,20},{17,21},{18,22},{19,23}} | collective-permute-start | bytes 1277960 | tf_op jit(solution)/shard_map/up/ppermute | solution.py:28
  72.6 0.7 collective-permute-start.19
  73.3 0.7 collective-permute-start.16
  74.0 0.7 collective-permute-start.21
  74.7 1.5 %fusion.18 = (bf16[32,2,3328]{2,0,1:T(8,128)(2,1)S(1)}, bf16[32,2,3328]{2,0,1:T(8,128)(2,1)S(1)}) fusion(bf16[32,2,3328]{2,0,1:T(8,128)(2,1)} %collective-permute-done.4, bf16[32,2,3328]{2,0,1:T(8,128)(2,1)S(1)} %collective-permute-done.6, bf16[4,32,2,3328]{3,1,0,2:T(8,128)(2,1)S(1)} %bitcast.88, s32[]{:T(128)S(6)} %min.17, ...), kind=kLoop, calls=%fused_computation.23 | loop fusion | flops 2129920 | bytes 3407880 | tf_op jit(solution)/shard_map/up/convert_element_type | solution.py:25
  76.2 2.0 %collective-permute-done.14 = bf16[32,2,3328]{2,0,1:T(8,128)(2,1)S(1)} collective-permute-done((bf16[32,2,3328]{2,0,1:T(8,128)(2,1)S(1)}, bf16[32,2,3328]{2,0,1:T(8,128)(2,1)S(1)}, u32[]{:S(2)}, u32[]{:S(2)}) %collective-permute-start.14) | collective-permute-done | bytes 426016 | tf_op jit(solution)/shard_map/up/ppermute | solution.py:28
  78.9 0.7 collective-permute-start.18
  79.6 0.7 collective-permute-start.7
  80.3 1.3 %collective-permute-start.12 = (bf16[32,2,3328]{2,0,1:T(8,128)(2,1)S(1)}, bf16[32,2,3328]{2,0,1:T(8,128)(2,1)S(1)}, u32[]{:S(2)}, u32[]{:S(2)}) collective-permute-start(bf16[32,2,3328]{2,0,1:T(8,128)(2,1)S(1)} %get-tuple-element.8), channel_id=1, source_target_pairs={{4,0},{8,4},{5,1},{9,5},{6,2},{10,6},{7,3},{11,7},{20,16},{24,20},... | collective-permute-start | bytes 1277960 | tf_op jit(solution)/shard_map/down/ppermute | solution.py:38
  82.0 14.4 %collective-permute-start.13 = (bf16[32,2,3328]{2,0,1:T(8,128)(2,1)S(1)}, bf16[32,2,3328]{2,0,1:T(8,128)(2,1)S(1)}, u32[]{:S(2)}, u32[]{:S(2)}) collective-permute-start(bf16[32,2,3328]{2,0,1:T(8,128)(2,1)S(1)} %get-tuple-element.22), channel_id=1, source_target_pairs={{0,4},{1,5},{2,6},{3,7},{16,20},{17,21},{18,22},{19,23}} | collective-permute-start | bytes 1277960 | tf_op jit(solution)/shard_map/up/ppermute | solution.py:28
  97.1 1.3 %collective-permute-start.22 = (bf16[32,2,3328]{2,0,1:T(8,128)(2,1)S(1)}, bf16[32,2,3328]{2,0,1:T(8,128)(2,1)S(1)}, u32[]{:S(2)}, u32[]{:S(2)}) collective-permute-start(bf16[32,2,3328]{2,0,1:T(8,128)(2,1)S(1)} %get-tuple-element.16), channel_id=1, source_target_pairs={{4,0},{8,4},{5,1},{9,5},{6,2},{10,6},{7,3},{11,7},{20,16},{24,20},... | collective-permute-start | bytes 1277960 | tf_op jit(solution)/shard_map/down/ppermute | solution.py:38
  98.4 3.9 %collective-permute-done.12 = bf16[32,2,3328]{2,0,1:T(8,128)(2,1)S(1)} collective-permute-done((bf16[32,2,3328]{2,0,1:T(8,128)(2,1)S(1)}, bf16[32,2,3328]{2,0,1:T(8,128)(2,1)S(1)}, u32[]{:S(2)}, u32[]{:S(2)}) %collective-permute-start.12) | collective-permute-done | bytes 426016 | tf_op jit(solution)/shard_map/down/ppermute | solution.py:38
  102.3 1.3 %fusion.19 = f32[32,2,3328]{2,0,1:T(8,128)S(1)} fusion(bf16[32,2,3328]{2,0,1:T(8,128)(2,1)S(1)} %collective-permute-done.8, bf16[32,2,3328]{2,0,1:T(8,128)(2,1)S(1)} %collective-permute-done.12, bf16[32,2,3328]{2,0,1:T(8,128)(2,1)} %collective-permute-done.3, bf16[32,2,3328]{2,0,1:T(8,128)(2,1)S(1)} %collective-permute-done.7, ...), kind=kLoop, calls=%fused_computation.25 | loop fusion | flops 1490944 | bytes 2981892 | tf_op jit(solution)/shard_map/add | solution.py:63
  103.7 4.2 %collective-permute-done.22 = bf16[32,2,3328]{2,0,1:T(8,128)(2,1)S(1)} collective-permute-done((bf16[32,2,3328]{2,0,1:T(8,128)(2,1)S(1)}, bf16[32,2,3328]{2,0,1:T(8,128)(2,1)S(1)}, u32[]{:S(2)}, u32[]{:S(2)}) %collective-permute-start.22) | collective-permute-done | bytes 426016 | tf_op jit(solution)/shard_map/down/ppermute | solution.py:38
  108.3 0.8 pad_maximum_fusion
  (42 shorter events, 4.7 us)
Async XLA Ops:
  0.0 5.8 %collective-permute-start = (bf16[32,2560]{1,0:T(8,128)(2,1)}, bf16[32,2560]{1,0:T(8,128)(2,1)S(1)}, u32[]{:S(2)}, u32[]{:S(2)}) collective-permute-start(bf16[32,2560]{1,0:T(8,128)(2,1)} %param.2), channel_id=1, source_target_pairs={{0,1},{1,2},{2,3},{3,0},{4,5},{5,6},{6,7},{7,4},{8,9},{9,10},{10,1... | collective-permute-start | bytes 491528 | tf_op jit(solution)/shard_map/ppermute | solution.py:15
  0.5 10.7 %collective-permute-start.2 = (bf16[32,2560]{1,0:T(8,128)(2,1)}, bf16[32,2560]{1,0:T(8,128)(2,1)S(1)}, u32[]{:S(2)}, u32[]{:S(2)}) collective-permute-start(bf16[32,2560]{1,0:T(8,128)(2,1)} %param.2), channel_id=1, source_target_pairs={{0,3},{1,0},{2,1},{3,2},{4,7},{5,4},{6,5},{7,6},{8,11},{9,8},{10,9... | collective-permute-start | bytes 491528 | tf_op jit(solution)/shard_map/ppermute | solution.py:15
  2.4 8.7 %collective-permute-start.1 = (bf16[32,2560]{1,0:T(8,128)(2,1)}, bf16[32,2560]{1,0:T(8,128)(2,1)S(1)}, u32[]{:S(2)}, u32[]{:S(2)}) collective-permute-start(bf16[32,2560]{1,0:T(8,128)(2,1)} %param.2), channel_id=1, source_target_pairs={{0,2},{1,3},{2,0},{3,1},{4,6},{5,7},{6,4},{7,5},{8,10},{9,11},{10,... | collective-permute-start | bytes 491528 | tf_op jit(solution)/shard_map/ppermute | solution.py:15
  11.2 13.4 %copy-start = (bf16[4,32,2560]{2,1,0:T(8,128)(2,1)}, bf16[4,32,2560]{2,1,0:T(8,128)(2,1)S(1)}, u32[]{:S(2)}) copy-start(bf16[4,32,2560]{2,1,0:T(8,128)(2,1)S(1)} %bitcast_dynamic-update-slice_fusion) | copy-start | bytes 1966084
  25.6 10.3 %collective-permute-start.10 = (bf16[32,2,3328]{2,0,1:T(8,128)(2,1)S(1)}, bf16[32,2,3328]{2,0,1:T(8,128)(2,1)S(1)}, u32[]{:S(2)}, u32[]{:S(2)}) collective-permute-start(bf16[32,2,3328]{2,0,1:T(8,128)(2,1)S(1)} %get-tuple-element.12), channel_id=1, source_target_pairs={{12,8},{13,9},{14,10},{15,11},{28,24},{29,25},{30,26},{31,27}} | collective-permute-start | bytes 1277960 | tf_op jit(solution)/shard_map/down/ppermute | solution.py:35
  26.3 14.2 %collective-permute-start.5 = (bf16[32,2,3328]{2,0,1:T(8,128)(2,1)S(1)}, bf16[32,2,3328]{2,0,1:T(8,128)(2,1)S(1)}, u32[]{:S(2)}, u32[]{:S(2)}) collective-permute-start(bf16[32,2,3328]{2,0,1:T(8,128)(2,1)S(1)} %get-tuple-element.13), channel_id=1, source_target_pairs={{0,4},{1,5},{2,6},{3,7},{16,20},{17,21},{18,22},{19,23}} | collective-permute-start | bytes 1277960 | tf_op jit(solution)/shard_map/up/ppermute | solution.py:28
  30.4 36.6 %collective-permute-start.9 = (bf16[32,2,3328]{2,0,1:T(8,128)(2,1)}, bf16[32,2,3328]{2,0,1:T(8,128)(2,1)}, u32[]{:S(2)}, u32[]{:S(2)}) collective-permute-start(bf16[32,2,3328]{2,0,1:T(8,128)(2,1)} %get-tuple-element.11), channel_id=1, source_target_pairs={{12,8},{13,9},{14,10},{15,11},{28,24},{29,25},{30,26},{31,27}} | collective-permute-start | bytes 1277960 | tf_op jit(solution)/shard_map/down/ppermute | solution.py:35
  31.8 50.1 %collective-permute-start.3 = (bf16[32,2,3328]{2,0,1:T(8,128)(2,1)}, bf16[32,2,3328]{2,0,1:T(8,128)(2,1)}, u32[]{:S(2)}, u32[]{:S(2)}) collective-permute-start(bf16[32,2,3328]{2,0,1:T(8,128)(2,1)} %get-tuple-element.11), channel_id=1, source_target_pairs={{0,4},{1,5},{2,6},{3,7},{16,20},{17,21},{18,22},{19,23}} | collective-permute-start | bytes 1277960 | tf_op jit(solution)/shard_map/up/ppermute | solution.py:28
  33.9 38.7 %collective-permute-start.4 = (bf16[32,2,3328]{2,0,1:T(8,128)(2,1)}, bf16[32,2,3328]{2,0,1:T(8,128)(2,1)}, u32[]{:S(2)}, u32[]{:S(2)}) collective-permute-start(bf16[32,2,3328]{2,0,1:T(8,128)(2,1)} %get-tuple-element.14), channel_id=1, source_target_pairs={{0,4},{1,5},{2,6},{3,7},{16,20},{17,21},{18,22},{19,23}} | collective-permute-start | bytes 1277960 | tf_op jit(solution)/shard_map/up/ppermute | solution.py:28
  35.9 4.6 %copy-start.1 = (bf16[32,2,3328]{2,0,1:T(8,128)(2,1)}, bf16[32,2,3328]{2,0,1:T(8,128)(2,1)S(1)}, u32[]{:S(2)}) copy-start(bf16[32,2,3328]{2,0,1:T(8,128)(2,1)S(1)} %collective-permute-done.10) | copy-start | bytes 1277956
  40.5 0.8 copy-start.3
  54.9 5.4 %copy-start.2 = (bf16[32,2,3328]{2,0,1:T(8,128)(2,1)S(1)}, bf16[32,2,3328]{2,0,1:T(8,128)(2,1)}, u32[]{:S(2)}) copy-start(bf16[32,2,3328]{2,0,1:T(8,128)(2,1)} %copy-done.1) | copy-start | bytes 1277956
  54.9 5.4 %copy-start.4 = (bf16[32,2,3328]{2,0,1:T(8,128)(2,1)S(1)}, bf16[32,2,3328]{2,0,1:T(8,128)(2,1)}, u32[]{:S(2)}) copy-start(bf16[32,2,3328]{2,0,1:T(8,128)(2,1)} %copy-done.3) | copy-start | bytes 1277956
  55.0 10.3 %collective-permute-start.15 = (bf16[32,2,3328]{2,0,1:T(8,128)(2,1)S(1)}, bf16[32,2,3328]{2,0,1:T(8,128)(2,1)S(1)}, u32[]{:S(2)}, u32[]{:S(2)}) collective-permute-start(bf16[32,2,3328]{2,0,1:T(8,128)(2,1)S(1)} %get-tuple-element.19), channel_id=1, source_target_pairs={{0,4},{1,5},{2,6},{3,7},{16,20},{17,21},{18,22},{19,23}} | collective-permute-start | bytes 1277960 | tf_op jit(solution)/shard_map/up/ppermute | solution.py:28
  59.6 6.5 %collective-permute-start.20 = (bf16[32,2,3328]{2,0,1:T(8,128)(2,1)S(1)}, bf16[32,2,3328]{2,0,1:T(8,128)(2,1)S(1)}, u32[]{:S(2)}, u32[]{:S(2)}) collective-permute-start(bf16[32,2,3328]{2,0,1:T(8,128)(2,1)S(1)} %get-tuple-element.20), channel_id=1, source_target_pairs={{12,8},{13,9},{14,10},{15,11},{28,24},{29,25},{30,26},{31,27}} | collective-permute-start | bytes 1277960 | tf_op jit(solution)/shard_map/down/ppermute | solution.py:35
  65.3 8.0 %collective-permute-start.6 = (bf16[32,2,3328]{2,0,1:T(8,128)(2,1)S(1)}, bf16[32,2,3328]{2,0,1:T(8,128)(2,1)S(1)}, u32[]{:S(2)}, u32[]{:S(2)}) collective-permute-start(bf16[32,2,3328]{2,0,1:T(8,128)(2,1)S(1)} %get-tuple-element.9), channel_id=1, source_target_pairs={{4,8},{5,9},{6,10},{7,11},{20,24},{21,25},{22,26},{23,27}} | collective-permute-start | bytes 1277960 | tf_op jit(solution)/shard_map/up/ppermute | solution.py:32
  66.0 8.0 %collective-permute-start.11 = (bf16[32,2,3328]{2,0,1:T(8,128)(2,1)S(1)}, bf16[32,2,3328]{2,0,1:T(8,128)(2,1)S(1)}, u32[]{:S(2)}, u32[]{:S(2)}) collective-permute-start(bf16[32,2,3328]{2,0,1:T(8,128)(2,1)S(1)} %get-tuple-element.10), channel_id=1, source_target_pairs={{8,4},{9,5},{10,6},{11,7},{24,20},{25,21},{26,22},{27,23}} | collective-permute-start | bytes 1277960 | tf_op jit(solution)/shard_map/down/ppermute | solution.py:38
  67.0 11.3 %collective-permute-start.14 = (bf16[32,2,3328]{2,0,1:T(8,128)(2,1)S(1)}, bf16[32,2,3328]{2,0,1:T(8,128)(2,1)S(1)}, u32[]{:S(2)}, u32[]{:S(2)}) collective-permute-start(bf16[32,2,3328]{2,0,1:T(8,128)(2,1)S(1)} %get-tuple-element.21), channel_id=1, source_target_pairs={{0,4},{1,5},{2,6},{3,7},{16,20},{17,21},{18,22},{19,23}} | collective-permute-start | bytes 1277960 | tf_op jit(solution)/shard_map/up/ppermute | solution.py:28
  72.6 6.3 %collective-permute-start.19 = (bf16[32,2,3328]{2,0,1:T(8,128)(2,1)S(1)}, bf16[32,2,3328]{2,0,1:T(8,128)(2,1)S(1)}, u32[]{:S(2)}, u32[]{:S(2)}) collective-permute-start(bf16[32,2,3328]{2,0,1:T(8,128)(2,1)S(1)} %get-tuple-element.22), channel_id=1, source_target_pairs={{12,8},{13,9},{14,10},{15,11},{28,24},{29,25},{30,26},{31,27}} | collective-permute-start | bytes 1277960 | tf_op jit(solution)/shard_map/down/ppermute | solution.py:35
  73.3 6.3 %collective-permute-start.16 = (bf16[32,2,3328]{2,0,1:T(8,128)(2,1)S(1)}, bf16[32,2,3328]{2,0,1:T(8,128)(2,1)S(1)}, u32[]{:S(2)}, u32[]{:S(2)}) collective-permute-start(bf16[32,2,3328]{2,0,1:T(8,128)(2,1)S(1)} %get-tuple-element.17), channel_id=1, source_target_pairs={{4,8},{5,9},{6,10},{7,11},{20,24},{21,25},{22,26},{23,27}} | collective-permute-start | bytes 1277960 | tf_op jit(solution)/shard_map/up/ppermute | solution.py:32
  74.0 6.3 %collective-permute-start.21 = (bf16[32,2,3328]{2,0,1:T(8,128)(2,1)S(1)}, bf16[32,2,3328]{2,0,1:T(8,128)(2,1)S(1)}, u32[]{:S(2)}, u32[]{:S(2)}) collective-permute-start(bf16[32,2,3328]{2,0,1:T(8,128)(2,1)S(1)} %get-tuple-element.18), channel_id=1, source_target_pairs={{8,4},{9,5},{10,6},{11,7},{24,20},{25,21},{26,22},{27,23}} | collective-permute-start | bytes 1277960 | tf_op jit(solution)/shard_map/down/ppermute | solution.py:38
  78.2 18.2 %collective-permute-start.8 = (bf16[32,2,3328]{2,0,1:T(8,128)(2,1)}, bf16[32,2,3328]{2,0,1:T(8,128)(2,1)S(1)}, u32[]{:S(2)}, u32[]{:S(2)}) collective-permute-start(bf16[32,2,3328]{2,0,1:T(8,128)(2,1)} %get-tuple-element.14), channel_id=1, source_target_pairs={{12,8},{13,9},{14,10},{15,11},{28,24},{29,25},{30,26},{31,27}} | collective-permute-start | bytes 1277960 | tf_op jit(solution)/shard_map/down/ppermute | solution.py:35
  78.9 24.8 %collective-permute-start.18 = (bf16[32,2,3328]{2,0,1:T(8,128)(2,1)S(1)}, bf16[32,2,3328]{2,0,1:T(8,128)(2,1)S(1)}, u32[]{:S(2)}, u32[]{:S(2)}) collective-permute-start(bf16[32,2,3328]{2,0,1:T(8,128)(2,1)S(1)} %get-tuple-element.21), channel_id=1, source_target_pairs={{12,8},{13,9},{14,10},{15,11},{28,24},{29,25},{30,26},{31,27}} | collective-permute-start | bytes 1277960 | tf_op jit(solution)/shard_map/down/ppermute | solution.py:35
  79.6 17.5 %collective-permute-start.7 = (bf16[32,2,3328]{2,0,1:T(8,128)(2,1)S(1)}, bf16[32,2,3328]{2,0,1:T(8,128)(2,1)S(1)}, u32[]{:S(2)}, u32[]{:S(2)}) collective-permute-start(bf16[32,2,3328]{2,0,1:T(8,128)(2,1)S(1)} %get-tuple-element.7), channel_id=1, source_target_pairs={{4,8},{8,12},{5,9},{9,13},{6,10},{10,14},{7,11},{11,15},{20,24},{2... | collective-permute-start | bytes 1277960 | tf_op jit(solution)/shard_map/up/ppermute | solution.py:32
  80.3 22.0 %collective-permute-start.12 = (bf16[32,2,3328]{2,0,1:T(8,128)(2,1)S(1)}, bf16[32,2,3328]{2,0,1:T(8,128)(2,1)S(1)}, u32[]{:S(2)}, u32[]{:S(2)}) collective-permute-start(bf16[32,2,3328]{2,0,1:T(8,128)(2,1)S(1)} %get-tuple-element.8), channel_id=1, source_target_pairs={{4,0},{8,4},{5,1},{9,5},{6,2},{10,6},{7,3},{11,7},{20,16},{24,20},... | collective-permute-start | bytes 1277960 | tf_op jit(solution)/shard_map/down/ppermute | solution.py:38
  82.0 21.7 %collective-permute-start.13 = (bf16[32,2,3328]{2,0,1:T(8,128)(2,1)S(1)}, bf16[32,2,3328]{2,0,1:T(8,128)(2,1)S(1)}, u32[]{:S(2)}, u32[]{:S(2)}) collective-permute-start(bf16[32,2,3328]{2,0,1:T(8,128)(2,1)S(1)} %get-tuple-element.22), channel_id=1, source_target_pairs={{0,4},{1,5},{2,6},{3,7},{16,20},{17,21},{18,22},{19,23}} | collective-permute-start | bytes 1277960 | tf_op jit(solution)/shard_map/up/ppermute | solution.py:28
  96.4 7.3 %collective-permute-start.17 = (bf16[32,2,3328]{2,0,1:T(8,128)(2,1)S(1)}, bf16[32,2,3328]{2,0,1:T(8,128)(2,1)S(1)}, u32[]{:S(2)}, u32[]{:S(2)}) collective-permute-start(bf16[32,2,3328]{2,0,1:T(8,128)(2,1)S(1)} %get-tuple-element.15), channel_id=1, source_target_pairs={{4,8},{8,12},{5,9},{9,13},{6,10},{10,14},{7,11},{11,15},{20,24},{2... | collective-permute-start | bytes 1277960 | tf_op jit(solution)/shard_map/up/ppermute | solution.py:32
  97.1 10.8 %collective-permute-start.22 = (bf16[32,2,3328]{2,0,1:T(8,128)(2,1)S(1)}, bf16[32,2,3328]{2,0,1:T(8,128)(2,1)S(1)}, u32[]{:S(2)}, u32[]{:S(2)}) collective-permute-start(bf16[32,2,3328]{2,0,1:T(8,128)(2,1)S(1)} %get-tuple-element.16), channel_id=1, source_target_pairs={{4,0},{8,4},{5,1},{9,5},{6,2},{10,6},{7,3},{11,7},{20,16},{24,20},... | collective-permute-start | bytes 1277960 | tf_op jit(solution)/shard_map/down/ppermute | solution.py:38

commit v5 on v4

--- a/solution.py
+++ b/solution.py
@@ -24,20 +24,28 @@
     def add(a, b):
         return (a.astype(jnp.float32) + b.astype(jnp.float32)).astype(jnp.bfloat16)
 
+    ends = [(0, 1), (n - 1, n - 2)]
+    if n > 3:
+        sent = [
+            lax.ppermute(block(jnp.where(p == 0, n - r, r - 1)), "row", ends) for r in range(1, n)
+        ]
+        zero = jnp.zeros_like(sent[0])
+        origin_up = [jnp.where(p == 1, s, zero) for s in sent]
+        origin_down = [jnp.where(p == n - 2, s, zero) for s in sent]
+    else:
+        origin_up = [lax.ppermute(part[n - r], "row", ends[:1]) for r in range(1, n)]
+        origin_down = [lax.ppermute(part[r - 1], "row", ends[1:]) for r in range(1, n)]
     with jax.named_scope("up"):
-        origin = [lax.ppermute(part[n - r], "row", [(0, 1)]) for r in range(1, n)]
-        first = origin[0]
-        plus = origin[0]
+        plus = origin_up[0]
         for r in range(2, n):
             sent = lax.ppermute(add(block(p + n - r), plus), "row", [(q, q + 1) for q in range(1, r)])
-            plus = origin[r - 1] + sent
+            plus = origin_up[r - 1] + sent
     with jax.named_scope("down"):
-        origin = [lax.ppermute(part[r - 1], "row", [(n - 1, n - 2)]) for r in range(1, n)]
-        minus = origin[0]
+        minus = origin_down[0]
         for r in range(2, n):
             sent = lax.ppermute(add(block(p - n + r), minus), "row", [(q, q - 1) for q in range(n - r, n - 1)])
-            minus = origin[r - 1] + sent
-    return plus, minus, (first, origin[0])
+            minus = origin_down[r - 1] + sent
+    return plus, minus, (origin_up[0], origin_down[0])
 
 
 def on_device(tokens, gate_up, n, m):

time: 110 us -> 127 us (1.15)
  waiting for transfers between devices: 24.9 us -> 58.4 us
  starting transfers between devices: 49 us -> 32.1 us
    ppermute x12 -> x6, waiting for transfers between devices: 11.5 us -> 34.4 us  [line_reduce(): lax.ppermute(block(jnp.where(p == 0, n - r, r - 1)), 'row', ends)]
    ppermute x12 -> x6, starting transfers between devices: 37.6 us -> 20.6 us  [line_reduce(): lax.ppermute(block(jnp.where(p == 0, n - r, r - 1)), 'row', ends)]
    ppermute x4, waiting for transfers between devices: 8.04 us -> 18.6 us  [line_reduce(): lax.ppermute(add(block(p - n + r), minus), 'row', [(q, q - 1) for q in ra...]
    squeeze x0 -> x2, local copies, waits for them, and re-layouts: none -> 2.09 us  [block(): lax.dynamic_index_in_dim(part, jnp.clip(d, 0, n - 1), 0, keepdims=False)]
  transfers between devices with their start and end apart: 23 -> 17, of which waited for: 6 -> 7; matrix products, arithmetic and copies ran while one was open for 17% -> 3% of each run, Pallas kernels for 0% -> 0%
where the time goes in v5:
time: 127 us; the launch traced here: 126 us
  waiting for transfers between devices  58.4 us (46%)
  starting transfers between devices  32.1 us (25%)
  matrix products  27 us (21%)
  other arithmetic  4.71 us (4%)
  local copies, waits for them, and re-layouts  3.14 us (2%)
    ppermute x6, waiting for transfers between devices, line_reduce(): lax.ppermute(block(jnp.where(p == 0, n - r, r - 1)), 'row', ends)  34.4 us
    dot_general x2, matrix products, on_device(): jnp.einsum('td,gdf->tgf', held, w, preferred_element_type=jnp.float32)  27 us
    ppermute x6, starting transfers between devices, line_reduce(): lax.ppermute(block(jnp.where(p == 0, n - r, r - 1)), 'row', ends)  20.6 us
    ppermute x4, waiting for transfers between devices, line_reduce(): lax.ppermute(add(block(p - n + r), minus), 'row', [(q, q - 1) for q in ra...  18.6 us
    ppermute x3, waiting for transfers between devices, gather_cols(): got = lax.ppermute(tokens, 'col', [(i, (i + s) % m) for i in range(m)])  5.35 us
    ppermute x3, starting transfers between devices, gather_cols(): got = lax.ppermute(tokens, 'col', [(i, (i + s) % m) for i in range(m)])  4.71 us
    ppermute x4, starting transfers between devices, line_reduce(): lax.ppermute(add(block(p - n + r), minus), 'row', [(q, q - 1) for q in ra...  3.96 us
    convert_element_type x4, other arithmetic, add(): return (a.astype(jnp.float32) + b.astype(jnp.float32)).astype(jnp.bfloat16)  3.12 us
  transfers between devices with their start and end apart: 17, of which 7 were waited for; matrix products, arithmetic and copies ran while one was open for 3% of the time, Pallas kernels for 0%

profile of v5, /device:TPU:0, one launch (start us, length us, event | category | flops | bytes accessed | tf_op | source)
XLA Modules:
  0.0 125.6 jit_solution(3633857721805040412)
XLA Ops:
  0.0 0.5 collective-permute-start
  0.5 1.9 %collective-permute-start.2 = (bf16[32,2560]{1,0:T(8,128)(2,1)}, bf16[32,2560]{1,0:T(8,128)(2,1)S(1)}, u32[]{:S(2)}, u32[]{:S(2)}) collective-permute-start(bf16[32,2560]{1,0:T(8,128)(2,1)} %param.2), channel_id=1, source_target_pairs={{0,3},{1,0},{2,1},{3,2},{4,7},{5,4},{6,5},{7,6},{8,11},{9,8},{10,9... | collective-permute-start | bytes 491528 | tf_op jit(solution)/shard_map/ppermute | solution.py:15
  2.4 2.3 %collective-permute-start.1 = (bf16[32,2560]{1,0:T(8,128)(2,1)}, bf16[32,2560]{1,0:T(8,128)(2,1)S(1)}, u32[]{:S(2)}, u32[]{:S(2)}) collective-permute-start(bf16[32,2560]{1,0:T(8,128)(2,1)} %param.2), channel_id=1, source_target_pairs={{0,2},{1,3},{2,0},{3,1},{4,6},{5,7},{6,4},{7,5},{8,10},{9,11},{10,... | collective-permute-start | bytes 491528 | tf_op jit(solution)/shard_map/ppermute | solution.py:15
  4.8 1.0 bitcast_dynamic-update-slice_fusion.3
  5.8 5.3 %collective-permute-done.1 = bf16[32,2560]{1,0:T(8,128)(2,1)S(1)} collective-permute-done((bf16[32,2560]{1,0:T(8,128)(2,1)}, bf16[32,2560]{1,0:T(8,128)(2,1)S(1)}, u32[]{:S(2)}, u32[]{:S(2)}) %collective-permute-start.1) | collective-permute-done | bytes 163872 | tf_op jit(solution)/shard_map/ppermute | solution.py:15
  11.2 13.4 %fusion.4 = bf16[128,2,3328]{2,0,1:T(8,128)(2,1)S(1)} fusion(bf16[128,2560,1]{1,0,2:T(8,128)(2,1)S(1)} %bitcast.107, bf16[2,2560,6656]{2,1,0:T(8,128)(2,1)} %param.3), kind=kOutput, calls=%fused_computation.4 | convolution fusion | flops 4362928128 | bytes 36438016 | tf_op jit(solution)/shard_map/td,gdf->tgf/dot_general | solution.py:65
  24.6 1.0 dynamic-slice_bitcast_fusion.5
  25.6 4.0 %collective-permute-start.5 = (bf16[32,2,3328]{2,0,1:T(8,128)(2,1)S(1)}, bf16[32,2,3328]{2,0,1:T(8,128)(2,1)S(1)}, u32[]{:S(2)}, u32[]{:S(2)}) collective-permute-start(bf16[32,2,3328]{2,0,1:T(8,128)(2,1)S(1)} %get-tuple-element.21), channel_id=1, source_target_pairs={{0,4},{12,8},{1,5},{13,9},{2,6},{14,10},{3,7},{15,11},{16,20},{28,... | collective-permute-start | bytes 1277960 | tf_op jit(solution)/shard_map/ppermute | solution.py:30
  29.7 7.6 %collective-permute-done.5 = bf16[32,2,3328]{2,0,1:T(8,128)(2,1)S(1)} collective-permute-done((bf16[32,2,3328]{2,0,1:T(8,128)(2,1)S(1)}, bf16[32,2,3328]{2,0,1:T(8,128)(2,1)S(1)}, u32[]{:S(2)}, u32[]{:S(2)}) %collective-permute-start.5) | collective-permute-done | bytes 426016 | tf_op jit(solution)/shard_map/ppermute | solution.py:30
  37.3 1.2 fusion.15
  38.4 13.6 %fusion.7 = bf16[128,2,3328]{2,0,1:T(8,128)(2,1)S(1)} fusion(bf16[2,2560,6656]{2,1,0:T(8,128)(2,1)} %param.3, bf16[128,2560]{1,0:T(8,128)(2,1)} %bitcast.108), kind=kOutput, calls=%fused_computation.5 | convolution fusion | flops 4362928128 | bytes 36438016 | tf_op jit(solution)/shard_map/td,gdf->tgf/dot_general | solution.py:65
  52.1 1.1 dynamic-slice_bitcast_fusion.2
  53.2 5.2 %collective-permute-start.12 = (bf16[32,2,3328]{2,0,1:T(8,128)(2,1)}, bf16[32,2,3328]{2,0,1:T(8,128)(2,1)}, u32[]{:S(2)}, u32[]{:S(2)}) collective-permute-start(bf16[32,2,3328]{2,0,1:T(8,128)(2,1)} %get-tuple-element.24), channel_id=1, source_target_pairs={{0,4},{12,8},{1,5},{13,9},{2,6},{14,10},{3,7},{15,11},{16,20},{28,... | collective-permute-start | bytes 1277960 | tf_op jit(solution)/shard_map/ppermute | solution.py:30
  58.3 1.4 %collective-permute-start.3 = (bf16[32,2,3328]{2,0,1:T(8,128)(2,1)}, bf16[32,2,3328]{2,0,1:T(8,128)(2,1)S(1)}, u32[]{:S(2)}, u32[]{:S(2)}) collective-permute-start(bf16[32,2,3328]{2,0,1:T(8,128)(2,1)} %get-tuple-element.19), channel_id=1, source_target_pairs={{0,4},{12,8},{1,5},{13,9},{2,6},{14,10},{3,7},{15,11},{16,20},{28,... | collective-permute-start | bytes 1277960 | tf_op jit(solution)/shard_map/ppermute | solution.py:30
  59.8 1.3 %collective-permute-start.4 = (bf16[32,2,3328]{2,0,1:T(8,128)(2,1)}, bf16[32,2,3328]{2,0,1:T(8,128)(2,1)S(1)}, u32[]{:S(2)}, u32[]{:S(2)}) collective-permute-start(bf16[32,2,3328]{2,0,1:T(8,128)(2,1)} %get-tuple-element.20), channel_id=1, source_target_pairs={{0,4},{12,8},{1,5},{13,9},{2,6},{14,10},{3,7},{15,11},{16,20},{28,... | collective-permute-start | bytes 1277960 | tf_op jit(solution)/shard_map/ppermute | solution.py:30
  61.1 0.7 collective-permute-start.8
  61.8 0.7 collective-permute-start.6
  62.5 5.6 %collective-permute-done.12 = bf16[32,2,3328]{2,0,1:T(8,128)(2,1)} collective-permute-done((bf16[32,2,3328]{2,0,1:T(8,128)(2,1)}, bf16[32,2,3328]{2,0,1:T(8,128)(2,1)}, u32[]{:S(2)}, u32[]{:S(2)}) %collective-permute-start.12) | collective-permute-done | bytes 426016 | tf_op jit(solution)/shard_map/ppermute | solution.py:30
  68.0 4.4 %collective-permute-start.10 = (bf16[32,2,3328]{2,0,1:T(8,128)(2,1)}, bf16[32,2,3328]{2,0,1:T(8,128)(2,1)S(1)}, u32[]{:S(2)}, u32[]{:S(2)}) collective-permute-start(bf16[32,2,3328]{2,0,1:T(8,128)(2,1)} %get-tuple-element.22), channel_id=1, source_target_pairs={{0,4},{12,8},{1,5},{13,9},{2,6},{14,10},{3,7},{15,11},{16,20},{28,... | collective-permute-start | bytes 1277960 | tf_op jit(solution)/shard_map/ppermute | solution.py:30
  72.5 1.2 fusion.12
  73.7 12.6 %collective-permute-done.4 = bf16[32,2,3328]{2,0,1:T(8,128)(2,1)S(1)} collective-permute-done((bf16[32,2,3328]{2,0,1:T(8,128)(2,1)}, bf16[32,2,3328]{2,0,1:T(8,128)(2,1)S(1)}, u32[]{:S(2)}, u32[]{:S(2)}) %collective-permute-start.4) | collective-permute-done | bytes 426016 | tf_op jit(solution)/shard_map/ppermute | solution.py:30
  86.3 4.3 %collective-permute-start.11 = (bf16[32,2,3328]{2,0,1:T(8,128)(2,1)S(1)}, bf16[32,2,3328]{2,0,1:T(8,128)(2,1)S(1)}, u32[]{:S(2)}, u32[]{:S(2)}) collective-permute-start(bf16[32,2,3328]{2,0,1:T(8,128)(2,1)S(1)} %copy-done.1), channel_id=1, source_target_pairs={{0,4},{12,8},{1,5},{13,9},{2,6},{14,10},{3,7},{15,11},{16,20},{28,... | collective-permute-start | bytes 1277960 | tf_op jit(solution)/shard_map/ppermute | solution.py:30
  90.6 0.7 collective-permute-start.13
  91.3 0.7 collective-permute-start.15
  92.4 8.7 %collective-permute-done.11 = bf16[32,2,3328]{2,0,1:T(8,128)(2,1)S(1)} collective-permute-done((bf16[32,2,3328]{2,0,1:T(8,128)(2,1)S(1)}, bf16[32,2,3328]{2,0,1:T(8,128)(2,1)S(1)}, u32[]{:S(2)}, u32[]{:S(2)}) %collective-permute-start.11) | collective-permute-done | bytes 426016 | tf_op jit(solution)/shard_map/ppermute | solution.py:30
  101.0 0.7 collective-permute-start.7
  101.7 1.3 %collective-permute-start.9 = (bf16[32,2,3328]{2,0,1:T(8,128)(2,1)S(1)}, bf16[32,2,3328]{2,0,1:T(8,128)(2,1)S(1)}, u32[]{:S(2)}, u32[]{:S(2)}) collective-permute-start(bf16[32,2,3328]{2,0,1:T(8,128)(2,1)S(1)} %get-tuple-element.12), channel_id=1, source_target_pairs={{4,0},{8,4},{5,1},{9,5},{6,2},{10,6},{7,3},{11,7},{20,16},{24,20},... | collective-permute-start | bytes 1277960 | tf_op jit(solution)/shard_map/down/ppermute | solution.py:46
  103.4 0.7 collective-permute-start.14
  104.1 1.3 %collective-permute-start.16 = (bf16[32,2,3328]{2,0,1:T(8,128)(2,1)S(1)}, bf16[32,2,3328]{2,0,1:T(8,128)(2,1)S(1)}, u32[]{:S(2)}, u32[]{:S(2)}) collective-permute-start(bf16[32,2,3328]{2,0,1:T(8,128)(2,1)S(1)} %get-tuple-element.14), channel_id=1, source_target_pairs={{4,0},{8,4},{5,1},{9,5},{6,2},{10,6},{7,3},{11,7},{20,16},{24,20},... | collective-permute-start | bytes 1277960 | tf_op jit(solution)/shard_map/down/ppermute | solution.py:46
  105.4 13.3 %collective-permute-done.9 = bf16[32,2,3328]{2,0,1:T(8,128)(2,1)S(1)} collective-permute-done((bf16[32,2,3328]{2,0,1:T(8,128)(2,1)S(1)}, bf16[32,2,3328]{2,0,1:T(8,128)(2,1)S(1)}, u32[]{:S(2)}, u32[]{:S(2)}) %collective-permute-start.9) | collective-permute-done | bytes 426016 | tf_op jit(solution)/shard_map/down/ppermute | solution.py:46
  119.2 5.3 %collective-permute-done.16 = bf16[32,2,3328]{2,0,1:T(8,128)(2,1)S(1)} collective-permute-done((bf16[32,2,3328]{2,0,1:T(8,128)(2,1)S(1)}, bf16[32,2,3328]{2,0,1:T(8,128)(2,1)S(1)}, u32[]{:S(2)}, u32[]{:S(2)}) %collective-permute-start.16) | collective-permute-done | bytes 426016 | tf_op jit(solution)/shard_map/down/ppermute | solution.py:46
  124.9 0.8 pad_maximum_fusion
  (24 shorter events, 1.6 us)
Async XLA Ops:
  0.0 5.8 %collective-permute-start = (bf16[32,2560]{1,0:T(8,128)(2,1)}, bf16[32,2560]{1,0:T(8,128)(2,1)S(1)}, u32[]{:S(2)}, u32[]{:S(2)}) collective-permute-start(bf16[32,2560]{1,0:T(8,128)(2,1)} %param.2), channel_id=1, source_target_pairs={{0,1},{1,2},{2,3},{3,0},{4,5},{5,6},{6,7},{7,4},{8,9},{9,10},{10,1... | collective-permute-start | bytes 491528 | tf_op jit(solution)/shard_map/ppermute | solution.py:15
  0.5 10.7 %collective-permute-start.2 = (bf16[32,2560]{1,0:T(8,128)(2,1)}, bf16[32,2560]{1,0:T(8,128)(2,1)S(1)}, u32[]{:S(2)}, u32[]{:S(2)}) collective-permute-start(bf16[32,2560]{1,0:T(8,128)(2,1)} %param.2), channel_id=1, source_target_pairs={{0,3},{1,0},{2,1},{3,2},{4,7},{5,4},{6,5},{7,6},{8,11},{9,8},{10,9... | collective-permute-start | bytes 491528 | tf_op jit(solution)/shard_map/ppermute | solution.py:15
  2.4 8.7 %collective-permute-start.1 = (bf16[32,2560]{1,0:T(8,128)(2,1)}, bf16[32,2560]{1,0:T(8,128)(2,1)S(1)}, u32[]{:S(2)}, u32[]{:S(2)}) collective-permute-start(bf16[32,2560]{1,0:T(8,128)(2,1)} %param.2), channel_id=1, source_target_pairs={{0,2},{1,3},{2,0},{3,1},{4,6},{5,7},{6,4},{7,5},{8,10},{9,11},{10,... | collective-permute-start | bytes 491528 | tf_op jit(solution)/shard_map/ppermute | solution.py:15
  11.2 13.4 %copy-start = (bf16[4,32,2560]{2,1,0:T(8,128)(2,1)}, bf16[4,32,2560]{2,1,0:T(8,128)(2,1)S(1)}, u32[]{:S(2)}) copy-start(bf16[4,32,2560]{2,1,0:T(8,128)(2,1)S(1)} %bitcast_dynamic-update-slice_fusion) | copy-start | bytes 1966084
  25.6 11.6 %collective-permute-start.5 = (bf16[32,2,3328]{2,0,1:T(8,128)(2,1)S(1)}, bf16[32,2,3328]{2,0,1:T(8,128)(2,1)S(1)}, u32[]{:S(2)}, u32[]{:S(2)}) collective-permute-start(bf16[32,2,3328]{2,0,1:T(8,128)(2,1)S(1)} %get-tuple-element.21), channel_id=1, source_target_pairs={{0,4},{12,8},{1,5},{13,9},{2,6},{14,10},{3,7},{15,11},{16,20},{28,... | collective-permute-start | bytes 1277960 | tf_op jit(solution)/shard_map/ppermute | solution.py:30
  53.2 14.9 %collective-permute-start.12 = (bf16[32,2,3328]{2,0,1:T(8,128)(2,1)}, bf16[32,2,3328]{2,0,1:T(8,128)(2,1)}, u32[]{:S(2)}, u32[]{:S(2)}) collective-permute-start(bf16[32,2,3328]{2,0,1:T(8,128)(2,1)} %get-tuple-element.24), channel_id=1, source_target_pairs={{0,4},{12,8},{1,5},{13,9},{2,6},{14,10},{3,7},{15,11},{16,20},{28,... | collective-permute-start | bytes 1277960 | tf_op jit(solution)/shard_map/ppermute | solution.py:30
  58.3 28.0 %copy-start.1 = (bf16[32,2,3328]{2,0,1:T(8,128)(2,1)S(1)}, bf16[32,2,3328]{2,0,1:T(8,128)(2,1)}, u32[]{:S(2)}) copy-start(bf16[32,2,3328]{2,0,1:T(8,128)(2,1)} %get-tuple-element.23) | copy-start | bytes 1277956
  58.3 45.8 %collective-permute-start.3 = (bf16[32,2,3328]{2,0,1:T(8,128)(2,1)}, bf16[32,2,3328]{2,0,1:T(8,128)(2,1)S(1)}, u32[]{:S(2)}, u32[]{:S(2)}) collective-permute-start(bf16[32,2,3328]{2,0,1:T(8,128)(2,1)} %get-tuple-element.19), channel_id=1, source_target_pairs={{0,4},{12,8},{1,5},{13,9},{2,6},{14,10},{3,7},{15,11},{16,20},{28,... | collective-permute-start | bytes 1277960 | tf_op jit(solution)/shard_map/ppermute | solution.py:30
  59.8 26.5 %collective-permute-start.4 = (bf16[32,2,3328]{2,0,1:T(8,128)(2,1)}, bf16[32,2,3328]{2,0,1:T(8,128)(2,1)S(1)}, u32[]{:S(2)}, u32[]{:S(2)}) collective-permute-start(bf16[32,2,3328]{2,0,1:T(8,128)(2,1)} %get-tuple-element.20), channel_id=1, source_target_pairs={{0,4},{12,8},{1,5},{13,9},{2,6},{14,10},{3,7},{15,11},{16,20},{28,... | collective-permute-start | bytes 1277960 | tf_op jit(solution)/shard_map/ppermute | solution.py:30
  61.1 29.5 %collective-permute-start.8 = (bf16[32,2,3328]{2,0,1:T(8,128)(2,1)}, bf16[32,2,3328]{2,0,1:T(8,128)(2,1)S(1)}, u32[]{:S(2)}, u32[]{:S(2)}) collective-permute-start(bf16[32,2,3328]{2,0,1:T(8,128)(2,1)} %get-tuple-element.9), channel_id=1, source_target_pairs={{8,4},{9,5},{10,6},{11,7},{24,20},{25,21},{26,22},{27,23}} | collective-permute-start | bytes 1277960 | tf_op jit(solution)/shard_map/down/ppermute | solution.py:46
  61.8 29.5 %collective-permute-start.6 = (bf16[32,2,3328]{2,0,1:T(8,128)(2,1)}, bf16[32,2,3328]{2,0,1:T(8,128)(2,1)S(1)}, u32[]{:S(2)}, u32[]{:S(2)}) collective-permute-start(bf16[32,2,3328]{2,0,1:T(8,128)(2,1)} %get-tuple-element.17), channel_id=1, source_target_pairs={{4,8},{5,9},{6,10},{7,11},{20,24},{21,25},{22,26},{23,27}} | collective-permute-start | bytes 1277960 | tf_op jit(solution)/shard_map/up/ppermute | solution.py:41
  68.0 51.1 %collective-permute-start.10 = (bf16[32,2,3328]{2,0,1:T(8,128)(2,1)}, bf16[32,2,3328]{2,0,1:T(8,128)(2,1)S(1)}, u32[]{:S(2)}, u32[]{:S(2)}) collective-permute-start(bf16[32,2,3328]{2,0,1:T(8,128)(2,1)} %get-tuple-element.22), channel_id=1, source_target_pairs={{0,4},{12,8},{1,5},{13,9},{2,6},{14,10},{3,7},{15,11},{16,20},{28,... | collective-permute-start | bytes 1277960 | tf_op jit(solution)/shard_map/ppermute | solution.py:30
  86.3 14.7 %collective-permute-start.11 = (bf16[32,2,3328]{2,0,1:T(8,128)(2,1)S(1)}, bf16[32,2,3328]{2,0,1:T(8,128)(2,1)S(1)}, u32[]{:S(2)}, u32[]{:S(2)}) collective-permute-start(bf16[32,2,3328]{2,0,1:T(8,128)(2,1)S(1)} %copy-done.1), channel_id=1, source_target_pairs={{0,4},{12,8},{1,5},{13,9},{2,6},{14,10},{3,7},{15,11},{16,20},{28,... | collective-permute-start | bytes 1277960 | tf_op jit(solution)/shard_map/ppermute | solution.py:30
  90.6 11.1 %collective-permute-start.13 = (bf16[32,2,3328]{2,0,1:T(8,128)(2,1)S(1)}, bf16[32,2,3328]{2,0,1:T(8,128)(2,1)S(1)}, u32[]{:S(2)}, u32[]{:S(2)}) collective-permute-start(bf16[32,2,3328]{2,0,1:T(8,128)(2,1)S(1)} %get-tuple-element.15), channel_id=1, source_target_pairs={{4,8},{5,9},{6,10},{7,11},{20,24},{21,25},{22,26},{23,27}} | collective-permute-start | bytes 1277960 | tf_op jit(solution)/shard_map/up/ppermute | solution.py:41
  91.3 11.7 %collective-permute-start.15 = (bf16[32,2,3328]{2,0,1:T(8,128)(2,1)S(1)}, bf16[32,2,3328]{2,0,1:T(8,128)(2,1)S(1)}, u32[]{:S(2)}, u32[]{:S(2)}) collective-permute-start(bf16[32,2,3328]{2,0,1:T(8,128)(2,1)S(1)} %get-tuple-element.16), channel_id=1, source_target_pairs={{8,4},{9,5},{10,6},{11,7},{24,20},{25,21},{26,22},{27,23}} | collective-permute-start | bytes 1277960 | tf_op jit(solution)/shard_map/down/ppermute | solution.py:46
  101.0 4.4 %collective-permute-start.7 = (bf16[32,2,3328]{2,0,1:T(8,128)(2,1)S(1)}, bf16[32,2,3328]{2,0,1:T(8,128)(2,1)S(1)}, u32[]{:S(2)}, u32[]{:S(2)}) collective-permute-start(bf16[32,2,3328]{2,0,1:T(8,128)(2,1)S(1)} %get-tuple-element.11), channel_id=1, source_target_pairs={{4,8},{8,12},{5,9},{9,13},{6,10},{10,14},{7,11},{11,15},{20,24},{2... | collective-permute-start | bytes 1277960 | tf_op jit(solution)/shard_map/up/ppermute | solution.py:41
  101.7 17.0 %collective-permute-start.9 = (bf16[32,2,3328]{2,0,1:T(8,128)(2,1)S(1)}, bf16[32,2,3328]{2,0,1:T(8,128)(2,1)S(1)}, u32[]{:S(2)}, u32[]{:S(2)}) collective-permute-start(bf16[32,2,3328]{2,0,1:T(8,128)(2,1)S(1)} %get-tuple-element.12), channel_id=1, source_target_pairs={{4,0},{8,4},{5,1},{9,5},{6,2},{10,6},{7,3},{11,7},{20,16},{24,20},... | collective-permute-start | bytes 1277960 | tf_op jit(solution)/shard_map/down/ppermute | solution.py:46
  103.4 15.8 %collective-permute-start.14 = (bf16[32,2,3328]{2,0,1:T(8,128)(2,1)S(1)}, bf16[32,2,3328]{2,0,1:T(8,128)(2,1)S(1)}, u32[]{:S(2)}, u32[]{:S(2)}) collective-permute-start(bf16[32,2,3328]{2,0,1:T(8,128)(2,1)S(1)} %get-tuple-element.13), channel_id=1, source_target_pairs={{4,8},{8,12},{5,9},{9,13},{6,10},{10,14},{7,11},{11,15},{20,24},{2... | collective-permute-start | bytes 1277960 | tf_op jit(solution)/shard_map/up/ppermute | solution.py:41
  104.1 20.3 %collective-permute-start.16 = (bf16[32,2,3328]{2,0,1:T(8,128)(2,1)S(1)}, bf16[32,2,3328]{2,0,1:T(8,128)(2,1)S(1)}, u32[]{:S(2)}, u32[]{:S(2)}) collective-permute-start(bf16[32,2,3328]{2,0,1:T(8,128)(2,1)S(1)} %get-tuple-element.14), channel_id=1, source_target_pairs={{4,0},{8,4},{5,1},{9,5},{6,2},{10,6},{7,3},{11,7},{20,16},{24,20},... | collective-permute-start | bytes 1277960 | tf_op jit(solution)/shard_map/down/ppermute | solution.py:46

commit v6 on v4

--- a/solution.py
+++ b/solution.py
@@ -1,6 +1,10 @@
+import math
+
 import jax
 import jax.numpy as jnp
 from jax import lax
+from jax.experimental import pallas as pl
+from jax.experimental.pallas import tpu as pltpu
 from jax.sharding import PartitionSpec as P
 
 CHUNKS = 2
@@ -17,22 +21,57 @@
     return buf.reshape(m * rows, tokens.shape[1])
 
 
+def tile_width(lo, width, depth):
+    step = 128
+    units = width // step
+    common = units if lo == 0 else math.gcd(lo // step, units)
+    best = 1
+    for g in range(1, common + 1):
+        if common % g == 0 and depth * step * g * 2 <= 9 * 2**20:
+            best = g
+    return step * best
+
+
+def project(x, w, lo, width):
+    t, d = x.shape
+    tf = tile_width(lo, width, d)
+    base = lo // tf
+
+    def kernel(x_ref, w_ref, o_ref):
+        o_ref[0] = jnp.dot(x_ref[...], w_ref[0], preferred_element_type=jnp.float32).astype(o_ref.dtype)
+
+    return pl.pallas_call(
+        kernel,
+        out_shape=jax.ShapeDtypeStruct((2, t, width), x.dtype),
+        grid=(2, width // tf),
+        in_specs=[
+            pl.BlockSpec((t, d), lambda g, j: (0, 0)),
+            pl.BlockSpec((1, d, tf), lambda g, j: (g, 0, base + j)),
+        ],
+        out_specs=pl.BlockSpec((1, t, tf), lambda g, j: (g, 0, j)),
+        compiler_params=pltpu.CompilerParams(vmem_limit_bytes=48 * 2**20),
+        cost_estimate=pl.CostEstimate(
+            flops=4 * t * d * width, bytes_accessed=4 * d * width + 2 * t * d + 4 * t * width, transcendentals=0
+        ),
+    )(x, w)
+
+
 def line_reduce(part, n, p):
     def block(d):
-        return lax.dynamic_index_in_dim(part, jnp.clip(d, 0, n - 1), 0, keepdims=False)
+        return lax.dynamic_index_in_dim(part, jnp.clip(d, 0, n - 1), 1, keepdims=False)
 
     def add(a, b):
         return (a.astype(jnp.float32) + b.astype(jnp.float32)).astype(jnp.bfloat16)
 
     with jax.named_scope("up"):
-        origin = [lax.ppermute(part[n - r], "row", [(0, 1)]) for r in range(1, n)]
+        origin = [lax.ppermute(part[:, n - r], "row", [(0, 1)]) for r in range(1, n)]
         first = origin[0]
         plus = origin[0]
         for r in range(2, n):
             sent = lax.ppermute(add(block(p + n - r), plus), "row", [(q, q + 1) for q in range(1, r)])
             plus = origin[r - 1] + sent
     with jax.named_scope("down"):
-        origin = [lax.ppermute(part[r - 1], "row", [(n - 1, n - 2)]) for r in range(1, n)]
+        origin = [lax.ppermute(part[:, r - 1], "row", [(n - 1, n - 2)]) for r in range(1, n)]
         minus = origin[0]
         for r in range(2, n):
             sent = lax.ppermute(add(block(p - n + r), minus), "row", [(q, q - 1) for q in range(n - r, n - 1)])
@@ -53,15 +92,14 @@
     outs = []
     held = gathered
     for i in range(k):
-        w = gate_up[:, :, edges[i] : edges[i + 1]]
-        part = jnp.einsum("td,gdf->tgf", held, w, preferred_element_type=jnp.float32).astype(jnp.bfloat16)
-        part = part.reshape(n, tb, 2, edges[i + 1] - edges[i])
-        own = lax.dynamic_index_in_dim(part, p, 0, keepdims=False).astype(jnp.float32)
+        part = project(held, gate_up, edges[i], edges[i + 1] - edges[i])
+        part = part.reshape(2, n, tb, edges[i + 1] - edges[i])
+        own = lax.dynamic_index_in_dim(part, p, 1, keepdims=False).astype(jnp.float32)
         if n > 1:
             plus, minus, first = line_reduce(part, n, p)
             held = lax.optimization_barrier((gathered, first))[0]
             own = own + plus.astype(jnp.float32) + minus.astype(jnp.float32)
-        outs.append((jax.nn.silu(own[:, 0]) * own[:, 1]).astype(jnp.bfloat16))
+        outs.append((jax.nn.silu(own[0]) * own[1]).astype(jnp.bfloat16))
     return jnp.concatenate(outs, axis=1)
 
 

time: 110 us -> 120 us (1.091)
  matrix products: 26.9 us -> 0 us
  Pallas kernels: 0 us -> 24.8 us
  waiting for transfers between devices: 24.9 us -> 31.1 us
  starting transfers between devices: 49 us -> 55 us
    dot_general x2 -> x0, matrix products: 26.9 us -> none  [on_device(): jnp.einsum('td,gdf->tgf', held, w, preferred_element_type=jnp.float32)]
    pallas_call x0 -> x2, Pallas kernels: none -> 24.8 us  [project(): pl.pallas_call(kernel, out_shape=jax.ShapeDtypeStruct((2, t, width), x.dt...]
    ppermute x12, starting transfers between devices: 37.6 us -> 43.5 us  [the longest x6 38.7 us: line_reduce(): lax.ppermute(part[:, n - r], 'row', [(0, 1)])]
    ppermute x12, waiting for transfers between devices: 11.5 us -> 15 us  [the longest x6 15 us: line_reduce(): lax.ppermute(part[:, n - r], 'row', [(0, 1)])]
    ppermute x4, waiting for transfers between devices: 8.04 us -> 10.8 us  [line_reduce(): lax.ppermute(add(block(p - n + r), minus), 'row', [(q, q - 1) for q in ra...]
    convert_element_type x4 -> x6, other arithmetic: 2.23 us -> 3.06 us  [add(): return (a.astype(jnp.float32) + b.astype(jnp.float32)).astype(jnp.bfloat16)]
  transfers between devices with their start and end apart: 23 -> 23, of which waited for: 6 -> 6; matrix products, arithmetic and copies ran while one was open for 17% -> 4% of each run, Pallas kernels for 0% -> 11%
where the time goes in v6:
time: 120 us; the launch traced here: 118 us
  starting transfers between devices  55 us (46%)
  waiting for transfers between devices  31.1 us (26%)
  Pallas kernels  24.8 us (21%)
  other arithmetic  4.59 us (4%)
  local copies, waits for them, and re-layouts  2.17 us (2%)
    ppermute x6, starting transfers between devices, line_reduce(): lax.ppermute(part[:, n - r], 'row', [(0, 1)])  38.7 us
    pallas_call x2, Pallas kernels, project(): pl.pallas_call(kernel, out_shape=jax.ShapeDtypeStruct((2, t, width), x.dt...  24.8 us
    ppermute x6, waiting for transfers between devices, line_reduce(): lax.ppermute(part[:, n - r], 'row', [(0, 1)])  15 us
    ppermute x4, waiting for transfers between devices, line_reduce(): lax.ppermute(add(block(p - n + r), minus), 'row', [(q, q - 1) for q in ra...  10.8 us
    ppermute x3, waiting for transfers between devices, gather_cols(): got = lax.ppermute(tokens, 'col', [(i, (i + s) % m) for i in range(m)])  5.37 us
    ppermute x6, starting transfers between devices, line_reduce(): lax.ppermute(part[:, r - 1], 'row', [(n - 1, n - 2)])  4.84 us
    ppermute x3, starting transfers between devices, gather_cols(): got = lax.ppermute(tokens, 'col', [(i, (i + s) % m) for i in range(m)])  4.71 us
    ppermute x4, starting transfers between devices, line_reduce(): lax.ppermute(add(block(p - n + r), minus), 'row', [(q, q - 1) for q in ra...  3.96 us
  transfers between devices with their start and end apart: 23, of which 6 were waited for; matrix products, arithmetic and copies ran while one was open for 4% of the time, Pallas kernels for 11%

profile of v6, /device:TPU:0, one launch (start us, length us, event | category | flops | bytes accessed | tf_op | source)
XLA Modules:
  0.0 118.1 jit_solution(7886706484691621166)
XLA Ops:
  0.5 1.9 %collective-permute-start.2 = (bf16[32,2560]{1,0:T(8,128)(2,1)}, bf16[32,2560]{1,0:T(8,128)(2,1)S(1)}, u32[]{:S(2)}, u32[]{:S(2)}) collective-permute-start(bf16[32,2560]{1,0:T(8,128)(2,1)} %param.2), channel_id=1, source_target_pairs={{0,3},{1,0},{2,1},{3,2},{4,7},{5,4},{6,5},{7,6},{8,11},{9,8},{10,9... | collective-permute-start | bytes 491528 | tf_op jit(solution)/shard_map/ppermute | solution.py:19
  2.4 2.3 %collective-permute-start.1 = (bf16[32,2560]{1,0:T(8,128)(2,1)}, bf16[32,2560]{1,0:T(8,128)(2,1)S(1)}, u32[]{:S(2)}, u32[]{:S(2)}) collective-permute-start(bf16[32,2560]{1,0:T(8,128)(2,1)} %param.2), channel_id=1, source_target_pairs={{0,2},{1,3},{2,0},{3,1},{4,6},{5,7},{6,4},{7,5},{8,10},{9,11},{10,... | collective-permute-start | bytes 491528 | tf_op jit(solution)/shard_map/ppermute | solution.py:19
  4.8 1.0 bitcast_dynamic-update-slice_fusion.3
  5.8 5.4 %collective-permute-done.1 = bf16[32,2560]{1,0:T(8,128)(2,1)S(1)} collective-permute-done((bf16[32,2560]{1,0:T(8,128)(2,1)}, bf16[32,2560]{1,0:T(8,128)(2,1)S(1)}, u32[]{:S(2)}, u32[]{:S(2)}) %collective-permute-start.1) | collective-permute-done | bytes 163872 | tf_op jit(solution)/shard_map/ppermute | solution.py:19
  11.2 12.4 %shard_map.28 = bf16[2,128,3328]{2,1,0:T(8,128)(2,1)S(1)} custom-call(bf16[128,2560]{1,0:T(8,128)(2,1)S(1)} %bitcast.123, bf16[2,2560,6656]{2,1,0:T(8,128)(2,1)} %w_ref.3), custom_call_target="tpu_custom_call" | custom-call | flops 4362076160 | bytes 36438016 | tf_op jit(solution)/shard_map/pallas_call | solution.py:43
  23.6 1.0 slice_bitcast_fusion.11
  24.6 4.8 %collective-permute-start.5 = (bf16[2,32,3328]{2,1,0:T(8,128)(2,1)}, bf16[2,32,3328]{2,1,0:T(8,128)(2,1)}, u32[]{:S(2)}, u32[]{:S(2)}) collective-permute-start(bf16[2,32,3328]{2,1,0:T(8,128)(2,1)} %get-tuple-element.10), channel_id=1, source_target_pairs={{0,4},{1,5},{2,6},{3,7},{16,20},{17,21},{18,22},{19,23}} | collective-permute-start | bytes 1277960 | tf_op jit(solution)/shard_map/up/ppermute | solution.py:67
  29.4 1.4 %collective-permute-start.10 = (bf16[2,32,3328]{2,1,0:T(8,128)(2,1)}, bf16[2,32,3328]{2,1,0:T(8,128)(2,1)}, u32[]{:S(2)}, u32[]{:S(2)}) collective-permute-start(bf16[2,32,3328]{2,1,0:T(8,128)(2,1)} %get-tuple-element.12), channel_id=1, source_target_pairs={{12,8},{13,9},{14,10},{15,11},{28,24},{29,25},{30,26},{31,27}} | collective-permute-start | bytes 1277960 | tf_op jit(solution)/shard_map/down/ppermute | solution.py:74
  31.5 1.3 %collective-permute-start.3 = (bf16[2,32,3328]{2,1,0:T(8,128)(2,1)S(1)}, bf16[2,32,3328]{2,1,0:T(8,128)(2,1)S(1)}, u32[]{:S(2)}, u32[]{:S(2)}) collective-permute-start(bf16[2,32,3328]{2,1,0:T(8,128)(2,1)S(1)} %get-tuple-element.9), channel_id=1, source_target_pairs={{0,4},{1,5},{2,6},{3,7},{16,20},{17,21},{18,22},{19,23}} | collective-permute-start | bytes 1277960 | tf_op jit(solution)/shard_map/up/ppermute | solution.py:67
  32.9 1.3 %collective-permute-start.4 = (bf16[2,32,3328]{2,1,0:T(8,128)(2,1)S(1)}, bf16[2,32,3328]{2,1,0:T(8,128)(2,1)S(1)}, u32[]{:S(2)}, u32[]{:S(2)}) collective-permute-start(bf16[2,32,3328]{2,1,0:T(8,128)(2,1)S(1)} %get-tuple-element.11), channel_id=1, source_target_pairs={{0,4},{1,5},{2,6},{3,7},{16,20},{17,21},{18,22},{19,23}} | collective-permute-start | bytes 1277960 | tf_op jit(solution)/shard_map/up/ppermute | solution.py:67
  34.2 5.0 %collective-permute-done.5 = bf16[2,32,3328]{2,1,0:T(8,128)(2,1)} collective-permute-done((bf16[2,32,3328]{2,1,0:T(8,128)(2,1)}, bf16[2,32,3328]{2,1,0:T(8,128)(2,1)}, u32[]{:S(2)}, u32[]{:S(2)}) %collective-permute-start.5) | collective-permute-done | bytes 426016 | tf_op jit(solution)/shard_map/up/ppermute | solution.py:67
  39.2 12.4 %shard_map.29 = bf16[2,128,3328]{2,1,0:T(8,128)(2,1)S(1)} custom-call(bf16[128,2560]{1,0:T(8,128)(2,1)S(1)} %bitcast.124, bf16[2,2560,6656]{2,1,0:T(8,128)(2,1)} %w_ref.3), custom_call_target="tpu_custom_call" | custom-call | flops 4362076160 | bytes 36438016 | tf_op jit(solution)/shard_map/pallas_call | solution.py:43
  51.7 4.4 %collective-permute-start.15 = (bf16[2,32,3328]{2,1,0:T(8,128)(2,1)S(1)}, bf16[2,32,3328]{2,1,0:T(8,128)(2,1)S(1)}, u32[]{:S(2)}, u32[]{:S(2)}) collective-permute-start(bf16[2,32,3328]{2,1,0:T(8,128)(2,1)S(1)} %get-tuple-element.15), channel_id=1, source_target_pairs={{0,4},{1,5},{2,6},{3,7},{16,20},{17,21},{18,22},{19,23}} | collective-permute-start | bytes 1277960 | tf_op jit(solution)/shard_map/up/ppermute | solution.py:67
  56.1 1.1 fusion.7
  57.2 0.7 collective-permute-start.6
  57.9 5.9 %collective-permute-done.15 = bf16[2,32,3328]{2,1,0:T(8,128)(2,1)S(1)} collective-permute-done((bf16[2,32,3328]{2,1,0:T(8,128)(2,1)S(1)}, bf16[2,32,3328]{2,1,0:T(8,128)(2,1)S(1)}, u32[]{:S(2)}, u32[]{:S(2)}) %collective-permute-start.15) | collective-permute-done | bytes 426016 | tf_op jit(solution)/shard_map/up/ppermute | solution.py:67
  64.7 4.4 %collective-permute-start.14 = (bf16[2,32,3328]{2,1,0:T(8,128)(2,1)S(1)}, bf16[2,32,3328]{2,1,0:T(8,128)(2,1)S(1)}, u32[]{:S(2)}, u32[]{:S(2)}) collective-permute-start(bf16[2,32,3328]{2,1,0:T(8,128)(2,1)S(1)} %get-tuple-element.16), channel_id=1, source_target_pairs={{0,4},{1,5},{2,6},{3,7},{16,20},{17,21},{18,22},{19,23}} | collective-permute-start | bytes 1277960 | tf_op jit(solution)/shard_map/up/ppermute | solution.py:67
  69.1 0.7 collective-permute-start.16
  69.8 1.3 %fusion.8 = (bf16[2,32,3328]{2,1,0:T(8,128)(2,1)S(1)}, bf16[2,32,3328]{2,1,0:T(8,128)(2,1)S(1)}) fusion(bf16[2,32,3328]{2,1,0:T(8,128)(2,1)S(1)} %collective-permute-done.4, bf16[2,32,3328]{2,1,0:T(8,128)(2,1)S(1)} %collective-permute-done.6, bf16[2,4,32,3328]{3,2,1,0:T(8,128)(2,1)S(1)} %bitcast.115, s32[]{:T(128)S(6)} %min.17, ...), kind=kLoop, calls=%fused_computation.17 | loop fusion | flops 1916928 | bytes 2981896 | tf_op jit(solution)/shard_map/up/convert_element_type | solution.py:64
  71.1 0.7 collective-permute-start.8
  71.8 4.1 %collective-permute-done.14 = bf16[2,32,3328]{2,1,0:T(8,128)(2,1)S(1)} collective-permute-done((bf16[2,32,3328]{2,1,0:T(8,128)(2,1)S(1)}, bf16[2,32,3328]{2,1,0:T(8,128)(2,1)S(1)}, u32[]{:S(2)}, u32[]{:S(2)}) %collective-permute-start.14) | collective-permute-done | bytes 426016 | tf_op jit(solution)/shard_map/up/ppermute | solution.py:67
  76.5 0.7 collective-permute-start.11
  77.5 0.7 collective-permute-start.19
  78.2 0.7 collective-permute-start.21
  79.1 0.7 collective-permute-start.7
  79.8 1.3 %collective-permute-start.12 = (bf16[2,32,3328]{2,1,0:T(8,128)(2,1)S(1)}, bf16[2,32,3328]{2,1,0:T(8,128)(2,1)S(1)}, u32[]{:S(2)}, u32[]{:S(2)}) collective-permute-start(bf16[2,32,3328]{2,1,0:T(8,128)(2,1)S(1)} %fusion.6), channel_id=1, source_target_pairs={{4,0},{8,4},{5,1},{9,5},{6,2},{10,6},{7,3},{11,7},{20,16},{24,20},... | collective-permute-start | bytes 1277960 | tf_op jit(solution)/shard_map/down/ppermute | solution.py:77
  81.3 22.4 %collective-permute-start.13 = (bf16[2,32,3328]{2,1,0:T(8,128)(2,1)S(1)}, bf16[2,32,3328]{2,1,0:T(8,128)(2,1)S(1)}, u32[]{:S(2)}, u32[]{:S(2)}) collective-permute-start(bf16[2,32,3328]{2,1,0:T(8,128)(2,1)S(1)} %get-tuple-element.17), channel_id=1, source_target_pairs={{0,4},{1,5},{2,6},{3,7},{16,20},{17,21},{18,22},{19,23}} | collective-permute-start | bytes 1277960 | tf_op jit(solution)/shard_map/up/ppermute | solution.py:67
  103.7 0.7 collective-permute-start.17
  104.4 1.3 %collective-permute-start.22 = (bf16[2,32,3328]{2,1,0:T(8,128)(2,1)S(1)}, bf16[2,32,3328]{2,1,0:T(8,128)(2,1)S(1)}, u32[]{:S(2)}, u32[]{:S(2)}) collective-permute-start(bf16[2,32,3328]{2,1,0:T(8,128)(2,1)S(1)} %fusion.1), channel_id=1, source_target_pairs={{4,0},{8,4},{5,1},{9,5},{6,2},{10,6},{7,3},{11,7},{20,16},{24,20},... | collective-permute-start | bytes 1277960 | tf_op jit(solution)/shard_map/down/ppermute | solution.py:77
  105.7 5.6 %collective-permute-done.12 = bf16[2,32,3328]{2,1,0:T(8,128)(2,1)S(1)} collective-permute-done((bf16[2,32,3328]{2,1,0:T(8,128)(2,1)S(1)}, bf16[2,32,3328]{2,1,0:T(8,128)(2,1)S(1)}, u32[]{:S(2)}, u32[]{:S(2)}) %collective-permute-start.12) | collective-permute-done | bytes 426016 | tf_op jit(solution)/shard_map/down/ppermute | solution.py:77
  111.7 5.2 %collective-permute-done.22 = bf16[2,32,3328]{2,1,0:T(8,128)(2,1)S(1)} collective-permute-done((bf16[2,32,3328]{2,1,0:T(8,128)(2,1)S(1)}, bf16[2,32,3328]{2,1,0:T(8,128)(2,1)S(1)}, u32[]{:S(2)}, u32[]{:S(2)}) %collective-permute-start.22) | collective-permute-done | bytes 426016 | tf_op jit(solution)/shard_map/down/ppermute | solution.py:77
  117.3 0.8 pad_maximum_fusion
  (34 shorter events, 4.2 us)
Async XLA Ops:
  0.0 5.8 %collective-permute-start = (bf16[32,2560]{1,0:T(8,128)(2,1)}, bf16[32,2560]{1,0:T(8,128)(2,1)S(1)}, u32[]{:S(2)}, u32[]{:S(2)}) collective-permute-start(bf16[32,2560]{1,0:T(8,128)(2,1)} %param.2), channel_id=1, source_target_pairs={{0,1},{1,2},{2,3},{3,0},{4,5},{5,6},{6,7},{7,4},{8,9},{9,10},{10,1... | collective-permute-start | bytes 491528 | tf_op jit(solution)/shard_map/ppermute | solution.py:19
  0.5 10.7 %collective-permute-start.2 = (bf16[32,2560]{1,0:T(8,128)(2,1)}, bf16[32,2560]{1,0:T(8,128)(2,1)S(1)}, u32[]{:S(2)}, u32[]{:S(2)}) collective-permute-start(bf16[32,2560]{1,0:T(8,128)(2,1)} %param.2), channel_id=1, source_target_pairs={{0,3},{1,0},{2,1},{3,2},{4,7},{5,4},{6,5},{7,6},{8,11},{9,8},{10,9... | collective-permute-start | bytes 491528 | tf_op jit(solution)/shard_map/ppermute | solution.py:19
  2.4 8.7 %collective-permute-start.1 = (bf16[32,2560]{1,0:T(8,128)(2,1)}, bf16[32,2560]{1,0:T(8,128)(2,1)S(1)}, u32[]{:S(2)}, u32[]{:S(2)}) collective-permute-start(bf16[32,2560]{1,0:T(8,128)(2,1)} %param.2), channel_id=1, source_target_pairs={{0,2},{1,3},{2,0},{3,1},{4,6},{5,7},{6,4},{7,5},{8,10},{9,11},{10,... | collective-permute-start | bytes 491528 | tf_op jit(solution)/shard_map/ppermute | solution.py:19
  24.6 14.5 %collective-permute-start.5 = (bf16[2,32,3328]{2,1,0:T(8,128)(2,1)}, bf16[2,32,3328]{2,1,0:T(8,128)(2,1)}, u32[]{:S(2)}, u32[]{:S(2)}) collective-permute-start(bf16[2,32,3328]{2,1,0:T(8,128)(2,1)} %get-tuple-element.10), channel_id=1, source_target_pairs={{0,4},{1,5},{2,6},{3,7},{16,20},{17,21},{18,22},{19,23}} | collective-permute-start | bytes 1277960 | tf_op jit(solution)/shard_map/up/ppermute | solution.py:67
  29.4 9.7 %collective-permute-start.10 = (bf16[2,32,3328]{2,1,0:T(8,128)(2,1)}, bf16[2,32,3328]{2,1,0:T(8,128)(2,1)}, u32[]{:S(2)}, u32[]{:S(2)}) collective-permute-start(bf16[2,32,3328]{2,1,0:T(8,128)(2,1)} %get-tuple-element.12), channel_id=1, source_target_pairs={{12,8},{13,9},{14,10},{15,11},{28,24},{29,25},{30,26},{31,27}} | collective-permute-start | bytes 1277960 | tf_op jit(solution)/shard_map/down/ppermute | solution.py:74
  30.9 46.6 %collective-permute-start.9 = (bf16[2,32,3328]{2,1,0:T(8,128)(2,1)S(1)}, bf16[2,32,3328]{2,1,0:T(8,128)(2,1)S(1)}, u32[]{:S(2)}, u32[]{:S(2)}) collective-permute-start(bf16[2,32,3328]{2,1,0:T(8,128)(2,1)S(1)} %get-tuple-element.9), channel_id=1, source_target_pairs={{12,8},{13,9},{14,10},{15,11},{28,24},{29,25},{30,26},{31,27}} | collective-permute-start | bytes 1277960 | tf_op jit(solution)/shard_map/down/ppermute | solution.py:74
  31.5 49.7 %collective-permute-start.3 = (bf16[2,32,3328]{2,1,0:T(8,128)(2,1)S(1)}, bf16[2,32,3328]{2,1,0:T(8,128)(2,1)S(1)}, u32[]{:S(2)}, u32[]{:S(2)}) collective-permute-start(bf16[2,32,3328]{2,1,0:T(8,128)(2,1)S(1)} %get-tuple-element.9), channel_id=1, source_target_pairs={{0,4},{1,5},{2,6},{3,7},{16,20},{17,21},{18,22},{19,23}} | collective-permute-start | bytes 1277960 | tf_op jit(solution)/shard_map/up/ppermute | solution.py:67
  32.9 31.8 %collective-permute-start.4 = (bf16[2,32,3328]{2,1,0:T(8,128)(2,1)S(1)}, bf16[2,32,3328]{2,1,0:T(8,128)(2,1)S(1)}, u32[]{:S(2)}, u32[]{:S(2)}) collective-permute-start(bf16[2,32,3328]{2,1,0:T(8,128)(2,1)S(1)} %get-tuple-element.11), channel_id=1, source_target_pairs={{0,4},{1,5},{2,6},{3,7},{16,20},{17,21},{18,22},{19,23}} | collective-permute-start | bytes 1277960 | tf_op jit(solution)/shard_map/up/ppermute | solution.py:67
  51.7 12.2 %collective-permute-start.15 = (bf16[2,32,3328]{2,1,0:T(8,128)(2,1)S(1)}, bf16[2,32,3328]{2,1,0:T(8,128)(2,1)S(1)}, u32[]{:S(2)}, u32[]{:S(2)}) collective-permute-start(bf16[2,32,3328]{2,1,0:T(8,128)(2,1)S(1)} %get-tuple-element.15), channel_id=1, source_target_pairs={{0,4},{1,5},{2,6},{3,7},{16,20},{17,21},{18,22},{19,23}} | collective-permute-start | bytes 1277960 | tf_op jit(solution)/shard_map/up/ppermute | solution.py:67
  57.2 11.9 %collective-permute-start.6 = (bf16[2,32,3328]{2,1,0:T(8,128)(2,1)S(1)}, bf16[2,32,3328]{2,1,0:T(8,128)(2,1)S(1)}, u32[]{:S(2)}, u32[]{:S(2)}) collective-permute-start(bf16[2,32,3328]{2,1,0:T(8,128)(2,1)S(1)} %fusion.7), channel_id=1, source_target_pairs={{4,8},{5,9},{6,10},{7,11},{20,24},{21,25},{22,26},{23,27}} | collective-permute-start | bytes 1277960 | tf_op jit(solution)/shard_map/up/ppermute | solution.py:71
  63.9 7.2 %collective-permute-start.20 = (bf16[2,32,3328]{2,1,0:T(8,128)(2,1)S(1)}, bf16[2,32,3328]{2,1,0:T(8,128)(2,1)S(1)}, u32[]{:S(2)}, u32[]{:S(2)}) collective-permute-start(bf16[2,32,3328]{2,1,0:T(8,128)(2,1)S(1)} %get-tuple-element.18), channel_id=1, source_target_pairs={{12,8},{13,9},{14,10},{15,11},{28,24},{29,25},{30,26},{31,27}} | collective-permute-start | bytes 1277960 | tf_op jit(solution)/shard_map/down/ppermute | solution.py:74
  64.7 11.2 %collective-permute-start.14 = (bf16[2,32,3328]{2,1,0:T(8,128)(2,1)S(1)}, bf16[2,32,3328]{2,1,0:T(8,128)(2,1)S(1)}, u32[]{:S(2)}, u32[]{:S(2)}) collective-permute-start(bf16[2,32,3328]{2,1,0:T(8,128)(2,1)S(1)} %get-tuple-element.16), channel_id=1, source_target_pairs={{0,4},{1,5},{2,6},{3,7},{16,20},{17,21},{18,22},{19,23}} | collective-permute-start | bytes 1277960 | tf_op jit(solution)/shard_map/up/ppermute | solution.py:67
  69.1 7.4 %collective-permute-start.16 = (bf16[2,32,3328]{2,1,0:T(8,128)(2,1)S(1)}, bf16[2,32,3328]{2,1,0:T(8,128)(2,1)S(1)}, u32[]{:S(2)}, u32[]{:S(2)}) collective-permute-start(bf16[2,32,3328]{2,1,0:T(8,128)(2,1)S(1)} %fusion.2), channel_id=1, source_target_pairs={{4,8},{5,9},{6,10},{7,11},{20,24},{21,25},{22,26},{23,27}} | collective-permute-start | bytes 1277960 | tf_op jit(solution)/shard_map/up/ppermute | solution.py:71
  71.1 32.6 %collective-permute-start.8 = (bf16[2,32,3328]{2,1,0:T(8,128)(2,1)S(1)}, bf16[2,32,3328]{2,1,0:T(8,128)(2,1)S(1)}, u32[]{:S(2)}, u32[]{:S(2)}) collective-permute-start(bf16[2,32,3328]{2,1,0:T(8,128)(2,1)S(1)} %get-tuple-element.11), channel_id=1, source_target_pairs={{12,8},{13,9},{14,10},{15,11},{28,24},{29,25},{30,26},{31,27}} | collective-permute-start | bytes 1277960 | tf_op jit(solution)/shard_map/down/ppermute | solution.py:74
  75.8 35.9 %collective-permute-start.18 = (bf16[2,32,3328]{2,1,0:T(8,128)(2,1)S(1)}, bf16[2,32,3328]{2,1,0:T(8,128)(2,1)S(1)}, u32[]{:S(2)}, u32[]{:S(2)}) collective-permute-start(bf16[2,32,3328]{2,1,0:T(8,128)(2,1)S(1)} %get-tuple-element.16), channel_id=1, source_target_pairs={{12,8},{13,9},{14,10},{15,11},{28,24},{29,25},{30,26},{31,27}} | collective-permute-start | bytes 1277960 | tf_op jit(solution)/shard_map/down/ppermute | solution.py:74
  76.5 1.7 %collective-permute-start.11 = (bf16[2,32,3328]{2,1,0:T(8,128)(2,1)S(1)}, bf16[2,32,3328]{2,1,0:T(8,128)(2,1)S(1)}, u32[]{:S(2)}, u32[]{:S(2)}) collective-permute-start(bf16[2,32,3328]{2,1,0:T(8,128)(2,1)S(1)} %get-tuple-element.8), channel_id=1, source_target_pairs={{8,4},{9,5},{10,6},{11,7},{24,20},{25,21},{26,22},{27,23}} | collective-permute-start | bytes 1277960 | tf_op jit(solution)/shard_map/down/ppermute | solution.py:77
  77.5 1.6 %collective-permute-start.19 = (bf16[2,32,3328]{2,1,0:T(8,128)(2,1)S(1)}, bf16[2,32,3328]{2,1,0:T(8,128)(2,1)S(1)}, u32[]{:S(2)}, u32[]{:S(2)}) collective-permute-start(bf16[2,32,3328]{2,1,0:T(8,128)(2,1)S(1)} %get-tuple-element.17), channel_id=1, source_target_pairs={{12,8},{13,9},{14,10},{15,11},{28,24},{29,25},{30,26},{31,27}} | collective-permute-start | bytes 1277960 | tf_op jit(solution)/shard_map/down/ppermute | solution.py:74
  78.2 1.6 %collective-permute-start.21 = (bf16[2,32,3328]{2,1,0:T(8,128)(2,1)S(1)}, bf16[2,32,3328]{2,1,0:T(8,128)(2,1)S(1)}, u32[]{:S(2)}, u32[]{:S(2)}) collective-permute-start(bf16[2,32,3328]{2,1,0:T(8,128)(2,1)S(1)} %get-tuple-element.14), channel_id=1, source_target_pairs={{8,4},{9,5},{10,6},{11,7},{24,20},{25,21},{26,22},{27,23}} | collective-permute-start | bytes 1277960 | tf_op jit(solution)/shard_map/down/ppermute | solution.py:77
  79.1 25.3 %collective-permute-start.7 = (bf16[2,32,3328]{2,1,0:T(8,128)(2,1)S(1)}, bf16[2,32,3328]{2,1,0:T(8,128)(2,1)S(1)}, u32[]{:S(2)}, u32[]{:S(2)}) collective-permute-start(bf16[2,32,3328]{2,1,0:T(8,128)(2,1)S(1)} %get-tuple-element.7), channel_id=1, source_target_pairs={{4,8},{8,12},{5,9},{9,13},{6,10},{10,14},{7,11},{11,15},{20,24},{2... | collective-permute-start | bytes 1277960 | tf_op jit(solution)/shard_map/up/ppermute | solution.py:71
  79.8 31.5 %collective-permute-start.12 = (bf16[2,32,3328]{2,1,0:T(8,128)(2,1)S(1)}, bf16[2,32,3328]{2,1,0:T(8,128)(2,1)S(1)}, u32[]{:S(2)}, u32[]{:S(2)}) collective-permute-start(bf16[2,32,3328]{2,1,0:T(8,128)(2,1)S(1)} %fusion.6), channel_id=1, source_target_pairs={{4,0},{8,4},{5,1},{9,5},{6,2},{10,6},{7,3},{11,7},{20,16},{24,20},... | collective-permute-start | bytes 1277960 | tf_op jit(solution)/shard_map/down/ppermute | solution.py:77
  81.3 30.5 %collective-permute-start.13 = (bf16[2,32,3328]{2,1,0:T(8,128)(2,1)S(1)}, bf16[2,32,3328]{2,1,0:T(8,128)(2,1)S(1)}, u32[]{:S(2)}, u32[]{:S(2)}) collective-permute-start(bf16[2,32,3328]{2,1,0:T(8,128)(2,1)S(1)} %get-tuple-element.17), channel_id=1, source_target_pairs={{0,4},{1,5},{2,6},{3,7},{16,20},{17,21},{18,22},{19,23}} | collective-permute-start | bytes 1277960 | tf_op jit(solution)/shard_map/up/ppermute | solution.py:67
  103.7 8.0 %collective-permute-start.17 = (bf16[2,32,3328]{2,1,0:T(8,128)(2,1)S(1)}, bf16[2,32,3328]{2,1,0:T(8,128)(2,1)S(1)}, u32[]{:S(2)}, u32[]{:S(2)}) collective-permute-start(bf16[2,32,3328]{2,1,0:T(8,128)(2,1)S(1)} %get-tuple-element.13), channel_id=1, source_target_pairs={{4,8},{8,12},{5,9},{9,13},{6,10},{10,14},{7,11},{11,15},{20,24},{2... | collective-permute-start | bytes 1277960 | tf_op jit(solution)/shard_map/up/ppermute | solution.py:71
  104.4 12.5 %collective-permute-start.22 = (bf16[2,32,3328]{2,1,0:T(8,128)(2,1)S(1)}, bf16[2,32,3328]{2,1,0:T(8,128)(2,1)S(1)}, u32[]{:S(2)}, u32[]{:S(2)}) collective-permute-start(bf16[2,32,3328]{2,1,0:T(8,128)(2,1)S(1)} %fusion.1), channel_id=1, source_target_pairs={{4,0},{8,4},{5,1},{9,5},{6,2},{10,6},{7,3},{11,7},{20,16},{24,20},... | collective-permute-start | bytes 1277960 | tf_op jit(solution)/shard_map/down/ppermute | solution.py:77

commit v7 on v6

--- a/solution.py
+++ b/solution.py
@@ -6,6 +6,7 @@
 from jax.experimental import pallas as pl
 from jax.experimental.pallas import tpu as pltpu
 from jax.sharding import PartitionSpec as P
+
 
 CHUNKS = 2
 
@@ -57,25 +58,29 @@
 
 
 def line_reduce(part, n, p):
-    def block(d):
-        return lax.dynamic_index_in_dim(part, jnp.clip(d, 0, n - 1), 1, keepdims=False)
+    down = lax.optimization_barrier(part)
+
+    def block(d, src=part):
+        return lax.dynamic_index_in_dim(src, jnp.clip(d, 0, n - 1), 1, keepdims=False)
 
     def add(a, b):
         return (a.astype(jnp.float32) + b.astype(jnp.float32)).astype(jnp.bfloat16)
 
-    with jax.named_scope("up"):
-        origin = [lax.ppermute(part[:, n - r], "row", [(0, 1)]) for r in range(1, n)]
-        first = origin[0]
-        plus = origin[0]
-        for r in range(2, n):
-            sent = lax.ppermute(add(block(p + n - r), plus), "row", [(q, q + 1) for q in range(1, r)])
-            plus = origin[r - 1] + sent
-    with jax.named_scope("down"):
-        origin = [lax.ppermute(part[:, r - 1], "row", [(n - 1, n - 2)]) for r in range(1, n)]
-        minus = origin[0]
-        for r in range(2, n):
-            sent = lax.ppermute(add(block(p - n + r), minus), "row", [(q, q - 1) for q in range(n - r, n - 1)])
-            minus = origin[r - 1] + sent
+    origin = []
+    for r in range(1, n):
+        origin.append(lax.ppermute(part[:, n - r], "row", [(0, 1)]))
+    first = origin[0]
+    plus = origin[0]
+    for r in range(2, n):
+        sent = lax.ppermute(add(block(p + n - r), plus), "row", [(q, q + 1) for q in range(1, r)])
+        plus = origin[r - 1] + sent
+    origin = []
+    for r in range(1, n):
+        origin.append(lax.ppermute(down[:, r - 1], "row", [(n - 1, n - 2)]))
+    minus = origin[0]
+    for r in range(2, n):
+        sent = lax.ppermute(add(block(p - n + r, down), minus), "row", [(q, q - 1) for q in range(n - r, n - 1)])
+        minus = origin[r - 1] + sent
     return plus, minus, (first, origin[0])
 
 

time: 120 us -> 124 us (1.033)
  starting transfers between devices: 55 us -> 59.5 us
    ppermute x16, starting transfers between devices: 47.5 us -> 52 us  [the longest x6 43.3 us: line_reduce(): origin.append(lax.ppermute(part[:, n - r], 'row', [(0, 1)]))]
    convert_element_type x6 -> x8, other arithmetic: 3.06 us -> 3.07 us  [add(): return (a.astype(jnp.float32) + b.astype(jnp.float32)).astype(jnp.bfloat16)]
  transfers between devices with their start and end apart: 23 -> 23, of which waited for: 6 -> 6; matrix products, arithmetic and copies ran while one was open for 4% -> 5% of each run, Pallas kernels for 11% -> 10%
where the time goes in v7:
time: 124 us; the launch traced here: 123 us
  starting transfers between devices  59.5 us (48%)
  waiting for transfers between devices  30.4 us (25%)
  Pallas kernels  24.8 us (20%)
  other arithmetic  4.61 us (4%)
  local copies, waits for them, and re-layouts  3.22 us (3%)
    ppermute x6, starting transfers between devices, line_reduce(): origin.append(lax.ppermute(part[:, n - r], 'row', [(0, 1)]))  43.3 us
    pallas_call x2, Pallas kernels, project(): pl.pallas_call(kernel, out_shape=jax.ShapeDtypeStruct((2, t, width), x.dt...  24.8 us
    ppermute x6, waiting for transfers between devices, line_reduce(): origin.append(lax.ppermute(part[:, n - r], 'row', [(0, 1)]))  20.5 us
    ppermute x3, waiting for transfers between devices, gather_cols(): got = lax.ppermute(tokens, 'col', [(i, (i + s) % m) for i in range(m)])  5.37 us
    ppermute x6, starting transfers between devices, line_reduce(): origin.append(lax.ppermute(down[:, r - 1], 'row', [(n - 1, n - 2)]))  4.85 us
    ppermute x3, starting transfers between devices, gather_cols(): got = lax.ppermute(tokens, 'col', [(i, (i + s) % m) for i in range(m)])  4.71 us
    ppermute x4, waiting for transfers between devices, line_reduce(): lax.ppermute(add(block(p - n + r, down), minus), 'row', [(q, q - 1) for q...  4.44 us
    ppermute x4, starting transfers between devices, line_reduce(): lax.ppermute(add(block(p - n + r, down), minus), 'row', [(q, q - 1) for q...  3.94 us
  transfers between devices with their start and end apart: 23, of which 6 were waited for; matrix products, arithmetic and copies ran while one was open for 5% of the time, Pallas kernels for 10%

profile of v7, /device:TPU:0, one launch (start us, length us, event | category | flops | bytes accessed | tf_op | source)
XLA Modules:
  0.0 123.0 jit_solution(4392302216197996797)
XLA Ops:
  0.5 1.9 %collective-permute-start.2 = (bf16[32,2560]{1,0:T(8,128)(2,1)}, bf16[32,2560]{1,0:T(8,128)(2,1)S(1)}, u32[]{:S(2)}, u32[]{:S(2)}) collective-permute-start(bf16[32,2560]{1,0:T(8,128)(2,1)} %param.2), channel_id=1, source_target_pairs={{0,3},{1,0},{2,1},{3,2},{4,7},{5,4},{6,5},{7,6},{8,11},{9,8},{10,9... | collective-permute-start | bytes 491528 | tf_op jit(solution)/shard_map/ppermute | solution.py:20
  2.4 2.3 %collective-permute-start.1 = (bf16[32,2560]{1,0:T(8,128)(2,1)}, bf16[32,2560]{1,0:T(8,128)(2,1)S(1)}, u32[]{:S(2)}, u32[]{:S(2)}) collective-permute-start(bf16[32,2560]{1,0:T(8,128)(2,1)} %param.2), channel_id=1, source_target_pairs={{0,2},{1,3},{2,0},{3,1},{4,6},{5,7},{6,4},{7,5},{8,10},{9,11},{10,... | collective-permute-start | bytes 491528 | tf_op jit(solution)/shard_map/ppermute | solution.py:20
  4.8 1.0 bitcast_dynamic-update-slice_fusion.3
  5.8 5.4 %collective-permute-done.1 = bf16[32,2560]{1,0:T(8,128)(2,1)S(1)} collective-permute-done((bf16[32,2560]{1,0:T(8,128)(2,1)}, bf16[32,2560]{1,0:T(8,128)(2,1)S(1)}, u32[]{:S(2)}, u32[]{:S(2)}) %collective-permute-start.1) | collective-permute-done | bytes 163872 | tf_op jit(solution)/shard_map/ppermute | solution.py:20
  11.2 12.4 %shard_map.28 = bf16[2,128,3328]{2,1,0:T(8,128)(2,1)S(1)} custom-call(bf16[128,2560]{1,0:T(8,128)(2,1)S(1)} %bitcast.143, bf16[2,2560,6656]{2,1,0:T(8,128)(2,1)} %w_ref.3), custom_call_target="tpu_custom_call" | custom-call | flops 4362076160 | bytes 36438016 | tf_op jit(solution)/shard_map/pallas_call | solution.py:44
  23.6 1.0 slice_bitcast_fusion.11
  24.6 1.4 %collective-permute-start.10 = (bf16[2,32,3328]{2,1,0:T(8,128)(2,1)}, bf16[2,32,3328]{2,1,0:T(8,128)(2,1)}, u32[]{:S(2)}, u32[]{:S(2)}) collective-permute-start(bf16[2,32,3328]{2,1,0:T(8,128)(2,1)} %get-tuple-element.12), channel_id=1, source_target_pairs={{12,8},{13,9},{14,10},{15,11},{28,24},{29,25},{30,26},{31,27}} | collective-permute-start | bytes 1277960 | tf_op jit(solution)/shard_map/ppermute | solution.py:79
  26.0 1.0 slice_bitcast_fusion.14
  27.0 4.8 %collective-permute-start.5 = (bf16[2,32,3328]{2,1,0:T(8,128)(2,1)}, bf16[2,32,3328]{2,1,0:T(8,128)(2,1)}, u32[]{:S(2)}, u32[]{:S(2)}) collective-permute-start(bf16[2,32,3328]{2,1,0:T(8,128)(2,1)} %get-tuple-element.9), channel_id=1, source_target_pairs={{0,4},{1,5},{2,6},{3,7},{16,20},{17,21},{18,22},{19,23}} | collective-permute-start | bytes 1277960 | tf_op jit(solution)/shard_map/ppermute | solution.py:71
  32.5 0.7 collective-permute-start.8
  33.2 1.3 %collective-permute-start.4 = (bf16[2,32,3328]{2,1,0:T(8,128)(2,1)}, bf16[2,32,3328]{2,1,0:T(8,128)(2,1)S(1)}, u32[]{:S(2)}, u32[]{:S(2)}) collective-permute-start(bf16[2,32,3328]{2,1,0:T(8,128)(2,1)} %get-tuple-element.7), channel_id=1, source_target_pairs={{0,4},{1,5},{2,6},{3,7},{16,20},{17,21},{18,22},{19,23}} | collective-permute-start | bytes 1277960 | tf_op jit(solution)/shard_map/ppermute | solution.py:71
  34.5 1.3 %collective-permute-start.3 = (bf16[2,32,3328]{2,1,0:T(8,128)(2,1)S(1)}, bf16[2,32,3328]{2,1,0:T(8,128)(2,1)S(1)}, u32[]{:S(2)}, u32[]{:S(2)}) collective-permute-start(bf16[2,32,3328]{2,1,0:T(8,128)(2,1)S(1)} %get-tuple-element.8), channel_id=1, source_target_pairs={{0,4},{1,5},{2,6},{3,7},{16,20},{17,21},{18,22},{19,23}} | collective-permute-start | bytes 1277960 | tf_op jit(solution)/shard_map/ppermute | solution.py:71
  35.8 5.7 %collective-permute-done.5 = bf16[2,32,3328]{2,1,0:T(8,128)(2,1)} collective-permute-done((bf16[2,32,3328]{2,1,0:T(8,128)(2,1)}, bf16[2,32,3328]{2,1,0:T(8,128)(2,1)}, u32[]{:S(2)}, u32[]{:S(2)}) %collective-permute-start.5) | collective-permute-done | bytes 426016 | tf_op jit(solution)/shard_map/ppermute | solution.py:71
  41.6 12.4 %shard_map.29 = bf16[2,128,3328]{2,1,0:T(8,128)(2,1)S(1)} custom-call(bf16[128,2560]{1,0:T(8,128)(2,1)S(1)} %bitcast.144, bf16[2,2560,6656]{2,1,0:T(8,128)(2,1)} %w_ref.3), custom_call_target="tpu_custom_call" | custom-call | flops 4362076160 | bytes 36438016 | tf_op jit(solution)/shard_map/pallas_call | solution.py:44
  54.1 1.1 fusion.5
  55.2 0.7 collective-permute-start.11
  56.0 1.1 fusion.7
  57.1 0.7 collective-permute-start.6
  57.8 0.7 collective-permute-start.20
  58.7 0.7 collective-permute-start.19
  60.3 12.9 %collective-permute-start.15 = (bf16[2,32,3328]{2,1,0:T(8,128)(2,1)S(1)}, bf16[2,32,3328]{2,1,0:T(8,128)(2,1)S(1)}, u32[]{:S(2)}, u32[]{:S(2)}) collective-permute-start(bf16[2,32,3328]{2,1,0:T(8,128)(2,1)S(1)} %get-tuple-element.13), channel_id=1, source_target_pairs={{0,4},{1,5},{2,6},{3,7},{16,20},{17,21},{18,22},{19,23}} | collective-permute-start | bytes 1277960 | tf_op jit(solution)/shard_map/ppermute | solution.py:71
  73.3 6.9 %collective-permute-done.15 = bf16[2,32,3328]{2,1,0:T(8,128)(2,1)S(1)} collective-permute-done((bf16[2,32,3328]{2,1,0:T(8,128)(2,1)S(1)}, bf16[2,32,3328]{2,1,0:T(8,128)(2,1)S(1)}, u32[]{:S(2)}, u32[]{:S(2)}) %collective-permute-start.15) | collective-permute-done | bytes 426016 | tf_op jit(solution)/shard_map/ppermute | solution.py:71
  81.0 5.0 %collective-permute-start.14 = (bf16[2,32,3328]{2,1,0:T(8,128)(2,1)S(1)}, bf16[2,32,3328]{2,1,0:T(8,128)(2,1)S(1)}, u32[]{:S(2)}, u32[]{:S(2)}) collective-permute-start(bf16[2,32,3328]{2,1,0:T(8,128)(2,1)S(1)} %get-tuple-element.14), channel_id=1, source_target_pairs={{0,4},{1,5},{2,6},{3,7},{16,20},{17,21},{18,22},{19,23}} | collective-permute-start | bytes 1277960 | tf_op jit(solution)/shard_map/ppermute | solution.py:71
  86.1 0.7 collective-permute-start.16
  86.9 4.7 %collective-permute-done.14 = bf16[2,32,3328]{2,1,0:T(8,128)(2,1)S(1)} collective-permute-done((bf16[2,32,3328]{2,1,0:T(8,128)(2,1)S(1)}, bf16[2,32,3328]{2,1,0:T(8,128)(2,1)S(1)}, u32[]{:S(2)}, u32[]{:S(2)}) %collective-permute-start.14) | collective-permute-done | bytes 426016 | tf_op jit(solution)/shard_map/ppermute | solution.py:71
  91.7 1.3 %collective-permute-start.12 = (bf16[2,32,3328]{2,1,0:T(8,128)(2,1)S(1)}, bf16[2,32,3328]{2,1,0:T(8,128)(2,1)S(1)}, u32[]{:S(2)}, u32[]{:S(2)}) collective-permute-start(bf16[2,32,3328]{2,1,0:T(8,128)(2,1)S(1)} %fusion.6), channel_id=1, source_target_pairs={{4,0},{8,4},{5,1},{9,5},{6,2},{10,6},{7,3},{11,7},{20,16},{24,20},... | collective-permute-start | bytes 1277960 | tf_op jit(solution)/shard_map/ppermute | solution.py:82
  93.0 0.7 collective-permute-start.7
  93.8 17.9 %collective-permute-start.13 = (bf16[2,32,3328]{2,1,0:T(8,128)(2,1)S(1)}, bf16[2,32,3328]{2,1,0:T(8,128)(2,1)S(1)}, u32[]{:S(2)}, u32[]{:S(2)}) collective-permute-start(bf16[2,32,3328]{2,1,0:T(8,128)(2,1)S(1)} %get-tuple-element.15), channel_id=1, source_target_pairs={{0,4},{1,5},{2,6},{3,7},{16,20},{17,21},{18,22},{19,23}} | collective-permute-start | bytes 1277960 | tf_op jit(solution)/shard_map/ppermute | solution.py:71
  111.8 1.3 %collective-permute-start.22 = (bf16[2,32,3328]{2,1,0:T(8,128)(2,1)S(1)}, bf16[2,32,3328]{2,1,0:T(8,128)(2,1)S(1)}, u32[]{:S(2)}, u32[]{:S(2)}) collective-permute-start(bf16[2,32,3328]{2,1,0:T(8,128)(2,1)S(1)} %fusion.1), channel_id=1, source_target_pairs={{4,0},{8,4},{5,1},{9,5},{6,2},{10,6},{7,3},{11,7},{20,16},{24,20},... | collective-permute-start | bytes 1277960 | tf_op jit(solution)/shard_map/ppermute | solution.py:82
  114.2 3.2 %collective-permute-done.13 = bf16[2,32,3328]{2,1,0:T(8,128)(2,1)S(1)} collective-permute-done((bf16[2,32,3328]{2,1,0:T(8,128)(2,1)S(1)}, bf16[2,32,3328]{2,1,0:T(8,128)(2,1)S(1)}, u32[]{:S(2)}, u32[]{:S(2)}) %collective-permute-start.13) | collective-permute-done | bytes 426016 | tf_op jit(solution)/shard_map/ppermute | solution.py:71
  117.4 4.4 %collective-permute-done.22 = bf16[2,32,3328]{2,1,0:T(8,128)(2,1)S(1)} collective-permute-done((bf16[2,32,3328]{2,1,0:T(8,128)(2,1)S(1)}, bf16[2,32,3328]{2,1,0:T(8,128)(2,1)S(1)}, u32[]{:S(2)}, u32[]{:S(2)}) %collective-permute-start.22) | collective-permute-done | bytes 426016 | tf_op jit(solution)/shard_map/ppermute | solution.py:82
  122.2 0.8 pad_maximum_fusion
  (38 shorter events, 5.1 us)
Async XLA Ops:
  0.0 5.8 %collective-permute-start = (bf16[32,2560]{1,0:T(8,128)(2,1)}, bf16[32,2560]{1,0:T(8,128)(2,1)S(1)}, u32[]{:S(2)}, u32[]{:S(2)}) collective-permute-start(bf16[32,2560]{1,0:T(8,128)(2,1)} %param.2), channel_id=1, source_target_pairs={{0,1},{1,2},{2,3},{3,0},{4,5},{5,6},{6,7},{7,4},{8,9},{9,10},{10,1... | collective-permute-start | bytes 491528 | tf_op jit(solution)/shard_map/ppermute | solution.py:20
  0.5 10.7 %collective-permute-start.2 = (bf16[32,2560]{1,0:T(8,128)(2,1)}, bf16[32,2560]{1,0:T(8,128)(2,1)S(1)}, u32[]{:S(2)}, u32[]{:S(2)}) collective-permute-start(bf16[32,2560]{1,0:T(8,128)(2,1)} %param.2), channel_id=1, source_target_pairs={{0,3},{1,0},{2,1},{3,2},{4,7},{5,4},{6,5},{7,6},{8,11},{9,8},{10,9... | collective-permute-start | bytes 491528 | tf_op jit(solution)/shard_map/ppermute | solution.py:20
  2.4 8.7 %collective-permute-start.1 = (bf16[32,2560]{1,0:T(8,128)(2,1)}, bf16[32,2560]{1,0:T(8,128)(2,1)S(1)}, u32[]{:S(2)}, u32[]{:S(2)}) collective-permute-start(bf16[32,2560]{1,0:T(8,128)(2,1)} %param.2), channel_id=1, source_target_pairs={{0,2},{1,3},{2,0},{3,1},{4,6},{5,7},{6,4},{7,5},{8,10},{9,11},{10,... | collective-permute-start | bytes 491528 | tf_op jit(solution)/shard_map/ppermute | solution.py:20
  24.6 9.9 %collective-permute-start.10 = (bf16[2,32,3328]{2,1,0:T(8,128)(2,1)}, bf16[2,32,3328]{2,1,0:T(8,128)(2,1)}, u32[]{:S(2)}, u32[]{:S(2)}) collective-permute-start(bf16[2,32,3328]{2,1,0:T(8,128)(2,1)} %get-tuple-element.12), channel_id=1, source_target_pairs={{12,8},{13,9},{14,10},{15,11},{28,24},{29,25},{30,26},{31,27}} | collective-permute-start | bytes 1277960 | tf_op jit(solution)/shard_map/ppermute | solution.py:79
  27.0 14.5 %collective-permute-start.5 = (bf16[2,32,3328]{2,1,0:T(8,128)(2,1)}, bf16[2,32,3328]{2,1,0:T(8,128)(2,1)}, u32[]{:S(2)}, u32[]{:S(2)}) collective-permute-start(bf16[2,32,3328]{2,1,0:T(8,128)(2,1)} %get-tuple-element.9), channel_id=1, source_target_pairs={{0,4},{1,5},{2,6},{3,7},{16,20},{17,21},{18,22},{19,23}} | collective-permute-start | bytes 1277960 | tf_op jit(solution)/shard_map/ppermute | solution.py:71
  31.8 25.3 %collective-permute-start.9 = (bf16[2,32,3328]{2,1,0:T(8,128)(2,1)}, bf16[2,32,3328]{2,1,0:T(8,128)(2,1)S(1)}, u32[]{:S(2)}, u32[]{:S(2)}) collective-permute-start(bf16[2,32,3328]{2,1,0:T(8,128)(2,1)} %get-tuple-element.10), channel_id=1, source_target_pairs={{12,8},{13,9},{14,10},{15,11},{28,24},{29,25},{30,26},{31,27}} | collective-permute-start | bytes 1277960 | tf_op jit(solution)/shard_map/ppermute | solution.py:79
  32.5 61.3 %collective-permute-start.8 = (bf16[2,32,3328]{2,1,0:T(8,128)(2,1)S(1)}, bf16[2,32,3328]{2,1,0:T(8,128)(2,1)S(1)}, u32[]{:S(2)}, u32[]{:S(2)}) collective-permute-start(bf16[2,32,3328]{2,1,0:T(8,128)(2,1)S(1)} %get-tuple-element.11), channel_id=1, source_target_pairs={{12,8},{13,9},{14,10},{15,11},{28,24},{29,25},{30,26},{31,27}} | collective-permute-start | bytes 1277960 | tf_op jit(solution)/shard_map/ppermute | solution.py:79
  33.2 25.5 %collective-permute-start.4 = (bf16[2,32,3328]{2,1,0:T(8,128)(2,1)}, bf16[2,32,3328]{2,1,0:T(8,128)(2,1)S(1)}, u32[]{:S(2)}, u32[]{:S(2)}) collective-permute-start(bf16[2,32,3328]{2,1,0:T(8,128)(2,1)} %get-tuple-element.7), channel_id=1, source_target_pairs={{0,4},{1,5},{2,6},{3,7},{16,20},{17,21},{18,22},{19,23}} | collective-permute-start | bytes 1277960 | tf_op jit(solution)/shard_map/ppermute | solution.py:71
  34.5 77.2 %collective-permute-start.3 = (bf16[2,32,3328]{2,1,0:T(8,128)(2,1)S(1)}, bf16[2,32,3328]{2,1,0:T(8,128)(2,1)S(1)}, u32[]{:S(2)}, u32[]{:S(2)}) collective-permute-start(bf16[2,32,3328]{2,1,0:T(8,128)(2,1)S(1)} %get-tuple-element.8), channel_id=1, source_target_pairs={{0,4},{1,5},{2,6},{3,7},{16,20},{17,21},{18,22},{19,23}} | collective-permute-start | bytes 1277960 | tf_op jit(solution)/shard_map/ppermute | solution.py:71
  55.2 2.6 %collective-permute-start.11 = (bf16[2,32,3328]{2,1,0:T(8,128)(2,1)S(1)}, bf16[2,32,3328]{2,1,0:T(8,128)(2,1)S(1)}, u32[]{:S(2)}, u32[]{:S(2)}) collective-permute-start(bf16[2,32,3328]{2,1,0:T(8,128)(2,1)S(1)} %fusion.5), channel_id=1, source_target_pairs={{8,4},{9,5},{10,6},{11,7},{24,20},{25,21},{26,22},{27,23}} | collective-permute-start | bytes 1277960 | tf_op jit(solution)/shard_map/ppermute | solution.py:82
  57.1 2.3 %collective-permute-start.6 = (bf16[2,32,3328]{2,1,0:T(8,128)(2,1)S(1)}, bf16[2,32,3328]{2,1,0:T(8,128)(2,1)S(1)}, u32[]{:S(2)}, u32[]{:S(2)}) collective-permute-start(bf16[2,32,3328]{2,1,0:T(8,128)(2,1)S(1)} %fusion.7), channel_id=1, source_target_pairs={{4,8},{5,9},{6,10},{7,11},{20,24},{21,25},{22,26},{23,27}} | collective-permute-start | bytes 1277960 | tf_op jit(solution)/shard_map/ppermute | solution.py:75
  57.8 2.4 %collective-permute-start.20 = (bf16[2,32,3328]{2,1,0:T(8,128)(2,1)S(1)}, bf16[2,32,3328]{2,1,0:T(8,128)(2,1)S(1)}, u32[]{:S(2)}, u32[]{:S(2)}) collective-permute-start(bf16[2,32,3328]{2,1,0:T(8,128)(2,1)S(1)} %get-tuple-element.16), channel_id=1, source_target_pairs={{12,8},{13,9},{14,10},{15,11},{28,24},{29,25},{30,26},{31,27}} | collective-permute-start | bytes 1277960 | tf_op jit(solution)/shard_map/ppermute | solution.py:79
  58.7 22.3 %collective-permute-start.19 = (bf16[2,32,3328]{2,1,0:T(8,128)(2,1)S(1)}, bf16[2,32,3328]{2,1,0:T(8,128)(2,1)S(1)}, u32[]{:S(2)}, u32[]{:S(2)}) collective-permute-start(bf16[2,32,3328]{2,1,0:T(8,128)(2,1)S(1)} %get-tuple-element.17), channel_id=1, source_target_pairs={{12,8},{13,9},{14,10},{15,11},{28,24},{29,25},{30,26},{31,27}} | collective-permute-start | bytes 1277960 | tf_op jit(solution)/shard_map/ppermute | solution.py:79
  59.4 54.8 %collective-permute-start.18 = (bf16[2,32,3328]{2,1,0:T(8,128)(2,1)S(1)}, bf16[2,32,3328]{2,1,0:T(8,128)(2,1)S(1)}, u32[]{:S(2)}, u32[]{:S(2)}) collective-permute-start(bf16[2,32,3328]{2,1,0:T(8,128)(2,1)S(1)} %get-tuple-element.18), channel_id=1, source_target_pairs={{12,8},{13,9},{14,10},{15,11},{28,24},{29,25},{30,26},{31,27}} | collective-permute-start | bytes 1277960 | tf_op jit(solution)/shard_map/ppermute | solution.py:79
  60.3 20.0 %collective-permute-start.15 = (bf16[2,32,3328]{2,1,0:T(8,128)(2,1)S(1)}, bf16[2,32,3328]{2,1,0:T(8,128)(2,1)S(1)}, u32[]{:S(2)}, u32[]{:S(2)}) collective-permute-start(bf16[2,32,3328]{2,1,0:T(8,128)(2,1)S(1)} %get-tuple-element.13), channel_id=1, source_target_pairs={{0,4},{1,5},{2,6},{3,7},{16,20},{17,21},{18,22},{19,23}} | collective-permute-start | bytes 1277960 | tf_op jit(solution)/shard_map/ppermute | solution.py:71
  80.2 5.8 %collective-permute-start.21 = (bf16[2,32,3328]{2,1,0:T(8,128)(2,1)S(1)}, bf16[2,32,3328]{2,1,0:T(8,128)(2,1)S(1)}, u32[]{:S(2)}, u32[]{:S(2)}) collective-permute-start(bf16[2,32,3328]{2,1,0:T(8,128)(2,1)S(1)} %fusion), channel_id=1, source_target_pairs={{8,4},{9,5},{10,6},{11,7},{24,20},{25,21},{26,22},{27,23}} | collective-permute-start | bytes 1277960 | tf_op jit(solution)/shard_map/ppermute | solution.py:82
  81.0 10.6 %collective-permute-start.14 = (bf16[2,32,3328]{2,1,0:T(8,128)(2,1)S(1)}, bf16[2,32,3328]{2,1,0:T(8,128)(2,1)S(1)}, u32[]{:S(2)}, u32[]{:S(2)}) collective-permute-start(bf16[2,32,3328]{2,1,0:T(8,128)(2,1)S(1)} %get-tuple-element.14), channel_id=1, source_target_pairs={{0,4},{1,5},{2,6},{3,7},{16,20},{17,21},{18,22},{19,23}} | collective-permute-start | bytes 1277960 | tf_op jit(solution)/shard_map/ppermute | solution.py:71
  86.1 6.9 %collective-permute-start.16 = (bf16[2,32,3328]{2,1,0:T(8,128)(2,1)S(1)}, bf16[2,32,3328]{2,1,0:T(8,128)(2,1)S(1)}, u32[]{:S(2)}, u32[]{:S(2)}) collective-permute-start(bf16[2,32,3328]{2,1,0:T(8,128)(2,1)S(1)} %fusion.2), channel_id=1, source_target_pairs={{4,8},{5,9},{6,10},{7,11},{20,24},{21,25},{22,26},{23,27}} | collective-permute-start | bytes 1277960 | tf_op jit(solution)/shard_map/ppermute | solution.py:75
  91.7 21.4 %collective-permute-start.12 = (bf16[2,32,3328]{2,1,0:T(8,128)(2,1)S(1)}, bf16[2,32,3328]{2,1,0:T(8,128)(2,1)S(1)}, u32[]{:S(2)}, u32[]{:S(2)}) collective-permute-start(bf16[2,32,3328]{2,1,0:T(8,128)(2,1)S(1)} %fusion.6), channel_id=1, source_target_pairs={{4,0},{8,4},{5,1},{9,5},{6,2},{10,6},{7,3},{11,7},{20,16},{24,20},... | collective-permute-start | bytes 1277960 | tf_op jit(solution)/shard_map/ppermute | solution.py:82
  93.0 20.8 %collective-permute-start.7 = (bf16[2,32,3328]{2,1,0:T(8,128)(2,1)S(1)}, bf16[2,32,3328]{2,1,0:T(8,128)(2,1)S(1)}, u32[]{:S(2)}, u32[]{:S(2)}) collective-permute-start(bf16[2,32,3328]{2,1,0:T(8,128)(2,1)S(1)} %fusion.8), channel_id=1, source_target_pairs={{4,8},{8,12},{5,9},{9,13},{6,10},{10,14},{7,11},{11,15},{20,24},{2... | collective-permute-start | bytes 1277960 | tf_op jit(solution)/shard_map/ppermute | solution.py:75
  93.8 23.5 %collective-permute-start.13 = (bf16[2,32,3328]{2,1,0:T(8,128)(2,1)S(1)}, bf16[2,32,3328]{2,1,0:T(8,128)(2,1)S(1)}, u32[]{:S(2)}, u32[]{:S(2)}) collective-permute-start(bf16[2,32,3328]{2,1,0:T(8,128)(2,1)S(1)} %get-tuple-element.15), channel_id=1, source_target_pairs={{0,4},{1,5},{2,6},{3,7},{16,20},{17,21},{18,22},{19,23}} | collective-permute-start | bytes 1277960 | tf_op jit(solution)/shard_map/ppermute | solution.py:71
  111.8 10.0 %collective-permute-start.22 = (bf16[2,32,3328]{2,1,0:T(8,128)(2,1)S(1)}, bf16[2,32,3328]{2,1,0:T(8,128)(2,1)S(1)}, u32[]{:S(2)}, u32[]{:S(2)}) collective-permute-start(bf16[2,32,3328]{2,1,0:T(8,128)(2,1)S(1)} %fusion.1), channel_id=1, source_target_pairs={{4,0},{8,4},{5,1},{9,5},{6,2},{10,6},{7,3},{11,7},{20,16},{24,20},... | collective-permute-start | bytes 1277960 | tf_op jit(solution)/shard_map/ppermute | solution.py:82
  113.1 8.7 %collective-permute-start.17 = (bf16[2,32,3328]{2,1,0:T(8,128)(2,1)S(1)}, bf16[2,32,3328]{2,1,0:T(8,128)(2,1)S(1)}, u32[]{:S(2)}, u32[]{:S(2)}) collective-permute-start(bf16[2,32,3328]{2,1,0:T(8,128)(2,1)S(1)} %fusion.3), channel_id=1, source_target_pairs={{4,8},{8,12},{5,9},{9,13},{6,10},{10,14},{7,11},{11,15},{20,24},{2... | collective-permute-start | bytes 1277960 | tf_op jit(solution)/shard_map/ppermute | solution.py:75

commit v8 on v4

--- a/solution.py
+++ b/solution.py
@@ -42,7 +42,7 @@
 
 def on_device(tokens, gate_up, n, m):
     p = lax.axis_index("row")
-    gathered = gather_cols(tokens, m)
+    gathered = lax.all_gather(tokens, "col", axis=0, tiled=True)
     t = gathered.shape[0]
     tb = t // n
     f = gate_up.shape[2]

time: 110 us -> 113 us (1.027)
  blocking collectives: 0 us -> 9.56 us
  starting transfers between devices: 49 us -> 43.3 us
    all_gather x0 -> x1, blocking collectives: none -> 9.56 us  [on_device(): gathered = lax.all_gather(tokens, 'col', axis=0, tiled=True)]
    ppermute x3 -> x0, waiting for transfers between devices: 5.37 us -> none  [gather_cols(): got = lax.ppermute(tokens, 'col', [(i, (i + s) % m) for i in range(m)])]
    ppermute x3 -> x0, starting transfers between devices: 4.71 us -> none  [gather_cols(): got = lax.ppermute(tokens, 'col', [(i, (i + s) % m) for i in range(m)])]
    ppermute x4, waiting for transfers between devices: 8.04 us -> 11 us  [line_reduce(): lax.ppermute(add(block(p - n + r), minus), 'row', [(q, q - 1) for q in ra...]
    ppermute x6, waiting for transfers between devices: 11.5 us -> 13.8 us  [line_reduce(): origin = [lax.ppermute(part[n - r], 'row', [(0, 1)]) for r in range(1, n)]]
  transfers between devices with their start and end apart: 23 -> 20, of which waited for: 6 -> 5; matrix products, arithmetic and copies ran while one was open for 17% -> 16% of each run, Pallas kernels for 0% -> 0%
where the time goes in v8:
time: 113 us
  starting transfers between devices  43.3 us (38%)
  matrix products  26.9 us (24%)
  waiting for transfers between devices  24.9 us (22%)
  blocking collectives  9.56 us (8%)
  other arithmetic  5.76 us (5%)
  local copies, waits for them, and re-layouts  1.9 us (2%)
    ppermute x6, starting transfers between devices, line_reduce(): origin = [lax.ppermute(part[n - r], 'row', [(0, 1)]) for r in range(1, n)]  31.7 us
    dot_general x2, matrix products, on_device(): jnp.einsum('td,gdf->tgf', held, w, preferred_element_type=jnp.float32)  26.9 us
    ppermute x6, waiting for transfers between devices, line_reduce(): origin = [lax.ppermute(part[n - r], 'row', [(0, 1)]) for r in range(1, n)]  13.8 us
    ppermute x4, waiting for transfers between devices, line_reduce(): lax.ppermute(add(block(p - n + r), minus), 'row', [(q, q - 1) for q in ra...  11 us
    all_gather x1, blocking collectives, on_device(): gathered = lax.all_gather(tokens, 'col', axis=0, tiled=True)  9.56 us
    ppermute x6, starting transfers between devices, line_reduce(): lax.ppermute(part[r - 1], 'row', [(n - 1, n - 2)])  4.84 us
    ppermute x4, starting transfers between devices, line_reduce(): lax.ppermute(add(block(p - n + r), minus), 'row', [(q, q - 1) for q in ra...  3.96 us
    convert_element_type x4, other arithmetic, add(): return (a.astype(jnp.float32) + b.astype(jnp.float32)).astype(jnp.bfloat16)  3.22 us
  transfers between devices with their start and end apart: 20, of which 5 were waited for; matrix products, arithmetic and copies ran while one was open for 16% of the time, Pallas kernels for 0%

profile of v8, /device:TPU:0, one launch (start us, length us, event | category | flops | bytes accessed | tf_op | source)
XLA Modules:
  0.0 112.6 jit_solution(8175538922295653616)
XLA Ops:
  0.0 9.6 %all_gather.3 = bf16[128,2560]{1,0:T(8,128)(2,1)S(1)} all-gather(bf16[32,2560]{1,0:T(8,128)(2,1)} %param.2), channel_id=1, replica_groups=mesh['grp'=2,'row'=4,'col'=4] {'col'}, dimensions={0}, use_global_device_ids=true | all-gather | bytes 819200 | tf_op jit(solution)/shard_map/all_gather | solution.py:45
  9.6 13.3 %fusion.4 = bf16[128,2,3328]{2,0,1:T(8,128)(2,1)S(1)} fusion(bf16[2,2560,6656]{2,1,0:T(8,128)(2,1)} %param.3, bf16[128,2560]{1,0:T(8,128)(2,1)S(1)} %all_gather.3), kind=kOutput, calls=%fused_computation.4 | convolution fusion | flops 4362928128 | bytes 36438016 | tf_op jit(solution)/shard_map/td,gdf->tgf/dot_general | solution.py:57
  22.9 1.0 fusion.26
  24.6 4.3 %collective-permute-start.2 = (bf16[32,2,3328]{2,0,1:T(8,128)(2,1)S(1)}, bf16[32,2,3328]{2,0,1:T(8,128)(2,1)}, u32[]{:S(2)}, u32[]{:S(2)}) collective-permute-start(bf16[32,2,3328]{2,0,1:T(8,128)(2,1)S(1)} %get-tuple-element.13), channel_id=1, source_target_pairs={{0,4},{1,5},{2,6},{3,7},{16,20},{17,21},{18,22},{19,23}} | collective-permute-start | bytes 1277960 | tf_op jit(solution)/shard_map/up/ppermute | solution.py:28
  28.9 1.4 %collective-permute-start.6 = (bf16[32,2,3328]{2,0,1:T(8,128)(2,1)}, bf16[32,2,3328]{2,0,1:T(8,128)(2,1)}, u32[]{:S(2)}, u32[]{:S(2)}) collective-permute-start(bf16[32,2,3328]{2,0,1:T(8,128)(2,1)} %get-tuple-element.11), channel_id=1, source_target_pairs={{12,8},{13,9},{14,10},{15,11},{28,24},{29,25},{30,26},{31,27}} | collective-permute-start | bytes 1277960 | tf_op jit(solution)/shard_map/down/ppermute | solution.py:35
  30.3 2.0 %collective-permute-start = (bf16[32,2,3328]{2,0,1:T(8,128)(2,1)}, bf16[32,2,3328]{2,0,1:T(8,128)(2,1)}, u32[]{:S(2)}, u32[]{:S(2)}) collective-permute-start(bf16[32,2,3328]{2,0,1:T(8,128)(2,1)} %get-tuple-element.11), channel_id=1, source_target_pairs={{0,4},{1,5},{2,6},{3,7},{16,20},{17,21},{18,22},{19,23}} | collective-permute-start | bytes 1277960 | tf_op jit(solution)/shard_map/up/ppermute | solution.py:28
  32.4 2.1 %collective-permute-start.1 = (bf16[32,2,3328]{2,0,1:T(8,128)(2,1)}, bf16[32,2,3328]{2,0,1:T(8,128)(2,1)}, u32[]{:S(2)}, u32[]{:S(2)}) collective-permute-start(bf16[32,2,3328]{2,0,1:T(8,128)(2,1)} %get-tuple-element.14), channel_id=1, source_target_pairs={{0,4},{1,5},{2,6},{3,7},{16,20},{17,21},{18,22},{19,23}} | collective-permute-start | bytes 1277960 | tf_op jit(solution)/shard_map/up/ppermute | solution.py:28
  34.4 0.8 copy-done.1
  35.2 3.1 %collective-permute-done.2 = bf16[32,2,3328]{2,0,1:T(8,128)(2,1)} collective-permute-done((bf16[32,2,3328]{2,0,1:T(8,128)(2,1)S(1)}, bf16[32,2,3328]{2,0,1:T(8,128)(2,1)}, u32[]{:S(2)}, u32[]{:S(2)}) %collective-permute-start.2) | collective-permute-done | bytes 426016 | tf_op jit(solution)/shard_map/up/ppermute | solution.py:28
  38.3 13.6 %fusion.7 = bf16[128,2,3328]{2,0,1:T(8,128)(2,1)S(1)} fusion(bf16[2,2560,6656]{2,1,0:T(8,128)(2,1)} %param.3, bf16[128,2560]{1,0:T(8,128)(2,1)} %copy-done), kind=kOutput, calls=%fused_computation.5 | convolution fusion | flops 4362928128 | bytes 36438016 | tf_op jit(solution)/shard_map/td,gdf->tgf/dot_general | solution.py:57
  52.0 4.5 %collective-permute-start.12 = (bf16[32,2,3328]{2,0,1:T(8,128)(2,1)S(1)}, bf16[32,2,3328]{2,0,1:T(8,128)(2,1)S(1)}, u32[]{:S(2)}, u32[]{:S(2)}) collective-permute-start(bf16[32,2,3328]{2,0,1:T(8,128)(2,1)S(1)} %get-tuple-element.19), channel_id=1, source_target_pairs={{0,4},{1,5},{2,6},{3,7},{16,20},{17,21},{18,22},{19,23}} | collective-permute-start | bytes 1277960 | tf_op jit(solution)/shard_map/up/ppermute | solution.py:28
  56.5 0.7 collective-permute-start.17
  57.2 1.2 %fusion.17 = (bf16[32,2,3328]{2,0,1:T(8,128)(2,1)S(1)}, bf16[32,2,3328]{2,0,1:T(8,128)(2,1)S(1)}) fusion(bf16[32,2,3328]{2,0,1:T(8,128)(2,1)} %collective-permute-done.2, bf16[4,32,2,3328]{3,1,0,2:T(8,128)(2,1)S(1)} %bitcast.78, s32[]{:T(128)S(6)} %min.18, bf16[32,2,3328]{2,0,1:T(8,128)(2,1)S(1)} %copy-done.2, s32[]{:T(128)S(6)} %min.20), kind=kLoop, calls=%fused_computation.21 | loop fusion | flops 1703936 | bytes 2555912 | tf_op jit(solution)/shard_map/up/convert_element_type | solution.py:25
  58.5 6.6 %collective-permute-done.12 = bf16[32,2,3328]{2,0,1:T(8,128)(2,1)S(1)} collective-permute-done((bf16[32,2,3328]{2,0,1:T(8,128)(2,1)S(1)}, bf16[32,2,3328]{2,0,1:T(8,128)(2,1)S(1)}, u32[]{:S(2)}, u32[]{:S(2)}) %collective-permute-start.12) | collective-permute-done | bytes 426016 | tf_op jit(solution)/shard_map/up/ppermute | solution.py:28
  65.1 0.7 collective-permute-start.3
  65.8 0.7 collective-permute-start.8
  66.7 5.6 %collective-permute-start.11 = (bf16[32,2,3328]{2,0,1:T(8,128)(2,1)S(1)}, bf16[32,2,3328]{2,0,1:T(8,128)(2,1)S(1)}, u32[]{:S(2)}, u32[]{:S(2)}) collective-permute-start(bf16[32,2,3328]{2,0,1:T(8,128)(2,1)S(1)} %get-tuple-element.21), channel_id=1, source_target_pairs={{0,4},{1,5},{2,6},{3,7},{16,20},{17,21},{18,22},{19,23}} | collective-permute-start | bytes 1277960 | tf_op jit(solution)/shard_map/up/ppermute | solution.py:28
  72.4 0.7 collective-permute-start.16
  73.1 0.7 collective-permute-start.13
  73.8 0.7 collective-permute-start.18
  74.5 1.5 %fusion.18 = (bf16[32,2,3328]{2,0,1:T(8,128)(2,1)S(1)}, bf16[32,2,3328]{2,0,1:T(8,128)(2,1)S(1)}) fusion(bf16[32,2,3328]{2,0,1:T(8,128)(2,1)} %collective-permute-done.1, bf16[32,2,3328]{2,0,1:T(8,128)(2,1)S(1)} %collective-permute-done.3, bf16[4,32,2,3328]{3,1,0,2:T(8,128)(2,1)S(1)} %bitcast.79, s32[]{:T(128)S(6)} %min.17, ...), kind=kLoop, calls=%fused_computation.23 | loop fusion | flops 2129920 | bytes 3407880 | tf_op jit(solution)/shard_map/up/convert_element_type | solution.py:25
  75.9 4.1 %collective-permute-done.11 = bf16[32,2,3328]{2,0,1:T(8,128)(2,1)S(1)} collective-permute-done((bf16[32,2,3328]{2,0,1:T(8,128)(2,1)S(1)}, bf16[32,2,3328]{2,0,1:T(8,128)(2,1)S(1)}, u32[]{:S(2)}, u32[]{:S(2)}) %collective-permute-start.11) | collective-permute-done | bytes 426016 | tf_op jit(solution)/shard_map/up/ppermute | solution.py:28
  80.7 0.7 collective-permute-start.15
  81.4 0.7 collective-permute-start.4
  82.1 1.3 %collective-permute-start.9 = (bf16[32,2,3328]{2,0,1:T(8,128)(2,1)S(1)}, bf16[32,2,3328]{2,0,1:T(8,128)(2,1)S(1)}, u32[]{:S(2)}, u32[]{:S(2)}) collective-permute-start(bf16[32,2,3328]{2,0,1:T(8,128)(2,1)S(1)} %get-tuple-element.8), channel_id=1, source_target_pairs={{4,0},{8,4},{5,1},{9,5},{6,2},{10,6},{7,3},{11,7},{20,16},{24,20},... | collective-permute-start | bytes 1277960 | tf_op jit(solution)/shard_map/down/ppermute | solution.py:38
  83.8 13.2 %collective-permute-start.10 = (bf16[32,2,3328]{2,0,1:T(8,128)(2,1)S(1)}, bf16[32,2,3328]{2,0,1:T(8,128)(2,1)S(1)}, u32[]{:S(2)}, u32[]{:S(2)}) collective-permute-start(bf16[32,2,3328]{2,0,1:T(8,128)(2,1)S(1)} %get-tuple-element.22), channel_id=1, source_target_pairs={{0,4},{1,5},{2,6},{3,7},{16,20},{17,21},{18,22},{19,23}} | collective-permute-start | bytes 1277960 | tf_op jit(solution)/shard_map/up/ppermute | solution.py:28
  97.0 0.7 collective-permute-start.14
  97.7 1.3 %collective-permute-start.19 = (bf16[32,2,3328]{2,0,1:T(8,128)(2,1)S(1)}, bf16[32,2,3328]{2,0,1:T(8,128)(2,1)S(1)}, u32[]{:S(2)}, u32[]{:S(2)}) collective-permute-start(bf16[32,2,3328]{2,0,1:T(8,128)(2,1)S(1)} %get-tuple-element.16), channel_id=1, source_target_pairs={{4,0},{8,4},{5,1},{9,5},{6,2},{10,6},{7,3},{11,7},{20,16},{24,20},... | collective-permute-start | bytes 1277960 | tf_op jit(solution)/shard_map/down/ppermute | solution.py:38
  99.0 5.1 %collective-permute-done.9 = bf16[32,2,3328]{2,0,1:T(8,128)(2,1)S(1)} collective-permute-done((bf16[32,2,3328]{2,0,1:T(8,128)(2,1)S(1)}, bf16[32,2,3328]{2,0,1:T(8,128)(2,1)S(1)}, u32[]{:S(2)}, u32[]{:S(2)}) %collective-permute-start.9) | collective-permute-done | bytes 426016 | tf_op jit(solution)/shard_map/down/ppermute | solution.py:38
  104.1 1.3 %fusion.19 = f32[32,2,3328]{2,0,1:T(8,128)S(1)} fusion(bf16[32,2,3328]{2,0,1:T(8,128)(2,1)S(1)} %collective-permute-done.5, bf16[32,2,3328]{2,0,1:T(8,128)(2,1)S(1)} %collective-permute-done.9, bf16[32,2,3328]{2,0,1:T(8,128)(2,1)} %collective-permute-done, bf16[32,2,3328]{2,0,1:T(8,128)(2,1)S(1)} %collective-permute-done.4, ...), kind=kLoop, calls=%fused_computation.25 | loop fusion | flops 1490944 | bytes 2981892 | tf_op jit(solution)/shard_map/add | solution.py:63
  105.5 6.0 %collective-permute-done.19 = bf16[32,2,3328]{2,0,1:T(8,128)(2,1)S(1)} collective-permute-done((bf16[32,2,3328]{2,0,1:T(8,128)(2,1)S(1)}, bf16[32,2,3328]{2,0,1:T(8,128)(2,1)S(1)}, u32[]{:S(2)}, u32[]{:S(2)}) %collective-permute-start.19) | collective-permute-done | bytes 426016 | tf_op jit(solution)/shard_map/down/ppermute | solution.py:38
  111.8 0.8 pad_maximum_fusion
  (28 shorter events, 2.6 us)
Async XLA Ops:
  9.6 13.4 %copy-start = (bf16[128,2560]{1,0:T(8,128)(2,1)}, bf16[128,2560]{1,0:T(8,128)(2,1)S(1)}, u32[]{:S(2)}) copy-start(bf16[128,2560]{1,0:T(8,128)(2,1)S(1)} %all_gather.3) | copy-start | bytes 1966084
  23.9 10.5 %collective-permute-start.7 = (bf16[32,2,3328]{2,0,1:T(8,128)(2,1)S(1)}, bf16[32,2,3328]{2,0,1:T(8,128)(2,1)S(1)}, u32[]{:S(2)}, u32[]{:S(2)}) collective-permute-start(bf16[32,2,3328]{2,0,1:T(8,128)(2,1)S(1)} %get-tuple-element.12), channel_id=1, source_target_pairs={{12,8},{13,9},{14,10},{15,11},{28,24},{29,25},{30,26},{31,27}} | collective-permute-start | bytes 1277960 | tf_op jit(solution)/shard_map/down/ppermute | solution.py:35
  24.6 13.7 %collective-permute-start.2 = (bf16[32,2,3328]{2,0,1:T(8,128)(2,1)S(1)}, bf16[32,2,3328]{2,0,1:T(8,128)(2,1)}, u32[]{:S(2)}, u32[]{:S(2)}) collective-permute-start(bf16[32,2,3328]{2,0,1:T(8,128)(2,1)S(1)} %get-tuple-element.13), channel_id=1, source_target_pairs={{0,4},{1,5},{2,6},{3,7},{16,20},{17,21},{18,22},{19,23}} | collective-permute-start | bytes 1277960 | tf_op jit(solution)/shard_map/up/ppermute | solution.py:28
  28.9 37.8 %collective-permute-start.6 = (bf16[32,2,3328]{2,0,1:T(8,128)(2,1)}, bf16[32,2,3328]{2,0,1:T(8,128)(2,1)}, u32[]{:S(2)}, u32[]{:S(2)}) collective-permute-start(bf16[32,2,3328]{2,0,1:T(8,128)(2,1)} %get-tuple-element.11), channel_id=1, source_target_pairs={{12,8},{13,9},{14,10},{15,11},{28,24},{29,25},{30,26},{31,27}} | collective-permute-start | bytes 1277960 | tf_op jit(solution)/shard_map/down/ppermute | solution.py:35
  30.3 53.4 %collective-permute-start = (bf16[32,2,3328]{2,0,1:T(8,128)(2,1)}, bf16[32,2,3328]{2,0,1:T(8,128)(2,1)}, u32[]{:S(2)}, u32[]{:S(2)}) collective-permute-start(bf16[32,2,3328]{2,0,1:T(8,128)(2,1)} %get-tuple-element.11), channel_id=1, source_target_pairs={{0,4},{1,5},{2,6},{3,7},{16,20},{17,21},{18,22},{19,23}} | collective-permute-start | bytes 1277960 | tf_op jit(solution)/shard_map/up/ppermute | solution.py:28
  32.4 40.0 %collective-permute-start.1 = (bf16[32,2,3328]{2,0,1:T(8,128)(2,1)}, bf16[32,2,3328]{2,0,1:T(8,128)(2,1)}, u32[]{:S(2)}, u32[]{:S(2)}) collective-permute-start(bf16[32,2,3328]{2,0,1:T(8,128)(2,1)} %get-tuple-element.14), channel_id=1, source_target_pairs={{0,4},{1,5},{2,6},{3,7},{16,20},{17,21},{18,22},{19,23}} | collective-permute-start | bytes 1277960 | tf_op jit(solution)/shard_map/up/ppermute | solution.py:28
  34.4 0.8 copy-start.1
  51.9 5.4 %copy-start.2 = (bf16[32,2,3328]{2,0,1:T(8,128)(2,1)S(1)}, bf16[32,2,3328]{2,0,1:T(8,128)(2,1)}, u32[]{:S(2)}) copy-start(bf16[32,2,3328]{2,0,1:T(8,128)(2,1)} %copy-done.1) | copy-start | bytes 1277956
  52.0 13.1 %collective-permute-start.12 = (bf16[32,2,3328]{2,0,1:T(8,128)(2,1)S(1)}, bf16[32,2,3328]{2,0,1:T(8,128)(2,1)S(1)}, u32[]{:S(2)}, u32[]{:S(2)}) collective-permute-start(bf16[32,2,3328]{2,0,1:T(8,128)(2,1)S(1)} %get-tuple-element.19), channel_id=1, source_target_pairs={{0,4},{1,5},{2,6},{3,7},{16,20},{17,21},{18,22},{19,23}} | collective-permute-start | bytes 1277960 | tf_op jit(solution)/shard_map/up/ppermute | solution.py:28
  56.5 9.2 %collective-permute-start.17 = (bf16[32,2,3328]{2,0,1:T(8,128)(2,1)S(1)}, bf16[32,2,3328]{2,0,1:T(8,128)(2,1)S(1)}, u32[]{:S(2)}, u32[]{:S(2)}) collective-permute-start(bf16[32,2,3328]{2,0,1:T(8,128)(2,1)S(1)} %get-tuple-element.20), channel_id=1, source_target_pairs={{12,8},{13,9},{14,10},{15,11},{28,24},{29,25},{30,26},{31,27}} | collective-permute-start | bytes 1277960 | tf_op jit(solution)/shard_map/down/ppermute | solution.py:35
  65.1 8.0 %collective-permute-start.3 = (bf16[32,2,3328]{2,0,1:T(8,128)(2,1)S(1)}, bf16[32,2,3328]{2,0,1:T(8,128)(2,1)S(1)}, u32[]{:S(2)}, u32[]{:S(2)}) collective-permute-start(bf16[32,2,3328]{2,0,1:T(8,128)(2,1)S(1)} %get-tuple-element.9), channel_id=1, source_target_pairs={{4,8},{5,9},{6,10},{7,11},{20,24},{21,25},{22,26},{23,27}} | collective-permute-start | bytes 1277960 | tf_op jit(solution)/shard_map/up/ppermute | solution.py:32
  65.8 8.0 %collective-permute-start.8 = (bf16[32,2,3328]{2,0,1:T(8,128)(2,1)S(1)}, bf16[32,2,3328]{2,0,1:T(8,128)(2,1)S(1)}, u32[]{:S(2)}, u32[]{:S(2)}) collective-permute-start(bf16[32,2,3328]{2,0,1:T(8,128)(2,1)S(1)} %get-tuple-element.10), channel_id=1, source_target_pairs={{8,4},{9,5},{10,6},{11,7},{24,20},{25,21},{26,22},{27,23}} | collective-permute-start | bytes 1277960 | tf_op jit(solution)/shard_map/down/ppermute | solution.py:38
  66.7 13.3 %collective-permute-start.11 = (bf16[32,2,3328]{2,0,1:T(8,128)(2,1)S(1)}, bf16[32,2,3328]{2,0,1:T(8,128)(2,1)S(1)}, u32[]{:S(2)}, u32[]{:S(2)}) collective-permute-start(bf16[32,2,3328]{2,0,1:T(8,128)(2,1)S(1)} %get-tuple-element.21), channel_id=1, source_target_pairs={{0,4},{1,5},{2,6},{3,7},{16,20},{17,21},{18,22},{19,23}} | collective-permute-start | bytes 1277960 | tf_op jit(solution)/shard_map/up/ppermute | solution.py:28
  72.4 8.4 %collective-permute-start.16 = (bf16[32,2,3328]{2,0,1:T(8,128)(2,1)S(1)}, bf16[32,2,3328]{2,0,1:T(8,128)(2,1)S(1)}, u32[]{:S(2)}, u32[]{:S(2)}) collective-permute-start(bf16[32,2,3328]{2,0,1:T(8,128)(2,1)S(1)} %get-tuple-element.22), channel_id=1, source_target_pairs={{12,8},{13,9},{14,10},{15,11},{28,24},{29,25},{30,26},{31,27}} | collective-permute-start | bytes 1277960 | tf_op jit(solution)/shard_map/down/ppermute | solution.py:35
  73.1 8.4 %collective-permute-start.13 = (bf16[32,2,3328]{2,0,1:T(8,128)(2,1)S(1)}, bf16[32,2,3328]{2,0,1:T(8,128)(2,1)S(1)}, u32[]{:S(2)}, u32[]{:S(2)}) collective-permute-start(bf16[32,2,3328]{2,0,1:T(8,128)(2,1)S(1)} %get-tuple-element.17), channel_id=1, source_target_pairs={{4,8},{5,9},{6,10},{7,11},{20,24},{21,25},{22,26},{23,27}} | collective-permute-start | bytes 1277960 | tf_op jit(solution)/shard_map/up/ppermute | solution.py:32
  73.8 8.4 %collective-permute-start.18 = (bf16[32,2,3328]{2,0,1:T(8,128)(2,1)S(1)}, bf16[32,2,3328]{2,0,1:T(8,128)(2,1)S(1)}, u32[]{:S(2)}, u32[]{:S(2)}) collective-permute-start(bf16[32,2,3328]{2,0,1:T(8,128)(2,1)S(1)} %get-tuple-element.18), channel_id=1, source_target_pairs={{8,4},{9,5},{10,6},{11,7},{24,20},{25,21},{26,22},{27,23}} | collective-permute-start | bytes 1277960 | tf_op jit(solution)/shard_map/down/ppermute | solution.py:38
  80.0 16.9 %collective-permute-start.5 = (bf16[32,2,3328]{2,0,1:T(8,128)(2,1)}, bf16[32,2,3328]{2,0,1:T(8,128)(2,1)S(1)}, u32[]{:S(2)}, u32[]{:S(2)}) collective-permute-start(bf16[32,2,3328]{2,0,1:T(8,128)(2,1)} %get-tuple-element.14), channel_id=1, source_target_pairs={{12,8},{13,9},{14,10},{15,11},{28,24},{29,25},{30,26},{31,27}} | collective-permute-start | bytes 1277960 | tf_op jit(solution)/shard_map/down/ppermute | solution.py:35
  80.7 24.7 %collective-permute-start.15 = (bf16[32,2,3328]{2,0,1:T(8,128)(2,1)S(1)}, bf16[32,2,3328]{2,0,1:T(8,128)(2,1)S(1)}, u32[]{:S(2)}, u32[]{:S(2)}) collective-permute-start(bf16[32,2,3328]{2,0,1:T(8,128)(2,1)S(1)} %get-tuple-element.21), channel_id=1, source_target_pairs={{12,8},{13,9},{14,10},{15,11},{28,24},{29,25},{30,26},{31,27}} | collective-permute-start | bytes 1277960 | tf_op jit(solution)/shard_map/down/ppermute | solution.py:35
  81.4 16.2 %collective-permute-start.4 = (bf16[32,2,3328]{2,0,1:T(8,128)(2,1)S(1)}, bf16[32,2,3328]{2,0,1:T(8,128)(2,1)S(1)}, u32[]{:S(2)}, u32[]{:S(2)}) collective-permute-start(bf16[32,2,3328]{2,0,1:T(8,128)(2,1)S(1)} %get-tuple-element.7), channel_id=1, source_target_pairs={{4,8},{8,12},{5,9},{9,13},{6,10},{10,14},{7,11},{11,15},{20,24},{2... | collective-permute-start | bytes 1277960 | tf_op jit(solution)/shard_map/up/ppermute | solution.py:32
  82.1 21.9 %collective-permute-start.9 = (bf16[32,2,3328]{2,0,1:T(8,128)(2,1)S(1)}, bf16[32,2,3328]{2,0,1:T(8,128)(2,1)S(1)}, u32[]{:S(2)}, u32[]{:S(2)}) collective-permute-start(bf16[32,2,3328]{2,0,1:T(8,128)(2,1)S(1)} %get-tuple-element.8), channel_id=1, source_target_pairs={{4,0},{8,4},{5,1},{9,5},{6,2},{10,6},{7,3},{11,7},{20,16},{24,20},... | collective-permute-start | bytes 1277960 | tf_op jit(solution)/shard_map/down/ppermute | solution.py:38
  83.8 21.7 %collective-permute-start.10 = (bf16[32,2,3328]{2,0,1:T(8,128)(2,1)S(1)}, bf16[32,2,3328]{2,0,1:T(8,128)(2,1)S(1)}, u32[]{:S(2)}, u32[]{:S(2)}) collective-permute-start(bf16[32,2,3328]{2,0,1:T(8,128)(2,1)S(1)} %get-tuple-element.22), channel_id=1, source_target_pairs={{0,4},{1,5},{2,6},{3,7},{16,20},{17,21},{18,22},{19,23}} | collective-permute-start | bytes 1277960 | tf_op jit(solution)/shard_map/up/ppermute | solution.py:28
  97.0 8.5 %collective-permute-start.14 = (bf16[32,2,3328]{2,0,1:T(8,128)(2,1)S(1)}, bf16[32,2,3328]{2,0,1:T(8,128)(2,1)S(1)}, u32[]{:S(2)}, u32[]{:S(2)}) collective-permute-start(bf16[32,2,3328]{2,0,1:T(8,128)(2,1)S(1)} %get-tuple-element.15), channel_id=1, source_target_pairs={{4,8},{8,12},{5,9},{9,13},{6,10},{10,14},{7,11},{11,15},{20,24},{2... | collective-permute-start | bytes 1277960 | tf_op jit(solution)/shard_map/up/ppermute | solution.py:32
  97.7 13.7 %collective-permute-start.19 = (bf16[32,2,3328]{2,0,1:T(8,128)(2,1)S(1)}, bf16[32,2,3328]{2,0,1:T(8,128)(2,1)S(1)}, u32[]{:S(2)}, u32[]{:S(2)}) collective-permute-start(bf16[32,2,3328]{2,0,1:T(8,128)(2,1)S(1)} %get-tuple-element.16), channel_id=1, source_target_pairs={{4,0},{8,4},{5,1},{9,5},{6,2},{10,6},{7,3},{11,7},{20,16},{24,20},... | collective-permute-start | bytes 1277960 | tf_op jit(solution)/shard_map/down/ppermute | solution.py:38

commit v9 on v4

--- a/solution.py
+++ b/solution.py
@@ -18,8 +18,10 @@
 
 
 def line_reduce(part, n, p):
-    def block(d):
-        return lax.dynamic_index_in_dim(part, jnp.clip(d, 0, n - 1), 0, keepdims=False)
+    down = lax.optimization_barrier(part)
+
+    def block(d, src=part):
+        return lax.dynamic_index_in_dim(src, jnp.clip(d, 0, n - 1), 0, keepdims=False)
 
     def add(a, b):
         return (a.astype(jnp.float32) + b.astype(jnp.float32)).astype(jnp.bfloat16)
@@ -32,10 +34,10 @@
             sent = lax.ppermute(add(block(p + n - r), plus), "row", [(q, q + 1) for q in range(1, r)])
             plus = origin[r - 1] + sent
     with jax.named_scope("down"):
-        origin = [lax.ppermute(part[r - 1], "row", [(n - 1, n - 2)]) for r in range(1, n)]
+        origin = [lax.ppermute(down[r - 1], "row", [(n - 1, n - 2)]) for r in range(1, n)]
         minus = origin[0]
         for r in range(2, n):
-            sent = lax.ppermute(add(block(p - n + r), minus), "row", [(q, q - 1) for q in range(n - r, n - 1)])
+            sent = lax.ppermute(add(block(p - n + r, down), minus), "row", [(q, q - 1) for q in range(n - r, n - 1)])
             minus = origin[r - 1] + sent
     return plus, minus, (first, origin[0])
 

time: 110 us -> 137 us (1.25)
  waiting for transfers between devices: 24.9 us -> 38 us
  starting transfers between devices: 49 us -> 60.3 us
  other arithmetic: 4.77 us -> 6.62 us
    ppermute x6, waiting for transfers between devices: 11.5 us -> 28.2 us  [line_reduce(): origin = [lax.ppermute(part[n - r], 'row', [(0, 1)]) for r in range(1, n)]]
    ppermute x6, starting transfers between devices: 32.8 us -> 42.6 us  [line_reduce(): origin = [lax.ppermute(part[n - r], 'row', [(0, 1)]) for r in range(1, n)]]
    ppermute x10, waiting for transfers between devices: 8.05 us -> 4.45 us  [the longest x4 4.44 us: line_reduce(): lax.ppermute(add(block(p - n + r, down), minus), 'row', [(q, q - 1) for q...]
    convert_element_type x4 -> x8, other arithmetic: 2.23 us -> 3.95 us  [add(): return (a.astype(jnp.float32) + b.astype(jnp.float32)).astype(jnp.bfloat16)]
    ppermute x10, starting transfers between devices: 8.82 us -> 10.3 us  [the longest x6 5.62 us: line_reduce(): lax.ppermute(down[r - 1], 'row', [(n - 1, n - 2)])]
  transfers between devices with their start and end apart: 23 -> 23, of which waited for: 6 -> 6; matrix products, arithmetic and copies ran while one was open for 17% -> 16% of each run, Pallas kernels for 0% -> 0%
where the time goes in v9:
time: 137 us; the launch traced here: 136 us
  starting transfers between devices  60.3 us (44%)
  waiting for transfers between devices  38 us (28%)
  matrix products  26.9 us (20%)
  other arithmetic  6.62 us (5%)
  local copies, waits for them, and re-layouts  4.12 us (3%)
    ppermute x6, starting transfers between devices, line_reduce(): origin = [lax.ppermute(part[n - r], 'row', [(0, 1)]) for r in range(1, n)]  42.6 us
    ppermute x6, waiting for transfers between devices, line_reduce(): origin = [lax.ppermute(part[n - r], 'row', [(0, 1)]) for r in range(1, n)]  28.2 us
    dot_general x2, matrix products, on_device(): jnp.einsum('td,gdf->tgf', held, w, preferred_element_type=jnp.float32)  26.9 us
    ppermute x6, starting transfers between devices, line_reduce(): lax.ppermute(down[r - 1], 'row', [(n - 1, n - 2)])  5.62 us
    ppermute x3, waiting for transfers between devices, gather_cols(): got = lax.ppermute(tokens, 'col', [(i, (i + s) % m) for i in range(m)])  5.35 us
    ppermute x3, starting transfers between devices, gather_cols(): got = lax.ppermute(tokens, 'col', [(i, (i + s) % m) for i in range(m)])  4.71 us
    ppermute x4, starting transfers between devices, line_reduce(): lax.ppermute(add(block(p - n + r, down), minus), 'row', [(q, q - 1) for q...  4.67 us
    ppermute x4, waiting for transfers between devices, line_reduce(): lax.ppermute(add(block(p - n + r, down), minus), 'row', [(q, q - 1) for q...  4.44 us
  transfers between devices with their start and end apart: 23, of which 6 were waited for; matrix products, arithmetic and copies ran while one was open for 16% of the time, Pallas kernels for 0%

profile of v9, /device:TPU:0, one launch (start us, length us, event | category | flops | bytes accessed | tf_op | source)
XLA Modules:
  0.0 136.5 jit_solution(8684107925565505695)
XLA Ops:
  0.5 1.9 %collective-permute-start.2 = (bf16[32,2560]{1,0:T(8,128)(2,1)}, bf16[32,2560]{1,0:T(8,128)(2,1)S(1)}, u32[]{:S(2)}, u32[]{:S(2)}) collective-permute-start(bf16[32,2560]{1,0:T(8,128)(2,1)} %param.2), channel_id=1, source_target_pairs={{0,3},{1,0},{2,1},{3,2},{4,7},{5,4},{6,5},{7,6},{8,11},{9,8},{10,9... | collective-permute-start | bytes 491528 | tf_op jit(solution)/shard_map/ppermute | solution.py:15
  2.4 2.3 %collective-permute-start.1 = (bf16[32,2560]{1,0:T(8,128)(2,1)}, bf16[32,2560]{1,0:T(8,128)(2,1)S(1)}, u32[]{:S(2)}, u32[]{:S(2)}) collective-permute-start(bf16[32,2560]{1,0:T(8,128)(2,1)} %param.2), channel_id=1, source_target_pairs={{0,2},{1,3},{2,0},{3,1},{4,6},{5,7},{6,4},{7,5},{8,10},{9,11},{10,... | collective-permute-start | bytes 491528 | tf_op jit(solution)/shard_map/ppermute | solution.py:15
  4.8 1.0 bitcast_dynamic-update-slice_fusion.3
  5.8 5.3 %collective-permute-done.1 = bf16[32,2560]{1,0:T(8,128)(2,1)S(1)} collective-permute-done((bf16[32,2560]{1,0:T(8,128)(2,1)}, bf16[32,2560]{1,0:T(8,128)(2,1)S(1)}, u32[]{:S(2)}, u32[]{:S(2)}) %collective-permute-start.1) | collective-permute-done | bytes 163872 | tf_op jit(solution)/shard_map/ppermute | solution.py:15
  11.2 13.4 %fusion.4 = bf16[128,2,3328]{2,0,1:T(8,128)(2,1)S(1)} fusion(bf16[128,2560,1]{1,0,2:T(8,128)(2,1)S(1)} %bitcast.123, bf16[2,2560,6656]{2,1,0:T(8,128)(2,1)} %param.3), kind=kOutput, calls=%fused_computation.4 | convolution fusion | flops 4362928128 | bytes 36438016 | tf_op jit(solution)/shard_map/td,gdf->tgf/dot_general | solution.py:59
  24.6 1.0 slice_bitcast_fusion.8
  26.3 1.0 fusion.25
  27.3 1.4 %collective-permute-start.9 = (bf16[32,2,3328]{2,0,1:T(8,128)(2,1)}, bf16[32,2,3328]{2,0,1:T(8,128)(2,1)}, u32[]{:S(2)}, u32[]{:S(2)}) collective-permute-start(bf16[32,2,3328]{2,0,1:T(8,128)(2,1)} %get-tuple-element.10), channel_id=1, source_target_pairs={{12,8},{13,9},{14,10},{15,11},{28,24},{29,25},{30,26},{31,27}} | collective-permute-start | bytes 1277960 | tf_op jit(solution)/shard_map/down/ppermute | solution.py:37
  28.7 1.5 %collective-permute-start.8 = (bf16[32,2,3328]{2,0,1:T(8,128)(2,1)}, bf16[32,2,3328]{2,0,1:T(8,128)(2,1)}, u32[]{:S(2)}, u32[]{:S(2)}) collective-permute-start(bf16[32,2,3328]{2,0,1:T(8,128)(2,1)} %get-tuple-element.11), channel_id=1, source_target_pairs={{12,8},{13,9},{14,10},{15,11},{28,24},{29,25},{30,26},{31,27}} | collective-permute-start | bytes 1277960 | tf_op jit(solution)/shard_map/down/ppermute | solution.py:37
  30.1 4.8 %collective-permute-start.4 = (bf16[32,2,3328]{2,0,1:T(8,128)(2,1)}, bf16[32,2,3328]{2,0,1:T(8,128)(2,1)}, u32[]{:S(2)}, u32[]{:S(2)}) collective-permute-start(bf16[32,2,3328]{2,0,1:T(8,128)(2,1)} %get-tuple-element.7), channel_id=1, source_target_pairs={{0,4},{1,5},{2,6},{3,7},{16,20},{17,21},{18,22},{19,23}} | collective-permute-start | bytes 1277960 | tf_op jit(solution)/shard_map/up/ppermute | solution.py:30
  34.9 1.3 collective-permute-start.5
  36.2 2.1 %collective-permute-start.3 = (bf16[32,2,3328]{2,0,1:T(8,128)(2,1)}, bf16[32,2,3328]{2,0,1:T(8,128)(2,1)}, u32[]{:S(2)}, u32[]{:S(2)}) collective-permute-start(bf16[32,2,3328]{2,0,1:T(8,128)(2,1)} %get-tuple-element.9), channel_id=1, source_target_pairs={{0,4},{1,5},{2,6},{3,7},{16,20},{17,21},{18,22},{19,23}} | collective-permute-start | bytes 1277960 | tf_op jit(solution)/shard_map/up/ppermute | solution.py:30
  38.3 0.9 fusion.15
  39.2 14.5 %collective-permute-done.5 = bf16[32,2,3328]{2,0,1:T(8,128)(2,1)S(1)} collective-permute-done((bf16[32,2,3328]{2,0,1:T(8,128)(2,1)S(1)}, bf16[32,2,3328]{2,0,1:T(8,128)(2,1)S(1)}, u32[]{:S(2)}, u32[]{:S(2)}) %collective-permute-start.5) | collective-permute-done | bytes 426016 | tf_op jit(solution)/shard_map/up/ppermute | solution.py:30
  53.7 1.4 %collective-permute-start.11 = (bf16[32,2,3328]{2,0,1:T(8,128)(2,1)}, bf16[32,2,3328]{2,0,1:T(8,128)(2,1)}, u32[]{:S(2)}, u32[]{:S(2)}) collective-permute-start(bf16[32,2,3328]{2,0,1:T(8,128)(2,1)} %fusion.15), channel_id=1, source_target_pairs={{8,4},{9,5},{10,6},{11,7},{24,20},{25,21},{26,22},{27,23}} | collective-permute-start | bytes 1277960 | tf_op jit(solution)/shard_map/down/ppermute | solution.py:40
  55.1 13.6 %fusion.7 = bf16[128,2,3328]{2,0,1:T(8,128)(2,1)S(1)} fusion(bf16[2,2560,6656]{2,1,0:T(8,128)(2,1)} %param.3, bf16[128,2560]{1,0:T(8,128)(2,1)} %bitcast.124), kind=kOutput, calls=%fused_computation.5 | convolution fusion | flops 4362928128 | bytes 36438016 | tf_op jit(solution)/shard_map/td,gdf->tgf/dot_general | solution.py:59
  68.9 0.9 copy-done.2
  69.9 0.7 collective-permute-start.6
  71.3 1.3 fusion.16
  72.6 0.7 collective-permute-start.19
  74.0 1.2 fusion.18
  75.2 11.8 %collective-permute-start.15 = (bf16[32,2,3328]{2,0,1:T(8,128)(2,1)S(1)}, bf16[32,2,3328]{2,0,1:T(8,128)(2,1)S(1)}, u32[]{:S(2)}, u32[]{:S(2)}) collective-permute-start(bf16[32,2,3328]{2,0,1:T(8,128)(2,1)S(1)} %get-tuple-element.13), channel_id=1, source_target_pairs={{0,4},{1,5},{2,6},{3,7},{16,20},{17,21},{18,22},{19,23}} | collective-permute-start | bytes 1277960 | tf_op jit(solution)/shard_map/up/ppermute | solution.py:30
  87.1 6.9 %collective-permute-done.15 = bf16[32,2,3328]{2,0,1:T(8,128)(2,1)S(1)} collective-permute-done((bf16[32,2,3328]{2,0,1:T(8,128)(2,1)S(1)}, bf16[32,2,3328]{2,0,1:T(8,128)(2,1)S(1)}, u32[]{:S(2)}, u32[]{:S(2)}) %collective-permute-start.15) | collective-permute-done | bytes 426016 | tf_op jit(solution)/shard_map/up/ppermute | solution.py:30
  94.8 5.0 %collective-permute-start.14 = (bf16[32,2,3328]{2,0,1:T(8,128)(2,1)S(1)}, bf16[32,2,3328]{2,0,1:T(8,128)(2,1)S(1)}, u32[]{:S(2)}, u32[]{:S(2)}) collective-permute-start(bf16[32,2,3328]{2,0,1:T(8,128)(2,1)S(1)} %get-tuple-element.14), channel_id=1, source_target_pairs={{0,4},{1,5},{2,6},{3,7},{16,20},{17,21},{18,22},{19,23}} | collective-permute-start | bytes 1277960 | tf_op jit(solution)/shard_map/up/ppermute | solution.py:30
  100.7 4.7 %collective-permute-done.14 = bf16[32,2,3328]{2,0,1:T(8,128)(2,1)S(1)} collective-permute-done((bf16[32,2,3328]{2,0,1:T(8,128)(2,1)S(1)}, bf16[32,2,3328]{2,0,1:T(8,128)(2,1)S(1)}, u32[]{:S(2)}, u32[]{:S(2)}) %collective-permute-start.14) | collective-permute-done | bytes 426016 | tf_op jit(solution)/shard_map/up/ppermute | solution.py:30
  105.4 1.3 collective-permute-start.12
  107.6 17.6 %collective-permute-start.13 = (bf16[32,2,3328]{2,0,1:T(8,128)(2,1)S(1)}, bf16[32,2,3328]{2,0,1:T(8,128)(2,1)S(1)}, u32[]{:S(2)}, u32[]{:S(2)}) collective-permute-start(bf16[32,2,3328]{2,0,1:T(8,128)(2,1)S(1)} %get-tuple-element.15), channel_id=1, source_target_pairs={{0,4},{1,5},{2,6},{3,7},{16,20},{17,21},{18,22},{19,23}} | collective-permute-start | bytes 1277960 | tf_op jit(solution)/shard_map/up/ppermute | solution.py:30
  125.3 1.3 collective-permute-start.22
  127.3 1.4 %fusion.19 = f32[32,2,3328]{2,0,1:T(8,128)S(1)} fusion(bf16[32,2,3328]{2,0,1:T(8,128)(2,1)} %collective-permute-done.8, bf16[32,2,3328]{2,0,1:T(8,128)(2,1)S(1)} %collective-permute-done.12, bf16[32,2,3328]{2,0,1:T(8,128)(2,1)} %collective-permute-done.3, bf16[32,2,3328]{2,0,1:T(8,128)(2,1)S(1)} %collective-permute-done.7, ...), kind=kLoop, calls=%fused_computation.25 | loop fusion | flops 1490944 | bytes 2981892 | tf_op jit(solution)/shard_map/add | solution.py:65
  128.8 2.0 %collective-permute-done.13 = bf16[32,2,3328]{2,0,1:T(8,128)(2,1)S(1)} collective-permute-done((bf16[32,2,3328]{2,0,1:T(8,128)(2,1)S(1)}, bf16[32,2,3328]{2,0,1:T(8,128)(2,1)S(1)}, u32[]{:S(2)}, u32[]{:S(2)}) %collective-permute-start.13) | collective-permute-done | bytes 426016 | tf_op jit(solution)/shard_map/up/ppermute | solution.py:30
  130.9 4.4 %collective-permute-done.22 = bf16[32,2,3328]{2,0,1:T(8,128)(2,1)S(1)} collective-permute-done((bf16[32,2,3328]{2,0,1:T(8,128)(2,1)S(1)}, bf16[32,2,3328]{2,0,1:T(8,128)(2,1)S(1)}, u32[]{:S(2)}, u32[]{:S(2)}) %collective-permute-start.22) | collective-permute-done | bytes 426016 | tf_op jit(solution)/shard_map/down/ppermute | solution.py:40
  135.7 0.8 pad_maximum_fusion
  (44 shorter events, 6.7 us)
Async XLA Ops:
  0.0 5.8 %collective-permute-start = (bf16[32,2560]{1,0:T(8,128)(2,1)}, bf16[32,2560]{1,0:T(8,128)(2,1)S(1)}, u32[]{:S(2)}, u32[]{:S(2)}) collective-permute-start(bf16[32,2560]{1,0:T(8,128)(2,1)} %param.2), channel_id=1, source_target_pairs={{0,1},{1,2},{2,3},{3,0},{4,5},{5,6},{6,7},{7,4},{8,9},{9,10},{10,1... | collective-permute-start | bytes 491528 | tf_op jit(solution)/shard_map/ppermute | solution.py:15
  0.5 10.7 %collective-permute-start.2 = (bf16[32,2560]{1,0:T(8,128)(2,1)}, bf16[32,2560]{1,0:T(8,128)(2,1)S(1)}, u32[]{:S(2)}, u32[]{:S(2)}) collective-permute-start(bf16[32,2560]{1,0:T(8,128)(2,1)} %param.2), channel_id=1, source_target_pairs={{0,3},{1,0},{2,1},{3,2},{4,7},{5,4},{6,5},{7,6},{8,11},{9,8},{10,9... | collective-permute-start | bytes 491528 | tf_op jit(solution)/shard_map/ppermute | solution.py:15
  2.4 8.7 %collective-permute-start.1 = (bf16[32,2560]{1,0:T(8,128)(2,1)}, bf16[32,2560]{1,0:T(8,128)(2,1)S(1)}, u32[]{:S(2)}, u32[]{:S(2)}) collective-permute-start(bf16[32,2560]{1,0:T(8,128)(2,1)} %param.2), channel_id=1, source_target_pairs={{0,2},{1,3},{2,0},{3,1},{4,6},{5,7},{6,4},{7,5},{8,10},{9,11},{10,... | collective-permute-start | bytes 491528 | tf_op jit(solution)/shard_map/ppermute | solution.py:15
  11.2 13.4 %copy-start = (bf16[4,32,2560]{2,1,0:T(8,128)(2,1)}, bf16[4,32,2560]{2,1,0:T(8,128)(2,1)S(1)}, u32[]{:S(2)}) copy-start(bf16[4,32,2560]{2,1,0:T(8,128)(2,1)S(1)} %bitcast_dynamic-update-slice_fusion) | copy-start | bytes 1966084
  25.6 10.6 %collective-permute-start.10 = (bf16[32,2,3328]{2,0,1:T(8,128)(2,1)S(1)}, bf16[32,2,3328]{2,0,1:T(8,128)(2,1)S(1)}, u32[]{:S(2)}, u32[]{:S(2)}) collective-permute-start(bf16[32,2,3328]{2,0,1:T(8,128)(2,1)S(1)} %get-tuple-element.12), channel_id=1, source_target_pairs={{12,8},{13,9},{14,10},{15,11},{28,24},{29,25},{30,26},{31,27}} | collective-permute-start | bytes 1277960 | tf_op jit(solution)/shard_map/down/ppermute | solution.py:37
  27.3 42.6 %collective-permute-start.9 = (bf16[32,2,3328]{2,0,1:T(8,128)(2,1)}, bf16[32,2,3328]{2,0,1:T(8,128)(2,1)}, u32[]{:S(2)}, u32[]{:S(2)}) collective-permute-start(bf16[32,2,3328]{2,0,1:T(8,128)(2,1)} %get-tuple-element.10), channel_id=1, source_target_pairs={{12,8},{13,9},{14,10},{15,11},{28,24},{29,25},{30,26},{31,27}} | collective-permute-start | bytes 1277960 | tf_op jit(solution)/shard_map/down/ppermute | solution.py:37
  28.7 78.9 %collective-permute-start.8 = (bf16[32,2,3328]{2,0,1:T(8,128)(2,1)}, bf16[32,2,3328]{2,0,1:T(8,128)(2,1)}, u32[]{:S(2)}, u32[]{:S(2)}) collective-permute-start(bf16[32,2,3328]{2,0,1:T(8,128)(2,1)} %get-tuple-element.11), channel_id=1, source_target_pairs={{12,8},{13,9},{14,10},{15,11},{28,24},{29,25},{30,26},{31,27}} | collective-permute-start | bytes 1277960 | tf_op jit(solution)/shard_map/down/ppermute | solution.py:37
  30.1 42.5 %collective-permute-start.4 = (bf16[32,2,3328]{2,0,1:T(8,128)(2,1)}, bf16[32,2,3328]{2,0,1:T(8,128)(2,1)}, u32[]{:S(2)}, u32[]{:S(2)}) collective-permute-start(bf16[32,2,3328]{2,0,1:T(8,128)(2,1)} %get-tuple-element.7), channel_id=1, source_target_pairs={{0,4},{1,5},{2,6},{3,7},{16,20},{17,21},{18,22},{19,23}} | collective-permute-start | bytes 1277960 | tf_op jit(solution)/shard_map/up/ppermute | solution.py:30
  34.9 18.8 %collective-permute-start.5 = (bf16[32,2,3328]{2,0,1:T(8,128)(2,1)S(1)}, bf16[32,2,3328]{2,0,1:T(8,128)(2,1)S(1)}, u32[]{:S(2)}, u32[]{:S(2)}) collective-permute-start(bf16[32,2,3328]{2,0,1:T(8,128)(2,1)S(1)} %get-tuple-element.8), channel_id=1, source_target_pairs={{0,4},{1,5},{2,6},{3,7},{16,20},{17,21},{18,22},{19,23}} | collective-permute-start | bytes 1277960 | tf_op jit(solution)/shard_map/up/ppermute | solution.py:30
  36.2 89.0 %collective-permute-start.3 = (bf16[32,2,3328]{2,0,1:T(8,128)(2,1)}, bf16[32,2,3328]{2,0,1:T(8,128)(2,1)}, u32[]{:S(2)}, u32[]{:S(2)}) collective-permute-start(bf16[32,2,3328]{2,0,1:T(8,128)(2,1)} %get-tuple-element.9), channel_id=1, source_target_pairs={{0,4},{1,5},{2,6},{3,7},{16,20},{17,21},{18,22},{19,23}} | collective-permute-start | bytes 1277960 | tf_op jit(solution)/shard_map/up/ppermute | solution.py:30
  53.7 1.4 %copy-start.1 = (bf16[32,2,3328]{2,0,1:T(8,128)(2,1)}, bf16[32,2,3328]{2,0,1:T(8,128)(2,1)S(1)}, u32[]{:S(2)}) copy-start(bf16[32,2,3328]{2,0,1:T(8,128)(2,1)S(1)} %collective-permute-done.5) | copy-start | bytes 1277956
  53.7 16.9 %collective-permute-start.11 = (bf16[32,2,3328]{2,0,1:T(8,128)(2,1)}, bf16[32,2,3328]{2,0,1:T(8,128)(2,1)}, u32[]{:S(2)}, u32[]{:S(2)}) collective-permute-start(bf16[32,2,3328]{2,0,1:T(8,128)(2,1)} %fusion.15), channel_id=1, source_target_pairs={{8,4},{9,5},{10,6},{11,7},{24,20},{25,21},{26,22},{27,23}} | collective-permute-start | bytes 1277960 | tf_op jit(solution)/shard_map/down/ppermute | solution.py:40
  68.8 1.0 copy-start.2
  69.9 3.4 %collective-permute-start.6 = (bf16[32,2,3328]{2,0,1:T(8,128)(2,1)S(1)}, bf16[32,2,3328]{2,0,1:T(8,128)(2,1)S(1)}, u32[]{:S(2)}, u32[]{:S(2)}) collective-permute-start(bf16[32,2,3328]{2,0,1:T(8,128)(2,1)S(1)} %fusion.17), channel_id=1, source_target_pairs={{4,8},{5,9},{6,10},{7,11},{20,24},{21,25},{22,26},{23,27}} | collective-permute-start | bytes 1277960 | tf_op jit(solution)/shard_map/up/ppermute | solution.py:34
  70.6 4.6 %collective-permute-start.20 = (bf16[32,2,3328]{2,0,1:T(8,128)(2,1)S(1)}, bf16[32,2,3328]{2,0,1:T(8,128)(2,1)S(1)}, u32[]{:S(2)}, u32[]{:S(2)}) collective-permute-start(bf16[32,2,3328]{2,0,1:T(8,128)(2,1)S(1)} %get-tuple-element.16), channel_id=1, source_target_pairs={{12,8},{13,9},{14,10},{15,11},{28,24},{29,25},{30,26},{31,27}} | collective-permute-start | bytes 1277960 | tf_op jit(solution)/shard_map/down/ppermute | solution.py:37
  72.6 22.2 %collective-permute-start.19 = (bf16[32,2,3328]{2,0,1:T(8,128)(2,1)S(1)}, bf16[32,2,3328]{2,0,1:T(8,128)(2,1)S(1)}, u32[]{:S(2)}, u32[]{:S(2)}) collective-permute-start(bf16[32,2,3328]{2,0,1:T(8,128)(2,1)S(1)} %get-tuple-element.17), channel_id=1, source_target_pairs={{12,8},{13,9},{14,10},{15,11},{28,24},{29,25},{30,26},{31,27}} | collective-permute-start | bytes 1277960 | tf_op jit(solution)/shard_map/down/ppermute | solution.py:37
  73.3 55.5 %collective-permute-start.18 = (bf16[32,2,3328]{2,0,1:T(8,128)(2,1)S(1)}, bf16[32,2,3328]{2,0,1:T(8,128)(2,1)S(1)}, u32[]{:S(2)}, u32[]{:S(2)}) collective-permute-start(bf16[32,2,3328]{2,0,1:T(8,128)(2,1)S(1)} %get-tuple-element.18), channel_id=1, source_target_pairs={{12,8},{13,9},{14,10},{15,11},{28,24},{29,25},{30,26},{31,27}} | collective-permute-start | bytes 1277960 | tf_op jit(solution)/shard_map/down/ppermute | solution.py:37
  75.2 18.8 %collective-permute-start.15 = (bf16[32,2,3328]{2,0,1:T(8,128)(2,1)S(1)}, bf16[32,2,3328]{2,0,1:T(8,128)(2,1)S(1)}, u32[]{:S(2)}, u32[]{:S(2)}) collective-permute-start(bf16[32,2,3328]{2,0,1:T(8,128)(2,1)S(1)} %get-tuple-element.13), channel_id=1, source_target_pairs={{0,4},{1,5},{2,6},{3,7},{16,20},{17,21},{18,22},{19,23}} | collective-permute-start | bytes 1277960 | tf_op jit(solution)/shard_map/up/ppermute | solution.py:30
  94.0 5.8 %collective-permute-start.21 = (bf16[32,2,3328]{2,0,1:T(8,128)(2,1)S(1)}, bf16[32,2,3328]{2,0,1:T(8,128)(2,1)S(1)}, u32[]{:S(2)}, u32[]{:S(2)}) collective-permute-start(bf16[32,2,3328]{2,0,1:T(8,128)(2,1)S(1)} %fusion.10), channel_id=1, source_target_pairs={{8,4},{9,5},{10,6},{11,7},{24,20},{25,21},{26,22},{27,23}} | collective-permute-start | bytes 1277960 | tf_op jit(solution)/shard_map/down/ppermute | solution.py:40
  94.8 10.6 %collective-permute-start.14 = (bf16[32,2,3328]{2,0,1:T(8,128)(2,1)S(1)}, bf16[32,2,3328]{2,0,1:T(8,128)(2,1)S(1)}, u32[]{:S(2)}, u32[]{:S(2)}) collective-permute-start(bf16[32,2,3328]{2,0,1:T(8,128)(2,1)S(1)} %get-tuple-element.14), channel_id=1, source_target_pairs={{0,4},{1,5},{2,6},{3,7},{16,20},{17,21},{18,22},{19,23}} | collective-permute-start | bytes 1277960 | tf_op jit(solution)/shard_map/up/ppermute | solution.py:30
  99.9 6.9 %collective-permute-start.16 = (bf16[32,2,3328]{2,0,1:T(8,128)(2,1)S(1)}, bf16[32,2,3328]{2,0,1:T(8,128)(2,1)S(1)}, u32[]{:S(2)}, u32[]{:S(2)}) collective-permute-start(bf16[32,2,3328]{2,0,1:T(8,128)(2,1)S(1)} %fusion.12), channel_id=1, source_target_pairs={{4,8},{5,9},{6,10},{7,11},{20,24},{21,25},{22,26},{23,27}} | collective-permute-start | bytes 1277960 | tf_op jit(solution)/shard_map/up/ppermute | solution.py:34
  105.4 21.1 %collective-permute-start.12 = (bf16[32,2,3328]{2,0,1:T(8,128)(2,1)S(1)}, bf16[32,2,3328]{2,0,1:T(8,128)(2,1)S(1)}, u32[]{:S(2)}, u32[]{:S(2)}) collective-permute-start(bf16[32,2,3328]{2,0,1:T(8,128)(2,1)S(1)} %fusion.16), channel_id=1, source_target_pairs={{4,0},{8,4},{5,1},{9,5},{6,2},{10,6},{7,3},{11,7},{20,16},{24,20},... | collective-permute-start | bytes 1277960 | tf_op jit(solution)/shard_map/down/ppermute | solution.py:40
  106.7 20.5 %collective-permute-start.7 = (bf16[32,2,3328]{2,0,1:T(8,128)(2,1)S(1)}, bf16[32,2,3328]{2,0,1:T(8,128)(2,1)S(1)}, u32[]{:S(2)}, u32[]{:S(2)}) collective-permute-start(bf16[32,2,3328]{2,0,1:T(8,128)(2,1)S(1)} %fusion.18), channel_id=1, source_target_pairs={{4,8},{8,12},{5,9},{9,13},{6,10},{10,14},{7,11},{11,15},{20,24},{2... | collective-permute-start | bytes 1277960 | tf_op jit(solution)/shard_map/up/ppermute | solution.py:34
  107.6 23.3 %collective-permute-start.13 = (bf16[32,2,3328]{2,0,1:T(8,128)(2,1)S(1)}, bf16[32,2,3328]{2,0,1:T(8,128)(2,1)S(1)}, u32[]{:S(2)}, u32[]{:S(2)}) collective-permute-start(bf16[32,2,3328]{2,0,1:T(8,128)(2,1)S(1)} %get-tuple-element.15), channel_id=1, source_target_pairs={{0,4},{1,5},{2,6},{3,7},{16,20},{17,21},{18,22},{19,23}} | collective-permute-start | bytes 1277960 | tf_op jit(solution)/shard_map/up/ppermute | solution.py:30
  125.3 10.0 %collective-permute-start.22 = (bf16[32,2,3328]{2,0,1:T(8,128)(2,1)S(1)}, bf16[32,2,3328]{2,0,1:T(8,128)(2,1)S(1)}, u32[]{:S(2)}, u32[]{:S(2)}) collective-permute-start(bf16[32,2,3328]{2,0,1:T(8,128)(2,1)S(1)} %fusion.11), channel_id=1, source_target_pairs={{4,0},{8,4},{5,1},{9,5},{6,2},{10,6},{7,3},{11,7},{20,16},{24,20},... | collective-permute-start | bytes 1277960 | tf_op jit(solution)/shard_map/down/ppermute | solution.py:40
  126.6 8.7 %collective-permute-start.17 = (bf16[32,2,3328]{2,0,1:T(8,128)(2,1)S(1)}, bf16[32,2,3328]{2,0,1:T(8,128)(2,1)S(1)}, u32[]{:S(2)}, u32[]{:S(2)}) collective-permute-start(bf16[32,2,3328]{2,0,1:T(8,128)(2,1)S(1)} %fusion.13), channel_id=1, source_target_pairs={{4,8},{8,12},{5,9},{9,13},{6,10},{10,14},{7,11},{11,15},{20,24},{2... | collective-permute-start | bytes 1277960 | tf_op jit(solution)/shard_map/up/ppermute | solution.py:34

commit v10 on v4

--- a/solution.py
+++ b/solution.py
@@ -3,7 +3,7 @@
 from jax import lax
 from jax.sharding import PartitionSpec as P
 
-CHUNKS = 2
+SHARES = (2, 1)
 
 
 def gather_cols(tokens, m):
@@ -47,8 +47,9 @@
     tb = t // n
     f = gate_up.shape[2]
     units = f // 128
-    k = min(CHUNKS, units)
-    edges = [128 * (units * i // k) for i in range(k + 1)]
+    shares = SHARES[: max(1, min(len(SHARES), units))]
+    k = len(shares)
+    edges = [128 * (units * sum(shares[:i]) // sum(shares)) for i in range(k + 1)]
     edges[-1] = f
     outs = []
     held = gathered

time: 110 us -> 128 us (1.16); the launches traced: 109 us -> 126 us
  waiting for transfers between devices: 24.9 us -> 48.7 us
  starting transfers between devices: 49 us -> 42.4 us
    ppermute x6, waiting for transfers between devices: 11.5 us -> 30.7 us  [line_reduce(): origin = [lax.ppermute(part[n - r], 'row', [(0, 1)]) for r in range(1, n)]]
    ppermute x6, starting transfers between devices: 32.8 us -> 25.9 us  [line_reduce(): origin = [lax.ppermute(part[n - r], 'row', [(0, 1)]) for r in range(1, n)]]
    ppermute x4, waiting for transfers between devices: 8.04 us -> 12.6 us  [line_reduce(): lax.ppermute(add(block(p - n + r), minus), 'row', [(q, q - 1) for q in ra...]
  transfers between devices with their start and end apart: 23 -> 23, of which waited for: 6 -> 8; matrix products, arithmetic and copies ran while one was open for 17% -> 3% of each run, Pallas kernels for 0% -> 0%
where the time goes in v10:
time: 128 us; the launch traced here: 126 us
  waiting for transfers between devices  48.7 us (38%)
  starting transfers between devices  42.4 us (33%)
  matrix products  26.4 us (21%)
  local copies, waits for them, and re-layouts  4.07 us (3%)
  other arithmetic  3.64 us (3%)
    ppermute x6, waiting for transfers between devices, line_reduce(): origin = [lax.ppermute(part[n - r], 'row', [(0, 1)]) for r in range(1, n)]  30.7 us
    dot_general x2, matrix products, on_device(): jnp.einsum('td,gdf->tgf', held, w, preferred_element_type=jnp.float32)  26.4 us
    ppermute x6, starting transfers between devices, line_reduce(): origin = [lax.ppermute(part[n - r], 'row', [(0, 1)]) for r in range(1, n)]  25.9 us
    ppermute x4, waiting for transfers between devices, line_reduce(): lax.ppermute(add(block(p - n + r), minus), 'row', [(q, q - 1) for q in ra...  12.6 us
    ppermute x3, waiting for transfers between devices, gather_cols(): got = lax.ppermute(tokens, 'col', [(i, (i + s) % m) for i in range(m)])  5.37 us
    ppermute x6, starting transfers between devices, line_reduce(): lax.ppermute(part[r - 1], 'row', [(n - 1, n - 2)])  4.92 us
    ppermute x3, starting transfers between devices, gather_cols(): got = lax.ppermute(tokens, 'col', [(i, (i + s) % m) for i in range(m)])  4.71 us
    ppermute x4, starting transfers between devices, line_reduce(): lax.ppermute(add(block(p - n + r), minus), 'row', [(q, q - 1) for q in ra...  4.09 us
  transfers between devices with their start and end apart: 23, of which 8 were waited for; matrix products, arithmetic and copies ran while one was open for 3% of the time, Pallas kernels for 0%

profile of v10, /device:TPU:0, one launch (start us, length us, event | category | flops | bytes accessed | tf_op | source)
XLA Modules:
  0.0 125.6 jit_solution(7509280208086773462)
XLA Ops:
  0.5 1.9 %collective-permute-start.2 = (bf16[32,2560]{1,0:T(8,128)(2,1)}, bf16[32,2560]{1,0:T(8,128)(2,1)S(1)}, u32[]{:S(2)}, u32[]{:S(2)}) collective-permute-start(bf16[32,2560]{1,0:T(8,128)(2,1)} %param.2), channel_id=1, source_target_pairs={{0,3},{1,0},{2,1},{3,2},{4,7},{5,4},{6,5},{7,6},{8,11},{9,8},{10,9... | collective-permute-start | bytes 491528 | tf_op jit(solution)/shard_map/ppermute | solution.py:15
  2.4 2.3 %collective-permute-start.1 = (bf16[32,2560]{1,0:T(8,128)(2,1)}, bf16[32,2560]{1,0:T(8,128)(2,1)S(1)}, u32[]{:S(2)}, u32[]{:S(2)}) collective-permute-start(bf16[32,2560]{1,0:T(8,128)(2,1)} %param.2), channel_id=1, source_target_pairs={{0,2},{1,3},{2,0},{3,1},{4,6},{5,7},{6,4},{7,5},{8,10},{9,11},{10,... | collective-permute-start | bytes 491528 | tf_op jit(solution)/shard_map/ppermute | solution.py:15
  4.8 1.0 bitcast_dynamic-update-slice_fusion.3
  5.8 5.4 %collective-permute-done.1 = bf16[32,2560]{1,0:T(8,128)(2,1)S(1)} collective-permute-done((bf16[32,2560]{1,0:T(8,128)(2,1)}, bf16[32,2560]{1,0:T(8,128)(2,1)S(1)}, u32[]{:S(2)}, u32[]{:S(2)}) %collective-permute-start.1) | collective-permute-done | bytes 163872 | tf_op jit(solution)/shard_map/ppermute | solution.py:15
  11.2 16.6 %fusion.4 = bf16[128,2,4352]{2,0,1:T(8,128)(2,1)S(1)} fusion(bf16[128,2560,1]{1,0,2:T(8,128)(2,1)S(1)} %bitcast.93, bf16[2,2560,6656]{2,1,0:T(8,128)(2,1)} %param.3), kind=kOutput, calls=%fused_computation.4 | convolution fusion | flops 5705367552 | bytes 47448064 | tf_op jit(solution)/shard_map/td,gdf->tgf/dot_general | solution.py:58
  27.8 1.2 fusion.25
  29.0 0.7 collective-permute-start.10
  29.6 4.1 %collective-permute-start.5 = (bf16[32,2,4352]{2,0,1:T(8,128)(2,1)S(1)}, bf16[32,2,4352]{2,0,1:T(8,128)(2,1)S(1)}, u32[]{:S(2)}, u32[]{:S(2)}) collective-permute-start(bf16[32,2,4352]{2,0,1:T(8,128)(2,1)S(1)} %get-tuple-element.13), channel_id=1, source_target_pairs={{0,4},{1,5},{2,6},{3,7},{16,20},{17,21},{18,22},{19,23}} | collective-permute-start | bytes 1671176 | tf_op jit(solution)/shard_map/up/ppermute | solution.py:28
  33.7 10.4 %collective-permute-done.5 = bf16[32,2,4352]{2,0,1:T(8,128)(2,1)S(1)} collective-permute-done((bf16[32,2,4352]{2,0,1:T(8,128)(2,1)S(1)}, bf16[32,2,4352]{2,0,1:T(8,128)(2,1)S(1)}, u32[]{:S(2)}, u32[]{:S(2)}) %collective-permute-start.5) | collective-permute-done | bytes 557088 | tf_op jit(solution)/shard_map/up/ppermute | solution.py:28
  44.1 0.8 copy-done.5
  44.9 9.8 %fusion.7 = bf16[128,2,2304]{2,0,1:T(8,128)(2,1)S(1)} fusion(bf16[2,2560,6656]{2,1,0:T(8,128)(2,1)} %param.3, bf16[128,2560]{1,0:T(8,128)(2,1)} %bitcast.94), kind=kOutput, calls=%fused_computation.5 | convolution fusion | flops 3020488704 | bytes 25427968 | tf_op jit(solution)/shard_map/td,gdf->tgf/dot_general | solution.py:58
  54.7 1.0 fusion.26
  55.8 5.1 %collective-permute-start.15 = (bf16[32,2,2304]{2,0,1:T(8,128)(2,1)}, bf16[32,2,2304]{2,0,1:T(8,128)(2,1)}, u32[]{:S(2)}, u32[]{:S(2)}) collective-permute-start(bf16[32,2,2304]{2,0,1:T(8,128)(2,1)} %get-tuple-element.19), channel_id=1, source_target_pairs={{0,4},{1,5},{2,6},{3,7},{16,20},{17,21},{18,22},{19,23}} | collective-permute-start | bytes 884744 | tf_op jit(solution)/shard_map/up/ppermute | solution.py:28
  60.8 1.4 %collective-permute-start.20 = (bf16[32,2,2304]{2,0,1:T(8,128)(2,1)}, bf16[32,2,2304]{2,0,1:T(8,128)(2,1)}, u32[]{:S(2)}, u32[]{:S(2)}) collective-permute-start(bf16[32,2,2304]{2,0,1:T(8,128)(2,1)} %get-tuple-element.20), channel_id=1, source_target_pairs={{12,8},{13,9},{14,10},{15,11},{28,24},{29,25},{30,26},{31,27}} | collective-permute-start | bytes 884744 | tf_op jit(solution)/shard_map/down/ppermute | solution.py:35
  62.2 0.8 collective-permute-start.9
  63.0 1.3 %collective-permute-start.14 = (bf16[32,2,2304]{2,0,1:T(8,128)(2,1)}, bf16[32,2,2304]{2,0,1:T(8,128)(2,1)S(1)}, u32[]{:S(2)}, u32[]{:S(2)}) collective-permute-start(bf16[32,2,2304]{2,0,1:T(8,128)(2,1)} %get-tuple-element.21), channel_id=1, source_target_pairs={{0,4},{1,5},{2,6},{3,7},{16,20},{17,21},{18,22},{19,23}} | collective-permute-start | bytes 884744 | tf_op jit(solution)/shard_map/up/ppermute | solution.py:28
  65.0 2.1 %collective-permute-done.15 = bf16[32,2,2304]{2,0,1:T(8,128)(2,1)} collective-permute-done((bf16[32,2,2304]{2,0,1:T(8,128)(2,1)}, bf16[32,2,2304]{2,0,1:T(8,128)(2,1)}, u32[]{:S(2)}, u32[]{:S(2)}) %collective-permute-start.15) | collective-permute-done | bytes 294944 | tf_op jit(solution)/shard_map/up/ppermute | solution.py:28
  67.1 1.2 fusion.18
  70.0 1.0 collective-permute-done.14
  71.0 9.8 %collective-permute-start.3 = (bf16[32,2,4352]{2,0,1:T(8,128)(2,1)S(1)}, bf16[32,2,4352]{2,0,1:T(8,128)(2,1)S(1)}, u32[]{:S(2)}, u32[]{:S(2)}) collective-permute-start(bf16[32,2,4352]{2,0,1:T(8,128)(2,1)S(1)} %copy-done.2), channel_id=1, source_target_pairs={{0,4},{1,5},{2,6},{3,7},{16,20},{17,21},{18,22},{19,23}} | collective-permute-start | bytes 1671176 | tf_op jit(solution)/shard_map/up/ppermute | solution.py:28
  80.8 1.3 %collective-permute-start.4 = (bf16[32,2,4352]{2,0,1:T(8,128)(2,1)S(1)}, bf16[32,2,4352]{2,0,1:T(8,128)(2,1)S(1)}, u32[]{:S(2)}, u32[]{:S(2)}) collective-permute-start(bf16[32,2,4352]{2,0,1:T(8,128)(2,1)S(1)} %copy-done.1), channel_id=1, source_target_pairs={{0,4},{1,5},{2,6},{3,7},{16,20},{17,21},{18,22},{19,23}} | collective-permute-start | bytes 1671176 | tf_op jit(solution)/shard_map/up/ppermute | solution.py:28
  82.2 0.7 collective-permute-start.6
  82.9 0.8 collective-permute-start.11
  84.7 16.2 %collective-permute-done.4 = bf16[32,2,4352]{2,0,1:T(8,128)(2,1)S(1)} collective-permute-done((bf16[32,2,4352]{2,0,1:T(8,128)(2,1)S(1)}, bf16[32,2,4352]{2,0,1:T(8,128)(2,1)S(1)}, u32[]{:S(2)}, u32[]{:S(2)}) %collective-permute-start.4) | collective-permute-done | bytes 557088 | tf_op jit(solution)/shard_map/up/ppermute | solution.py:28
  100.8 4.4 %collective-permute-start.13 = (bf16[32,2,2304]{2,0,1:T(8,128)(2,1)S(1)}, bf16[32,2,2304]{2,0,1:T(8,128)(2,1)S(1)}, u32[]{:S(2)}, u32[]{:S(2)}) collective-permute-start(bf16[32,2,2304]{2,0,1:T(8,128)(2,1)S(1)} %copy-done.7), channel_id=1, source_target_pairs={{0,4},{1,5},{2,6},{3,7},{16,20},{17,21},{18,22},{19,23}} | collective-permute-start | bytes 884744 | tf_op jit(solution)/shard_map/up/ppermute | solution.py:28
  105.9 1.3 %collective-permute-start.22 = (bf16[32,2,2304]{2,0,1:T(8,128)(2,1)S(1)}, bf16[32,2,2304]{2,0,1:T(8,128)(2,1)S(1)}, u32[]{:S(2)}, u32[]{:S(2)}) collective-permute-start(bf16[32,2,2304]{2,0,1:T(8,128)(2,1)S(1)} %get-tuple-element.16), channel_id=1, source_target_pairs={{4,0},{8,4},{5,1},{9,5},{6,2},{10,6},{7,3},{11,7},{20,16},{24,20},... | collective-permute-start | bytes 884744 | tf_op jit(solution)/shard_map/down/ppermute | solution.py:38
  107.7 0.7 collective-permute-start.8
  108.4 1.1 collective-permute-done.13
  110.1 1.3 %collective-permute-start.12 = (bf16[32,2,4352]{2,0,1:T(8,128)(2,1)S(1)}, bf16[32,2,4352]{2,0,1:T(8,128)(2,1)S(1)}, u32[]{:S(2)}, u32[]{:S(2)}) collective-permute-start(bf16[32,2,4352]{2,0,1:T(8,128)(2,1)S(1)} %get-tuple-element.8), channel_id=1, source_target_pairs={{4,0},{8,4},{5,1},{9,5},{6,2},{10,6},{7,3},{11,7},{20,16},{24,20},... | collective-permute-start | bytes 1671176 | tf_op jit(solution)/shard_map/down/ppermute | solution.py:38
  111.4 6.3 %collective-permute-done.22 = bf16[32,2,2304]{2,0,1:T(8,128)(2,1)S(1)} collective-permute-done((bf16[32,2,2304]{2,0,1:T(8,128)(2,1)S(1)}, bf16[32,2,2304]{2,0,1:T(8,128)(2,1)S(1)}, u32[]{:S(2)}, u32[]{:S(2)}) %collective-permute-start.22) | collective-permute-done | bytes 294944 | tf_op jit(solution)/shard_map/down/ppermute | solution.py:38
  118.0 6.3 %collective-permute-done.12 = bf16[32,2,4352]{2,0,1:T(8,128)(2,1)S(1)} collective-permute-done((bf16[32,2,4352]{2,0,1:T(8,128)(2,1)S(1)}, bf16[32,2,4352]{2,0,1:T(8,128)(2,1)S(1)}, u32[]{:S(2)}, u32[]{:S(2)}) %collective-permute-start.12) | collective-permute-done | bytes 557088 | tf_op jit(solution)/shard_map/down/ppermute | solution.py:38
  124.8 0.8 pad_maximum_fusion
  (50 shorter events, 6.4 us)
Async XLA Ops:
  0.0 5.8 %collective-permute-start = (bf16[32,2560]{1,0:T(8,128)(2,1)}, bf16[32,2560]{1,0:T(8,128)(2,1)S(1)}, u32[]{:S(2)}, u32[]{:S(2)}) collective-permute-start(bf16[32,2560]{1,0:T(8,128)(2,1)} %param.2), channel_id=1, source_target_pairs={{0,1},{1,2},{2,3},{3,0},{4,5},{5,6},{6,7},{7,4},{8,9},{9,10},{10,1... | collective-permute-start | bytes 491528 | tf_op jit(solution)/shard_map/ppermute | solution.py:15
  0.5 10.7 %collective-permute-start.2 = (bf16[32,2560]{1,0:T(8,128)(2,1)}, bf16[32,2560]{1,0:T(8,128)(2,1)S(1)}, u32[]{:S(2)}, u32[]{:S(2)}) collective-permute-start(bf16[32,2560]{1,0:T(8,128)(2,1)} %param.2), channel_id=1, source_target_pairs={{0,3},{1,0},{2,1},{3,2},{4,7},{5,4},{6,5},{7,6},{8,11},{9,8},{10,9... | collective-permute-start | bytes 491528 | tf_op jit(solution)/shard_map/ppermute | solution.py:15
  2.4 8.7 %collective-permute-start.1 = (bf16[32,2560]{1,0:T(8,128)(2,1)}, bf16[32,2560]{1,0:T(8,128)(2,1)S(1)}, u32[]{:S(2)}, u32[]{:S(2)}) collective-permute-start(bf16[32,2560]{1,0:T(8,128)(2,1)} %param.2), channel_id=1, source_target_pairs={{0,2},{1,3},{2,0},{3,1},{4,6},{5,7},{6,4},{7,5},{8,10},{9,11},{10,... | collective-permute-start | bytes 491528 | tf_op jit(solution)/shard_map/ppermute | solution.py:15
  11.2 16.6 %copy-start = (bf16[4,32,2560]{2,1,0:T(8,128)(2,1)}, bf16[4,32,2560]{2,1,0:T(8,128)(2,1)S(1)}, u32[]{:S(2)}) copy-start(bf16[4,32,2560]{2,1,0:T(8,128)(2,1)S(1)} %bitcast_dynamic-update-slice_fusion) | copy-start | bytes 1966084
  29.0 4.8 %collective-permute-start.10 = (bf16[32,2,4352]{2,0,1:T(8,128)(2,1)S(1)}, bf16[32,2,4352]{2,0,1:T(8,128)(2,1)S(1)}, u32[]{:S(2)}, u32[]{:S(2)}) collective-permute-start(bf16[32,2,4352]{2,0,1:T(8,128)(2,1)S(1)} %get-tuple-element.12), channel_id=1, source_target_pairs={{12,8},{13,9},{14,10},{15,11},{28,24},{29,25},{30,26},{31,27}} | collective-permute-start | bytes 1671176 | tf_op jit(solution)/shard_map/down/ppermute | solution.py:35
  29.6 14.5 %collective-permute-start.5 = (bf16[32,2,4352]{2,0,1:T(8,128)(2,1)S(1)}, bf16[32,2,4352]{2,0,1:T(8,128)(2,1)S(1)}, u32[]{:S(2)}, u32[]{:S(2)}) collective-permute-start(bf16[32,2,4352]{2,0,1:T(8,128)(2,1)S(1)} %get-tuple-element.13), channel_id=1, source_target_pairs={{0,4},{1,5},{2,6},{3,7},{16,20},{17,21},{18,22},{19,23}} | collective-permute-start | bytes 1671176 | tf_op jit(solution)/shard_map/up/ppermute | solution.py:28
  33.7 10.4 %copy-start.3 = (bf16[32,2,4352]{2,0,1:T(8,128)(2,1)}, bf16[32,2,4352]{2,0,1:T(8,128)(2,1)S(1)}, u32[]{:S(2)}) copy-start(bf16[32,2,4352]{2,0,1:T(8,128)(2,1)S(1)} %collective-permute-done.10) | copy-start | bytes 1671172
  44.1 0.8 copy-start.5
  55.8 11.3 %collective-permute-start.15 = (bf16[32,2,2304]{2,0,1:T(8,128)(2,1)}, bf16[32,2,2304]{2,0,1:T(8,128)(2,1)}, u32[]{:S(2)}, u32[]{:S(2)}) collective-permute-start(bf16[32,2,2304]{2,0,1:T(8,128)(2,1)} %get-tuple-element.19), channel_id=1, source_target_pairs={{0,4},{1,5},{2,6},{3,7},{16,20},{17,21},{18,22},{19,23}} | collective-permute-start | bytes 884744 | tf_op jit(solution)/shard_map/up/ppermute | solution.py:28
  60.8 6.2 %collective-permute-start.20 = (bf16[32,2,2304]{2,0,1:T(8,128)(2,1)}, bf16[32,2,2304]{2,0,1:T(8,128)(2,1)}, u32[]{:S(2)}, u32[]{:S(2)}) collective-permute-start(bf16[32,2,2304]{2,0,1:T(8,128)(2,1)} %get-tuple-element.20), channel_id=1, source_target_pairs={{12,8},{13,9},{14,10},{15,11},{28,24},{29,25},{30,26},{31,27}} | collective-permute-start | bytes 884744 | tf_op jit(solution)/shard_map/down/ppermute | solution.py:35
  62.2 7.5 %copy-start.4 = (bf16[32,2,4352]{2,0,1:T(8,128)(2,1)S(1)}, bf16[32,2,4352]{2,0,1:T(8,128)(2,1)}, u32[]{:S(2)}) copy-start(bf16[32,2,4352]{2,0,1:T(8,128)(2,1)} %copy-done.3) | copy-start | bytes 1671172
  62.2 7.5 %copy-start.6 = (bf16[32,2,4352]{2,0,1:T(8,128)(2,1)S(1)}, bf16[32,2,4352]{2,0,1:T(8,128)(2,1)}, u32[]{:S(2)}) copy-start(bf16[32,2,4352]{2,0,1:T(8,128)(2,1)} %copy-done.5) | copy-start | bytes 1671172
  62.2 21.7 %collective-permute-start.9 = (bf16[32,2,4352]{2,0,1:T(8,128)(2,1)}, bf16[32,2,4352]{2,0,1:T(8,128)(2,1)S(1)}, u32[]{:S(2)}, u32[]{:S(2)}) collective-permute-start(bf16[32,2,4352]{2,0,1:T(8,128)(2,1)} %get-tuple-element.11), channel_id=1, source_target_pairs={{12,8},{13,9},{14,10},{15,11},{28,24},{29,25},{30,26},{31,27}} | collective-permute-start | bytes 1671176 | tf_op jit(solution)/shard_map/down/ppermute | solution.py:35
  63.0 8.0 %collective-permute-start.14 = (bf16[32,2,2304]{2,0,1:T(8,128)(2,1)}, bf16[32,2,2304]{2,0,1:T(8,128)(2,1)S(1)}, u32[]{:S(2)}, u32[]{:S(2)}) collective-permute-start(bf16[32,2,2304]{2,0,1:T(8,128)(2,1)} %get-tuple-element.21), channel_id=1, source_target_pairs={{0,4},{1,5},{2,6},{3,7},{16,20},{17,21},{18,22},{19,23}} | collective-permute-start | bytes 884744 | tf_op jit(solution)/shard_map/up/ppermute | solution.py:28
  64.3 16.4 %collective-permute-start.19 = (bf16[32,2,2304]{2,0,1:T(8,128)(2,1)}, bf16[32,2,2304]{2,0,1:T(8,128)(2,1)S(1)}, u32[]{:S(2)}, u32[]{:S(2)}) collective-permute-start(bf16[32,2,2304]{2,0,1:T(8,128)(2,1)} %get-tuple-element.22), channel_id=1, source_target_pairs={{12,8},{13,9},{14,10},{15,11},{28,24},{29,25},{30,26},{31,27}} | collective-permute-start | bytes 884744 | tf_op jit(solution)/shard_map/down/ppermute | solution.py:35
  68.3 13.9 %collective-permute-start.16 = (bf16[32,2,2304]{2,0,1:T(8,128)(2,1)S(1)}, bf16[32,2,2304]{2,0,1:T(8,128)(2,1)S(1)}, u32[]{:S(2)}, u32[]{:S(2)}) collective-permute-start(bf16[32,2,2304]{2,0,1:T(8,128)(2,1)S(1)} %get-tuple-element.17), channel_id=1, source_target_pairs={{4,8},{5,9},{6,10},{7,11},{20,24},{21,25},{22,26},{23,27}} | collective-permute-start | bytes 884744 | tf_op jit(solution)/shard_map/up/ppermute | solution.py:32
  69.0 13.9 %collective-permute-start.21 = (bf16[32,2,2304]{2,0,1:T(8,128)(2,1)S(1)}, bf16[32,2,2304]{2,0,1:T(8,128)(2,1)S(1)}, u32[]{:S(2)}, u32[]{:S(2)}) collective-permute-start(bf16[32,2,2304]{2,0,1:T(8,128)(2,1)S(1)} %get-tuple-element.18), channel_id=1, source_target_pairs={{8,4},{9,5},{10,6},{11,7},{24,20},{25,21},{26,22},{27,23}} | collective-permute-start | bytes 884744 | tf_op jit(solution)/shard_map/down/ppermute | solution.py:38
  69.7 1.3 %copy-start.2 = (bf16[32,2,4352]{2,0,1:T(8,128)(2,1)S(1)}, bf16[32,2,4352]{2,0,1:T(8,128)(2,1)}, u32[]{:S(2)}) copy-start(bf16[32,2,4352]{2,0,1:T(8,128)(2,1)} %get-tuple-element.11) | copy-start | bytes 1671172
  69.7 11.1 %copy-start.1 = (bf16[32,2,4352]{2,0,1:T(8,128)(2,1)S(1)}, bf16[32,2,4352]{2,0,1:T(8,128)(2,1)}, u32[]{:S(2)}) copy-start(bf16[32,2,4352]{2,0,1:T(8,128)(2,1)} %get-tuple-element.14) | copy-start | bytes 1671172
  71.0 47.0 %collective-permute-start.3 = (bf16[32,2,4352]{2,0,1:T(8,128)(2,1)S(1)}, bf16[32,2,4352]{2,0,1:T(8,128)(2,1)S(1)}, u32[]{:S(2)}, u32[]{:S(2)}) collective-permute-start(bf16[32,2,4352]{2,0,1:T(8,128)(2,1)S(1)} %copy-done.2), channel_id=1, source_target_pairs={{0,4},{1,5},{2,6},{3,7},{16,20},{17,21},{18,22},{19,23}} | collective-permute-start | bytes 1671176 | tf_op jit(solution)/shard_map/up/ppermute | solution.py:28
  80.8 20.0 %collective-permute-start.4 = (bf16[32,2,4352]{2,0,1:T(8,128)(2,1)S(1)}, bf16[32,2,4352]{2,0,1:T(8,128)(2,1)S(1)}, u32[]{:S(2)}, u32[]{:S(2)}) collective-permute-start(bf16[32,2,4352]{2,0,1:T(8,128)(2,1)S(1)} %copy-done.1), channel_id=1, source_target_pairs={{0,4},{1,5},{2,6},{3,7},{16,20},{17,21},{18,22},{19,23}} | collective-permute-start | bytes 1671176 | tf_op jit(solution)/shard_map/up/ppermute | solution.py:28
  82.2 23.1 %collective-permute-start.6 = (bf16[32,2,4352]{2,0,1:T(8,128)(2,1)S(1)}, bf16[32,2,4352]{2,0,1:T(8,128)(2,1)S(1)}, u32[]{:S(2)}, u32[]{:S(2)}) collective-permute-start(bf16[32,2,4352]{2,0,1:T(8,128)(2,1)S(1)} %get-tuple-element.9), channel_id=1, source_target_pairs={{4,8},{5,9},{6,10},{7,11},{20,24},{21,25},{22,26},{23,27}} | collective-permute-start | bytes 1671176 | tf_op jit(solution)/shard_map/up/ppermute | solution.py:32
  82.9 1.1 copy-start.8
  82.9 18.0 %copy-start.7 = (bf16[32,2,2304]{2,0,1:T(8,128)(2,1)S(1)}, bf16[32,2,2304]{2,0,1:T(8,128)(2,1)}, u32[]{:S(2)}) copy-start(bf16[32,2,2304]{2,0,1:T(8,128)(2,1)} %get-tuple-element.22) | copy-start | bytes 884740
  82.9 23.1 %collective-permute-start.11 = (bf16[32,2,4352]{2,0,1:T(8,128)(2,1)S(1)}, bf16[32,2,4352]{2,0,1:T(8,128)(2,1)S(1)}, u32[]{:S(2)}, u32[]{:S(2)}) collective-permute-start(bf16[32,2,4352]{2,0,1:T(8,128)(2,1)S(1)} %get-tuple-element.10), channel_id=1, source_target_pairs={{8,4},{9,5},{10,6},{11,7},{24,20},{25,21},{26,22},{27,23}} | collective-permute-start | bytes 1671176 | tf_op jit(solution)/shard_map/down/ppermute | solution.py:38
  84.0 23.7 %collective-permute-start.18 = (bf16[32,2,2304]{2,0,1:T(8,128)(2,1)S(1)}, bf16[32,2,2304]{2,0,1:T(8,128)(2,1)S(1)}, u32[]{:S(2)}, u32[]{:S(2)}) collective-permute-start(bf16[32,2,2304]{2,0,1:T(8,128)(2,1)S(1)} %copy-done.8), channel_id=1, source_target_pairs={{12,8},{13,9},{14,10},{15,11},{28,24},{29,25},{30,26},{31,27}} | collective-permute-start | bytes 884744 | tf_op jit(solution)/shard_map/down/ppermute | solution.py:35
  100.8 8.6 %collective-permute-start.13 = (bf16[32,2,2304]{2,0,1:T(8,128)(2,1)S(1)}, bf16[32,2,2304]{2,0,1:T(8,128)(2,1)S(1)}, u32[]{:S(2)}, u32[]{:S(2)}) collective-permute-start(bf16[32,2,2304]{2,0,1:T(8,128)(2,1)S(1)} %copy-done.7), channel_id=1, source_target_pairs={{0,4},{1,5},{2,6},{3,7},{16,20},{17,21},{18,22},{19,23}} | collective-permute-start | bytes 884744 | tf_op jit(solution)/shard_map/up/ppermute | solution.py:28
  105.2 4.9 %collective-permute-start.17 = (bf16[32,2,2304]{2,0,1:T(8,128)(2,1)S(1)}, bf16[32,2,2304]{2,0,1:T(8,128)(2,1)S(1)}, u32[]{:S(2)}, u32[]{:S(2)}) collective-permute-start(bf16[32,2,2304]{2,0,1:T(8,128)(2,1)S(1)} %get-tuple-element.15), channel_id=1, source_target_pairs={{4,8},{8,12},{5,9},{9,13},{6,10},{10,14},{7,11},{11,15},{20,24},{2... | collective-permute-start | bytes 884744 | tf_op jit(solution)/shard_map/up/ppermute | solution.py:32
  105.9 11.8 %collective-permute-start.22 = (bf16[32,2,2304]{2,0,1:T(8,128)(2,1)S(1)}, bf16[32,2,2304]{2,0,1:T(8,128)(2,1)S(1)}, u32[]{:S(2)}, u32[]{:S(2)}) collective-permute-start(bf16[32,2,2304]{2,0,1:T(8,128)(2,1)S(1)} %get-tuple-element.16), channel_id=1, source_target_pairs={{4,0},{8,4},{5,1},{9,5},{6,2},{10,6},{7,3},{11,7},{20,16},{24,20},... | collective-permute-start | bytes 884744 | tf_op jit(solution)/shard_map/down/ppermute | solution.py:38
  107.7 10.3 %collective-permute-start.8 = (bf16[32,2,4352]{2,0,1:T(8,128)(2,1)S(1)}, bf16[32,2,4352]{2,0,1:T(8,128)(2,1)S(1)}, u32[]{:S(2)}, u32[]{:S(2)}) collective-permute-start(bf16[32,2,4352]{2,0,1:T(8,128)(2,1)S(1)} %copy-done.1), channel_id=1, source_target_pairs={{12,8},{13,9},{14,10},{15,11},{28,24},{29,25},{30,26},{31,27}} | collective-permute-start | bytes 1671176 | tf_op jit(solution)/shard_map/down/ppermute | solution.py:35
  109.4 8.6 %collective-permute-start.7 = (bf16[32,2,4352]{2,0,1:T(8,128)(2,1)S(1)}, bf16[32,2,4352]{2,0,1:T(8,128)(2,1)S(1)}, u32[]{:S(2)}, u32[]{:S(2)}) collective-permute-start(bf16[32,2,4352]{2,0,1:T(8,128)(2,1)S(1)} %get-tuple-element.7), channel_id=1, source_target_pairs={{4,8},{8,12},{5,9},{9,13},{6,10},{10,14},{7,11},{11,15},{20,24},{2... | collective-permute-start | bytes 1671176 | tf_op jit(solution)/shard_map/up/ppermute | solution.py:32
  110.1 14.2 %collective-permute-start.12 = (bf16[32,2,4352]{2,0,1:T(8,128)(2,1)S(1)}, bf16[32,2,4352]{2,0,1:T(8,128)(2,1)S(1)}, u32[]{:S(2)}, u32[]{:S(2)}) collective-permute-start(bf16[32,2,4352]{2,0,1:T(8,128)(2,1)S(1)} %get-tuple-element.8), channel_id=1, source_target_pairs={{4,0},{8,4},{5,1},{9,5},{6,2},{10,6},{7,3},{11,7},{20,16},{24,20},... | collective-permute-start | bytes 1671176 | tf_op jit(solution)/shard_map/down/ppermute | solution.py:38

commit v11 on v10

--- a/solution.py
+++ b/solution.py
@@ -3,7 +3,7 @@
 from jax import lax
 from jax.sharding import PartitionSpec as P
 
-SHARES = (2, 1)
+SHARES = (1, 1, 1)
 
 
 def gather_cols(tokens, m):

time: 128 us -> 132 us (1.031); the launches traced: 126 us -> 132 us
  starting transfers between devices: 42.4 us -> 56.4 us
  waiting for transfers between devices: 48.7 us -> 42.8 us
  local copies, waits for them, and re-layouts: 4.07 us -> 1.3 us
  matrix products: 26.4 us -> 27.8 us
    ppermute x6 -> x9, waiting for transfers between devices: 30.7 us -> 17.6 us  [line_reduce(): origin = [lax.ppermute(part[n - r], 'row', [(0, 1)]) for r in range(1, n)]]
    ppermute x6 -> x9, starting transfers between devices: 25.9 us -> 36 us  [line_reduce(): origin = [lax.ppermute(part[n - r], 'row', [(0, 1)]) for r in range(1, n)]]
    ppermute x4 -> x6, waiting for transfers between devices: 12.6 us -> 19.8 us  [line_reduce(): lax.ppermute(add(block(p - n + r), minus), 'row', [(q, q - 1) for q in ra...]
    slice x2 -> x3, local copies, waits for them, and re-layouts: 2.19 us -> 0.26 us  [line_reduce(): origin = [lax.ppermute(part[n - r], 'row', [(0, 1)]) for r in range(1, n)]]
    ppermute x4 -> x6, starting transfers between devices: 4.09 us -> 5.89 us  [line_reduce(): lax.ppermute(add(block(p - n + r), minus), 'row', [(q, q - 1) for q in ra...]
    dot_general x2 -> x3, matrix products: 26.4 us -> 27.8 us  [on_device(): jnp.einsum('td,gdf->tgf', held, w, preferred_element_type=jnp.float32)]
    ppermute x4 -> x6, starting transfers between devices: 2.74 us -> 4.06 us  [line_reduce(): lax.ppermute(add(block(p + n - r), plus), 'row', [(q, q + 1) for q in ran...]
    ppermute x6 -> x9, starting transfers between devices: 4.92 us -> 6.07 us  [line_reduce(): lax.ppermute(part[r - 1], 'row', [(n - 1, n - 2)])]
  transfers between devices with their start and end apart: 23 -> 33, of which waited for: 8 -> 11; matrix products, arithmetic and copies ran while one was open for 3% -> 16% of each run, Pallas kernels for 0% -> 0%
where the time goes in v11:
time: 132 us
  starting transfers between devices  56.4 us (43%)
  waiting for transfers between devices  42.8 us (32%)
  matrix products  27.8 us (21%)
  other arithmetic  2.7 us (2%)
    ppermute x9, starting transfers between devices, line_reduce(): origin = [lax.ppermute(part[n - r], 'row', [(0, 1)]) for r in range(1, n)]  36 us
    dot_general x3, matrix products, on_device(): jnp.einsum('td,gdf->tgf', held, w, preferred_element_type=jnp.float32)  27.8 us
    ppermute x6, waiting for transfers between devices, line_reduce(): lax.ppermute(add(block(p - n + r), minus), 'row', [(q, q - 1) for q in ra...  19.8 us
    ppermute x9, waiting for transfers between devices, line_reduce(): origin = [lax.ppermute(part[n - r], 'row', [(0, 1)]) for r in range(1, n)]  17.6 us
    ppermute x9, starting transfers between devices, line_reduce(): lax.ppermute(part[r - 1], 'row', [(n - 1, n - 2)])  6.07 us
    ppermute x6, starting transfers between devices, line_reduce(): lax.ppermute(add(block(p - n + r), minus), 'row', [(q, q - 1) for q in ra...  5.89 us
    ppermute x3, waiting for transfers between devices, gather_cols(): got = lax.ppermute(tokens, 'col', [(i, (i + s) % m) for i in range(m)])  5.3 us
    ppermute x3, starting transfers between devices, gather_cols(): got = lax.ppermute(tokens, 'col', [(i, (i + s) % m) for i in range(m)])  4.43 us
  transfers between devices with their start and end apart: 33, of which 11 were waited for; matrix products, arithmetic and copies ran while one was open for 16% of the time, Pallas kernels for 0%

profile of v11, /device:TPU:0, one launch (start us, length us, event | category | flops | bytes accessed | tf_op | source)
XLA Modules:
  0.0 131.6 jit_solution(574773108133398986)
XLA Ops:
  0.5 2.5 %collective-permute-start.1 = (bf16[32,2560]{1,0:T(8,128)(2,1)}, bf16[32,2560]{1,0:T(8,128)(2,1)S(1)}, u32[]{:S(2)}, u32[]{:S(2)}) collective-permute-start(bf16[32,2560]{1,0:T(8,128)(2,1)} %param.2), channel_id=1, source_target_pairs={{0,2},{1,3},{2,0},{3,1},{4,6},{5,7},{6,4},{7,5},{8,10},{9,11},{10,... | collective-permute-start | bytes 491528 | tf_op jit(solution)/shard_map/ppermute | solution.py:15
  3.0 1.5 %collective-permute-start.2 = (bf16[32,2560]{1,0:T(8,128)(2,1)}, bf16[32,2560]{1,0:T(8,128)(2,1)S(1)}, u32[]{:S(2)}, u32[]{:S(2)}) collective-permute-start(bf16[32,2560]{1,0:T(8,128)(2,1)} %param.2), channel_id=1, source_target_pairs={{0,3},{1,0},{2,1},{3,2},{4,7},{5,4},{6,5},{7,6},{8,11},{9,8},{10,9... | collective-permute-start | bytes 491528 | tf_op jit(solution)/shard_map/ppermute | solution.py:15
  4.5 1.0 bitcast_dynamic-update-slice_fusion.3
  5.5 1.0 collective-permute-done
  6.5 1.7 %collective-permute-done.1 = bf16[32,2560]{1,0:T(8,128)(2,1)S(1)} collective-permute-done((bf16[32,2560]{1,0:T(8,128)(2,1)}, bf16[32,2560]{1,0:T(8,128)(2,1)S(1)}, u32[]{:S(2)}, u32[]{:S(2)}) %collective-permute-start.1) | collective-permute-done | bytes 163872 | tf_op jit(solution)/shard_map/ppermute | solution.py:15
  8.2 2.6 %collective-permute-done.2 = bf16[32,2560]{1,0:T(8,128)(2,1)S(1)} collective-permute-done((bf16[32,2560]{1,0:T(8,128)(2,1)}, bf16[32,2560]{1,0:T(8,128)(2,1)S(1)}, u32[]{:S(2)}, u32[]{:S(2)}) %collective-permute-start.2) | collective-permute-done | bytes 163872 | tf_op jit(solution)/shard_map/ppermute | solution.py:15
  10.8 9.1 %fusion.6 = bf16[128,2,2176]{2,0,1:T(8,128)(2,1)S(1)} fusion(bf16[128,2560,1]{1,0,2:T(8,128)(2,1)S(1)} %bitcast.135, bf16[2,2560,6656]{2,1,0:T(8,128)(2,1)} %param.3), kind=kOutput, calls=%fused_computation.6 | convolution fusion | flops 2852683776 | bytes 24051712 | tf_op jit(solution)/shard_map/td,gdf->tgf/dot_general | solution.py:58
  20.0 0.7 collective-permute-start.10
  20.7 3.5 %collective-permute-start.5 = (bf16[32,2,2176]{2,0,1:T(8,128)(2,1)S(1)}, bf16[32,2,2176]{2,0,1:T(8,128)(2,1)S(1)}, u32[]{:S(2)}, u32[]{:S(2)}) collective-permute-start(bf16[32,2,2176]{2,0,1:T(8,128)(2,1)S(1)} %get-tuple-element.23), channel_id=1, source_target_pairs={{0,4},{1,5},{2,6},{3,7},{16,20},{17,21},{18,22},{19,23}} | collective-permute-start | bytes 835592 | tf_op jit(solution)/shard_map/up/ppermute | solution.py:28
  24.9 1.3 collective-permute-start.3
  26.2 1.3 collective-permute-start.4
  27.5 3.7 %collective-permute-done.5 = bf16[32,2,2176]{2,0,1:T(8,128)(2,1)S(1)} collective-permute-done((bf16[32,2,2176]{2,0,1:T(8,128)(2,1)S(1)}, bf16[32,2,2176]{2,0,1:T(8,128)(2,1)S(1)}, u32[]{:S(2)}, u32[]{:S(2)}) %collective-permute-start.5) | collective-permute-done | bytes 278560 | tf_op jit(solution)/shard_map/up/ppermute | solution.py:28
  31.2 9.1 %fusion.9 = bf16[128,2,2176]{2,0,1:T(8,128)(2,1)S(1)} fusion(bf16[2,2560,6656]{2,1,0:T(8,128)(2,1)} %param.3, bf16[128,2560]{1,0:T(8,128)(2,1)S(1)} %bitcast.136), kind=kOutput, calls=%fused_computation.7 | convolution fusion | flops 2852683776 | bytes 24051712 | tf_op jit(solution)/shard_map/td,gdf->tgf/dot_general | solution.py:58
  40.4 4.4 %collective-permute-start.15 = (bf16[32,2,2176]{2,0,1:T(8,128)(2,1)S(1)}, bf16[32,2,2176]{2,0,1:T(8,128)(2,1)S(1)}, u32[]{:S(2)}, u32[]{:S(2)}) collective-permute-start(bf16[32,2,2176]{2,0,1:T(8,128)(2,1)S(1)} %get-tuple-element.31), channel_id=1, source_target_pairs={{0,4},{1,5},{2,6},{3,7},{16,20},{17,21},{18,22},{19,23}} | collective-permute-start | bytes 835592 | tf_op jit(solution)/shard_map/up/ppermute | solution.py:28
  45.7 4.8 %collective-permute-done.15 = bf16[32,2,2176]{2,0,1:T(8,128)(2,1)S(1)} collective-permute-done((bf16[32,2,2176]{2,0,1:T(8,128)(2,1)S(1)}, bf16[32,2,2176]{2,0,1:T(8,128)(2,1)S(1)}, u32[]{:S(2)}, u32[]{:S(2)}) %collective-permute-start.15) | collective-permute-done | bytes 278560 | tf_op jit(solution)/shard_map/up/ppermute | solution.py:28
  51.8 9.6 %fusion.12 = bf16[128,2,2304]{2,0,1:T(8,128)(2,1)S(1)} fusion(bf16[2,2560,6656]{2,1,0:T(8,128)(2,1)} %param.3, bf16[128,2560]{1,0:T(8,128)(2,1)S(1)} %bitcast.137), kind=kOutput, calls=%fused_computation.8 | convolution fusion | flops 3020488704 | bytes 25427968 | tf_op jit(solution)/shard_map/td,gdf->tgf/dot_general | solution.py:58
  61.6 8.9 %collective-permute-start.14 = (bf16[32,2,2176]{2,0,1:T(8,128)(2,1)S(1)}, bf16[32,2,2176]{2,0,1:T(8,128)(2,1)S(1)}, u32[]{:S(2)}, u32[]{:S(2)}) collective-permute-start(bf16[32,2,2176]{2,0,1:T(8,128)(2,1)S(1)} %get-tuple-element.32), channel_id=1, source_target_pairs={{0,4},{1,5},{2,6},{3,7},{16,20},{17,21},{18,22},{19,23}} | collective-permute-start | bytes 835592 | tf_op jit(solution)/shard_map/up/ppermute | solution.py:28
  72.9 1.8 %collective-permute-done.14 = bf16[32,2,2176]{2,0,1:T(8,128)(2,1)S(1)} collective-permute-done((bf16[32,2,2176]{2,0,1:T(8,128)(2,1)S(1)}, bf16[32,2,2176]{2,0,1:T(8,128)(2,1)S(1)}, u32[]{:S(2)}, u32[]{:S(2)}) %collective-permute-start.14) | collective-permute-done | bytes 278560 | tf_op jit(solution)/shard_map/up/ppermute | solution.py:28
  75.5 4.4 %collective-permute-start.13 = (bf16[32,2,2176]{2,0,1:T(8,128)(2,1)S(1)}, bf16[32,2,2176]{2,0,1:T(8,128)(2,1)S(1)}, u32[]{:S(2)}, u32[]{:S(2)}) collective-permute-start(bf16[32,2,2176]{2,0,1:T(8,128)(2,1)S(1)} %get-tuple-element.29), channel_id=1, source_target_pairs={{0,4},{1,5},{2,6},{3,7},{16,20},{17,21},{18,22},{19,23}} | collective-permute-start | bytes 835592 | tf_op jit(solution)/shard_map/up/ppermute | solution.py:28
  79.9 1.3 collective-permute-start.12
  82.8 5.2 %collective-permute-start.25 = (bf16[32,2,2304]{2,0,1:T(8,128)(2,1)S(1)}, bf16[32,2,2304]{2,0,1:T(8,128)(2,1)S(1)}, u32[]{:S(2)}, u32[]{:S(2)}) collective-permute-start(bf16[32,2,2304]{2,0,1:T(8,128)(2,1)S(1)} %get-tuple-element.13), channel_id=1, source_target_pairs={{0,4},{1,5},{2,6},{3,7},{16,20},{17,21},{18,22},{19,23}} | collective-permute-start | bytes 884744 | tf_op jit(solution)/shard_map/up/ppermute | solution.py:28
  89.0 0.7 collective-permute-start.29
  90.0 2.2 %collective-permute-done.25 = bf16[32,2,2304]{2,0,1:T(8,128)(2,1)S(1)} collective-permute-done((bf16[32,2,2304]{2,0,1:T(8,128)(2,1)S(1)}, bf16[32,2,2304]{2,0,1:T(8,128)(2,1)S(1)}, u32[]{:S(2)}, u32[]{:S(2)}) %collective-permute-start.25) | collective-permute-done | bytes 294944 | tf_op jit(solution)/shard_map/up/ppermute | solution.py:28
  92.9 1.3 collective-permute-start.22
  94.4 5.7 %collective-permute-start.23 = (bf16[32,2,2304]{2,0,1:T(8,128)(2,1)S(1)}, bf16[32,2,2304]{2,0,1:T(8,128)(2,1)S(1)}, u32[]{:S(2)}, u32[]{:S(2)}) collective-permute-start(bf16[32,2,2304]{2,0,1:T(8,128)(2,1)S(1)} %get-tuple-element.16), channel_id=1, source_target_pairs={{0,4},{1,5},{2,6},{3,7},{16,20},{17,21},{18,22},{19,23}} | collective-permute-start | bytes 884744 | tf_op jit(solution)/shard_map/up/ppermute | solution.py:28
  100.0 1.3 collective-permute-start.24
  101.4 0.7 collective-permute-start.26
  103.3 5.1 %collective-permute-done.24 = bf16[32,2,2304]{2,0,1:T(8,128)(2,1)S(1)} collective-permute-done((bf16[32,2,2304]{2,0,1:T(8,128)(2,1)S(1)}, bf16[32,2,2304]{2,0,1:T(8,128)(2,1)S(1)}, u32[]{:S(2)}, u32[]{:S(2)}) %collective-permute-start.24) | collective-permute-done | bytes 294944 | tf_op jit(solution)/shard_map/up/ppermute | solution.py:28
  109.3 0.7 collective-permute-start.27
  110.0 1.3 collective-permute-start.32
  111.4 19.1 %collective-permute-done.32 = bf16[32,2,2304]{2,0,1:T(8,128)(2,1)S(1)} collective-permute-done((bf16[32,2,2304]{2,0,1:T(8,128)(2,1)S(1)}, bf16[32,2,2304]{2,0,1:T(8,128)(2,1)S(1)}, u32[]{:S(2)}, u32[]{:S(2)}) %collective-permute-start.32) | collective-permute-done | bytes 294944 | tf_op jit(solution)/shard_map/down/ppermute | solution.py:38
  130.8 0.8 pad_maximum_fusion
  (58 shorter events, 12.9 us)
Async XLA Ops:
  0.0 6.5 %collective-permute-start = (bf16[32,2560]{1,0:T(8,128)(2,1)}, bf16[32,2560]{1,0:T(8,128)(2,1)S(1)}, u32[]{:S(2)}, u32[]{:S(2)}) collective-permute-start(bf16[32,2560]{1,0:T(8,128)(2,1)} %param.2), channel_id=1, source_target_pairs={{0,1},{1,2},{2,3},{3,0},{4,5},{5,6},{6,7},{7,4},{8,9},{9,10},{10,1... | collective-permute-start | bytes 491528 | tf_op jit(solution)/shard_map/ppermute | solution.py:15
  0.5 7.7 %collective-permute-start.1 = (bf16[32,2560]{1,0:T(8,128)(2,1)}, bf16[32,2560]{1,0:T(8,128)(2,1)S(1)}, u32[]{:S(2)}, u32[]{:S(2)}) collective-permute-start(bf16[32,2560]{1,0:T(8,128)(2,1)} %param.2), channel_id=1, source_target_pairs={{0,2},{1,3},{2,0},{3,1},{4,6},{5,7},{6,4},{7,5},{8,10},{9,11},{10,... | collective-permute-start | bytes 491528 | tf_op jit(solution)/shard_map/ppermute | solution.py:15
  3.0 7.8 %collective-permute-start.2 = (bf16[32,2560]{1,0:T(8,128)(2,1)}, bf16[32,2560]{1,0:T(8,128)(2,1)S(1)}, u32[]{:S(2)}, u32[]{:S(2)}) collective-permute-start(bf16[32,2560]{1,0:T(8,128)(2,1)} %param.2), channel_id=1, source_target_pairs={{0,3},{1,0},{2,1},{3,2},{4,7},{5,4},{6,5},{7,6},{8,11},{9,8},{10,9... | collective-permute-start | bytes 491528 | tf_op jit(solution)/shard_map/ppermute | solution.py:15
  20.0 7.5 %collective-permute-start.10 = (bf16[32,2,2176]{2,0,1:T(8,128)(2,1)S(1)}, bf16[32,2,2176]{2,0,1:T(8,128)(2,1)S(1)}, u32[]{:S(2)}, u32[]{:S(2)}) collective-permute-start(bf16[32,2,2176]{2,0,1:T(8,128)(2,1)S(1)} %get-tuple-element.22), channel_id=1, source_target_pairs={{12,8},{13,9},{14,10},{15,11},{28,24},{29,25},{30,26},{31,27}} | collective-permute-start | bytes 835592 | tf_op jit(solution)/shard_map/down/ppermute | solution.py:35
  20.7 10.5 %collective-permute-start.5 = (bf16[32,2,2176]{2,0,1:T(8,128)(2,1)S(1)}, bf16[32,2,2176]{2,0,1:T(8,128)(2,1)S(1)}, u32[]{:S(2)}, u32[]{:S(2)}) collective-permute-start(bf16[32,2,2176]{2,0,1:T(8,128)(2,1)S(1)} %get-tuple-element.23), channel_id=1, source_target_pairs={{0,4},{1,5},{2,6},{3,7},{16,20},{17,21},{18,22},{19,23}} | collective-permute-start | bytes 835592 | tf_op jit(solution)/shard_map/up/ppermute | solution.py:28
  24.2 46.3 %collective-permute-start.9 = (bf16[32,2,2176]{2,0,1:T(8,128)(2,1)S(1)}, bf16[32,2,2176]{2,0,1:T(8,128)(2,1)S(1)}, u32[]{:S(2)}, u32[]{:S(2)}) collective-permute-start(bf16[32,2,2176]{2,0,1:T(8,128)(2,1)S(1)} %get-tuple-element.21), channel_id=1, source_target_pairs={{12,8},{13,9},{14,10},{15,11},{28,24},{29,25},{30,26},{31,27}} | collective-permute-start | bytes 835592 | tf_op jit(solution)/shard_map/down/ppermute | solution.py:35
  24.9 57.2 %collective-permute-start.3 = (bf16[32,2,2176]{2,0,1:T(8,128)(2,1)S(1)}, bf16[32,2,2176]{2,0,1:T(8,128)(2,1)S(1)}, u32[]{:S(2)}, u32[]{:S(2)}) collective-permute-start(bf16[32,2,2176]{2,0,1:T(8,128)(2,1)S(1)} %get-tuple-element.21), channel_id=1, source_target_pairs={{0,4},{1,5},{2,6},{3,7},{16,20},{17,21},{18,22},{19,23}} | collective-permute-start | bytes 835592 | tf_op jit(solution)/shard_map/up/ppermute | solution.py:28
  26.2 35.4 %collective-permute-start.4 = (bf16[32,2,2176]{2,0,1:T(8,128)(2,1)S(1)}, bf16[32,2,2176]{2,0,1:T(8,128)(2,1)S(1)}, u32[]{:S(2)}, u32[]{:S(2)}) collective-permute-start(bf16[32,2,2176]{2,0,1:T(8,128)(2,1)S(1)} %get-tuple-element.24), channel_id=1, source_target_pairs={{0,4},{1,5},{2,6},{3,7},{16,20},{17,21},{18,22},{19,23}} | collective-permute-start | bytes 835592 | tf_op jit(solution)/shard_map/up/ppermute | solution.py:28
  40.4 10.0 %collective-permute-start.15 = (bf16[32,2,2176]{2,0,1:T(8,128)(2,1)S(1)}, bf16[32,2,2176]{2,0,1:T(8,128)(2,1)S(1)}, u32[]{:S(2)}, u32[]{:S(2)}) collective-permute-start(bf16[32,2,2176]{2,0,1:T(8,128)(2,1)S(1)} %get-tuple-element.31), channel_id=1, source_target_pairs={{0,4},{1,5},{2,6},{3,7},{16,20},{17,21},{18,22},{19,23}} | collective-permute-start | bytes 835592 | tf_op jit(solution)/shard_map/up/ppermute | solution.py:28
  44.8 6.3 %collective-permute-start.20 = (bf16[32,2,2176]{2,0,1:T(8,128)(2,1)S(1)}, bf16[32,2,2176]{2,0,1:T(8,128)(2,1)S(1)}, u32[]{:S(2)}, u32[]{:S(2)}) collective-permute-start(bf16[32,2,2176]{2,0,1:T(8,128)(2,1)S(1)} %get-tuple-element.30), channel_id=1, source_target_pairs={{12,8},{13,9},{14,10},{15,11},{28,24},{29,25},{30,26},{31,27}} | collective-permute-start | bytes 835592 | tf_op jit(solution)/shard_map/down/ppermute | solution.py:35
  50.5 20.8 %collective-permute-start.11 = (bf16[32,2,2176]{2,0,1:T(8,128)(2,1)S(1)}, bf16[32,2,2176]{2,0,1:T(8,128)(2,1)S(1)}, u32[]{:S(2)}, u32[]{:S(2)}) collective-permute-start(bf16[32,2,2176]{2,0,1:T(8,128)(2,1)S(1)} %get-tuple-element.20), channel_id=1, source_target_pairs={{8,4},{9,5},{10,6},{11,7},{24,20},{25,21},{26,22},{27,23}} | collective-permute-start | bytes 835592 | tf_op jit(solution)/shard_map/down/ppermute | solution.py:38
  51.2 20.8 %collective-permute-start.6 = (bf16[32,2,2176]{2,0,1:T(8,128)(2,1)S(1)}, bf16[32,2,2176]{2,0,1:T(8,128)(2,1)S(1)}, u32[]{:S(2)}, u32[]{:S(2)}) collective-permute-start(bf16[32,2,2176]{2,0,1:T(8,128)(2,1)S(1)} %get-tuple-element.19), channel_id=1, source_target_pairs={{4,8},{5,9},{6,10},{7,11},{20,24},{21,25},{22,26},{23,27}} | collective-permute-start | bytes 835592 | tf_op jit(solution)/shard_map/up/ppermute | solution.py:32
  61.6 13.1 %collective-permute-start.14 = (bf16[32,2,2176]{2,0,1:T(8,128)(2,1)S(1)}, bf16[32,2,2176]{2,0,1:T(8,128)(2,1)S(1)}, u32[]{:S(2)}, u32[]{:S(2)}) collective-permute-start(bf16[32,2,2176]{2,0,1:T(8,128)(2,1)S(1)} %get-tuple-element.32), channel_id=1, source_target_pairs={{0,4},{1,5},{2,6},{3,7},{16,20},{17,21},{18,22},{19,23}} | collective-permute-start | bytes 835592 | tf_op jit(solution)/shard_map/up/ppermute | solution.py:28
  70.6 4.9 %collective-permute-start.19 = (bf16[32,2,2176]{2,0,1:T(8,128)(2,1)S(1)}, bf16[32,2,2176]{2,0,1:T(8,128)(2,1)S(1)}, u32[]{:S(2)}, u32[]{:S(2)}) collective-permute-start(bf16[32,2,2176]{2,0,1:T(8,128)(2,1)S(1)} %get-tuple-element.29), channel_id=1, source_target_pairs={{12,8},{13,9},{14,10},{15,11},{28,24},{29,25},{30,26},{31,27}} | collective-permute-start | bytes 835592 | tf_op jit(solution)/shard_map/down/ppermute | solution.py:35
  71.3 8.6 %collective-permute-start.16 = (bf16[32,2,2176]{2,0,1:T(8,128)(2,1)S(1)}, bf16[32,2,2176]{2,0,1:T(8,128)(2,1)S(1)}, u32[]{:S(2)}, u32[]{:S(2)}) collective-permute-start(bf16[32,2,2176]{2,0,1:T(8,128)(2,1)S(1)} %get-tuple-element.27), channel_id=1, source_target_pairs={{4,8},{5,9},{6,10},{7,11},{20,24},{21,25},{22,26},{23,27}} | collective-permute-start | bytes 835592 | tf_op jit(solution)/shard_map/up/ppermute | solution.py:32
  72.0 9.2 %collective-permute-start.21 = (bf16[32,2,2176]{2,0,1:T(8,128)(2,1)S(1)}, bf16[32,2,2176]{2,0,1:T(8,128)(2,1)S(1)}, u32[]{:S(2)}, u32[]{:S(2)}) collective-permute-start(bf16[32,2,2176]{2,0,1:T(8,128)(2,1)S(1)} %get-tuple-element.28), channel_id=1, source_target_pairs={{8,4},{9,5},{10,6},{11,7},{24,20},{25,21},{26,22},{27,23}} | collective-permute-start | bytes 835592 | tf_op jit(solution)/shard_map/down/ppermute | solution.py:38
  74.8 8.0 %collective-permute-start.8 = (bf16[32,2,2176]{2,0,1:T(8,128)(2,1)S(1)}, bf16[32,2,2176]{2,0,1:T(8,128)(2,1)S(1)}, u32[]{:S(2)}, u32[]{:S(2)}) collective-permute-start(bf16[32,2,2176]{2,0,1:T(8,128)(2,1)S(1)} %get-tuple-element.24), channel_id=1, source_target_pairs={{12,8},{13,9},{14,10},{15,11},{28,24},{29,25},{30,26},{31,27}} | collective-permute-start | bytes 835592 | tf_op jit(solution)/shard_map/down/ppermute | solution.py:35
  75.5 18.9 %collective-permute-start.13 = (bf16[32,2,2176]{2,0,1:T(8,128)(2,1)S(1)}, bf16[32,2,2176]{2,0,1:T(8,128)(2,1)S(1)}, u32[]{:S(2)}, u32[]{:S(2)}) collective-permute-start(bf16[32,2,2176]{2,0,1:T(8,128)(2,1)S(1)} %get-tuple-element.29), channel_id=1, source_target_pairs={{0,4},{1,5},{2,6},{3,7},{16,20},{17,21},{18,22},{19,23}} | collective-permute-start | bytes 835592 | tf_op jit(solution)/shard_map/up/ppermute | solution.py:28
  79.9 8.4 %collective-permute-start.12 = (bf16[32,2,2176]{2,0,1:T(8,128)(2,1)S(1)}, bf16[32,2,2176]{2,0,1:T(8,128)(2,1)S(1)}, u32[]{:S(2)}, u32[]{:S(2)}) collective-permute-start(bf16[32,2,2176]{2,0,1:T(8,128)(2,1)S(1)} %get-tuple-element.18), channel_id=1, source_target_pairs={{4,0},{8,4},{5,1},{9,5},{6,2},{10,6},{7,3},{11,7},{20,16},{24,20},... | collective-permute-start | bytes 835592 | tf_op jit(solution)/shard_map/down/ppermute | solution.py:38
  81.2 7.8 %collective-permute-start.7 = (bf16[32,2,2176]{2,0,1:T(8,128)(2,1)S(1)}, bf16[32,2,2176]{2,0,1:T(8,128)(2,1)S(1)}, u32[]{:S(2)}, u32[]{:S(2)}) collective-permute-start(bf16[32,2,2176]{2,0,1:T(8,128)(2,1)S(1)} %get-tuple-element.17), channel_id=1, source_target_pairs={{4,8},{8,12},{5,9},{9,13},{6,10},{10,14},{7,11},{11,15},{20,24},{2... | collective-permute-start | bytes 835592 | tf_op jit(solution)/shard_map/up/ppermute | solution.py:32
  82.1 17.9 %collective-permute-start.18 = (bf16[32,2,2176]{2,0,1:T(8,128)(2,1)S(1)}, bf16[32,2,2176]{2,0,1:T(8,128)(2,1)S(1)}, u32[]{:S(2)}, u32[]{:S(2)}) collective-permute-start(bf16[32,2,2176]{2,0,1:T(8,128)(2,1)S(1)} %get-tuple-element.32), channel_id=1, source_target_pairs={{12,8},{13,9},{14,10},{15,11},{28,24},{29,25},{30,26},{31,27}} | collective-permute-start | bytes 835592 | tf_op jit(solution)/shard_map/down/ppermute | solution.py:35
  82.8 9.4 %collective-permute-start.25 = (bf16[32,2,2304]{2,0,1:T(8,128)(2,1)S(1)}, bf16[32,2,2304]{2,0,1:T(8,128)(2,1)S(1)}, u32[]{:S(2)}, u32[]{:S(2)}) collective-permute-start(bf16[32,2,2304]{2,0,1:T(8,128)(2,1)S(1)} %get-tuple-element.13), channel_id=1, source_target_pairs={{0,4},{1,5},{2,6},{3,7},{16,20},{17,21},{18,22},{19,23}} | collective-permute-start | bytes 884744 | tf_op jit(solution)/shard_map/up/ppermute | solution.py:28
  88.3 4.6 %collective-permute-start.30 = (bf16[32,2,2304]{2,0,1:T(8,128)(2,1)S(1)}, bf16[32,2,2304]{2,0,1:T(8,128)(2,1)S(1)}, u32[]{:S(2)}, u32[]{:S(2)}) collective-permute-start(bf16[32,2,2304]{2,0,1:T(8,128)(2,1)S(1)} %get-tuple-element.14), channel_id=1, source_target_pairs={{12,8},{13,9},{14,10},{15,11},{28,24},{29,25},{30,26},{31,27}} | collective-permute-start | bytes 884744 | tf_op jit(solution)/shard_map/down/ppermute | solution.py:35
  89.0 20.0 %collective-permute-start.29 = (bf16[32,2,2304]{2,0,1:T(8,128)(2,1)S(1)}, bf16[32,2,2304]{2,0,1:T(8,128)(2,1)S(1)}, u32[]{:S(2)}, u32[]{:S(2)}) collective-permute-start(bf16[32,2,2304]{2,0,1:T(8,128)(2,1)S(1)} %get-tuple-element.16), channel_id=1, source_target_pairs={{12,8},{13,9},{14,10},{15,11},{28,24},{29,25},{30,26},{31,27}} | collective-permute-start | bytes 884744 | tf_op jit(solution)/shard_map/down/ppermute | solution.py:35
  92.2 9.1 %collective-permute-start.17 = (bf16[32,2,2176]{2,0,1:T(8,128)(2,1)S(1)}, bf16[32,2,2176]{2,0,1:T(8,128)(2,1)S(1)}, u32[]{:S(2)}, u32[]{:S(2)}) collective-permute-start(bf16[32,2,2176]{2,0,1:T(8,128)(2,1)S(1)} %get-tuple-element.25), channel_id=1, source_target_pairs={{4,8},{8,12},{5,9},{9,13},{6,10},{10,14},{7,11},{11,15},{20,24},{2... | collective-permute-start | bytes 835592 | tf_op jit(solution)/shard_map/up/ppermute | solution.py:32
  92.9 9.5 %collective-permute-start.22 = (bf16[32,2,2176]{2,0,1:T(8,128)(2,1)S(1)}, bf16[32,2,2176]{2,0,1:T(8,128)(2,1)S(1)}, u32[]{:S(2)}, u32[]{:S(2)}) collective-permute-start(bf16[32,2,2176]{2,0,1:T(8,128)(2,1)S(1)} %get-tuple-element.26), channel_id=1, source_target_pairs={{4,0},{8,4},{5,1},{9,5},{6,2},{10,6},{7,3},{11,7},{20,16},{24,20},... | collective-permute-start | bytes 835592 | tf_op jit(solution)/shard_map/down/ppermute | solution.py:38
  94.4 17.0 %collective-permute-start.23 = (bf16[32,2,2304]{2,0,1:T(8,128)(2,1)S(1)}, bf16[32,2,2304]{2,0,1:T(8,128)(2,1)S(1)}, u32[]{:S(2)}, u32[]{:S(2)}) collective-permute-start(bf16[32,2,2304]{2,0,1:T(8,128)(2,1)S(1)} %get-tuple-element.16), channel_id=1, source_target_pairs={{0,4},{1,5},{2,6},{3,7},{16,20},{17,21},{18,22},{19,23}} | collective-permute-start | bytes 884744 | tf_op jit(solution)/shard_map/up/ppermute | solution.py:28
  100.0 8.3 %collective-permute-start.24 = (bf16[32,2,2304]{2,0,1:T(8,128)(2,1)S(1)}, bf16[32,2,2304]{2,0,1:T(8,128)(2,1)S(1)}, u32[]{:S(2)}, u32[]{:S(2)}) collective-permute-start(bf16[32,2,2304]{2,0,1:T(8,128)(2,1)S(1)} %get-tuple-element.15), channel_id=1, source_target_pairs={{0,4},{1,5},{2,6},{3,7},{16,20},{17,21},{18,22},{19,23}} | collective-permute-start | bytes 884744 | tf_op jit(solution)/shard_map/up/ppermute | solution.py:28
  101.4 7.7 %collective-permute-start.26 = (bf16[32,2,2304]{2,0,1:T(8,128)(2,1)S(1)}, bf16[32,2,2304]{2,0,1:T(8,128)(2,1)S(1)}, u32[]{:S(2)}, u32[]{:S(2)}) collective-permute-start(bf16[32,2,2304]{2,0,1:T(8,128)(2,1)S(1)} %get-tuple-element.11), channel_id=1, source_target_pairs={{4,8},{5,9},{6,10},{7,11},{20,24},{21,25},{22,26},{23,27}} | collective-permute-start | bytes 884744 | tf_op jit(solution)/shard_map/up/ppermute | solution.py:32
  102.4 6.6 %collective-permute-start.31 = (bf16[32,2,2304]{2,0,1:T(8,128)(2,1)S(1)}, bf16[32,2,2304]{2,0,1:T(8,128)(2,1)S(1)}, u32[]{:S(2)}, u32[]{:S(2)}) collective-permute-start(bf16[32,2,2304]{2,0,1:T(8,128)(2,1)S(1)} %get-tuple-element.12), channel_id=1, source_target_pairs={{8,4},{9,5},{10,6},{11,7},{24,20},{25,21},{26,22},{27,23}} | collective-permute-start | bytes 884744 | tf_op jit(solution)/shard_map/down/ppermute | solution.py:38
  108.3 3.0 %collective-permute-start.28 = (bf16[32,2,2304]{2,0,1:T(8,128)(2,1)S(1)}, bf16[32,2,2304]{2,0,1:T(8,128)(2,1)S(1)}, u32[]{:S(2)}, u32[]{:S(2)}) collective-permute-start(bf16[32,2,2304]{2,0,1:T(8,128)(2,1)S(1)} %get-tuple-element.15), channel_id=1, source_target_pairs={{12,8},{13,9},{14,10},{15,11},{28,24},{29,25},{30,26},{31,27}} | collective-permute-start | bytes 884744 | tf_op jit(solution)/shard_map/down/ppermute | solution.py:35
  110.0 20.5 %collective-permute-start.32 = (bf16[32,2,2304]{2,0,1:T(8,128)(2,1)S(1)}, bf16[32,2,2304]{2,0,1:T(8,128)(2,1)S(1)}, u32[]{:S(2)}, u32[]{:S(2)}) collective-permute-start(bf16[32,2,2304]{2,0,1:T(8,128)(2,1)S(1)} %get-tuple-element.10), channel_id=1, source_target_pairs={{4,0},{8,4},{5,1},{9,5},{6,2},{10,6},{7,3},{11,7},{20,16},{24,20},... | collective-permute-start | bytes 884744 | tf_op jit(solution)/shard_map/down/ppermute | solution.py:38
  (1 other events, 2.1 us)

commit v12 on v7

--- a/solution.py
+++ b/solution.py
@@ -9,17 +9,6 @@
 
 
 CHUNKS = 2
-
-
-def gather_cols(tokens, m):
-    c = lax.axis_index("col")
-    rows = tokens.shape[0]
-    buf = jnp.zeros((m, rows, tokens.shape[1]), tokens.dtype)
-    buf = lax.dynamic_update_index_in_dim(buf, tokens, c, 0)
-    for s in range(1, m):
-        got = lax.ppermute(tokens, "col", [(i, (i + s) % m) for i in range(m)])
-        buf = lax.dynamic_update_index_in_dim(buf, got, (c - s + m) % m, 0)
-    return buf.reshape(m * rows, tokens.shape[1])
 
 
 def tile_width(lo, width, depth):
@@ -58,10 +47,8 @@
 
 
 def line_reduce(part, n, p):
-    down = lax.optimization_barrier(part)
-
-    def block(d, src=part):
-        return lax.dynamic_index_in_dim(src, jnp.clip(d, 0, n - 1), 1, keepdims=False)
+    def block(d):
+        return lax.dynamic_index_in_dim(part, jnp.clip(d, 0, n - 1), 1, keepdims=False)
 
     def add(a, b):
         return (a.astype(jnp.float32) + b.astype(jnp.float32)).astype(jnp.bfloat16)
@@ -76,17 +63,17 @@
         plus = origin[r - 1] + sent
     origin = []
     for r in range(1, n):
-        origin.append(lax.ppermute(down[:, r - 1], "row", [(n - 1, n - 2)]))
+        origin.append(lax.ppermute(part[:, r - 1], "row", [(n - 1, n - 2)]))
     minus = origin[0]
     for r in range(2, n):
-        sent = lax.ppermute(add(block(p - n + r, down), minus), "row", [(q, q - 1) for q in range(n - r, n - 1)])
+        sent = lax.ppermute(add(block(p - n + r), minus), "row", [(q, q - 1) for q in range(n - r, n - 1)])
         minus = origin[r - 1] + sent
     return plus, minus, (first, origin[0])
 
 
-def on_device(tokens, gate_up, n, m):
+def on_device(tokens, gate_up, n):
     p = lax.axis_index("row")
-    gathered = gather_cols(tokens, m)
+    gathered = lax.all_gather(tokens, "col", axis=0, tiled=True)
     t = gathered.shape[0]
     tb = t // n
     f = gate_up.shape[2]
@@ -110,11 +97,10 @@
 
 def solution(mesh):
     n = mesh.shape["row"]
-    m = mesh.shape["col"]
     placed = (P(("grp", "col"), "row"), P(None, "row", "col"))
 
     def body(tokens, gate_up):
-        return on_device(tokens, gate_up, n, m)
+        return on_device(tokens, gate_up, n)
 
     return jax.shard_map(
         body, mesh=mesh, in_specs=placed, out_specs=P(("grp", "row"), "col"), check_vma=False

time: 124 us -> 124 us (level)
  blocking collectives: 0 us -> 9.56 us
  starting transfers between devices: 59.5 us -> 53.1 us
  local copies, waits for them, and re-layouts: 3.22 us -> 1.19 us
  waiting for transfers between devices: 30.4 us -> 28.8 us
    all_gather x0 -> x1, blocking collectives: none -> 9.56 us  [on_device(): gathered = lax.all_gather(tokens, 'col', axis=0, tiled=True)]
    ppermute x13 -> x10, starting transfers between devices: 13.5 us -> 9.52 us  [the longest x6 5.56 us: line_reduce(): origin.append(lax.ppermute(part[:, r - 1], 'row', [(n - 1, n - 2)]))]
    ppermute x6, waiting for transfers between devices: 20.5 us -> 17.3 us  [line_reduce(): origin.append(lax.ppermute(part[:, n - r], 'row', [(0, 1)]))]
    ppermute x6, starting transfers between devices: 43.3 us -> 40.8 us  [line_reduce(): origin.append(lax.ppermute(part[:, n - r], 'row', [(0, 1)]))]
    ppermute x13 -> x10, waiting for transfers between devices: 9.82 us -> 11.5 us  [the longest x4 11.5 us: line_reduce(): lax.ppermute(add(block(p - n + r), minus), 'row', [(q, q - 1) for q in ra...]
    convert_element_type x8 -> x6, other arithmetic: 3.07 us -> 4.19 us  [add(): return (a.astype(jnp.float32) + b.astype(jnp.float32)).astype(jnp.bfloat16)]
  transfers between devices with their start and end apart: 23 -> 20, of which waited for: 6 -> 5; matrix products, arithmetic and copies ran while one was open for 5% -> 4% of each run, Pallas kernels for 10% -> 10%
where the time goes in v12:
time: 124 us; the launch traced here: 123 us
  starting transfers between devices  53.1 us (43%)
  waiting for transfers between devices  28.8 us (23%)
  Pallas kernels  24.8 us (20%)
  blocking collectives  9.56 us (8%)
  other arithmetic  5.72 us (5%)
    ppermute x6, starting transfers between devices, line_reduce(): origin.append(lax.ppermute(part[:, n - r], 'row', [(0, 1)]))  40.8 us
    pallas_call x2, Pallas kernels, project(): pl.pallas_call(kernel, out_shape=jax.ShapeDtypeStruct((2, t, width), x.dt...  24.8 us
    ppermute x6, waiting for transfers between devices, line_reduce(): origin.append(lax.ppermute(part[:, n - r], 'row', [(0, 1)]))  17.3 us
    ppermute x4, waiting for transfers between devices, line_reduce(): lax.ppermute(add(block(p - n + r), minus), 'row', [(q, q - 1) for q in ra...  11.5 us
    all_gather x1, blocking collectives, on_device(): gathered = lax.all_gather(tokens, 'col', axis=0, tiled=True)  9.56 us
    ppermute x6, starting transfers between devices, line_reduce(): origin.append(lax.ppermute(part[:, r - 1], 'row', [(n - 1, n - 2)]))  5.56 us
    convert_element_type x6, other arithmetic, add(): return (a.astype(jnp.float32) + b.astype(jnp.float32)).astype(jnp.bfloat16)  4.19 us
    ppermute x4, starting transfers between devices, line_reduce(): lax.ppermute(add(block(p - n + r), minus), 'row', [(q, q - 1) for q in ra...  3.96 us
  transfers between devices with their start and end apart: 20, of which 5 were waited for; matrix products, arithmetic and copies ran while one was open for 4% of the time, Pallas kernels for 10%

profile of v12, /device:TPU:0, one launch (start us, length us, event | category | flops | bytes accessed | tf_op | source)
XLA Modules:
  0.0 123.5 jit_solution(5183976150378409355)
XLA Ops:
  0.0 9.6 %all_gather.3.x_ref = bf16[128,2560]{1,0:T(8,128)(2,1)S(1)} all-gather(bf16[32,2560]{1,0:T(8,128)(2,1)} %param.2), channel_id=1, replica_groups=mesh['grp'=2,'row'=4,'col'=4] {'col'}, dimensions={0}, use_global_device_ids=true | all-gather | bytes 819200 | tf_op jit(solution)/shard_map/all_gather | solution.py:76
  9.6 12.4 %shard_map.28 = bf16[2,128,3328]{2,1,0:T(8,128)(2,1)S(1)} custom-call(bf16[128,2560]{1,0:T(8,128)(2,1)S(1)} %all_gather.3.x_ref, bf16[2,2560,6656]{2,1,0:T(8,128)(2,1)} %w_ref.3), custom_call_target="tpu_custom_call" | custom-call | flops 4362076160 | bytes 36438016 | tf_op jit(solution)/shard_map/pallas_call | solution.py:33
  22.0 1.1 slice_bitcast_fusion.11
  23.0 4.2 %collective-permute-start.2 = (bf16[2,32,3328]{2,1,0:T(8,128)(2,1)}, bf16[2,32,3328]{2,1,0:T(8,128)(2,1)}, u32[]{:S(2)}, u32[]{:S(2)}) collective-permute-start(bf16[2,32,3328]{2,1,0:T(8,128)(2,1)} %get-tuple-element.10), channel_id=1, source_target_pairs={{0,4},{1,5},{2,6},{3,7},{16,20},{17,21},{18,22},{19,23}} | collective-permute-start | bytes 1277960 | tf_op jit(solution)/shard_map/ppermute | solution.py:58
  27.3 1.4 %collective-permute-start.7 = (bf16[2,32,3328]{2,1,0:T(8,128)(2,1)}, bf16[2,32,3328]{2,1,0:T(8,128)(2,1)}, u32[]{:S(2)}, u32[]{:S(2)}) collective-permute-start(bf16[2,32,3328]{2,1,0:T(8,128)(2,1)} %get-tuple-element.12), channel_id=1, source_target_pairs={{12,8},{13,9},{14,10},{15,11},{28,24},{29,25},{30,26},{31,27}} | collective-permute-start | bytes 1277960 | tf_op jit(solution)/shard_map/ppermute | solution.py:66
  28.7 1.4 %collective-permute-start.6 = (bf16[2,32,3328]{2,1,0:T(8,128)(2,1)}, bf16[2,32,3328]{2,1,0:T(8,128)(2,1)}, u32[]{:S(2)}, u32[]{:S(2)}) collective-permute-start(bf16[2,32,3328]{2,1,0:T(8,128)(2,1)} %get-tuple-element.9), channel_id=1, source_target_pairs={{12,8},{13,9},{14,10},{15,11},{28,24},{29,25},{30,26},{31,27}} | collective-permute-start | bytes 1277960 | tf_op jit(solution)/shard_map/ppermute | solution.py:66
  30.1 1.3 %collective-permute-start = (bf16[2,32,3328]{2,1,0:T(8,128)(2,1)}, bf16[2,32,3328]{2,1,0:T(8,128)(2,1)S(1)}, u32[]{:S(2)}, u32[]{:S(2)}) collective-permute-start(bf16[2,32,3328]{2,1,0:T(8,128)(2,1)} %get-tuple-element.9), channel_id=1, source_target_pairs={{0,4},{1,5},{2,6},{3,7},{16,20},{17,21},{18,22},{19,23}} | collective-permute-start | bytes 1277960 | tf_op jit(solution)/shard_map/ppermute | solution.py:58
  31.4 2.1 %collective-permute-start.1 = (bf16[2,32,3328]{2,1,0:T(8,128)(2,1)S(1)}, bf16[2,32,3328]{2,1,0:T(8,128)(2,1)}, u32[]{:S(2)}, u32[]{:S(2)}) collective-permute-start(bf16[2,32,3328]{2,1,0:T(8,128)(2,1)S(1)} %get-tuple-element.11), channel_id=1, source_target_pairs={{0,4},{1,5},{2,6},{3,7},{16,20},{17,21},{18,22},{19,23}} | collective-permute-start | bytes 1277960 | tf_op jit(solution)/shard_map/ppermute | solution.py:58
  33.5 3.5 %collective-permute-done.2 = bf16[2,32,3328]{2,1,0:T(8,128)(2,1)} collective-permute-done((bf16[2,32,3328]{2,1,0:T(8,128)(2,1)}, bf16[2,32,3328]{2,1,0:T(8,128)(2,1)}, u32[]{:S(2)}, u32[]{:S(2)}) %collective-permute-start.2) | collective-permute-done | bytes 426016 | tf_op jit(solution)/shard_map/ppermute | solution.py:58
  37.0 12.4 %shard_map.29 = bf16[2,128,3328]{2,1,0:T(8,128)(2,1)S(1)} custom-call(bf16[128,2560]{1,0:T(8,128)(2,1)S(1)} %all_gather.3.x_ref, bf16[2,2560,6656]{2,1,0:T(8,128)(2,1)} %w_ref.3), custom_call_target="tpu_custom_call" | custom-call | flops 4362076160 | bytes 36438016 | tf_op jit(solution)/shard_map/pallas_call | solution.py:33
  49.6 4.4 %collective-permute-start.12 = (bf16[2,32,3328]{2,1,0:T(8,128)(2,1)S(1)}, bf16[2,32,3328]{2,1,0:T(8,128)(2,1)S(1)}, u32[]{:S(2)}, u32[]{:S(2)}) collective-permute-start(bf16[2,32,3328]{2,1,0:T(8,128)(2,1)S(1)} %get-tuple-element.15), channel_id=1, source_target_pairs={{0,4},{1,5},{2,6},{3,7},{16,20},{17,21},{18,22},{19,23}} | collective-permute-start | bytes 1277960 | tf_op jit(solution)/shard_map/ppermute | solution.py:58
  54.0 1.1 fusion.7
  55.1 0.7 collective-permute-start.3
  55.8 7.9 %collective-permute-done.12 = bf16[2,32,3328]{2,1,0:T(8,128)(2,1)S(1)} collective-permute-done((bf16[2,32,3328]{2,1,0:T(8,128)(2,1)S(1)}, bf16[2,32,3328]{2,1,0:T(8,128)(2,1)S(1)}, u32[]{:S(2)}, u32[]{:S(2)}) %collective-permute-start.12) | collective-permute-done | bytes 426016 | tf_op jit(solution)/shard_map/ppermute | solution.py:58
  63.7 0.7 collective-permute-start.17
  64.5 4.4 %collective-permute-start.11 = (bf16[2,32,3328]{2,1,0:T(8,128)(2,1)S(1)}, bf16[2,32,3328]{2,1,0:T(8,128)(2,1)S(1)}, u32[]{:S(2)}, u32[]{:S(2)}) collective-permute-start(bf16[2,32,3328]{2,1,0:T(8,128)(2,1)S(1)} %get-tuple-element.16), channel_id=1, source_target_pairs={{0,4},{1,5},{2,6},{3,7},{16,20},{17,21},{18,22},{19,23}} | collective-permute-start | bytes 1277960 | tf_op jit(solution)/shard_map/ppermute | solution.py:58
  68.9 0.7 collective-permute-start.13
  69.6 1.4 %fusion.8 = (bf16[2,32,3328]{2,1,0:T(8,128)(2,1)S(1)}, bf16[2,32,3328]{2,1,0:T(8,128)(2,1)S(1)}) fusion(bf16[2,32,3328]{2,1,0:T(8,128)(2,1)} %collective-permute-done.1, bf16[2,32,3328]{2,1,0:T(8,128)(2,1)S(1)} %collective-permute-done.3, bf16[2,4,32,3328]{3,2,1,0:T(8,128)(2,1)S(1)} %bitcast.106, s32[]{:T(128)S(6)} %min.17, ...), kind=kLoop, calls=%fused_computation.17 | loop fusion | flops 1916928 | bytes 2981896 | tf_op jit(solution)/shard_map/convert_element_type | solution.py:54
  71.0 0.7 collective-permute-start.5
  71.7 5.9 %collective-permute-done.11 = bf16[2,32,3328]{2,1,0:T(8,128)(2,1)S(1)} collective-permute-done((bf16[2,32,3328]{2,1,0:T(8,128)(2,1)S(1)}, bf16[2,32,3328]{2,1,0:T(8,128)(2,1)S(1)}, u32[]{:S(2)}, u32[]{:S(2)}) %collective-permute-start.11) | collective-permute-done | bytes 426016 | tf_op jit(solution)/shard_map/ppermute | solution.py:58
  78.3 0.7 collective-permute-start.8
  79.3 0.7 collective-permute-start.16
  80.0 0.7 collective-permute-start.18
  80.7 1.2 fusion.6
  81.8 0.7 collective-permute-start.4
  82.5 1.3 %collective-permute-start.9 = (bf16[2,32,3328]{2,1,0:T(8,128)(2,1)S(1)}, bf16[2,32,3328]{2,1,0:T(8,128)(2,1)S(1)}, u32[]{:S(2)}, u32[]{:S(2)}) collective-permute-start(bf16[2,32,3328]{2,1,0:T(8,128)(2,1)S(1)} %fusion.6), channel_id=1, source_target_pairs={{4,0},{8,4},{5,1},{9,5},{6,2},{10,6},{7,3},{11,7},{20,16},{24,20},... | collective-permute-start | bytes 1277960 | tf_op jit(solution)/shard_map/ppermute | solution.py:69
  84.0 24.4 %collective-permute-start.10 = (bf16[2,32,3328]{2,1,0:T(8,128)(2,1)S(1)}, bf16[2,32,3328]{2,1,0:T(8,128)(2,1)S(1)}, u32[]{:S(2)}, u32[]{:S(2)}) collective-permute-start(bf16[2,32,3328]{2,1,0:T(8,128)(2,1)S(1)} %get-tuple-element.17), channel_id=1, source_target_pairs={{0,4},{1,5},{2,6},{3,7},{16,20},{17,21},{18,22},{19,23}} | collective-permute-start | bytes 1277960 | tf_op jit(solution)/shard_map/ppermute | solution.py:58
  108.4 0.7 collective-permute-start.14
  109.2 1.3 %collective-permute-start.19 = (bf16[2,32,3328]{2,1,0:T(8,128)(2,1)S(1)}, bf16[2,32,3328]{2,1,0:T(8,128)(2,1)S(1)}, u32[]{:S(2)}, u32[]{:S(2)}) collective-permute-start(bf16[2,32,3328]{2,1,0:T(8,128)(2,1)S(1)} %fusion.1), channel_id=1, source_target_pairs={{4,0},{8,4},{5,1},{9,5},{6,2},{10,6},{7,3},{11,7},{20,16},{24,20},... | collective-permute-start | bytes 1277960 | tf_op jit(solution)/shard_map/ppermute | solution.py:69
  110.5 5.6 %collective-permute-done.9 = bf16[2,32,3328]{2,1,0:T(8,128)(2,1)S(1)} collective-permute-done((bf16[2,32,3328]{2,1,0:T(8,128)(2,1)S(1)}, bf16[2,32,3328]{2,1,0:T(8,128)(2,1)S(1)}, u32[]{:S(2)}, u32[]{:S(2)}) %collective-permute-start.9) | collective-permute-done | bytes 426016 | tf_op jit(solution)/shard_map/ppermute | solution.py:69
  116.5 5.8 %collective-permute-done.19 = bf16[2,32,3328]{2,1,0:T(8,128)(2,1)S(1)} collective-permute-done((bf16[2,32,3328]{2,1,0:T(8,128)(2,1)S(1)}, bf16[2,32,3328]{2,1,0:T(8,128)(2,1)S(1)}, u32[]{:S(2)}, u32[]{:S(2)}) %collective-permute-start.19) | collective-permute-done | bytes 426016 | tf_op jit(solution)/shard_map/ppermute | solution.py:69
  122.7 0.8 pad_maximum_fusion
  (24 shorter events, 2.1 us)
Async XLA Ops:
  23.0 14.0 %collective-permute-start.2 = (bf16[2,32,3328]{2,1,0:T(8,128)(2,1)}, bf16[2,32,3328]{2,1,0:T(8,128)(2,1)}, u32[]{:S(2)}, u32[]{:S(2)}) collective-permute-start(bf16[2,32,3328]{2,1,0:T(8,128)(2,1)} %get-tuple-element.10), channel_id=1, source_target_pairs={{0,4},{1,5},{2,6},{3,7},{16,20},{17,21},{18,22},{19,23}} | collective-permute-start | bytes 1277960 | tf_op jit(solution)/shard_map/ppermute | solution.py:58
  27.3 9.7 %collective-permute-start.7 = (bf16[2,32,3328]{2,1,0:T(8,128)(2,1)}, bf16[2,32,3328]{2,1,0:T(8,128)(2,1)}, u32[]{:S(2)}, u32[]{:S(2)}) collective-permute-start(bf16[2,32,3328]{2,1,0:T(8,128)(2,1)} %get-tuple-element.12), channel_id=1, source_target_pairs={{12,8},{13,9},{14,10},{15,11},{28,24},{29,25},{30,26},{31,27}} | collective-permute-start | bytes 1277960 | tf_op jit(solution)/shard_map/ppermute | solution.py:66
  28.7 50.6 %collective-permute-start.6 = (bf16[2,32,3328]{2,1,0:T(8,128)(2,1)}, bf16[2,32,3328]{2,1,0:T(8,128)(2,1)}, u32[]{:S(2)}, u32[]{:S(2)}) collective-permute-start(bf16[2,32,3328]{2,1,0:T(8,128)(2,1)} %get-tuple-element.9), channel_id=1, source_target_pairs={{12,8},{13,9},{14,10},{15,11},{28,24},{29,25},{30,26},{31,27}} | collective-permute-start | bytes 1277960 | tf_op jit(solution)/shard_map/ppermute | solution.py:66
  30.1 53.9 %collective-permute-start = (bf16[2,32,3328]{2,1,0:T(8,128)(2,1)}, bf16[2,32,3328]{2,1,0:T(8,128)(2,1)S(1)}, u32[]{:S(2)}, u32[]{:S(2)}) collective-permute-start(bf16[2,32,3328]{2,1,0:T(8,128)(2,1)} %get-tuple-element.9), channel_id=1, source_target_pairs={{0,4},{1,5},{2,6},{3,7},{16,20},{17,21},{18,22},{19,23}} | collective-permute-start | bytes 1277960 | tf_op jit(solution)/shard_map/ppermute | solution.py:58
  31.4 33.1 %collective-permute-start.1 = (bf16[2,32,3328]{2,1,0:T(8,128)(2,1)S(1)}, bf16[2,32,3328]{2,1,0:T(8,128)(2,1)}, u32[]{:S(2)}, u32[]{:S(2)}) collective-permute-start(bf16[2,32,3328]{2,1,0:T(8,128)(2,1)S(1)} %get-tuple-element.11), channel_id=1, source_target_pairs={{0,4},{1,5},{2,6},{3,7},{16,20},{17,21},{18,22},{19,23}} | collective-permute-start | bytes 1277960 | tf_op jit(solution)/shard_map/ppermute | solution.py:58
  49.6 14.1 %collective-permute-start.12 = (bf16[2,32,3328]{2,1,0:T(8,128)(2,1)S(1)}, bf16[2,32,3328]{2,1,0:T(8,128)(2,1)S(1)}, u32[]{:S(2)}, u32[]{:S(2)}) collective-permute-start(bf16[2,32,3328]{2,1,0:T(8,128)(2,1)S(1)} %get-tuple-element.15), channel_id=1, source_target_pairs={{0,4},{1,5},{2,6},{3,7},{16,20},{17,21},{18,22},{19,23}} | collective-permute-start | bytes 1277960 | tf_op jit(solution)/shard_map/ppermute | solution.py:58
  55.1 13.8 %collective-permute-start.3 = (bf16[2,32,3328]{2,1,0:T(8,128)(2,1)S(1)}, bf16[2,32,3328]{2,1,0:T(8,128)(2,1)S(1)}, u32[]{:S(2)}, u32[]{:S(2)}) collective-permute-start(bf16[2,32,3328]{2,1,0:T(8,128)(2,1)S(1)} %fusion.7), channel_id=1, source_target_pairs={{4,8},{5,9},{6,10},{7,11},{20,24},{21,25},{22,26},{23,27}} | collective-permute-start | bytes 1277960 | tf_op jit(solution)/shard_map/ppermute | solution.py:62
  63.7 7.3 %collective-permute-start.17 = (bf16[2,32,3328]{2,1,0:T(8,128)(2,1)S(1)}, bf16[2,32,3328]{2,1,0:T(8,128)(2,1)S(1)}, u32[]{:S(2)}, u32[]{:S(2)}) collective-permute-start(bf16[2,32,3328]{2,1,0:T(8,128)(2,1)S(1)} %get-tuple-element.18), channel_id=1, source_target_pairs={{12,8},{13,9},{14,10},{15,11},{28,24},{29,25},{30,26},{31,27}} | collective-permute-start | bytes 1277960 | tf_op jit(solution)/shard_map/ppermute | solution.py:66
  64.5 13.1 %collective-permute-start.11 = (bf16[2,32,3328]{2,1,0:T(8,128)(2,1)S(1)}, bf16[2,32,3328]{2,1,0:T(8,128)(2,1)S(1)}, u32[]{:S(2)}, u32[]{:S(2)}) collective-permute-start(bf16[2,32,3328]{2,1,0:T(8,128)(2,1)S(1)} %get-tuple-element.16), channel_id=1, source_target_pairs={{0,4},{1,5},{2,6},{3,7},{16,20},{17,21},{18,22},{19,23}} | collective-permute-start | bytes 1277960 | tf_op jit(solution)/shard_map/ppermute | solution.py:58
  68.9 9.4 %collective-permute-start.13 = (bf16[2,32,3328]{2,1,0:T(8,128)(2,1)S(1)}, bf16[2,32,3328]{2,1,0:T(8,128)(2,1)S(1)}, u32[]{:S(2)}, u32[]{:S(2)}) collective-permute-start(bf16[2,32,3328]{2,1,0:T(8,128)(2,1)S(1)} %fusion.2), channel_id=1, source_target_pairs={{4,8},{5,9},{6,10},{7,11},{20,24},{21,25},{22,26},{23,27}} | collective-permute-start | bytes 1277960 | tf_op jit(solution)/shard_map/ppermute | solution.py:62
  71.0 37.4 %collective-permute-start.5 = (bf16[2,32,3328]{2,1,0:T(8,128)(2,1)S(1)}, bf16[2,32,3328]{2,1,0:T(8,128)(2,1)S(1)}, u32[]{:S(2)}, u32[]{:S(2)}) collective-permute-start(bf16[2,32,3328]{2,1,0:T(8,128)(2,1)S(1)} %get-tuple-element.11), channel_id=1, source_target_pairs={{12,8},{13,9},{14,10},{15,11},{28,24},{29,25},{30,26},{31,27}} | collective-permute-start | bytes 1277960 | tf_op jit(solution)/shard_map/ppermute | solution.py:66
  77.6 38.9 %collective-permute-start.15 = (bf16[2,32,3328]{2,1,0:T(8,128)(2,1)S(1)}, bf16[2,32,3328]{2,1,0:T(8,128)(2,1)S(1)}, u32[]{:S(2)}, u32[]{:S(2)}) collective-permute-start(bf16[2,32,3328]{2,1,0:T(8,128)(2,1)S(1)} %get-tuple-element.16), channel_id=1, source_target_pairs={{12,8},{13,9},{14,10},{15,11},{28,24},{29,25},{30,26},{31,27}} | collective-permute-start | bytes 1277960 | tf_op jit(solution)/shard_map/ppermute | solution.py:66
  78.3 1.7 %collective-permute-start.8 = (bf16[2,32,3328]{2,1,0:T(8,128)(2,1)S(1)}, bf16[2,32,3328]{2,1,0:T(8,128)(2,1)S(1)}, u32[]{:S(2)}, u32[]{:S(2)}) collective-permute-start(bf16[2,32,3328]{2,1,0:T(8,128)(2,1)S(1)} %get-tuple-element.8), channel_id=1, source_target_pairs={{8,4},{9,5},{10,6},{11,7},{24,20},{25,21},{26,22},{27,23}} | collective-permute-start | bytes 1277960 | tf_op jit(solution)/shard_map/ppermute | solution.py:69
  79.3 2.6 %collective-permute-start.16 = (bf16[2,32,3328]{2,1,0:T(8,128)(2,1)S(1)}, bf16[2,32,3328]{2,1,0:T(8,128)(2,1)S(1)}, u32[]{:S(2)}, u32[]{:S(2)}) collective-permute-start(bf16[2,32,3328]{2,1,0:T(8,128)(2,1)S(1)} %get-tuple-element.17), channel_id=1, source_target_pairs={{12,8},{13,9},{14,10},{15,11},{28,24},{29,25},{30,26},{31,27}} | collective-permute-start | bytes 1277960 | tf_op jit(solution)/shard_map/ppermute | solution.py:66
  80.0 2.6 %collective-permute-start.18 = (bf16[2,32,3328]{2,1,0:T(8,128)(2,1)S(1)}, bf16[2,32,3328]{2,1,0:T(8,128)(2,1)S(1)}, u32[]{:S(2)}, u32[]{:S(2)}) collective-permute-start(bf16[2,32,3328]{2,1,0:T(8,128)(2,1)S(1)} %get-tuple-element.14), channel_id=1, source_target_pairs={{8,4},{9,5},{10,6},{11,7},{24,20},{25,21},{26,22},{27,23}} | collective-permute-start | bytes 1277960 | tf_op jit(solution)/shard_map/ppermute | solution.py:69
  81.8 27.3 %collective-permute-start.4 = (bf16[2,32,3328]{2,1,0:T(8,128)(2,1)S(1)}, bf16[2,32,3328]{2,1,0:T(8,128)(2,1)S(1)}, u32[]{:S(2)}, u32[]{:S(2)}) collective-permute-start(bf16[2,32,3328]{2,1,0:T(8,128)(2,1)S(1)} %get-tuple-element.7), channel_id=1, source_target_pairs={{4,8},{8,12},{5,9},{9,13},{6,10},{10,14},{7,11},{11,15},{20,24},{2... | collective-permute-start | bytes 1277960 | tf_op jit(solution)/shard_map/ppermute | solution.py:62
  82.5 33.5 %collective-permute-start.9 = (bf16[2,32,3328]{2,1,0:T(8,128)(2,1)S(1)}, bf16[2,32,3328]{2,1,0:T(8,128)(2,1)S(1)}, u32[]{:S(2)}, u32[]{:S(2)}) collective-permute-start(bf16[2,32,3328]{2,1,0:T(8,128)(2,1)S(1)} %fusion.6), channel_id=1, source_target_pairs={{4,0},{8,4},{5,1},{9,5},{6,2},{10,6},{7,3},{11,7},{20,16},{24,20},... | collective-permute-start | bytes 1277960 | tf_op jit(solution)/shard_map/ppermute | solution.py:69
  84.0 32.5 %collective-permute-start.10 = (bf16[2,32,3328]{2,1,0:T(8,128)(2,1)S(1)}, bf16[2,32,3328]{2,1,0:T(8,128)(2,1)S(1)}, u32[]{:S(2)}, u32[]{:S(2)}) collective-permute-start(bf16[2,32,3328]{2,1,0:T(8,128)(2,1)S(1)} %get-tuple-element.17), channel_id=1, source_target_pairs={{0,4},{1,5},{2,6},{3,7},{16,20},{17,21},{18,22},{19,23}} | collective-permute-start | bytes 1277960 | tf_op jit(solution)/shard_map/ppermute | solution.py:58
  108.4 8.0 %collective-permute-start.14 = (bf16[2,32,3328]{2,1,0:T(8,128)(2,1)S(1)}, bf16[2,32,3328]{2,1,0:T(8,128)(2,1)S(1)}, u32[]{:S(2)}, u32[]{:S(2)}) collective-permute-start(bf16[2,32,3328]{2,1,0:T(8,128)(2,1)S(1)} %get-tuple-element.13), channel_id=1, source_target_pairs={{4,8},{8,12},{5,9},{9,13},{6,10},{10,14},{7,11},{11,15},{20,24},{2... | collective-permute-start | bytes 1277960 | tf_op jit(solution)/shard_map/ppermute | solution.py:62
  109.2 13.2 %collective-permute-start.19 = (bf16[2,32,3328]{2,1,0:T(8,128)(2,1)S(1)}, bf16[2,32,3328]{2,1,0:T(8,128)(2,1)S(1)}, u32[]{:S(2)}, u32[]{:S(2)}) collective-permute-start(bf16[2,32,3328]{2,1,0:T(8,128)(2,1)S(1)} %fusion.1), channel_id=1, source_target_pairs={{4,0},{8,4},{5,1},{9,5},{6,2},{10,6},{7,3},{11,7},{20,16},{24,20},... | collective-permute-start | bytes 1277960 | tf_op jit(solution)/shard_map/ppermute | solution.py:69

commit v13 on v3

--- a/solution.py
+++ b/solution.py
@@ -3,7 +3,8 @@
 from jax import lax
 from jax.sharding import PartitionSpec as P
 
-CHUNKS = 1
+
+CHUNKS = 2
 
 
 def gather_cols(tokens, m):
@@ -24,19 +25,22 @@
     def add(a, b):
         return (a.astype(jnp.float32) + b.astype(jnp.float32)).astype(jnp.bfloat16)
 
-    with jax.named_scope("up"):
-        origin = [lax.ppermute(part[n - r], "row", [(0, 1)]) for r in range(1, n)]
-        plus = origin[0]
-        for r in range(2, n):
-            sent = lax.ppermute(add(block(p + n - r), plus), "row", [(q, q + 1) for q in range(1, r)])
-            plus = origin[r - 1] + sent
-    with jax.named_scope("down"):
-        origin = [lax.ppermute(part[r - 1], "row", [(n - 1, n - 2)]) for r in range(1, n)]
-        minus = origin[0]
-        for r in range(2, n):
-            sent = lax.ppermute(add(block(p - n + r), minus), "row", [(q, q - 1) for q in range(n - r, n - 1)])
-            minus = origin[r - 1] + sent
-    return plus, minus
+    origin = []
+    for r in range(1, n):
+        origin.append(lax.ppermute(part[n - r], "row", [(0, 1)]))
+    first = origin[0]
+    plus = origin[0]
+    for r in range(2, n):
+        sent = lax.ppermute(add(block(p + n - r), plus), "row", [(q, q + 1) for q in range(1, r)])
+        plus = origin[r - 1] + sent
+    origin = []
+    for r in range(1, n):
+        origin.append(lax.ppermute(part[r - 1], "row", [(n - 1, n - 2)]))
+    minus = origin[0]
+    for r in range(2, n):
+        sent = lax.ppermute(add(block(p - n + r), minus), "row", [(q, q - 1) for q in range(n - r, n - 1)])
+        minus = origin[r - 1] + sent
+    return plus, minus, (first, origin[0])
 
 
 def on_device(tokens, gate_up, n, m):
@@ -56,7 +60,7 @@
         part = part.reshape(n, tb, 2, edges[i + 1] - edges[i])
         own = lax.dynamic_index_in_dim(part, p, 0, keepdims=False).astype(jnp.float32)
         if n > 1:
-            plus, minus = line_reduce(part, n, p)
+            plus, minus, _ = line_reduce(part, n, p)
             own = own + plus.astype(jnp.float32) + minus.astype(jnp.float32)
         outs.append((jax.nn.silu(own[:, 0]) * own[:, 1]).astype(jnp.bfloat16))
     return jnp.concatenate(outs, axis=1)

time: 118 us -> 126 us (1.068)
  the two profiles are of different devices: /device:TPU:14 before, /device:TPU:0 now
where the time goes in v13:
time: 126 us
  waiting for transfers between devices  53.6 us (43%)
  starting transfers between devices  37.6 us (30%)
  matrix products  26.9 us (21%)
  other arithmetic  4.66 us (4%)
  local copies, waits for them, and re-layouts  2.39 us (2%)
    ppermute x6, waiting for transfers between devices, line_reduce(): origin.append(lax.ppermute(part[n - r], 'row', [(0, 1)]))  29.6 us
    dot_general x2, matrix products, on_device(): jnp.einsum('td,gdf->tgf', gathered, w, preferred_element_type=jnp.float32)  26.9 us
    ppermute x6, starting transfers between devices, line_reduce(): origin.append(lax.ppermute(part[n - r], 'row', [(0, 1)]))  21.5 us
    ppermute x4, waiting for transfers between devices, line_reduce(): lax.ppermute(add(block(p - n + r), minus), 'row', [(q, q - 1) for q in ra...  18.8 us
    ppermute x3, waiting for transfers between devices, gather_cols(): got = lax.ppermute(tokens, 'col', [(i, (i + s) % m) for i in range(m)])  5.28 us
    ppermute x6, starting transfers between devices, line_reduce(): origin.append(lax.ppermute(part[r - 1], 'row', [(n - 1, n - 2)]))  4.84 us
    ppermute x3, starting transfers between devices, gather_cols(): got = lax.ppermute(tokens, 'col', [(i, (i + s) % m) for i in range(m)])  4.43 us
    ppermute x4, starting transfers between devices, line_reduce(): lax.ppermute(add(block(p - n + r), minus), 'row', [(q, q - 1) for q in ra...  4.07 us
  transfers between devices with their start and end apart: 23, of which 8 were waited for; matrix products, arithmetic and copies ran while one was open for 15% of the time, Pallas kernels for 0%

profile of v13, /device:TPU:0, one launch (start us, length us, event | category | flops | bytes accessed | tf_op | source)
XLA Modules:
  0.0 125.6 jit_solution(1346977251747432818)
XLA Ops:
  0.5 2.5 %collective-permute-start.1 = (bf16[32,2560]{1,0:T(8,128)(2,1)}, bf16[32,2560]{1,0:T(8,128)(2,1)S(1)}, u32[]{:S(2)}, u32[]{:S(2)}) collective-permute-start(bf16[32,2560]{1,0:T(8,128)(2,1)} %param.2), channel_id=1, source_target_pairs={{0,2},{1,3},{2,0},{3,1},{4,6},{5,7},{6,4},{7,5},{8,10},{9,11},{10,... | collective-permute-start | bytes 491528 | tf_op jit(solution)/shard_map/ppermute | solution.py:16
  3.0 1.5 %collective-permute-start.2 = (bf16[32,2560]{1,0:T(8,128)(2,1)}, bf16[32,2560]{1,0:T(8,128)(2,1)S(1)}, u32[]{:S(2)}, u32[]{:S(2)}) collective-permute-start(bf16[32,2560]{1,0:T(8,128)(2,1)} %param.2), channel_id=1, source_target_pairs={{0,3},{1,0},{2,1},{3,2},{4,7},{5,4},{6,5},{7,6},{8,11},{9,8},{10,9... | collective-permute-start | bytes 491528 | tf_op jit(solution)/shard_map/ppermute | solution.py:16
  4.5 1.0 bitcast_dynamic-update-slice_fusion.3
  5.5 1.0 collective-permute-done
  6.5 1.7 %collective-permute-done.1 = bf16[32,2560]{1,0:T(8,128)(2,1)S(1)} collective-permute-done((bf16[32,2560]{1,0:T(8,128)(2,1)}, bf16[32,2560]{1,0:T(8,128)(2,1)S(1)}, u32[]{:S(2)}, u32[]{:S(2)}) %collective-permute-start.1) | collective-permute-done | bytes 163872 | tf_op jit(solution)/shard_map/ppermute | solution.py:16
  8.2 2.6 %collective-permute-done.2 = bf16[32,2560]{1,0:T(8,128)(2,1)S(1)} collective-permute-done((bf16[32,2560]{1,0:T(8,128)(2,1)}, bf16[32,2560]{1,0:T(8,128)(2,1)S(1)}, u32[]{:S(2)}, u32[]{:S(2)}) %collective-permute-start.2) | collective-permute-done | bytes 163872 | tf_op jit(solution)/shard_map/ppermute | solution.py:16
  10.8 13.4 %fusion.4 = bf16[128,2,3328]{2,0,1:T(8,128)(2,1)S(1)} fusion(bf16[128,2560,1]{1,0,2:T(8,128)(2,1)S(1)} %bitcast.91, bf16[2,2560,6656]{2,1,0:T(8,128)(2,1)} %param.3), kind=kOutput, calls=%fused_computation.4 | convolution fusion | flops 4362928128 | bytes 36438016 | tf_op jit(solution)/shard_map/td,gdf->tgf/dot_general | solution.py:59
  24.2 1.2 fusion.24
  25.4 1.4 %collective-permute-start.9 = (bf16[32,2,3328]{2,0,1:T(8,128)(2,1)}, bf16[32,2,3328]{2,0,1:T(8,128)(2,1)}, u32[]{:S(2)}, u32[]{:S(2)}) collective-permute-start(bf16[32,2,3328]{2,0,1:T(8,128)(2,1)} %get-tuple-element.12), channel_id=1, source_target_pairs={{12,8},{13,9},{14,10},{15,11},{28,24},{29,25},{30,26},{31,27}} | collective-permute-start | bytes 1277960 | tf_op jit(solution)/shard_map/ppermute | solution.py:38
  26.9 4.2 %collective-permute-start.3 = (bf16[32,2,3328]{2,0,1:T(8,128)(2,1)}, bf16[32,2,3328]{2,0,1:T(8,128)(2,1)}, u32[]{:S(2)}, u32[]{:S(2)}) collective-permute-start(bf16[32,2,3328]{2,0,1:T(8,128)(2,1)} %get-tuple-element.12), channel_id=1, source_target_pairs={{0,4},{1,5},{2,6},{3,7},{16,20},{17,21},{18,22},{19,23}} | collective-permute-start | bytes 1277960 | tf_op jit(solution)/shard_map/ppermute | solution.py:30
  31.1 13.6 %fusion.7 = bf16[128,2,3328]{2,0,1:T(8,128)(2,1)S(1)} fusion(bf16[128,2560,1]{1,0,2:T(8,128)(2,1)} %bitcast.92, bf16[2,2560,6656]{2,1,0:T(8,128)(2,1)} %param.3), kind=kOutput, calls=%fused_computation.5 | convolution fusion | flops 4362928128 | bytes 36438016 | tf_op jit(solution)/shard_map/td,gdf->tgf/dot_general | solution.py:59
  44.7 0.7 collective-permute-start.10
  45.4 1.3 %collective-permute-start.5 = (bf16[32,2,3328]{2,0,1:T(8,128)(2,1)}, bf16[32,2,3328]{2,0,1:T(8,128)(2,1)S(1)}, u32[]{:S(2)}, u32[]{:S(2)}) collective-permute-start(bf16[32,2,3328]{2,0,1:T(8,128)(2,1)} %get-tuple-element.9), channel_id=1, source_target_pairs={{0,4},{1,5},{2,6},{3,7},{16,20},{17,21},{18,22},{19,23}} | collective-permute-start | bytes 1277960 | tf_op jit(solution)/shard_map/ppermute | solution.py:30
  46.7 1.3 %collective-permute-start.4 = (bf16[32,2,3328]{2,0,1:T(8,128)(2,1)}, bf16[32,2,3328]{2,0,1:T(8,128)(2,1)S(1)}, u32[]{:S(2)}, u32[]{:S(2)}) collective-permute-start(bf16[32,2,3328]{2,0,1:T(8,128)(2,1)} %get-tuple-element.11), channel_id=1, source_target_pairs={{0,4},{1,5},{2,6},{3,7},{16,20},{17,21},{18,22},{19,23}} | collective-permute-start | bytes 1277960 | tf_op jit(solution)/shard_map/ppermute | solution.py:30
  48.2 1.3 %collective-permute-start.15 = (bf16[32,2,3328]{2,0,1:T(8,128)(2,1)S(1)}, bf16[32,2,3328]{2,0,1:T(8,128)(2,1)S(1)}, u32[]{:S(2)}, u32[]{:S(2)}) collective-permute-start(bf16[32,2,3328]{2,0,1:T(8,128)(2,1)S(1)} %get-tuple-element.17), channel_id=1, source_target_pairs={{0,4},{1,5},{2,6},{3,7},{16,20},{17,21},{18,22},{19,23}} | collective-permute-start | bytes 1277960 | tf_op jit(solution)/shard_map/ppermute | solution.py:30
  49.5 7.7 %collective-permute-done.5 = bf16[32,2,3328]{2,0,1:T(8,128)(2,1)S(1)} collective-permute-done((bf16[32,2,3328]{2,0,1:T(8,128)(2,1)}, bf16[32,2,3328]{2,0,1:T(8,128)(2,1)S(1)}, u32[]{:S(2)}, u32[]{:S(2)}) %collective-permute-start.5) | collective-permute-done | bytes 426016 | tf_op jit(solution)/shard_map/ppermute | solution.py:30
  58.1 17.0 %collective-permute-done.15 = bf16[32,2,3328]{2,0,1:T(8,128)(2,1)S(1)} collective-permute-done((bf16[32,2,3328]{2,0,1:T(8,128)(2,1)S(1)}, bf16[32,2,3328]{2,0,1:T(8,128)(2,1)S(1)}, u32[]{:S(2)}, u32[]{:S(2)}) %collective-permute-start.15) | collective-permute-done | bytes 426016 | tf_op jit(solution)/shard_map/ppermute | solution.py:30
  76.7 8.9 %collective-permute-start.14 = (bf16[32,2,3328]{2,0,1:T(8,128)(2,1)S(1)}, bf16[32,2,3328]{2,0,1:T(8,128)(2,1)S(1)}, u32[]{:S(2)}, u32[]{:S(2)}) collective-permute-start(bf16[32,2,3328]{2,0,1:T(8,128)(2,1)S(1)} %get-tuple-element.19), channel_id=1, source_target_pairs={{0,4},{1,5},{2,6},{3,7},{16,20},{17,21},{18,22},{19,23}} | collective-permute-start | bytes 1277960 | tf_op jit(solution)/shard_map/ppermute | solution.py:30
  85.6 0.7 collective-permute-start.19
  86.4 0.7 collective-permute-start.16
  87.1 0.8 collective-permute-start.21
  87.9 1.4 %fusion.18 = (bf16[32,2,3328]{2,0,1:T(8,128)(2,1)S(1)}, bf16[32,2,3328]{2,0,1:T(8,128)(2,1)S(1)}) fusion(bf16[32,2,3328]{2,0,1:T(8,128)(2,1)S(1)} %collective-permute-done.4, bf16[32,2,3328]{2,0,1:T(8,128)(2,1)S(1)} %collective-permute-done.6, bf16[4,32,2,3328]{3,1,0,2:T(8,128)(2,1)S(1)} %bitcast.89, s32[]{:T(128)S(6)} %min.17, ...), kind=kLoop, calls=%fused_computation.23 | loop fusion | flops 2129920 | bytes 3407880 | tf_op jit(solution)/shard_map/convert_element_type | solution.py:26
  89.3 4.9 %collective-permute-done.14 = bf16[32,2,3328]{2,0,1:T(8,128)(2,1)S(1)} collective-permute-done((bf16[32,2,3328]{2,0,1:T(8,128)(2,1)S(1)}, bf16[32,2,3328]{2,0,1:T(8,128)(2,1)S(1)}, u32[]{:S(2)}, u32[]{:S(2)}) %collective-permute-start.14) | collective-permute-done | bytes 426016 | tf_op jit(solution)/shard_map/ppermute | solution.py:30
  94.8 4.4 %collective-permute-start.13 = (bf16[32,2,3328]{2,0,1:T(8,128)(2,1)S(1)}, bf16[32,2,3328]{2,0,1:T(8,128)(2,1)S(1)}, u32[]{:S(2)}, u32[]{:S(2)}) collective-permute-start(bf16[32,2,3328]{2,0,1:T(8,128)(2,1)S(1)} %get-tuple-element.20), channel_id=1, source_target_pairs={{0,4},{1,5},{2,6},{3,7},{16,20},{17,21},{18,22},{19,23}} | collective-permute-start | bytes 1277960 | tf_op jit(solution)/shard_map/ppermute | solution.py:30
  99.2 1.3 %collective-permute-start.12 = (bf16[32,2,3328]{2,0,1:T(8,128)(2,1)S(1)}, bf16[32,2,3328]{2,0,1:T(8,128)(2,1)S(1)}, u32[]{:S(2)}, u32[]{:S(2)}) collective-permute-start(bf16[32,2,3328]{2,0,1:T(8,128)(2,1)S(1)} %get-tuple-element.6), channel_id=1, source_target_pairs={{4,0},{8,4},{5,1},{9,5},{6,2},{10,6},{7,3},{11,7},{20,16},{24,20},... | collective-permute-start | bytes 1277960 | tf_op jit(solution)/shard_map/ppermute | solution.py:41
  100.6 0.7 collective-permute-start.7
  101.6 0.7 collective-permute-start.18
  103.0 9.0 %collective-permute-done.12 = bf16[32,2,3328]{2,0,1:T(8,128)(2,1)S(1)} collective-permute-done((bf16[32,2,3328]{2,0,1:T(8,128)(2,1)S(1)}, bf16[32,2,3328]{2,0,1:T(8,128)(2,1)S(1)}, u32[]{:S(2)}, u32[]{:S(2)}) %collective-permute-start.12) | collective-permute-done | bytes 426016 | tf_op jit(solution)/shard_map/ppermute | solution.py:41
  112.0 1.3 %collective-permute-start.22 = (bf16[32,2,3328]{2,0,1:T(8,128)(2,1)S(1)}, bf16[32,2,3328]{2,0,1:T(8,128)(2,1)S(1)}, u32[]{:S(2)}, u32[]{:S(2)}) collective-permute-start(bf16[32,2,3328]{2,0,1:T(8,128)(2,1)S(1)} %get-tuple-element.14), channel_id=1, source_target_pairs={{4,0},{8,4},{5,1},{9,5},{6,2},{10,6},{7,3},{11,7},{20,16},{24,20},... | collective-permute-start | bytes 1277960 | tf_op jit(solution)/shard_map/ppermute | solution.py:41
  113.3 1.3 %fusion.19 = f32[32,2,3328]{2,0,1:T(8,128)S(1)} fusion(bf16[32,2,3328]{2,0,1:T(8,128)(2,1)S(1)} %collective-permute-done.8, bf16[32,2,3328]{2,0,1:T(8,128)(2,1)S(1)} %collective-permute-done.12, bf16[32,2,3328]{2,0,1:T(8,128)(2,1)} %collective-permute-done.3, bf16[32,2,3328]{2,0,1:T(8,128)(2,1)S(1)} %collective-permute-done.7, ...), kind=kLoop, calls=%fused_computation.25 | loop fusion | flops 1490944 | bytes 2981892 | tf_op jit(solution)/shard_map/add | solution.py:64
  114.8 9.7 %collective-permute-done.22 = bf16[32,2,3328]{2,0,1:T(8,128)(2,1)S(1)} collective-permute-done((bf16[32,2,3328]{2,0,1:T(8,128)(2,1)S(1)}, bf16[32,2,3328]{2,0,1:T(8,128)(2,1)S(1)}, u32[]{:S(2)}, u32[]{:S(2)}) %collective-permute-start.22) | collective-permute-done | bytes 426016 | tf_op jit(solution)/shard_map/ppermute | solution.py:41
  124.9 0.8 pad_maximum_fusion
  (36 shorter events, 5.4 us)
Async XLA Ops:
  0.0 6.5 %collective-permute-start = (bf16[32,2560]{1,0:T(8,128)(2,1)}, bf16[32,2560]{1,0:T(8,128)(2,1)S(1)}, u32[]{:S(2)}, u32[]{:S(2)}) collective-permute-start(bf16[32,2560]{1,0:T(8,128)(2,1)} %param.2), channel_id=1, source_target_pairs={{0,1},{1,2},{2,3},{3,0},{4,5},{5,6},{6,7},{7,4},{8,9},{9,10},{10,1... | collective-permute-start | bytes 491528 | tf_op jit(solution)/shard_map/ppermute | solution.py:16
  0.5 7.7 %collective-permute-start.1 = (bf16[32,2560]{1,0:T(8,128)(2,1)}, bf16[32,2560]{1,0:T(8,128)(2,1)S(1)}, u32[]{:S(2)}, u32[]{:S(2)}) collective-permute-start(bf16[32,2560]{1,0:T(8,128)(2,1)} %param.2), channel_id=1, source_target_pairs={{0,2},{1,3},{2,0},{3,1},{4,6},{5,7},{6,4},{7,5},{8,10},{9,11},{10,... | collective-permute-start | bytes 491528 | tf_op jit(solution)/shard_map/ppermute | solution.py:16
  3.0 7.8 %collective-permute-start.2 = (bf16[32,2560]{1,0:T(8,128)(2,1)}, bf16[32,2560]{1,0:T(8,128)(2,1)S(1)}, u32[]{:S(2)}, u32[]{:S(2)}) collective-permute-start(bf16[32,2560]{1,0:T(8,128)(2,1)} %param.2), channel_id=1, source_target_pairs={{0,3},{1,0},{2,1},{3,2},{4,7},{5,4},{6,5},{7,6},{8,11},{9,8},{10,9... | collective-permute-start | bytes 491528 | tf_op jit(solution)/shard_map/ppermute | solution.py:16
  10.8 13.4 %copy-start = (bf16[4,32,2560]{2,1,0:T(8,128)(2,1)}, bf16[4,32,2560]{2,1,0:T(8,128)(2,1)S(1)}, u32[]{:S(2)}) copy-start(bf16[4,32,2560]{2,1,0:T(8,128)(2,1)S(1)} %bitcast_dynamic-update-slice_fusion) | copy-start | bytes 1966084
  25.4 60.2 %collective-permute-start.9 = (bf16[32,2,3328]{2,0,1:T(8,128)(2,1)}, bf16[32,2,3328]{2,0,1:T(8,128)(2,1)}, u32[]{:S(2)}, u32[]{:S(2)}) collective-permute-start(bf16[32,2,3328]{2,0,1:T(8,128)(2,1)} %get-tuple-element.12), channel_id=1, source_target_pairs={{12,8},{13,9},{14,10},{15,11},{28,24},{29,25},{30,26},{31,27}} | collective-permute-start | bytes 1277960 | tf_op jit(solution)/shard_map/ppermute | solution.py:38
  26.9 74.7 %collective-permute-start.3 = (bf16[32,2,3328]{2,0,1:T(8,128)(2,1)}, bf16[32,2,3328]{2,0,1:T(8,128)(2,1)}, u32[]{:S(2)}, u32[]{:S(2)}) collective-permute-start(bf16[32,2,3328]{2,0,1:T(8,128)(2,1)} %get-tuple-element.12), channel_id=1, source_target_pairs={{0,4},{1,5},{2,6},{3,7},{16,20},{17,21},{18,22},{19,23}} | collective-permute-start | bytes 1277960 | tf_op jit(solution)/shard_map/ppermute | solution.py:30
  44.7 3.5 %collective-permute-start.10 = (bf16[32,2,3328]{2,0,1:T(8,128)(2,1)}, bf16[32,2,3328]{2,0,1:T(8,128)(2,1)S(1)}, u32[]{:S(2)}, u32[]{:S(2)}) collective-permute-start(bf16[32,2,3328]{2,0,1:T(8,128)(2,1)} %get-tuple-element.10), channel_id=1, source_target_pairs={{12,8},{13,9},{14,10},{15,11},{28,24},{29,25},{30,26},{31,27}} | collective-permute-start | bytes 1277960 | tf_op jit(solution)/shard_map/ppermute | solution.py:38
  45.4 11.8 %collective-permute-start.5 = (bf16[32,2,3328]{2,0,1:T(8,128)(2,1)}, bf16[32,2,3328]{2,0,1:T(8,128)(2,1)S(1)}, u32[]{:S(2)}, u32[]{:S(2)}) collective-permute-start(bf16[32,2,3328]{2,0,1:T(8,128)(2,1)} %get-tuple-element.9), channel_id=1, source_target_pairs={{0,4},{1,5},{2,6},{3,7},{16,20},{17,21},{18,22},{19,23}} | collective-permute-start | bytes 1277960 | tf_op jit(solution)/shard_map/ppermute | solution.py:30
  46.7 30.0 %collective-permute-start.4 = (bf16[32,2,3328]{2,0,1:T(8,128)(2,1)}, bf16[32,2,3328]{2,0,1:T(8,128)(2,1)S(1)}, u32[]{:S(2)}, u32[]{:S(2)}) collective-permute-start(bf16[32,2,3328]{2,0,1:T(8,128)(2,1)} %get-tuple-element.11), channel_id=1, source_target_pairs={{0,4},{1,5},{2,6},{3,7},{16,20},{17,21},{18,22},{19,23}} | collective-permute-start | bytes 1277960 | tf_op jit(solution)/shard_map/ppermute | solution.py:30
  48.2 26.9 %collective-permute-start.15 = (bf16[32,2,3328]{2,0,1:T(8,128)(2,1)S(1)}, bf16[32,2,3328]{2,0,1:T(8,128)(2,1)S(1)}, u32[]{:S(2)}, u32[]{:S(2)}) collective-permute-start(bf16[32,2,3328]{2,0,1:T(8,128)(2,1)S(1)} %get-tuple-element.17), channel_id=1, source_target_pairs={{0,4},{1,5},{2,6},{3,7},{16,20},{17,21},{18,22},{19,23}} | collective-permute-start | bytes 1277960 | tf_op jit(solution)/shard_map/ppermute | solution.py:30
  57.2 18.6 %collective-permute-start.20 = (bf16[32,2,3328]{2,0,1:T(8,128)(2,1)S(1)}, bf16[32,2,3328]{2,0,1:T(8,128)(2,1)S(1)}, u32[]{:S(2)}, u32[]{:S(2)}) collective-permute-start(bf16[32,2,3328]{2,0,1:T(8,128)(2,1)S(1)} %get-tuple-element.18), channel_id=1, source_target_pairs={{12,8},{13,9},{14,10},{15,11},{28,24},{29,25},{30,26},{31,27}} | collective-permute-start | bytes 1277960 | tf_op jit(solution)/shard_map/ppermute | solution.py:38
  75.1 11.3 %collective-permute-start.11 = (bf16[32,2,3328]{2,0,1:T(8,128)(2,1)S(1)}, bf16[32,2,3328]{2,0,1:T(8,128)(2,1)S(1)}, u32[]{:S(2)}, u32[]{:S(2)}) collective-permute-start(bf16[32,2,3328]{2,0,1:T(8,128)(2,1)S(1)} %get-tuple-element.8), channel_id=1, source_target_pairs={{8,4},{9,5},{10,6},{11,7},{24,20},{25,21},{26,22},{27,23}} | collective-permute-start | bytes 1277960 | tf_op jit(solution)/shard_map/ppermute | solution.py:41
  75.8 11.3 %collective-permute-start.6 = (bf16[32,2,3328]{2,0,1:T(8,128)(2,1)S(1)}, bf16[32,2,3328]{2,0,1:T(8,128)(2,1)S(1)}, u32[]{:S(2)}, u32[]{:S(2)}) collective-permute-start(bf16[32,2,3328]{2,0,1:T(8,128)(2,1)S(1)} %get-tuple-element.7), channel_id=1, source_target_pairs={{4,8},{5,9},{6,10},{7,11},{20,24},{21,25},{22,26},{23,27}} | collective-permute-start | bytes 1277960 | tf_op jit(solution)/shard_map/ppermute | solution.py:34
  76.7 17.4 %collective-permute-start.14 = (bf16[32,2,3328]{2,0,1:T(8,128)(2,1)S(1)}, bf16[32,2,3328]{2,0,1:T(8,128)(2,1)S(1)}, u32[]{:S(2)}, u32[]{:S(2)}) collective-permute-start(bf16[32,2,3328]{2,0,1:T(8,128)(2,1)S(1)} %get-tuple-element.19), channel_id=1, source_target_pairs={{0,4},{1,5},{2,6},{3,7},{16,20},{17,21},{18,22},{19,23}} | collective-permute-start | bytes 1277960 | tf_op jit(solution)/shard_map/ppermute | solution.py:30
  85.6 9.2 %collective-permute-start.19 = (bf16[32,2,3328]{2,0,1:T(8,128)(2,1)S(1)}, bf16[32,2,3328]{2,0,1:T(8,128)(2,1)S(1)}, u32[]{:S(2)}, u32[]{:S(2)}) collective-permute-start(bf16[32,2,3328]{2,0,1:T(8,128)(2,1)S(1)} %get-tuple-element.20), channel_id=1, source_target_pairs={{12,8},{13,9},{14,10},{15,11},{28,24},{29,25},{30,26},{31,27}} | collective-permute-start | bytes 1277960 | tf_op jit(solution)/shard_map/ppermute | solution.py:38
  86.4 12.9 %collective-permute-start.16 = (bf16[32,2,3328]{2,0,1:T(8,128)(2,1)S(1)}, bf16[32,2,3328]{2,0,1:T(8,128)(2,1)S(1)}, u32[]{:S(2)}, u32[]{:S(2)}) collective-permute-start(bf16[32,2,3328]{2,0,1:T(8,128)(2,1)S(1)} %get-tuple-element.15), channel_id=1, source_target_pairs={{4,8},{5,9},{6,10},{7,11},{20,24},{21,25},{22,26},{23,27}} | collective-permute-start | bytes 1277960 | tf_op jit(solution)/shard_map/ppermute | solution.py:34
  87.1 7.1 %copy-start.1 = (bf16[32,2,3328]{2,0,1:T(8,128)(2,1)S(1)}, bf16[32,2,3328]{2,0,1:T(8,128)(2,1)}, u32[]{:S(2)}) copy-start(bf16[32,2,3328]{2,0,1:T(8,128)(2,1)} %get-tuple-element.11) | copy-start | bytes 1277956
  87.1 13.5 %collective-permute-start.21 = (bf16[32,2,3328]{2,0,1:T(8,128)(2,1)S(1)}, bf16[32,2,3328]{2,0,1:T(8,128)(2,1)S(1)}, u32[]{:S(2)}, u32[]{:S(2)}) collective-permute-start(bf16[32,2,3328]{2,0,1:T(8,128)(2,1)S(1)} %get-tuple-element.16), channel_id=1, source_target_pairs={{8,4},{9,5},{10,6},{11,7},{24,20},{25,21},{26,22},{27,23}} | collective-permute-start | bytes 1277960 | tf_op jit(solution)/shard_map/ppermute | solution.py:41
  94.1 8.2 %collective-permute-start.8 = (bf16[32,2,3328]{2,0,1:T(8,128)(2,1)S(1)}, bf16[32,2,3328]{2,0,1:T(8,128)(2,1)S(1)}, u32[]{:S(2)}, u32[]{:S(2)}) collective-permute-start(bf16[32,2,3328]{2,0,1:T(8,128)(2,1)S(1)} %copy-done.1), channel_id=1, source_target_pairs={{12,8},{13,9},{14,10},{15,11},{28,24},{29,25},{30,26},{31,27}} | collective-permute-start | bytes 1277960 | tf_op jit(solution)/shard_map/ppermute | solution.py:38
  94.8 19.9 %collective-permute-start.13 = (bf16[32,2,3328]{2,0,1:T(8,128)(2,1)S(1)}, bf16[32,2,3328]{2,0,1:T(8,128)(2,1)S(1)}, u32[]{:S(2)}, u32[]{:S(2)}) collective-permute-start(bf16[32,2,3328]{2,0,1:T(8,128)(2,1)S(1)} %get-tuple-element.20), channel_id=1, source_target_pairs={{0,4},{1,5},{2,6},{3,7},{16,20},{17,21},{18,22},{19,23}} | collective-permute-start | bytes 1277960 | tf_op jit(solution)/shard_map/ppermute | solution.py:30
  99.2 12.8 %collective-permute-start.12 = (bf16[32,2,3328]{2,0,1:T(8,128)(2,1)S(1)}, bf16[32,2,3328]{2,0,1:T(8,128)(2,1)S(1)}, u32[]{:S(2)}, u32[]{:S(2)}) collective-permute-start(bf16[32,2,3328]{2,0,1:T(8,128)(2,1)S(1)} %get-tuple-element.6), channel_id=1, source_target_pairs={{4,0},{8,4},{5,1},{9,5},{6,2},{10,6},{7,3},{11,7},{20,16},{24,20},... | collective-permute-start | bytes 1277960 | tf_op jit(solution)/shard_map/ppermute | solution.py:41
  100.6 12.8 %collective-permute-start.7 = (bf16[32,2,3328]{2,0,1:T(8,128)(2,1)S(1)}, bf16[32,2,3328]{2,0,1:T(8,128)(2,1)S(1)}, u32[]{:S(2)}, u32[]{:S(2)}) collective-permute-start(bf16[32,2,3328]{2,0,1:T(8,128)(2,1)S(1)} %get-tuple-element.5), channel_id=1, source_target_pairs={{4,8},{8,12},{5,9},{9,13},{6,10},{10,14},{7,11},{11,15},{20,24},{2... | collective-permute-start | bytes 1277960 | tf_op jit(solution)/shard_map/ppermute | solution.py:34
  101.6 13.2 %collective-permute-start.18 = (bf16[32,2,3328]{2,0,1:T(8,128)(2,1)S(1)}, bf16[32,2,3328]{2,0,1:T(8,128)(2,1)S(1)}, u32[]{:S(2)}, u32[]{:S(2)}) collective-permute-start(bf16[32,2,3328]{2,0,1:T(8,128)(2,1)S(1)} %get-tuple-element.19), channel_id=1, source_target_pairs={{12,8},{13,9},{14,10},{15,11},{28,24},{29,25},{30,26},{31,27}} | collective-permute-start | bytes 1277960 | tf_op jit(solution)/shard_map/ppermute | solution.py:38
  102.3 12.5 %collective-permute-start.17 = (bf16[32,2,3328]{2,0,1:T(8,128)(2,1)S(1)}, bf16[32,2,3328]{2,0,1:T(8,128)(2,1)S(1)}, u32[]{:S(2)}, u32[]{:S(2)}) collective-permute-start(bf16[32,2,3328]{2,0,1:T(8,128)(2,1)S(1)} %get-tuple-element.13), channel_id=1, source_target_pairs={{4,8},{8,12},{5,9},{9,13},{6,10},{10,14},{7,11},{11,15},{20,24},{2... | collective-permute-start | bytes 1277960 | tf_op jit(solution)/shard_map/ppermute | solution.py:34
  112.0 12.4 %collective-permute-start.22 = (bf16[32,2,3328]{2,0,1:T(8,128)(2,1)S(1)}, bf16[32,2,3328]{2,0,1:T(8,128)(2,1)S(1)}, u32[]{:S(2)}, u32[]{:S(2)}) collective-permute-start(bf16[32,2,3328]{2,0,1:T(8,128)(2,1)S(1)} %get-tuple-element.14), channel_id=1, source_target_pairs={{4,0},{8,4},{5,1},{9,5},{6,2},{10,6},{7,3},{11,7},{20,16},{24,20},... | collective-permute-start | bytes 1277960 | tf_op jit(solution)/shard_map/ppermute | solution.py:41

commit v14 on v4

--- a/solution.py
+++ b/solution.py
@@ -55,6 +55,10 @@
     for i in range(k):
         w = gate_up[:, :, edges[i] : edges[i + 1]]
         part = jnp.einsum("td,gdf->tgf", held, w, preferred_element_type=jnp.float32).astype(jnp.bfloat16)
+        if i == k - 1 and k > 1:
+            own = lax.psum_scatter(part, "row", scatter_dimension=0, tiled=True).astype(jnp.float32)
+            outs.append((jax.nn.silu(own[:, 0]) * own[:, 1]).astype(jnp.bfloat16))
+            continue
         part = part.reshape(n, tb, 2, edges[i + 1] - edges[i])
         own = lax.dynamic_index_in_dim(part, p, 0, keepdims=False).astype(jnp.float32)
         if n > 1:

time: 110 us -> 126 us (1.15)
  waiting for transfers between devices: 24.9 us -> 47.7 us
  starting transfers between devices: 49 us -> 26.9 us
  between operations: 0.46 us -> 13.6 us
  other arithmetic: 4.77 us -> 7.95 us
    ppermute x6 -> x3, starting transfers between devices: 32.8 us -> 14.8 us  [line_reduce(): origin = [lax.ppermute(part[n - r], 'row', [(0, 1)]) for r in range(1, n)]]
    ppermute x4 -> x2, waiting for transfers between devices: 8.04 us -> 23.1 us  [line_reduce(): lax.ppermute(add(block(p - n + r), minus), 'row', [(q, q - 1) for q in ra...]
    ppermute x6 -> x3, waiting for transfers between devices: 11.5 us -> 17.5 us  [line_reduce(): origin = [lax.ppermute(part[n - r], 'row', [(0, 1)]) for r in range(1, n)]]
    convert_element_type x4 -> x2, other arithmetic: 2.23 us -> 4.6 us  [add(): return (a.astype(jnp.float32) + b.astype(jnp.float32)).astype(jnp.bfloat16)]
    ppermute x6 -> x3, starting transfers between devices: 4.86 us -> 2.82 us  [line_reduce(): lax.ppermute(part[r - 1], 'row', [(n - 1, n - 2)])]
    reduce_scatter x0 -> x1, waiting for transfers between devices: none -> 1.75 us  [on_device(): lax.psum_scatter(part, 'row', scatter_dimension=0, tiled=True)]
    ppermute x4 -> x2, starting transfers between devices: 3.96 us -> 2.7 us  [line_reduce(): lax.ppermute(add(block(p - n + r), minus), 'row', [(q, q - 1) for q in ra...]
    ppermute x4 -> x2, starting transfers between devices: 2.74 us -> 2.11 us  [line_reduce(): lax.ppermute(add(block(p + n - r), plus), 'row', [(q, q + 1) for q in ran...]
  transfers between devices with their start and end apart: 23 -> 14, of which waited for: 6 -> 7; matrix products, arithmetic and copies ran while one was open for 17% -> 17% of each run, Pallas kernels for 0% -> 0%
where the time goes in v14:
time: 126 us
  waiting for transfers between devices  47.7 us (38%)
  matrix products  27.7 us (22%)
  starting transfers between devices  26.9 us (21%)
  between operations  13.6 us (11%)
  other arithmetic  7.95 us (6%)
  local copies, waits for them, and re-layouts  2.28 us (2%)
    dot_general x2, matrix products, on_device(): jnp.einsum('td,gdf->tgf', held, w, preferred_element_type=jnp.float32)  27.7 us
    ppermute x2, waiting for transfers between devices, line_reduce(): lax.ppermute(add(block(p - n + r), minus), 'row', [(q, q - 1) for q in ra...  23.1 us
    ppermute x3, waiting for transfers between devices, line_reduce(): origin = [lax.ppermute(part[n - r], 'row', [(0, 1)]) for r in range(1, n)]  17.5 us
    ppermute x3, starting transfers between devices, line_reduce(): origin = [lax.ppermute(part[n - r], 'row', [(0, 1)]) for r in range(1, n)]  14.8 us
    ppermute x3, waiting for transfers between devices, gather_cols(): got = lax.ppermute(tokens, 'col', [(i, (i + s) % m) for i in range(m)])  5.3 us
    convert_element_type x2, other arithmetic, add(): return (a.astype(jnp.float32) + b.astype(jnp.float32)).astype(jnp.bfloat16)  4.6 us
    ppermute x3, starting transfers between devices, gather_cols(): got = lax.ppermute(tokens, 'col', [(i, (i + s) % m) for i in range(m)])  4.43 us
    ppermute x3, starting transfers between devices, line_reduce(): lax.ppermute(part[r - 1], 'row', [(n - 1, n - 2)])  2.82 us
  transfers between devices with their start and end apart: 14, of which 7 were waited for; matrix products, arithmetic and copies ran while one was open for 17% of the time, Pallas kernels for 0%

profile of v14, /device:TPU:0, one launch (start us, length us, event | category | flops | bytes accessed | tf_op | source)
XLA Modules:
  0.0 126.1 jit_solution(2326104338113907601)
XLA Ops:
  6.5 0.5 collective-permute-start
  7.0 2.5 %collective-permute-start.1 = (bf16[32,2560]{1,0:T(8,128)(2,1)}, bf16[32,2560]{1,0:T(8,128)(2,1)S(1)}, u32[]{:S(2)}, u32[]{:S(2)}) collective-permute-start(bf16[32,2560]{1,0:T(8,128)(2,1)} %param.2), channel_id=1, source_target_pairs={{0,2},{1,3},{2,0},{3,1},{4,6},{5,7},{6,4},{7,5},{8,10},{9,11},{10,... | collective-permute-start | bytes 491528 | tf_op jit(solution)/shard_map/ppermute | solution.py:15
  9.5 1.5 %collective-permute-start.2 = (bf16[32,2560]{1,0:T(8,128)(2,1)}, bf16[32,2560]{1,0:T(8,128)(2,1)S(1)}, u32[]{:S(2)}, u32[]{:S(2)}) collective-permute-start(bf16[32,2560]{1,0:T(8,128)(2,1)} %param.2), channel_id=1, source_target_pairs={{0,3},{1,0},{2,1},{3,2},{4,7},{5,4},{6,5},{7,6},{8,11},{9,8},{10,9... | collective-permute-start | bytes 491528 | tf_op jit(solution)/shard_map/ppermute | solution.py:15
  11.0 1.0 bitcast_dynamic-update-slice_fusion.3
  12.0 1.0 collective-permute-done
  13.1 1.7 %collective-permute-done.1 = bf16[32,2560]{1,0:T(8,128)(2,1)S(1)} collective-permute-done((bf16[32,2560]{1,0:T(8,128)(2,1)}, bf16[32,2560]{1,0:T(8,128)(2,1)S(1)}, u32[]{:S(2)}, u32[]{:S(2)}) %collective-permute-start.1) | collective-permute-done | bytes 163872 | tf_op jit(solution)/shard_map/ppermute | solution.py:15
  14.8 2.6 %collective-permute-done.2 = bf16[32,2560]{1,0:T(8,128)(2,1)S(1)} collective-permute-done((bf16[32,2560]{1,0:T(8,128)(2,1)}, bf16[32,2560]{1,0:T(8,128)(2,1)S(1)}, u32[]{:S(2)}, u32[]{:S(2)}) %collective-permute-start.2) | collective-permute-done | bytes 163872 | tf_op jit(solution)/shard_map/ppermute | solution.py:15
  17.4 13.3 %fusion.4 = bf16[128,2,3328]{2,0,1:T(8,128)(2,1)S(1)} fusion(bf16[128,2560,1]{1,0,2:T(8,128)(2,1)S(1)} %bitcast.64, bf16[2,2560,6656]{2,1,0:T(8,128)(2,1)} %param.3), kind=kOutput, calls=%fused_computation.4 | convolution fusion | flops 4362928128 | bytes 36438016 | tf_op jit(solution)/shard_map/td,gdf->tgf/dot_general | solution.py:57
  30.7 1.2 fusion.20
  32.0 4.2 %collective-permute-start.5 = (bf16[32,2,3328]{2,0,1:T(8,128)(2,1)}, bf16[32,2,3328]{2,0,1:T(8,128)(2,1)}, u32[]{:S(2)}, u32[]{:S(2)}) collective-permute-start(bf16[32,2,3328]{2,0,1:T(8,128)(2,1)} %get-tuple-element.13), channel_id=1, source_target_pairs={{0,4},{1,5},{2,6},{3,7},{16,20},{17,21},{18,22},{19,23}} | collective-permute-start | bytes 1277960 | tf_op jit(solution)/shard_map/up/ppermute | solution.py:28
  36.2 1.4 %collective-permute-start.10 = (bf16[32,2,3328]{2,0,1:T(8,128)(2,1)}, bf16[32,2,3328]{2,0,1:T(8,128)(2,1)}, u32[]{:S(2)}, u32[]{:S(2)}) collective-permute-start(bf16[32,2,3328]{2,0,1:T(8,128)(2,1)} %get-tuple-element.12), channel_id=1, source_target_pairs={{12,8},{13,9},{14,10},{15,11},{28,24},{29,25},{30,26},{31,27}} | collective-permute-start | bytes 1277960 | tf_op jit(solution)/shard_map/down/ppermute | solution.py:35
  37.6 1.3 %collective-permute-start.4 = (bf16[32,2,3328]{2,0,1:T(8,128)(2,1)}, bf16[32,2,3328]{2,0,1:T(8,128)(2,1)S(1)}, u32[]{:S(2)}, u32[]{:S(2)}) collective-permute-start(bf16[32,2,3328]{2,0,1:T(8,128)(2,1)} %get-tuple-element.14), channel_id=1, source_target_pairs={{0,4},{1,5},{2,6},{3,7},{16,20},{17,21},{18,22},{19,23}} | collective-permute-start | bytes 1277960 | tf_op jit(solution)/shard_map/up/ppermute | solution.py:28
  39.0 0.7 collective-permute-start.9
  39.7 6.3 %collective-permute-done.5 = bf16[32,2,3328]{2,0,1:T(8,128)(2,1)} collective-permute-done((bf16[32,2,3328]{2,0,1:T(8,128)(2,1)}, bf16[32,2,3328]{2,0,1:T(8,128)(2,1)}, u32[]{:S(2)}, u32[]{:S(2)}) %collective-permute-start.5) | collective-permute-done | bytes 426016 | tf_op jit(solution)/shard_map/up/ppermute | solution.py:28
  45.9 2.2 %fusion.12 = (bf16[32,2,3328]{2,0,1:T(8,128)(2,1)}, bf16[32,2,3328]{2,0,1:T(8,128)(2,1)}) fusion(bf16[32,2,3328]{2,0,1:T(8,128)(2,1)} %collective-permute-done.5, bf16[4,32,2,3328]{3,1,0,2:T(8,128)(2,1)S(1)} %bitcast.61, s32[]{:T(128)S(6)} %min.14, bf16[32,2,3328]{2,0,1:T(8,128)(2,1)} %collective-permute-done.10, s32[]{:T(128)S(6)} %min.16), kind=kLoop, calls=%fused_computation.11 | loop fusion | flops 1703936 | bytes 2555912 | tf_op jit(solution)/shard_map/up/convert_element_type | solution.py:25
  48.2 1.4 %collective-permute-start.6 = (bf16[32,2,3328]{2,0,1:T(8,128)(2,1)}, bf16[32,2,3328]{2,0,1:T(8,128)(2,1)}, u32[]{:S(2)}, u32[]{:S(2)}) collective-permute-start(bf16[32,2,3328]{2,0,1:T(8,128)(2,1)} %get-tuple-element.9), channel_id=1, source_target_pairs={{4,8},{5,9},{6,10},{7,11},{20,24},{21,25},{22,26},{23,27}} | collective-permute-start | bytes 1277960 | tf_op jit(solution)/shard_map/up/ppermute | solution.py:32
  49.6 1.4 %collective-permute-start.11 = (bf16[32,2,3328]{2,0,1:T(8,128)(2,1)}, bf16[32,2,3328]{2,0,1:T(8,128)(2,1)}, u32[]{:S(2)}, u32[]{:S(2)}) collective-permute-start(bf16[32,2,3328]{2,0,1:T(8,128)(2,1)} %get-tuple-element.10), channel_id=1, source_target_pairs={{8,4},{9,5},{10,6},{11,7},{24,20},{25,21},{26,22},{27,23}} | collective-permute-start | bytes 1277960 | tf_op jit(solution)/shard_map/down/ppermute | solution.py:38
  51.0 14.3 %fusion.7 = bf16[128,2,3328]{2,0,1:T(8,128)(2,1)} fusion(bf16[2,2560,6656]{2,1,0:T(8,128)(2,1)} %param.3, bf16[128,2560]{1,0:T(8,128)(2,1)S(1)} %bitcast.65), kind=kOutput, calls=%fused_computation.5 | convolution fusion | flops 4362928128 | bytes 36438016 | tf_op jit(solution)/shard_map/td,gdf->tgf/dot_general | solution.py:57
  65.3 0.0 reduce-scatter.2.cloned.1.call-update
  65.4 0.7 collective-permute-start.8
  66.1 9.3 %collective-permute-start.3 = (bf16[32,2,3328]{2,0,1:T(8,128)(2,1)}, bf16[32,2,3328]{2,0,1:T(8,128)(2,1)}, u32[]{:S(2)}, u32[]{:S(2)}) collective-permute-start(bf16[32,2,3328]{2,0,1:T(8,128)(2,1)} %get-tuple-element.11), channel_id=1, source_target_pairs={{0,4},{1,5},{2,6},{3,7},{16,20},{17,21},{18,22},{19,23}} | collective-permute-start | bytes 1277960 | tf_op jit(solution)/shard_map/up/ppermute | solution.py:28
  75.4 2.4 %fusion.13 = (bf16[32,2,3328]{2,0,1:T(8,128)(2,1)}, bf16[32,2,3328]{2,0,1:T(8,128)(2,1)}) fusion(bf16[32,2,3328]{2,0,1:T(8,128)(2,1)S(1)} %collective-permute-done.4, bf16[32,2,3328]{2,0,1:T(8,128)(2,1)} %collective-permute-done.6, bf16[4,32,2,3328]{3,1,0,2:T(8,128)(2,1)S(1)} %bitcast.62, s32[]{:T(128)S(6)} %min.13, ...), kind=kLoop, calls=%fused_computation.13 | loop fusion | flops 2129920 | bytes 3407880 | tf_op jit(solution)/shard_map/up/convert_element_type | solution.py:25
  77.8 1.3 %collective-permute-start.12 = (bf16[32,2,3328]{2,0,1:T(8,128)(2,1)}, bf16[32,2,3328]{2,0,1:T(8,128)(2,1)S(1)}, u32[]{:S(2)}, u32[]{:S(2)}) collective-permute-start(bf16[32,2,3328]{2,0,1:T(8,128)(2,1)} %get-tuple-element.8), channel_id=1, source_target_pairs={{4,0},{8,4},{5,1},{9,5},{6,2},{10,6},{7,3},{11,7},{20,16},{24,20},... | collective-permute-start | bytes 1277960 | tf_op jit(solution)/shard_map/down/ppermute | solution.py:38
  79.0 0.7 collective-permute-start.7
  79.7 11.2 %collective-permute-done.3 = bf16[32,2,3328]{2,0,1:T(8,128)(2,1)} collective-permute-done((bf16[32,2,3328]{2,0,1:T(8,128)(2,1)}, bf16[32,2,3328]{2,0,1:T(8,128)(2,1)}, u32[]{:S(2)}, u32[]{:S(2)}) %collective-permute-start.3) | collective-permute-done | bytes 426016 | tf_op jit(solution)/shard_map/up/ppermute | solution.py:28
  91.0 23.1 %collective-permute-done.12 = bf16[32,2,3328]{2,0,1:T(8,128)(2,1)S(1)} collective-permute-done((bf16[32,2,3328]{2,0,1:T(8,128)(2,1)}, bf16[32,2,3328]{2,0,1:T(8,128)(2,1)S(1)}, u32[]{:S(2)}, u32[]{:S(2)}) %collective-permute-start.12) | collective-permute-done | bytes 426016 | tf_op jit(solution)/shard_map/down/ppermute | solution.py:38
  114.1 1.3 fusion.14
  115.4 0.1 fusion.19
  115.5 1.7 %reduce-scatter.2.cloned.1.call-done = bf16[32,2,3328]{2,0,1:T(8,128)(2,1)} async-done(((bf16[128,2,3328]{2,0,1:T(8,128)(2,1)}), bf16[32,2,3328]{2,0,1:T(8,128)(2,1)}) %reduce-scatter.2.cloned.1.call-update) | async-done | bytes 426000 | tf_op jit(solution)/shard_map/reduce_scatter | solution.py:59
  117.2 1.1 convert_element_type.98
  118.3 0.1 fusion.17
  118.4 0.8 pad_maximum_fusion
  (12 shorter events, 0.1 us)
Async XLA Ops:
  6.5 110.7 %reduce-scatter.2.cloned.1.call-start = ((), (), s32[]{:S(2)}) async-start(), calls=%async_computation.1 | async-start | bytes 2129920 | tf_op jit(solution)/shard_map/reduce_scatter | solution.py:59
  6.5 6.5 %collective-permute-start = (bf16[32,2560]{1,0:T(8,128)(2,1)}, bf16[32,2560]{1,0:T(8,128)(2,1)S(1)}, u32[]{:S(2)}, u32[]{:S(2)}) collective-permute-start(bf16[32,2560]{1,0:T(8,128)(2,1)} %param.2), channel_id=1, source_target_pairs={{0,1},{1,2},{2,3},{3,0},{4,5},{5,6},{6,7},{7,4},{8,9},{9,10},{10,1... | collective-permute-start | bytes 491528 | tf_op jit(solution)/shard_map/ppermute | solution.py:15
  7.0 7.7 %collective-permute-start.1 = (bf16[32,2560]{1,0:T(8,128)(2,1)}, bf16[32,2560]{1,0:T(8,128)(2,1)S(1)}, u32[]{:S(2)}, u32[]{:S(2)}) collective-permute-start(bf16[32,2560]{1,0:T(8,128)(2,1)} %param.2), channel_id=1, source_target_pairs={{0,2},{1,3},{2,0},{3,1},{4,6},{5,7},{6,4},{7,5},{8,10},{9,11},{10,... | collective-permute-start | bytes 491528 | tf_op jit(solution)/shard_map/ppermute | solution.py:15
  9.5 7.8 %collective-permute-start.2 = (bf16[32,2560]{1,0:T(8,128)(2,1)}, bf16[32,2560]{1,0:T(8,128)(2,1)S(1)}, u32[]{:S(2)}, u32[]{:S(2)}) collective-permute-start(bf16[32,2560]{1,0:T(8,128)(2,1)} %param.2), channel_id=1, source_target_pairs={{0,3},{1,0},{2,1},{3,2},{4,7},{5,4},{6,5},{7,6},{8,11},{9,8},{10,9... | collective-permute-start | bytes 491528 | tf_op jit(solution)/shard_map/ppermute | solution.py:15
  32.0 14.0 %collective-permute-start.5 = (bf16[32,2,3328]{2,0,1:T(8,128)(2,1)}, bf16[32,2,3328]{2,0,1:T(8,128)(2,1)}, u32[]{:S(2)}, u32[]{:S(2)}) collective-permute-start(bf16[32,2,3328]{2,0,1:T(8,128)(2,1)} %get-tuple-element.13), channel_id=1, source_target_pairs={{0,4},{1,5},{2,6},{3,7},{16,20},{17,21},{18,22},{19,23}} | collective-permute-start | bytes 1277960 | tf_op jit(solution)/shard_map/up/ppermute | solution.py:28
  36.2 9.7 %collective-permute-start.10 = (bf16[32,2,3328]{2,0,1:T(8,128)(2,1)}, bf16[32,2,3328]{2,0,1:T(8,128)(2,1)}, u32[]{:S(2)}, u32[]{:S(2)}) collective-permute-start(bf16[32,2,3328]{2,0,1:T(8,128)(2,1)} %get-tuple-element.12), channel_id=1, source_target_pairs={{12,8},{13,9},{14,10},{15,11},{28,24},{29,25},{30,26},{31,27}} | collective-permute-start | bytes 1277960 | tf_op jit(solution)/shard_map/down/ppermute | solution.py:35
  37.6 28.4 %collective-permute-start.4 = (bf16[32,2,3328]{2,0,1:T(8,128)(2,1)}, bf16[32,2,3328]{2,0,1:T(8,128)(2,1)S(1)}, u32[]{:S(2)}, u32[]{:S(2)}) collective-permute-start(bf16[32,2,3328]{2,0,1:T(8,128)(2,1)} %get-tuple-element.14), channel_id=1, source_target_pairs={{0,4},{1,5},{2,6},{3,7},{16,20},{17,21},{18,22},{19,23}} | collective-permute-start | bytes 1277960 | tf_op jit(solution)/shard_map/up/ppermute | solution.py:28
  39.0 36.4 %collective-permute-start.9 = (bf16[32,2,3328]{2,0,1:T(8,128)(2,1)}, bf16[32,2,3328]{2,0,1:T(8,128)(2,1)S(1)}, u32[]{:S(2)}, u32[]{:S(2)}) collective-permute-start(bf16[32,2,3328]{2,0,1:T(8,128)(2,1)} %get-tuple-element.11), channel_id=1, source_target_pairs={{12,8},{13,9},{14,10},{15,11},{28,24},{29,25},{30,26},{31,27}} | collective-permute-start | bytes 1277960 | tf_op jit(solution)/shard_map/down/ppermute | solution.py:35
  48.2 27.2 %collective-permute-start.6 = (bf16[32,2,3328]{2,0,1:T(8,128)(2,1)}, bf16[32,2,3328]{2,0,1:T(8,128)(2,1)}, u32[]{:S(2)}, u32[]{:S(2)}) collective-permute-start(bf16[32,2,3328]{2,0,1:T(8,128)(2,1)} %get-tuple-element.9), channel_id=1, source_target_pairs={{4,8},{5,9},{6,10},{7,11},{20,24},{21,25},{22,26},{23,27}} | collective-permute-start | bytes 1277960 | tf_op jit(solution)/shard_map/up/ppermute | solution.py:32
  49.6 25.8 %collective-permute-start.11 = (bf16[32,2,3328]{2,0,1:T(8,128)(2,1)}, bf16[32,2,3328]{2,0,1:T(8,128)(2,1)}, u32[]{:S(2)}, u32[]{:S(2)}) collective-permute-start(bf16[32,2,3328]{2,0,1:T(8,128)(2,1)} %get-tuple-element.10), channel_id=1, source_target_pairs={{8,4},{9,5},{10,6},{11,7},{24,20},{25,21},{26,22},{27,23}} | collective-permute-start | bytes 1277960 | tf_op jit(solution)/shard_map/down/ppermute | solution.py:38
  65.4 14.4 %collective-permute-start.8 = (bf16[32,2,3328]{2,0,1:T(8,128)(2,1)}, bf16[32,2,3328]{2,0,1:T(8,128)(2,1)S(1)}, u32[]{:S(2)}, u32[]{:S(2)}) collective-permute-start(bf16[32,2,3328]{2,0,1:T(8,128)(2,1)} %get-tuple-element.14), channel_id=1, source_target_pairs={{12,8},{13,9},{14,10},{15,11},{28,24},{29,25},{30,26},{31,27}} | collective-permute-start | bytes 1277960 | tf_op jit(solution)/shard_map/down/ppermute | solution.py:35
  66.1 24.9 %collective-permute-start.3 = (bf16[32,2,3328]{2,0,1:T(8,128)(2,1)}, bf16[32,2,3328]{2,0,1:T(8,128)(2,1)}, u32[]{:S(2)}, u32[]{:S(2)}) collective-permute-start(bf16[32,2,3328]{2,0,1:T(8,128)(2,1)} %get-tuple-element.11), channel_id=1, source_target_pairs={{0,4},{1,5},{2,6},{3,7},{16,20},{17,21},{18,22},{19,23}} | collective-permute-start | bytes 1277960 | tf_op jit(solution)/shard_map/up/ppermute | solution.py:28
  77.8 36.4 %collective-permute-start.12 = (bf16[32,2,3328]{2,0,1:T(8,128)(2,1)}, bf16[32,2,3328]{2,0,1:T(8,128)(2,1)S(1)}, u32[]{:S(2)}, u32[]{:S(2)}) collective-permute-start(bf16[32,2,3328]{2,0,1:T(8,128)(2,1)} %get-tuple-element.8), channel_id=1, source_target_pairs={{4,0},{8,4},{5,1},{9,5},{6,2},{10,6},{7,3},{11,7},{20,16},{24,20},... | collective-permute-start | bytes 1277960 | tf_op jit(solution)/shard_map/down/ppermute | solution.py:38
  79.0 35.1 %collective-permute-start.7 = (bf16[32,2,3328]{2,0,1:T(8,128)(2,1)}, bf16[32,2,3328]{2,0,1:T(8,128)(2,1)S(1)}, u32[]{:S(2)}, u32[]{:S(2)}) collective-permute-start(bf16[32,2,3328]{2,0,1:T(8,128)(2,1)} %get-tuple-element.7), channel_id=1, source_target_pairs={{4,8},{8,12},{5,9},{9,13},{6,10},{10,14},{7,11},{11,15},{20,24},{2... | collective-permute-start | bytes 1277960 | tf_op jit(solution)/shard_map/up/ppermute | solution.py:32
Sparse Core Ops, SparseCore 0:
  65.5 51.7 reduce-scatter.1

commit v15 on v4

--- a/solution.py
+++ b/solution.py
@@ -10,10 +10,20 @@
     c = lax.axis_index("col")
     rows = tokens.shape[0]
     buf = jnp.zeros((m, rows, tokens.shape[1]), tokens.dtype)
-    buf = lax.dynamic_update_index_in_dim(buf, tokens, c, 0)
-    for s in range(1, m):
-        got = lax.ppermute(tokens, "col", [(i, (i + s) % m) for i in range(m)])
-        buf = lax.dynamic_update_index_in_dim(buf, got, (c - s + m) % m, 0)
+    if m % 2:
+        buf = lax.dynamic_update_index_in_dim(buf, tokens, c, 0)
+        for s in range(1, m):
+            got = lax.ppermute(tokens, "col", [(i, (i + s) % m) for i in range(m)])
+            buf = lax.dynamic_update_index_in_dim(buf, got, (c - s + m) % m, 0)
+        return buf.reshape(m * rows, tokens.shape[1])
+    mine = [tokens] + [
+        lax.ppermute(tokens, "col", [(i, (i + 2 * s) % m) for i in range(m)]) for s in range(1, m // 2)
+    ]
+    other = lax.ppermute(jnp.stack(mine), "col", [(i, i + 1 - 2 * (i % 2)) for i in range(m)])
+    partner = c + 1 - 2 * (c % 2)
+    for s in range(m // 2):
+        buf = lax.dynamic_update_index_in_dim(buf, mine[s], (c - 2 * s + m) % m, 0)
+        buf = lax.dynamic_update_index_in_dim(buf, other[s], (partner - 2 * s + m) % m, 0)
     return buf.reshape(m * rows, tokens.shape[1])
 
 

time: 110 us -> 113 us (1.027)
  waiting for transfers between devices: 24.9 us -> 31.4 us
  starting transfers between devices: 49 us -> 45 us
    ppermute x4, waiting for transfers between devices: 8.04 us -> 11.9 us  [line_reduce(): lax.ppermute(add(block(p - n + r), minus), 'row', [(q, q - 1) for q in ra...]
    ppermute x6, waiting for transfers between devices: 11.5 us -> 14.5 us  [line_reduce(): origin = [lax.ppermute(part[n - r], 'row', [(0, 1)]) for r in range(1, n)]]
    ppermute x6, starting transfers between devices: 32.8 us -> 30.4 us  [line_reduce(): origin = [lax.ppermute(part[n - r], 'row', [(0, 1)]) for r in range(1, n)]]
    ppermute x3 -> x2, starting transfers between devices: 4.71 us -> 3.04 us  [the longest x1 2.97 us: gather_cols(): lax.ppermute(tokens, 'col', [(i, (i + 2 * s) % m) for i in range(m)])]
    ppermute x3 -> x2, waiting for transfers between devices: 5.37 us -> 4.97 us  [the longest x1 4.41 us: gather_cols(): lax.ppermute(tokens, 'col', [(i, (i + 2 * s) % m) for i in range(m)])]
  transfers between devices with their start and end apart: 23 -> 22, of which waited for: 6 -> 7; matrix products, arithmetic and copies ran while one was open for 17% -> 16% of each run, Pallas kernels for 0% -> 0%
where the time goes in v15:
time: 113 us; the launch traced here: 112 us
  starting transfers between devices  45 us (40%)
  waiting for transfers between devices  31.4 us (28%)
  matrix products  26.9 us (24%)
  other arithmetic  5.71 us (5%)
  local copies, waits for them, and re-layouts  2.95 us (3%)
    ppermute x6, starting transfers between devices, line_reduce(): origin = [lax.ppermute(part[n - r], 'row', [(0, 1)]) for r in range(1, n)]  30.4 us
    dot_general x2, matrix products, on_device(): jnp.einsum('td,gdf->tgf', held, w, preferred_element_type=jnp.float32)  26.9 us
    ppermute x6, waiting for transfers between devices, line_reduce(): origin = [lax.ppermute(part[n - r], 'row', [(0, 1)]) for r in range(1, n)]  14.5 us
    ppermute x4, waiting for transfers between devices, line_reduce(): lax.ppermute(add(block(p - n + r), minus), 'row', [(q, q - 1) for q in ra...  11.9 us
    ppermute x6, starting transfers between devices, line_reduce(): lax.ppermute(part[r - 1], 'row', [(n - 1, n - 2)])  4.87 us
    ppermute x1, waiting for transfers between devices, gather_cols(): lax.ppermute(tokens, 'col', [(i, (i + 2 * s) % m) for i in range(m)])  4.41 us
    ppermute x4, starting transfers between devices, line_reduce(): lax.ppermute(add(block(p - n + r), minus), 'row', [(q, q - 1) for q in ra...  3.96 us
    ppermute x1, starting transfers between devices, gather_cols(): lax.ppermute(tokens, 'col', [(i, (i + 2 * s) % m) for i in range(m)])  2.97 us
  transfers between devices with their start and end apart: 22, of which 7 were waited for; matrix products, arithmetic and copies ran while one was open for 16% of the time, Pallas kernels for 0%

profile of v15, /device:TPU:0, one launch (start us, length us, event | category | flops | bytes accessed | tf_op | source)
XLA Modules:
  0.0 112.4 jit_solution(2925365010983920838)
XLA Ops:
  0.0 3.0 %collective-permute-start = (bf16[32,2560]{1,0:T(8,128)(2,1)}, bf16[32,2560]{1,0:T(8,128)(2,1)S(1)}, u32[]{:S(2)}, u32[]{:S(2)}) collective-permute-start(bf16[32,2560]{1,0:T(8,128)(2,1)} %param.2), channel_id=1, source_target_pairs={{0,2},{1,3},{2,0},{3,1},{4,6},{5,7},{6,4},{7,5},{8,10},{9,11},{10,... | collective-permute-start | bytes 491528 | tf_op jit(solution)/shard_map/ppermute | solution.py:20
  3.0 4.4 %collective-permute-done = bf16[32,2560]{1,0:T(8,128)(2,1)S(1)} collective-permute-done((bf16[32,2560]{1,0:T(8,128)(2,1)}, bf16[32,2560]{1,0:T(8,128)(2,1)S(1)}, u32[]{:S(2)}, u32[]{:S(2)}) %collective-permute-start) | collective-permute-done | bytes 163872 | tf_op jit(solution)/shard_map/ppermute | solution.py:20
  7.4 0.9 pad_maximum_fusion.1
  8.5 0.9 constant_dynamic-update-slice_fusion.1
  10.1 13.4 %fusion.4 = bf16[128,2,3328]{2,0,1:T(8,128)(2,1)S(1)} fusion(bf16[128,2560,1]{1,0,2:T(8,128)(2,1)S(1)} %bitcast.91, bf16[2,2560,6656]{2,1,0:T(8,128)(2,1)} %param.3), kind=kOutput, calls=%fused_computation.4 | convolution fusion | flops 4362928128 | bytes 36438016 | tf_op jit(solution)/shard_map/td,gdf->tgf/dot_general | solution.py:67
  23.5 1.0 fusion.25
  25.2 3.8 %collective-permute-start.4 = (bf16[32,2,3328]{2,0,1:T(8,128)(2,1)S(1)}, bf16[32,2,3328]{2,0,1:T(8,128)(2,1)S(1)}, u32[]{:S(2)}, u32[]{:S(2)}) collective-permute-start(bf16[32,2,3328]{2,0,1:T(8,128)(2,1)S(1)} %get-tuple-element.13), channel_id=1, source_target_pairs={{0,4},{1,5},{2,6},{3,7},{16,20},{17,21},{18,22},{19,23}} | collective-permute-start | bytes 1277960 | tf_op jit(solution)/shard_map/up/ppermute | solution.py:38
  29.0 1.5 %collective-permute-start.8 = (bf16[32,2,3328]{2,0,1:T(8,128)(2,1)}, bf16[32,2,3328]{2,0,1:T(8,128)(2,1)}, u32[]{:S(2)}, u32[]{:S(2)}) collective-permute-start(bf16[32,2,3328]{2,0,1:T(8,128)(2,1)} %get-tuple-element.11), channel_id=1, source_target_pairs={{12,8},{13,9},{14,10},{15,11},{28,24},{29,25},{30,26},{31,27}} | collective-permute-start | bytes 1277960 | tf_op jit(solution)/shard_map/down/ppermute | solution.py:45
  30.4 2.0 %collective-permute-start.2 = (bf16[32,2,3328]{2,0,1:T(8,128)(2,1)}, bf16[32,2,3328]{2,0,1:T(8,128)(2,1)}, u32[]{:S(2)}, u32[]{:S(2)}) collective-permute-start(bf16[32,2,3328]{2,0,1:T(8,128)(2,1)} %get-tuple-element.11), channel_id=1, source_target_pairs={{0,4},{1,5},{2,6},{3,7},{16,20},{17,21},{18,22},{19,23}} | collective-permute-start | bytes 1277960 | tf_op jit(solution)/shard_map/up/ppermute | solution.py:38
  32.5 2.1 %collective-permute-start.3 = (bf16[32,2,3328]{2,0,1:T(8,128)(2,1)}, bf16[32,2,3328]{2,0,1:T(8,128)(2,1)}, u32[]{:S(2)}, u32[]{:S(2)}) collective-permute-start(bf16[32,2,3328]{2,0,1:T(8,128)(2,1)} %get-tuple-element.14), channel_id=1, source_target_pairs={{0,4},{1,5},{2,6},{3,7},{16,20},{17,21},{18,22},{19,23}} | collective-permute-start | bytes 1277960 | tf_op jit(solution)/shard_map/up/ppermute | solution.py:38
  34.5 4.6 %collective-permute-done.4 = bf16[32,2,3328]{2,0,1:T(8,128)(2,1)S(1)} collective-permute-done((bf16[32,2,3328]{2,0,1:T(8,128)(2,1)S(1)}, bf16[32,2,3328]{2,0,1:T(8,128)(2,1)S(1)}, u32[]{:S(2)}, u32[]{:S(2)}) %collective-permute-start.4) | collective-permute-done | bytes 426016 | tf_op jit(solution)/shard_map/up/ppermute | solution.py:38
  39.1 0.8 copy-done.3
  39.9 13.6 %fusion.7 = bf16[128,2,3328]{2,0,1:T(8,128)(2,1)S(1)} fusion(bf16[2,2560,6656]{2,1,0:T(8,128)(2,1)} %param.3, bf16[128,2560]{1,0:T(8,128)(2,1)} %bitcast.92), kind=kOutput, calls=%fused_computation.5 | convolution fusion | flops 4362928128 | bytes 36438016 | tf_op jit(solution)/shard_map/td,gdf->tgf/dot_general | solution.py:67
  53.6 4.5 %collective-permute-start.14 = (bf16[32,2,3328]{2,0,1:T(8,128)(2,1)S(1)}, bf16[32,2,3328]{2,0,1:T(8,128)(2,1)S(1)}, u32[]{:S(2)}, u32[]{:S(2)}) collective-permute-start(bf16[32,2,3328]{2,0,1:T(8,128)(2,1)S(1)} %get-tuple-element.19), channel_id=1, source_target_pairs={{0,4},{1,5},{2,6},{3,7},{16,20},{17,21},{18,22},{19,23}} | collective-permute-start | bytes 1277960 | tf_op jit(solution)/shard_map/up/ppermute | solution.py:38
  58.2 0.7 collective-permute-start.19
  59.1 6.7 %collective-permute-done.14 = bf16[32,2,3328]{2,0,1:T(8,128)(2,1)S(1)} collective-permute-done((bf16[32,2,3328]{2,0,1:T(8,128)(2,1)S(1)}, bf16[32,2,3328]{2,0,1:T(8,128)(2,1)S(1)}, u32[]{:S(2)}, u32[]{:S(2)}) %collective-permute-start.14) | collective-permute-done | bytes 426016 | tf_op jit(solution)/shard_map/up/ppermute | solution.py:38
  66.5 0.7 collective-permute-start.10
  67.4 5.6 %collective-permute-start.13 = (bf16[32,2,3328]{2,0,1:T(8,128)(2,1)S(1)}, bf16[32,2,3328]{2,0,1:T(8,128)(2,1)S(1)}, u32[]{:S(2)}, u32[]{:S(2)}) collective-permute-start(bf16[32,2,3328]{2,0,1:T(8,128)(2,1)S(1)} %get-tuple-element.21), channel_id=1, source_target_pairs={{0,4},{1,5},{2,6},{3,7},{16,20},{17,21},{18,22},{19,23}} | collective-permute-start | bytes 1277960 | tf_op jit(solution)/shard_map/up/ppermute | solution.py:38
  73.1 0.7 collective-permute-start.18
  73.8 0.7 collective-permute-start.15
  75.2 1.5 %fusion.18 = (bf16[32,2,3328]{2,0,1:T(8,128)(2,1)S(1)}, bf16[32,2,3328]{2,0,1:T(8,128)(2,1)S(1)}) fusion(bf16[32,2,3328]{2,0,1:T(8,128)(2,1)} %collective-permute-done.3, bf16[32,2,3328]{2,0,1:T(8,128)(2,1)S(1)} %collective-permute-done.5, bf16[4,32,2,3328]{3,1,0,2:T(8,128)(2,1)S(1)} %bitcast.84, s32[]{:T(128)S(6)} %min.17, ...), kind=kLoop, calls=%fused_computation.23 | loop fusion | flops 2129920 | bytes 3407880 | tf_op jit(solution)/shard_map/up/convert_element_type | solution.py:35
  76.7 3.2 %collective-permute-done.13 = bf16[32,2,3328]{2,0,1:T(8,128)(2,1)S(1)} collective-permute-done((bf16[32,2,3328]{2,0,1:T(8,128)(2,1)S(1)}, bf16[32,2,3328]{2,0,1:T(8,128)(2,1)S(1)}, u32[]{:S(2)}, u32[]{:S(2)}) %collective-permute-start.13) | collective-permute-done | bytes 426016 | tf_op jit(solution)/shard_map/up/ppermute | solution.py:38
  80.5 0.7 collective-permute-start.17
  81.2 0.7 collective-permute-start.6
  82.0 1.3 %collective-permute-start.11 = (bf16[32,2,3328]{2,0,1:T(8,128)(2,1)S(1)}, bf16[32,2,3328]{2,0,1:T(8,128)(2,1)S(1)}, u32[]{:S(2)}, u32[]{:S(2)}) collective-permute-start(bf16[32,2,3328]{2,0,1:T(8,128)(2,1)S(1)} %get-tuple-element.8), channel_id=1, source_target_pairs={{4,0},{8,4},{5,1},{9,5},{6,2},{10,6},{7,3},{11,7},{20,16},{24,20},... | collective-permute-start | bytes 1277960 | tf_op jit(solution)/shard_map/down/ppermute | solution.py:48
  83.6 12.3 %collective-permute-start.12 = (bf16[32,2,3328]{2,0,1:T(8,128)(2,1)S(1)}, bf16[32,2,3328]{2,0,1:T(8,128)(2,1)S(1)}, u32[]{:S(2)}, u32[]{:S(2)}) collective-permute-start(bf16[32,2,3328]{2,0,1:T(8,128)(2,1)S(1)} %get-tuple-element.22), channel_id=1, source_target_pairs={{0,4},{1,5},{2,6},{3,7},{16,20},{17,21},{18,22},{19,23}} | collective-permute-start | bytes 1277960 | tf_op jit(solution)/shard_map/up/ppermute | solution.py:38
  95.9 0.7 collective-permute-start.16
  96.6 1.3 %collective-permute-start.21 = (bf16[32,2,3328]{2,0,1:T(8,128)(2,1)S(1)}, bf16[32,2,3328]{2,0,1:T(8,128)(2,1)S(1)}, u32[]{:S(2)}, u32[]{:S(2)}) collective-permute-start(bf16[32,2,3328]{2,0,1:T(8,128)(2,1)S(1)} %get-tuple-element.16), channel_id=1, source_target_pairs={{4,0},{8,4},{5,1},{9,5},{6,2},{10,6},{7,3},{11,7},{20,16},{24,20},... | collective-permute-start | bytes 1277960 | tf_op jit(solution)/shard_map/down/ppermute | solution.py:48
  97.9 4.7 %collective-permute-done.11 = bf16[32,2,3328]{2,0,1:T(8,128)(2,1)S(1)} collective-permute-done((bf16[32,2,3328]{2,0,1:T(8,128)(2,1)S(1)}, bf16[32,2,3328]{2,0,1:T(8,128)(2,1)S(1)}, u32[]{:S(2)}, u32[]{:S(2)}) %collective-permute-start.11) | collective-permute-done | bytes 426016 | tf_op jit(solution)/shard_map/down/ppermute | solution.py:48
  102.6 1.3 %fusion.19 = f32[32,2,3328]{2,0,1:T(8,128)S(1)} fusion(bf16[32,2,3328]{2,0,1:T(8,128)(2,1)S(1)} %collective-permute-done.7, bf16[32,2,3328]{2,0,1:T(8,128)(2,1)S(1)} %collective-permute-done.11, bf16[32,2,3328]{2,0,1:T(8,128)(2,1)} %collective-permute-done.2, bf16[32,2,3328]{2,0,1:T(8,128)(2,1)S(1)} %collective-permute-done.6, ...), kind=kLoop, calls=%fused_computation.25 | loop fusion | flops 1490944 | bytes 2981892 | tf_op jit(solution)/shard_map/add | solution.py:73
  104.0 7.2 %collective-permute-done.21 = bf16[32,2,3328]{2,0,1:T(8,128)(2,1)S(1)} collective-permute-done((bf16[32,2,3328]{2,0,1:T(8,128)(2,1)S(1)}, bf16[32,2,3328]{2,0,1:T(8,128)(2,1)S(1)}, u32[]{:S(2)}, u32[]{:S(2)}) %collective-permute-start.21) | collective-permute-done | bytes 426016 | tf_op jit(solution)/shard_map/down/ppermute | solution.py:48
  111.6 0.8 pad_maximum_fusion
  (41 shorter events, 4.9 us)
Async XLA Ops:
  0.0 7.4 %collective-permute-start = (bf16[32,2560]{1,0:T(8,128)(2,1)}, bf16[32,2560]{1,0:T(8,128)(2,1)S(1)}, u32[]{:S(2)}, u32[]{:S(2)}) collective-permute-start(bf16[32,2560]{1,0:T(8,128)(2,1)} %param.2), channel_id=1, source_target_pairs={{0,2},{1,3},{2,0},{3,1},{4,6},{5,7},{6,4},{7,5},{8,10},{9,11},{10,... | collective-permute-start | bytes 491528 | tf_op jit(solution)/shard_map/ppermute | solution.py:20
  8.3 1.7 %collective-permute-start.1 = (bf16[2,32,2560]{2,1,0:T(8,128)(2,1)S(1)}, bf16[2,32,2560]{2,1,0:T(8,128)(2,1)S(1)}, u32[]{:S(2)}, u32[]{:S(2)}) collective-permute-start(bf16[2,32,2560]{2,1,0:T(8,128)(2,1)S(1)} %pad_maximum_fusion.1), channel_id=1, source_target_pairs={{0,1},{1,0},{2,3},{3,2},{4,5},{5,4},{6,7},{7,6},{8,9},{9,8},{10,11... | collective-permute-start | bytes 983048 | tf_op jit(solution)/shard_map/ppermute | solution.py:22
  10.1 13.4 %copy-start = (bf16[4,32,2560]{2,1,0:T(8,128)(2,1)}, bf16[4,32,2560]{2,1,0:T(8,128)(2,1)S(1)}, u32[]{:S(2)}) copy-start(bf16[4,32,2560]{2,1,0:T(8,128)(2,1)S(1)} %slice_dynamic-update-slice_fusion) | copy-start | bytes 1966084
  24.5 10.0 %collective-permute-start.9 = (bf16[32,2,3328]{2,0,1:T(8,128)(2,1)S(1)}, bf16[32,2,3328]{2,0,1:T(8,128)(2,1)S(1)}, u32[]{:S(2)}, u32[]{:S(2)}) collective-permute-start(bf16[32,2,3328]{2,0,1:T(8,128)(2,1)S(1)} %get-tuple-element.12), channel_id=1, source_target_pairs={{12,8},{13,9},{14,10},{15,11},{28,24},{29,25},{30,26},{31,27}} | collective-permute-start | bytes 1277960 | tf_op jit(solution)/shard_map/down/ppermute | solution.py:45
  25.2 13.9 %collective-permute-start.4 = (bf16[32,2,3328]{2,0,1:T(8,128)(2,1)S(1)}, bf16[32,2,3328]{2,0,1:T(8,128)(2,1)S(1)}, u32[]{:S(2)}, u32[]{:S(2)}) collective-permute-start(bf16[32,2,3328]{2,0,1:T(8,128)(2,1)S(1)} %get-tuple-element.13), channel_id=1, source_target_pairs={{0,4},{1,5},{2,6},{3,7},{16,20},{17,21},{18,22},{19,23}} | collective-permute-start | bytes 1277960 | tf_op jit(solution)/shard_map/up/ppermute | solution.py:38
  29.0 38.4 %collective-permute-start.8 = (bf16[32,2,3328]{2,0,1:T(8,128)(2,1)}, bf16[32,2,3328]{2,0,1:T(8,128)(2,1)}, u32[]{:S(2)}, u32[]{:S(2)}) collective-permute-start(bf16[32,2,3328]{2,0,1:T(8,128)(2,1)} %get-tuple-element.11), channel_id=1, source_target_pairs={{12,8},{13,9},{14,10},{15,11},{28,24},{29,25},{30,26},{31,27}} | collective-permute-start | bytes 1277960 | tf_op jit(solution)/shard_map/down/ppermute | solution.py:45
  30.4 53.2 %collective-permute-start.2 = (bf16[32,2,3328]{2,0,1:T(8,128)(2,1)}, bf16[32,2,3328]{2,0,1:T(8,128)(2,1)}, u32[]{:S(2)}, u32[]{:S(2)}) collective-permute-start(bf16[32,2,3328]{2,0,1:T(8,128)(2,1)} %get-tuple-element.11), channel_id=1, source_target_pairs={{0,4},{1,5},{2,6},{3,7},{16,20},{17,21},{18,22},{19,23}} | collective-permute-start | bytes 1277960 | tf_op jit(solution)/shard_map/up/ppermute | solution.py:38
  32.5 40.6 %collective-permute-start.3 = (bf16[32,2,3328]{2,0,1:T(8,128)(2,1)}, bf16[32,2,3328]{2,0,1:T(8,128)(2,1)}, u32[]{:S(2)}, u32[]{:S(2)}) collective-permute-start(bf16[32,2,3328]{2,0,1:T(8,128)(2,1)} %get-tuple-element.14), channel_id=1, source_target_pairs={{0,4},{1,5},{2,6},{3,7},{16,20},{17,21},{18,22},{19,23}} | collective-permute-start | bytes 1277960 | tf_op jit(solution)/shard_map/up/ppermute | solution.py:38
  34.5 4.6 %copy-start.1 = (bf16[32,2,3328]{2,0,1:T(8,128)(2,1)}, bf16[32,2,3328]{2,0,1:T(8,128)(2,1)S(1)}, u32[]{:S(2)}) copy-start(bf16[32,2,3328]{2,0,1:T(8,128)(2,1)S(1)} %collective-permute-done.9) | copy-start | bytes 1277956
  39.1 0.8 copy-start.3
  53.5 5.4 %copy-start.2 = (bf16[32,2,3328]{2,0,1:T(8,128)(2,1)S(1)}, bf16[32,2,3328]{2,0,1:T(8,128)(2,1)}, u32[]{:S(2)}) copy-start(bf16[32,2,3328]{2,0,1:T(8,128)(2,1)} %copy-done.1) | copy-start | bytes 1277956
  53.5 5.4 %copy-start.4 = (bf16[32,2,3328]{2,0,1:T(8,128)(2,1)S(1)}, bf16[32,2,3328]{2,0,1:T(8,128)(2,1)}, u32[]{:S(2)}) copy-start(bf16[32,2,3328]{2,0,1:T(8,128)(2,1)} %copy-done.3) | copy-start | bytes 1277956
  53.6 12.2 %collective-permute-start.14 = (bf16[32,2,3328]{2,0,1:T(8,128)(2,1)S(1)}, bf16[32,2,3328]{2,0,1:T(8,128)(2,1)S(1)}, u32[]{:S(2)}, u32[]{:S(2)}) collective-permute-start(bf16[32,2,3328]{2,0,1:T(8,128)(2,1)S(1)} %get-tuple-element.19), channel_id=1, source_target_pairs={{0,4},{1,5},{2,6},{3,7},{16,20},{17,21},{18,22},{19,23}} | collective-permute-start | bytes 1277960 | tf_op jit(solution)/shard_map/up/ppermute | solution.py:38
  58.2 8.3 %collective-permute-start.19 = (bf16[32,2,3328]{2,0,1:T(8,128)(2,1)S(1)}, bf16[32,2,3328]{2,0,1:T(8,128)(2,1)S(1)}, u32[]{:S(2)}, u32[]{:S(2)}) collective-permute-start(bf16[32,2,3328]{2,0,1:T(8,128)(2,1)S(1)} %get-tuple-element.20), channel_id=1, source_target_pairs={{12,8},{13,9},{14,10},{15,11},{28,24},{29,25},{30,26},{31,27}} | collective-permute-start | bytes 1277960 | tf_op jit(solution)/shard_map/down/ppermute | solution.py:45
  65.8 8.0 %collective-permute-start.5 = (bf16[32,2,3328]{2,0,1:T(8,128)(2,1)S(1)}, bf16[32,2,3328]{2,0,1:T(8,128)(2,1)S(1)}, u32[]{:S(2)}, u32[]{:S(2)}) collective-permute-start(bf16[32,2,3328]{2,0,1:T(8,128)(2,1)S(1)} %get-tuple-element.9), channel_id=1, source_target_pairs={{4,8},{5,9},{6,10},{7,11},{20,24},{21,25},{22,26},{23,27}} | collective-permute-start | bytes 1277960 | tf_op jit(solution)/shard_map/up/ppermute | solution.py:42
  66.5 8.0 %collective-permute-start.10 = (bf16[32,2,3328]{2,0,1:T(8,128)(2,1)S(1)}, bf16[32,2,3328]{2,0,1:T(8,128)(2,1)S(1)}, u32[]{:S(2)}, u32[]{:S(2)}) collective-permute-start(bf16[32,2,3328]{2,0,1:T(8,128)(2,1)S(1)} %get-tuple-element.10), channel_id=1, source_target_pairs={{8,4},{9,5},{10,6},{11,7},{24,20},{25,21},{26,22},{27,23}} | collective-permute-start | bytes 1277960 | tf_op jit(solution)/shard_map/down/ppermute | solution.py:48
  67.4 12.4 %collective-permute-start.13 = (bf16[32,2,3328]{2,0,1:T(8,128)(2,1)S(1)}, bf16[32,2,3328]{2,0,1:T(8,128)(2,1)S(1)}, u32[]{:S(2)}, u32[]{:S(2)}) collective-permute-start(bf16[32,2,3328]{2,0,1:T(8,128)(2,1)S(1)} %get-tuple-element.21), channel_id=1, source_target_pairs={{0,4},{1,5},{2,6},{3,7},{16,20},{17,21},{18,22},{19,23}} | collective-permute-start | bytes 1277960 | tf_op jit(solution)/shard_map/up/ppermute | solution.py:38
  73.1 7.5 %collective-permute-start.18 = (bf16[32,2,3328]{2,0,1:T(8,128)(2,1)S(1)}, bf16[32,2,3328]{2,0,1:T(8,128)(2,1)S(1)}, u32[]{:S(2)}, u32[]{:S(2)}) collective-permute-start(bf16[32,2,3328]{2,0,1:T(8,128)(2,1)S(1)} %get-tuple-element.22), channel_id=1, source_target_pairs={{12,8},{13,9},{14,10},{15,11},{28,24},{29,25},{30,26},{31,27}} | collective-permute-start | bytes 1277960 | tf_op jit(solution)/shard_map/down/ppermute | solution.py:45
  73.8 7.5 %collective-permute-start.15 = (bf16[32,2,3328]{2,0,1:T(8,128)(2,1)S(1)}, bf16[32,2,3328]{2,0,1:T(8,128)(2,1)S(1)}, u32[]{:S(2)}, u32[]{:S(2)}) collective-permute-start(bf16[32,2,3328]{2,0,1:T(8,128)(2,1)S(1)} %get-tuple-element.17), channel_id=1, source_target_pairs={{4,8},{5,9},{6,10},{7,11},{20,24},{21,25},{22,26},{23,27}} | collective-permute-start | bytes 1277960 | tf_op jit(solution)/shard_map/up/ppermute | solution.py:42
  74.5 7.5 %collective-permute-start.20 = (bf16[32,2,3328]{2,0,1:T(8,128)(2,1)S(1)}, bf16[32,2,3328]{2,0,1:T(8,128)(2,1)S(1)}, u32[]{:S(2)}, u32[]{:S(2)}) collective-permute-start(bf16[32,2,3328]{2,0,1:T(8,128)(2,1)S(1)} %get-tuple-element.18), channel_id=1, source_target_pairs={{8,4},{9,5},{10,6},{11,7},{24,20},{25,21},{26,22},{27,23}} | collective-permute-start | bytes 1277960 | tf_op jit(solution)/shard_map/down/ppermute | solution.py:48
  79.8 16.1 %collective-permute-start.7 = (bf16[32,2,3328]{2,0,1:T(8,128)(2,1)}, bf16[32,2,3328]{2,0,1:T(8,128)(2,1)S(1)}, u32[]{:S(2)}, u32[]{:S(2)}) collective-permute-start(bf16[32,2,3328]{2,0,1:T(8,128)(2,1)} %get-tuple-element.14), channel_id=1, source_target_pairs={{12,8},{13,9},{14,10},{15,11},{28,24},{29,25},{30,26},{31,27}} | collective-permute-start | bytes 1277960 | tf_op jit(solution)/shard_map/down/ppermute | solution.py:45
  80.5 23.4 %collective-permute-start.17 = (bf16[32,2,3328]{2,0,1:T(8,128)(2,1)S(1)}, bf16[32,2,3328]{2,0,1:T(8,128)(2,1)S(1)}, u32[]{:S(2)}, u32[]{:S(2)}) collective-permute-start(bf16[32,2,3328]{2,0,1:T(8,128)(2,1)S(1)} %get-tuple-element.21), channel_id=1, source_target_pairs={{12,8},{13,9},{14,10},{15,11},{28,24},{29,25},{30,26},{31,27}} | collective-permute-start | bytes 1277960 | tf_op jit(solution)/shard_map/down/ppermute | solution.py:45
  81.2 15.4 %collective-permute-start.6 = (bf16[32,2,3328]{2,0,1:T(8,128)(2,1)S(1)}, bf16[32,2,3328]{2,0,1:T(8,128)(2,1)S(1)}, u32[]{:S(2)}, u32[]{:S(2)}) collective-permute-start(bf16[32,2,3328]{2,0,1:T(8,128)(2,1)S(1)} %get-tuple-element.7), channel_id=1, source_target_pairs={{4,8},{8,12},{5,9},{9,13},{6,10},{10,14},{7,11},{11,15},{20,24},{2... | collective-permute-start | bytes 1277960 | tf_op jit(solution)/shard_map/up/ppermute | solution.py:42
  82.0 20.6 %collective-permute-start.11 = (bf16[32,2,3328]{2,0,1:T(8,128)(2,1)S(1)}, bf16[32,2,3328]{2,0,1:T(8,128)(2,1)S(1)}, u32[]{:S(2)}, u32[]{:S(2)}) collective-permute-start(bf16[32,2,3328]{2,0,1:T(8,128)(2,1)S(1)} %get-tuple-element.8), channel_id=1, source_target_pairs={{4,0},{8,4},{5,1},{9,5},{6,2},{10,6},{7,3},{11,7},{20,16},{24,20},... | collective-permute-start | bytes 1277960 | tf_op jit(solution)/shard_map/down/ppermute | solution.py:48
  83.6 20.4 %collective-permute-start.12 = (bf16[32,2,3328]{2,0,1:T(8,128)(2,1)S(1)}, bf16[32,2,3328]{2,0,1:T(8,128)(2,1)S(1)}, u32[]{:S(2)}, u32[]{:S(2)}) collective-permute-start(bf16[32,2,3328]{2,0,1:T(8,128)(2,1)S(1)} %get-tuple-element.22), channel_id=1, source_target_pairs={{0,4},{1,5},{2,6},{3,7},{16,20},{17,21},{18,22},{19,23}} | collective-permute-start | bytes 1277960 | tf_op jit(solution)/shard_map/up/ppermute | solution.py:38
  95.9 8.1 %collective-permute-start.16 = (bf16[32,2,3328]{2,0,1:T(8,128)(2,1)S(1)}, bf16[32,2,3328]{2,0,1:T(8,128)(2,1)S(1)}, u32[]{:S(2)}, u32[]{:S(2)}) collective-permute-start(bf16[32,2,3328]{2,0,1:T(8,128)(2,1)S(1)} %get-tuple-element.15), channel_id=1, source_target_pairs={{4,8},{8,12},{5,9},{9,13},{6,10},{10,14},{7,11},{11,15},{20,24},{2... | collective-permute-start | bytes 1277960 | tf_op jit(solution)/shard_map/up/ppermute | solution.py:42
  96.6 14.6 %collective-permute-start.21 = (bf16[32,2,3328]{2,0,1:T(8,128)(2,1)S(1)}, bf16[32,2,3328]{2,0,1:T(8,128)(2,1)S(1)}, u32[]{:S(2)}, u32[]{:S(2)}) collective-permute-start(bf16[32,2,3328]{2,0,1:T(8,128)(2,1)S(1)} %get-tuple-element.16), channel_id=1, source_target_pairs={{4,0},{8,4},{5,1},{9,5},{6,2},{10,6},{7,3},{11,7},{20,16},{24,20},... | collective-permute-start | bytes 1277960 | tf_op jit(solution)/shard_map/down/ppermute | solution.py:48

commit v16 on v4

--- a/solution.py
+++ b/solution.py
@@ -37,7 +37,7 @@
         for r in range(2, n):
             sent = lax.ppermute(add(block(p - n + r), minus), "row", [(q, q - 1) for q in range(n - r, n - 1)])
             minus = origin[r - 1] + sent
-    return plus, minus, (first, origin[0])
+    return plus, minus, first
 
 
 def on_device(tokens, gate_up, n, m):

time: 110 us -> 109 us (level)
  waiting for transfers between devices: 24.9 us -> 23.3 us
    ppermute x6, waiting for transfers between devices: 11.5 us -> 9.47 us  [line_reduce(): origin = [lax.ppermute(part[n - r], 'row', [(0, 1)]) for r in range(1, n)]]
    ppermute x6, starting transfers between devices: 32.8 us -> 30.9 us  [line_reduce(): origin = [lax.ppermute(part[n - r], 'row', [(0, 1)]) for r in range(1, n)]]
    ppermute x6, starting transfers between devices: 4.86 us -> 6.37 us  [line_reduce(): lax.ppermute(part[r - 1], 'row', [(n - 1, n - 2)])]
  transfers between devices with their start and end apart: 23 -> 23, of which waited for: 6 -> 6; matrix products, arithmetic and copies ran while one was open for 17% -> 18% of each run, Pallas kernels for 0% -> 0%
where the time goes in v16:
time: 109 us; the launch traced here: 108 us
  starting transfers between devices  48.7 us (45%)
  matrix products  26.9 us (25%)
  waiting for transfers between devices  23.3 us (21%)
  other arithmetic  5.79 us (5%)
  local copies, waits for them, and re-layouts  3.01 us (3%)
    ppermute x6, starting transfers between devices, line_reduce(): origin = [lax.ppermute(part[n - r], 'row', [(0, 1)]) for r in range(1, n)]  30.9 us
    dot_general x2, matrix products, on_device(): jnp.einsum('td,gdf->tgf', held, w, preferred_element_type=jnp.float32)  26.9 us
    ppermute x6, waiting for transfers between devices, line_reduce(): origin = [lax.ppermute(part[n - r], 'row', [(0, 1)]) for r in range(1, n)]  9.47 us
    ppermute x4, waiting for transfers between devices, line_reduce(): lax.ppermute(add(block(p - n + r), minus), 'row', [(q, q - 1) for q in ra...  8.44 us
    ppermute x6, starting transfers between devices, line_reduce(): lax.ppermute(part[r - 1], 'row', [(n - 1, n - 2)])  6.37 us
    ppermute x3, waiting for transfers between devices, gather_cols(): got = lax.ppermute(tokens, 'col', [(i, (i + s) % m) for i in range(m)])  5.37 us
    ppermute x3, starting transfers between devices, gather_cols(): got = lax.ppermute(tokens, 'col', [(i, (i + s) % m) for i in range(m)])  4.71 us
    ppermute x4, starting transfers between devices, line_reduce(): lax.ppermute(add(block(p - n + r), minus), 'row', [(q, q - 1) for q in ra...  3.96 us
  transfers between devices with their start and end apart: 23, of which 6 were waited for; matrix products, arithmetic and copies ran while one was open for 18% of the time, Pallas kernels for 0%

profile of v16, /device:TPU:0, one launch (start us, length us, event | category | flops | bytes accessed | tf_op | source)
XLA Modules:
  0.0 108.1 jit_solution(3778817469900106825)
XLA Ops:
  0.5 1.9 %collective-permute-start.2 = (bf16[32,2560]{1,0:T(8,128)(2,1)}, bf16[32,2560]{1,0:T(8,128)(2,1)S(1)}, u32[]{:S(2)}, u32[]{:S(2)}) collective-permute-start(bf16[32,2560]{1,0:T(8,128)(2,1)} %param.2), channel_id=1, source_target_pairs={{0,3},{1,0},{2,1},{3,2},{4,7},{5,4},{6,5},{7,6},{8,11},{9,8},{10,9... | collective-permute-start | bytes 491528 | tf_op jit(solution)/shard_map/ppermute | solution.py:15
  2.4 2.3 %collective-permute-start.1 = (bf16[32,2560]{1,0:T(8,128)(2,1)}, bf16[32,2560]{1,0:T(8,128)(2,1)S(1)}, u32[]{:S(2)}, u32[]{:S(2)}) collective-permute-start(bf16[32,2560]{1,0:T(8,128)(2,1)} %param.2), channel_id=1, source_target_pairs={{0,2},{1,3},{2,0},{3,1},{4,6},{5,7},{6,4},{7,5},{8,10},{9,11},{10,... | collective-permute-start | bytes 491528 | tf_op jit(solution)/shard_map/ppermute | solution.py:15
  4.8 1.0 bitcast_dynamic-update-slice_fusion.3
  5.8 5.4 %collective-permute-done.1 = bf16[32,2560]{1,0:T(8,128)(2,1)S(1)} collective-permute-done((bf16[32,2560]{1,0:T(8,128)(2,1)}, bf16[32,2560]{1,0:T(8,128)(2,1)S(1)}, u32[]{:S(2)}, u32[]{:S(2)}) %collective-permute-start.1) | collective-permute-done | bytes 163872 | tf_op jit(solution)/shard_map/ppermute | solution.py:15
  11.2 13.4 %fusion.4 = bf16[128,2,3328]{2,0,1:T(8,128)(2,1)S(1)} fusion(bf16[128,2560,1]{1,0,2:T(8,128)(2,1)S(1)} %bitcast.93, bf16[2,2560,6656]{2,1,0:T(8,128)(2,1)} %param.3), kind=kOutput, calls=%fused_computation.4 | convolution fusion | flops 4362928128 | bytes 36438016 | tf_op jit(solution)/shard_map/td,gdf->tgf/dot_general | solution.py:57
  24.6 1.1 fusion.25
  25.7 4.0 %collective-permute-start.5 = (bf16[32,2,3328]{2,0,1:T(8,128)(2,1)S(1)}, bf16[32,2,3328]{2,0,1:T(8,128)(2,1)S(1)}, u32[]{:S(2)}, u32[]{:S(2)}) collective-permute-start(bf16[32,2,3328]{2,0,1:T(8,128)(2,1)S(1)} %get-tuple-element.12), channel_id=1, source_target_pairs={{0,4},{1,5},{2,6},{3,7},{16,20},{17,21},{18,22},{19,23}} | collective-permute-start | bytes 1277960 | tf_op jit(solution)/shard_map/up/ppermute | solution.py:28
  29.7 1.5 %collective-permute-start.8 = (bf16[32,2,3328]{2,0,1:T(8,128)(2,1)}, bf16[32,2,3328]{2,0,1:T(8,128)(2,1)}, u32[]{:S(2)}, u32[]{:S(2)}) collective-permute-start(bf16[32,2,3328]{2,0,1:T(8,128)(2,1)} %get-tuple-element.13), channel_id=1, source_target_pairs={{12,8},{13,9},{14,10},{15,11},{28,24},{29,25},{30,26},{31,27}} | collective-permute-start | bytes 1277960 | tf_op jit(solution)/shard_map/down/ppermute | solution.py:35
  31.2 2.1 %collective-permute-start.4 = (bf16[32,2,3328]{2,0,1:T(8,128)(2,1)}, bf16[32,2,3328]{2,0,1:T(8,128)(2,1)}, u32[]{:S(2)}, u32[]{:S(2)}) collective-permute-start(bf16[32,2,3328]{2,0,1:T(8,128)(2,1)} %get-tuple-element.13), channel_id=1, source_target_pairs={{0,4},{1,5},{2,6},{3,7},{16,20},{17,21},{18,22},{19,23}} | collective-permute-start | bytes 1277960 | tf_op jit(solution)/shard_map/up/ppermute | solution.py:28
  33.2 1.4 %collective-permute-start.10 = (bf16[32,2,3328]{2,0,1:T(8,128)(2,1)}, bf16[32,2,3328]{2,0,1:T(8,128)(2,1)}, u32[]{:S(2)}, u32[]{:S(2)}) collective-permute-start(bf16[32,2,3328]{2,0,1:T(8,128)(2,1)} %get-tuple-element.11), channel_id=1, source_target_pairs={{12,8},{13,9},{14,10},{15,11},{28,24},{29,25},{30,26},{31,27}} | collective-permute-start | bytes 1277960 | tf_op jit(solution)/shard_map/down/ppermute | solution.py:35
  34.7 1.4 %collective-permute-start.9 = (bf16[32,2,3328]{2,0,1:T(8,128)(2,1)}, bf16[32,2,3328]{2,0,1:T(8,128)(2,1)}, u32[]{:S(2)}, u32[]{:S(2)}) collective-permute-start(bf16[32,2,3328]{2,0,1:T(8,128)(2,1)} %get-tuple-element.14), channel_id=1, source_target_pairs={{12,8},{13,9},{14,10},{15,11},{28,24},{29,25},{30,26},{31,27}} | collective-permute-start | bytes 1277960 | tf_op jit(solution)/shard_map/down/ppermute | solution.py:35
  36.1 3.8 %collective-permute-done.5 = bf16[32,2,3328]{2,0,1:T(8,128)(2,1)S(1)} collective-permute-done((bf16[32,2,3328]{2,0,1:T(8,128)(2,1)S(1)}, bf16[32,2,3328]{2,0,1:T(8,128)(2,1)S(1)}, u32[]{:S(2)}, u32[]{:S(2)}) %collective-permute-start.5) | collective-permute-done | bytes 426016 | tf_op jit(solution)/shard_map/up/ppermute | solution.py:28
  39.9 0.8 copy-done.1
  40.6 13.6 %fusion.7 = bf16[128,2,3328]{2,0,1:T(8,128)(2,1)S(1)} fusion(bf16[2,2560,6656]{2,1,0:T(8,128)(2,1)} %param.3, bf16[128,2560]{1,0:T(8,128)(2,1)} %bitcast.94), kind=kOutput, calls=%fused_computation.5 | convolution fusion | flops 4362928128 | bytes 36438016 | tf_op jit(solution)/shard_map/td,gdf->tgf/dot_general | solution.py:57
  54.4 4.4 %collective-permute-start.15 = (bf16[32,2,3328]{2,0,1:T(8,128)(2,1)S(1)}, bf16[32,2,3328]{2,0,1:T(8,128)(2,1)S(1)}, u32[]{:S(2)}, u32[]{:S(2)}) collective-permute-start(bf16[32,2,3328]{2,0,1:T(8,128)(2,1)S(1)} %get-tuple-element.19), channel_id=1, source_target_pairs={{0,4},{1,5},{2,6},{3,7},{16,20},{17,21},{18,22},{19,23}} | collective-permute-start | bytes 1277960 | tf_op jit(solution)/shard_map/up/ppermute | solution.py:28
  59.5 1.2 %fusion.17 = (bf16[32,2,3328]{2,0,1:T(8,128)(2,1)S(1)}, bf16[32,2,3328]{2,0,1:T(8,128)(2,1)S(1)}) fusion(bf16[32,2,3328]{2,0,1:T(8,128)(2,1)S(1)} %copy-done.2, bf16[4,32,2,3328]{3,1,0,2:T(8,128)(2,1)S(1)} %bitcast.87, s32[]{:T(128)S(6)} %min.18, bf16[32,2,3328]{2,0,1:T(8,128)(2,1)} %collective-permute-done.10, s32[]{:T(128)S(6)} %min.20), kind=kLoop, calls=%fused_computation.21 | loop fusion | flops 1703936 | bytes 2555912 | tf_op jit(solution)/shard_map/up/convert_element_type | solution.py:25
  60.7 3.7 %collective-permute-done.15 = bf16[32,2,3328]{2,0,1:T(8,128)(2,1)S(1)} collective-permute-done((bf16[32,2,3328]{2,0,1:T(8,128)(2,1)S(1)}, bf16[32,2,3328]{2,0,1:T(8,128)(2,1)S(1)}, u32[]{:S(2)}, u32[]{:S(2)}) %collective-permute-start.15) | collective-permute-done | bytes 426016 | tf_op jit(solution)/shard_map/up/ppermute | solution.py:28
  65.1 0.7 collective-permute-start.11
  66.0 5.6 %collective-permute-start.14 = (bf16[32,2,3328]{2,0,1:T(8,128)(2,1)S(1)}, bf16[32,2,3328]{2,0,1:T(8,128)(2,1)S(1)}, u32[]{:S(2)}, u32[]{:S(2)}) collective-permute-start(bf16[32,2,3328]{2,0,1:T(8,128)(2,1)S(1)} %get-tuple-element.21), channel_id=1, source_target_pairs={{0,4},{1,5},{2,6},{3,7},{16,20},{17,21},{18,22},{19,23}} | collective-permute-start | bytes 1277960 | tf_op jit(solution)/shard_map/up/ppermute | solution.py:28
  71.7 0.7 collective-permute-start.19
  72.4 0.7 collective-permute-start.16
  73.8 1.5 %fusion.18 = (bf16[32,2,3328]{2,0,1:T(8,128)(2,1)S(1)}, bf16[32,2,3328]{2,0,1:T(8,128)(2,1)S(1)}) fusion(bf16[32,2,3328]{2,0,1:T(8,128)(2,1)} %collective-permute-done.4, bf16[32,2,3328]{2,0,1:T(8,128)(2,1)S(1)} %collective-permute-done.6, bf16[4,32,2,3328]{3,1,0,2:T(8,128)(2,1)S(1)} %bitcast.88, s32[]{:T(128)S(6)} %min.17, ...), kind=kLoop, calls=%fused_computation.23 | loop fusion | flops 2129920 | bytes 3407880 | tf_op jit(solution)/shard_map/up/convert_element_type | solution.py:25
  75.3 2.0 %collective-permute-done.14 = bf16[32,2,3328]{2,0,1:T(8,128)(2,1)S(1)} collective-permute-done((bf16[32,2,3328]{2,0,1:T(8,128)(2,1)S(1)}, bf16[32,2,3328]{2,0,1:T(8,128)(2,1)S(1)}, u32[]{:S(2)}, u32[]{:S(2)}) %collective-permute-start.14) | collective-permute-done | bytes 426016 | tf_op jit(solution)/shard_map/up/ppermute | solution.py:28
  77.3 6.7 %collective-permute-start.3 = (bf16[32,2,3328]{2,0,1:T(8,128)(2,1)}, bf16[32,2,3328]{2,0,1:T(8,128)(2,1)S(1)}, u32[]{:S(2)}, u32[]{:S(2)}) collective-permute-start(bf16[32,2,3328]{2,0,1:T(8,128)(2,1)} %get-tuple-element.14), channel_id=1, source_target_pairs={{0,4},{1,5},{2,6},{3,7},{16,20},{17,21},{18,22},{19,23}} | collective-permute-start | bytes 1277960 | tf_op jit(solution)/shard_map/up/ppermute | solution.py:28
  83.9 0.7 collective-permute-start.18
  85.4 1.3 %collective-permute-start.12 = (bf16[32,2,3328]{2,0,1:T(8,128)(2,1)S(1)}, bf16[32,2,3328]{2,0,1:T(8,128)(2,1)S(1)}, u32[]{:S(2)}, u32[]{:S(2)}) collective-permute-start(bf16[32,2,3328]{2,0,1:T(8,128)(2,1)S(1)} %get-tuple-element.8), channel_id=1, source_target_pairs={{4,0},{8,4},{5,1},{9,5},{6,2},{10,6},{7,3},{11,7},{20,16},{24,20},... | collective-permute-start | bytes 1277960 | tf_op jit(solution)/shard_map/down/ppermute | solution.py:38
  87.0 8.1 %collective-permute-start.13 = (bf16[32,2,3328]{2,0,1:T(8,128)(2,1)S(1)}, bf16[32,2,3328]{2,0,1:T(8,128)(2,1)S(1)}, u32[]{:S(2)}, u32[]{:S(2)}) collective-permute-start(bf16[32,2,3328]{2,0,1:T(8,128)(2,1)S(1)} %get-tuple-element.22), channel_id=1, source_target_pairs={{0,4},{1,5},{2,6},{3,7},{16,20},{17,21},{18,22},{19,23}} | collective-permute-start | bytes 1277960 | tf_op jit(solution)/shard_map/up/ppermute | solution.py:28
  95.8 1.3 %collective-permute-start.22 = (bf16[32,2,3328]{2,0,1:T(8,128)(2,1)S(1)}, bf16[32,2,3328]{2,0,1:T(8,128)(2,1)S(1)}, u32[]{:S(2)}, u32[]{:S(2)}) collective-permute-start(bf16[32,2,3328]{2,0,1:T(8,128)(2,1)S(1)} %get-tuple-element.16), channel_id=1, source_target_pairs={{4,0},{8,4},{5,1},{9,5},{6,2},{10,6},{7,3},{11,7},{20,16},{24,20},... | collective-permute-start | bytes 1277960 | tf_op jit(solution)/shard_map/down/ppermute | solution.py:38
  97.1 4.3 %collective-permute-done.12 = bf16[32,2,3328]{2,0,1:T(8,128)(2,1)S(1)} collective-permute-done((bf16[32,2,3328]{2,0,1:T(8,128)(2,1)S(1)}, bf16[32,2,3328]{2,0,1:T(8,128)(2,1)S(1)}, u32[]{:S(2)}, u32[]{:S(2)}) %collective-permute-start.12) | collective-permute-done | bytes 426016 | tf_op jit(solution)/shard_map/down/ppermute | solution.py:38
  101.4 1.3 %fusion.19 = f32[32,2,3328]{2,0,1:T(8,128)S(1)} fusion(bf16[32,2,3328]{2,0,1:T(8,128)(2,1)} %collective-permute-done.8, bf16[32,2,3328]{2,0,1:T(8,128)(2,1)S(1)} %collective-permute-done.12, bf16[32,2,3328]{2,0,1:T(8,128)(2,1)S(1)} %collective-permute-done.3, bf16[32,2,3328]{2,0,1:T(8,128)(2,1)S(1)} %collective-permute-done.7, ...), kind=kLoop, calls=%fused_computation.25 | loop fusion | flops 1490944 | bytes 2981892 | tf_op jit(solution)/shard_map/add | solution.py:63
  102.8 4.1 %collective-permute-done.22 = bf16[32,2,3328]{2,0,1:T(8,128)(2,1)S(1)} collective-permute-done((bf16[32,2,3328]{2,0,1:T(8,128)(2,1)S(1)}, bf16[32,2,3328]{2,0,1:T(8,128)(2,1)S(1)}, u32[]{:S(2)}, u32[]{:S(2)}) %collective-permute-start.22) | collective-permute-done | bytes 426016 | tf_op jit(solution)/shard_map/down/ppermute | solution.py:38
  107.4 0.8 pad_maximum_fusion
  (38 shorter events, 5.2 us)
Async XLA Ops:
  0.0 5.8 %collective-permute-start = (bf16[32,2560]{1,0:T(8,128)(2,1)}, bf16[32,2560]{1,0:T(8,128)(2,1)S(1)}, u32[]{:S(2)}, u32[]{:S(2)}) collective-permute-start(bf16[32,2560]{1,0:T(8,128)(2,1)} %param.2), channel_id=1, source_target_pairs={{0,1},{1,2},{2,3},{3,0},{4,5},{5,6},{6,7},{7,4},{8,9},{9,10},{10,1... | collective-permute-start | bytes 491528 | tf_op jit(solution)/shard_map/ppermute | solution.py:15
  0.5 10.7 %collective-permute-start.2 = (bf16[32,2560]{1,0:T(8,128)(2,1)}, bf16[32,2560]{1,0:T(8,128)(2,1)S(1)}, u32[]{:S(2)}, u32[]{:S(2)}) collective-permute-start(bf16[32,2560]{1,0:T(8,128)(2,1)} %param.2), channel_id=1, source_target_pairs={{0,3},{1,0},{2,1},{3,2},{4,7},{5,4},{6,5},{7,6},{8,11},{9,8},{10,9... | collective-permute-start | bytes 491528 | tf_op jit(solution)/shard_map/ppermute | solution.py:15
  2.4 8.7 %collective-permute-start.1 = (bf16[32,2560]{1,0:T(8,128)(2,1)}, bf16[32,2560]{1,0:T(8,128)(2,1)S(1)}, u32[]{:S(2)}, u32[]{:S(2)}) collective-permute-start(bf16[32,2560]{1,0:T(8,128)(2,1)} %param.2), channel_id=1, source_target_pairs={{0,2},{1,3},{2,0},{3,1},{4,6},{5,7},{6,4},{7,5},{8,10},{9,11},{10,... | collective-permute-start | bytes 491528 | tf_op jit(solution)/shard_map/ppermute | solution.py:15
  11.2 13.4 %copy-start = (bf16[4,32,2560]{2,1,0:T(8,128)(2,1)}, bf16[4,32,2560]{2,1,0:T(8,128)(2,1)S(1)}, u32[]{:S(2)}) copy-start(bf16[4,32,2560]{2,1,0:T(8,128)(2,1)S(1)} %bitcast_dynamic-update-slice_fusion) | copy-start | bytes 1966084
  25.7 14.2 %collective-permute-start.5 = (bf16[32,2,3328]{2,0,1:T(8,128)(2,1)S(1)}, bf16[32,2,3328]{2,0,1:T(8,128)(2,1)S(1)}, u32[]{:S(2)}, u32[]{:S(2)}) collective-permute-start(bf16[32,2,3328]{2,0,1:T(8,128)(2,1)S(1)} %get-tuple-element.12), channel_id=1, source_target_pairs={{0,4},{1,5},{2,6},{3,7},{16,20},{17,21},{18,22},{19,23}} | collective-permute-start | bytes 1277960 | tf_op jit(solution)/shard_map/up/ppermute | solution.py:28
  29.7 57.3 %collective-permute-start.8 = (bf16[32,2,3328]{2,0,1:T(8,128)(2,1)}, bf16[32,2,3328]{2,0,1:T(8,128)(2,1)}, u32[]{:S(2)}, u32[]{:S(2)}) collective-permute-start(bf16[32,2,3328]{2,0,1:T(8,128)(2,1)} %get-tuple-element.13), channel_id=1, source_target_pairs={{12,8},{13,9},{14,10},{15,11},{28,24},{29,25},{30,26},{31,27}} | collective-permute-start | bytes 1277960 | tf_op jit(solution)/shard_map/down/ppermute | solution.py:35
  31.2 34.8 %collective-permute-start.4 = (bf16[32,2,3328]{2,0,1:T(8,128)(2,1)}, bf16[32,2,3328]{2,0,1:T(8,128)(2,1)}, u32[]{:S(2)}, u32[]{:S(2)}) collective-permute-start(bf16[32,2,3328]{2,0,1:T(8,128)(2,1)} %get-tuple-element.13), channel_id=1, source_target_pairs={{0,4},{1,5},{2,6},{3,7},{16,20},{17,21},{18,22},{19,23}} | collective-permute-start | bytes 1277960 | tf_op jit(solution)/shard_map/up/ppermute | solution.py:28
  33.2 25.6 %collective-permute-start.10 = (bf16[32,2,3328]{2,0,1:T(8,128)(2,1)}, bf16[32,2,3328]{2,0,1:T(8,128)(2,1)}, u32[]{:S(2)}, u32[]{:S(2)}) collective-permute-start(bf16[32,2,3328]{2,0,1:T(8,128)(2,1)} %get-tuple-element.11), channel_id=1, source_target_pairs={{12,8},{13,9},{14,10},{15,11},{28,24},{29,25},{30,26},{31,27}} | collective-permute-start | bytes 1277960 | tf_op jit(solution)/shard_map/down/ppermute | solution.py:35
  34.7 37.0 %collective-permute-start.9 = (bf16[32,2,3328]{2,0,1:T(8,128)(2,1)}, bf16[32,2,3328]{2,0,1:T(8,128)(2,1)}, u32[]{:S(2)}, u32[]{:S(2)}) collective-permute-start(bf16[32,2,3328]{2,0,1:T(8,128)(2,1)} %get-tuple-element.14), channel_id=1, source_target_pairs={{12,8},{13,9},{14,10},{15,11},{28,24},{29,25},{30,26},{31,27}} | collective-permute-start | bytes 1277960 | tf_op jit(solution)/shard_map/down/ppermute | solution.py:35
  39.9 0.8 copy-start.1
  54.2 5.3 %copy-start.2 = (bf16[32,2,3328]{2,0,1:T(8,128)(2,1)S(1)}, bf16[32,2,3328]{2,0,1:T(8,128)(2,1)}, u32[]{:S(2)}) copy-start(bf16[32,2,3328]{2,0,1:T(8,128)(2,1)} %copy-done.1) | copy-start | bytes 1277956
  54.4 10.0 %collective-permute-start.15 = (bf16[32,2,3328]{2,0,1:T(8,128)(2,1)S(1)}, bf16[32,2,3328]{2,0,1:T(8,128)(2,1)S(1)}, u32[]{:S(2)}, u32[]{:S(2)}) collective-permute-start(bf16[32,2,3328]{2,0,1:T(8,128)(2,1)S(1)} %get-tuple-element.19), channel_id=1, source_target_pairs={{0,4},{1,5},{2,6},{3,7},{16,20},{17,21},{18,22},{19,23}} | collective-permute-start | bytes 1277960 | tf_op jit(solution)/shard_map/up/ppermute | solution.py:28
  58.8 6.3 %collective-permute-start.20 = (bf16[32,2,3328]{2,0,1:T(8,128)(2,1)S(1)}, bf16[32,2,3328]{2,0,1:T(8,128)(2,1)S(1)}, u32[]{:S(2)}, u32[]{:S(2)}) collective-permute-start(bf16[32,2,3328]{2,0,1:T(8,128)(2,1)S(1)} %get-tuple-element.20), channel_id=1, source_target_pairs={{12,8},{13,9},{14,10},{15,11},{28,24},{29,25},{30,26},{31,27}} | collective-permute-start | bytes 1277960 | tf_op jit(solution)/shard_map/down/ppermute | solution.py:35
  64.4 8.0 %collective-permute-start.6 = (bf16[32,2,3328]{2,0,1:T(8,128)(2,1)S(1)}, bf16[32,2,3328]{2,0,1:T(8,128)(2,1)S(1)}, u32[]{:S(2)}, u32[]{:S(2)}) collective-permute-start(bf16[32,2,3328]{2,0,1:T(8,128)(2,1)S(1)} %get-tuple-element.9), channel_id=1, source_target_pairs={{4,8},{5,9},{6,10},{7,11},{20,24},{21,25},{22,26},{23,27}} | collective-permute-start | bytes 1277960 | tf_op jit(solution)/shard_map/up/ppermute | solution.py:32
  65.1 8.0 %collective-permute-start.11 = (bf16[32,2,3328]{2,0,1:T(8,128)(2,1)S(1)}, bf16[32,2,3328]{2,0,1:T(8,128)(2,1)S(1)}, u32[]{:S(2)}, u32[]{:S(2)}) collective-permute-start(bf16[32,2,3328]{2,0,1:T(8,128)(2,1)S(1)} %get-tuple-element.10), channel_id=1, source_target_pairs={{8,4},{9,5},{10,6},{11,7},{24,20},{25,21},{26,22},{27,23}} | collective-permute-start | bytes 1277960 | tf_op jit(solution)/shard_map/down/ppermute | solution.py:38
  66.0 11.3 %collective-permute-start.14 = (bf16[32,2,3328]{2,0,1:T(8,128)(2,1)S(1)}, bf16[32,2,3328]{2,0,1:T(8,128)(2,1)S(1)}, u32[]{:S(2)}, u32[]{:S(2)}) collective-permute-start(bf16[32,2,3328]{2,0,1:T(8,128)(2,1)S(1)} %get-tuple-element.21), channel_id=1, source_target_pairs={{0,4},{1,5},{2,6},{3,7},{16,20},{17,21},{18,22},{19,23}} | collective-permute-start | bytes 1277960 | tf_op jit(solution)/shard_map/up/ppermute | solution.py:28
  71.7 12.3 %collective-permute-start.19 = (bf16[32,2,3328]{2,0,1:T(8,128)(2,1)S(1)}, bf16[32,2,3328]{2,0,1:T(8,128)(2,1)S(1)}, u32[]{:S(2)}, u32[]{:S(2)}) collective-permute-start(bf16[32,2,3328]{2,0,1:T(8,128)(2,1)S(1)} %get-tuple-element.22), channel_id=1, source_target_pairs={{12,8},{13,9},{14,10},{15,11},{28,24},{29,25},{30,26},{31,27}} | collective-permute-start | bytes 1277960 | tf_op jit(solution)/shard_map/down/ppermute | solution.py:35
  72.4 12.3 %collective-permute-start.16 = (bf16[32,2,3328]{2,0,1:T(8,128)(2,1)S(1)}, bf16[32,2,3328]{2,0,1:T(8,128)(2,1)S(1)}, u32[]{:S(2)}, u32[]{:S(2)}) collective-permute-start(bf16[32,2,3328]{2,0,1:T(8,128)(2,1)S(1)} %get-tuple-element.17), channel_id=1, source_target_pairs={{4,8},{5,9},{6,10},{7,11},{20,24},{21,25},{22,26},{23,27}} | collective-permute-start | bytes 1277960 | tf_op jit(solution)/shard_map/up/ppermute | solution.py:32
  73.1 12.3 %collective-permute-start.21 = (bf16[32,2,3328]{2,0,1:T(8,128)(2,1)S(1)}, bf16[32,2,3328]{2,0,1:T(8,128)(2,1)S(1)}, u32[]{:S(2)}, u32[]{:S(2)}) collective-permute-start(bf16[32,2,3328]{2,0,1:T(8,128)(2,1)S(1)} %get-tuple-element.18), channel_id=1, source_target_pairs={{8,4},{9,5},{10,6},{11,7},{24,20},{25,21},{26,22},{27,23}} | collective-permute-start | bytes 1277960 | tf_op jit(solution)/shard_map/down/ppermute | solution.py:38
  77.3 17.8 %collective-permute-start.3 = (bf16[32,2,3328]{2,0,1:T(8,128)(2,1)}, bf16[32,2,3328]{2,0,1:T(8,128)(2,1)S(1)}, u32[]{:S(2)}, u32[]{:S(2)}) collective-permute-start(bf16[32,2,3328]{2,0,1:T(8,128)(2,1)} %get-tuple-element.14), channel_id=1, source_target_pairs={{0,4},{1,5},{2,6},{3,7},{16,20},{17,21},{18,22},{19,23}} | collective-permute-start | bytes 1277960 | tf_op jit(solution)/shard_map/up/ppermute | solution.py:28
  83.9 18.8 %collective-permute-start.18 = (bf16[32,2,3328]{2,0,1:T(8,128)(2,1)S(1)}, bf16[32,2,3328]{2,0,1:T(8,128)(2,1)S(1)}, u32[]{:S(2)}, u32[]{:S(2)}) collective-permute-start(bf16[32,2,3328]{2,0,1:T(8,128)(2,1)S(1)} %get-tuple-element.21), channel_id=1, source_target_pairs={{12,8},{13,9},{14,10},{15,11},{28,24},{29,25},{30,26},{31,27}} | collective-permute-start | bytes 1277960 | tf_op jit(solution)/shard_map/down/ppermute | solution.py:35
  84.6 11.1 %collective-permute-start.7 = (bf16[32,2,3328]{2,0,1:T(8,128)(2,1)S(1)}, bf16[32,2,3328]{2,0,1:T(8,128)(2,1)S(1)}, u32[]{:S(2)}, u32[]{:S(2)}) collective-permute-start(bf16[32,2,3328]{2,0,1:T(8,128)(2,1)S(1)} %get-tuple-element.7), channel_id=1, source_target_pairs={{4,8},{8,12},{5,9},{9,13},{6,10},{10,14},{7,11},{11,15},{20,24},{2... | collective-permute-start | bytes 1277960 | tf_op jit(solution)/shard_map/up/ppermute | solution.py:32
  85.4 16.0 %collective-permute-start.12 = (bf16[32,2,3328]{2,0,1:T(8,128)(2,1)S(1)}, bf16[32,2,3328]{2,0,1:T(8,128)(2,1)S(1)}, u32[]{:S(2)}, u32[]{:S(2)}) collective-permute-start(bf16[32,2,3328]{2,0,1:T(8,128)(2,1)S(1)} %get-tuple-element.8), channel_id=1, source_target_pairs={{4,0},{8,4},{5,1},{9,5},{6,2},{10,6},{7,3},{11,7},{20,16},{24,20},... | collective-permute-start | bytes 1277960 | tf_op jit(solution)/shard_map/down/ppermute | solution.py:38
  87.0 15.8 %collective-permute-start.13 = (bf16[32,2,3328]{2,0,1:T(8,128)(2,1)S(1)}, bf16[32,2,3328]{2,0,1:T(8,128)(2,1)S(1)}, u32[]{:S(2)}, u32[]{:S(2)}) collective-permute-start(bf16[32,2,3328]{2,0,1:T(8,128)(2,1)S(1)} %get-tuple-element.22), channel_id=1, source_target_pairs={{0,4},{1,5},{2,6},{3,7},{16,20},{17,21},{18,22},{19,23}} | collective-permute-start | bytes 1277960 | tf_op jit(solution)/shard_map/up/ppermute | solution.py:28
  95.1 7.7 %collective-permute-start.17 = (bf16[32,2,3328]{2,0,1:T(8,128)(2,1)S(1)}, bf16[32,2,3328]{2,0,1:T(8,128)(2,1)S(1)}, u32[]{:S(2)}, u32[]{:S(2)}) collective-permute-start(bf16[32,2,3328]{2,0,1:T(8,128)(2,1)S(1)} %get-tuple-element.15), channel_id=1, source_target_pairs={{4,8},{8,12},{5,9},{9,13},{6,10},{10,14},{7,11},{11,15},{20,24},{2... | collective-permute-start | bytes 1277960 | tf_op jit(solution)/shard_map/up/ppermute | solution.py:32
  95.8 11.2 %collective-permute-start.22 = (bf16[32,2,3328]{2,0,1:T(8,128)(2,1)S(1)}, bf16[32,2,3328]{2,0,1:T(8,128)(2,1)S(1)}, u32[]{:S(2)}, u32[]{:S(2)}) collective-permute-start(bf16[32,2,3328]{2,0,1:T(8,128)(2,1)S(1)} %get-tuple-element.16), channel_id=1, source_target_pairs={{4,0},{8,4},{5,1},{9,5},{6,2},{10,6},{7,3},{11,7},{20,16},{24,20},... | collective-permute-start | bytes 1277960 | tf_op jit(solution)/shard_map/down/ppermute | solution.py:38

commit v17 on v16

--- a/solution.py
+++ b/solution.py
@@ -37,7 +37,7 @@
         for r in range(2, n):
             sent = lax.ppermute(add(block(p - n + r), minus), "row", [(q, q - 1) for q in range(n - r, n - 1)])
             minus = origin[r - 1] + sent
-    return plus, minus, first
+    return plus, minus, origin[0]
 
 
 def on_device(tokens, gate_up, n, m):

time: 109 us -> 106 us (0.972)
  waiting for transfers between devices: 23.3 us -> 21.5 us
  transfers between devices with their start and end apart: 23 -> 23, of which waited for: 6 -> 5; matrix products, arithmetic and copies ran while one was open for 18% -> 18% of each run, Pallas kernels for 0% -> 0%
where the time goes in v17:
time: 106 us
  starting transfers between devices  48.3 us (46%)
  matrix products  26.9 us (25%)
  waiting for transfers between devices  21.5 us (20%)
  other arithmetic  5.78 us (5%)
  local copies, waits for them, and re-layouts  3.01 us (3%)
    ppermute x6, starting transfers between devices, line_reduce(): origin = [lax.ppermute(part[n - r], 'row', [(0, 1)]) for r in range(1, n)]  31.3 us
    dot_general x2, matrix products, on_device(): jnp.einsum('td,gdf->tgf', held, w, preferred_element_type=jnp.float32)  26.9 us
    ppermute x6, waiting for transfers between devices, line_reduce(): origin = [lax.ppermute(part[n - r], 'row', [(0, 1)]) for r in range(1, n)]  8.51 us
    ppermute x4, waiting for transfers between devices, line_reduce(): lax.ppermute(add(block(p - n + r), minus), 'row', [(q, q - 1) for q in ra...  7.56 us
    ppermute x6, starting transfers between devices, line_reduce(): lax.ppermute(part[r - 1], 'row', [(n - 1, n - 2)])  5.63 us
    ppermute x3, waiting for transfers between devices, gather_cols(): got = lax.ppermute(tokens, 'col', [(i, (i + s) % m) for i in range(m)])  5.37 us
    ppermute x3, starting transfers between devices, gather_cols(): got = lax.ppermute(tokens, 'col', [(i, (i + s) % m) for i in range(m)])  4.71 us
    ppermute x4, starting transfers between devices, line_reduce(): lax.ppermute(add(block(p - n + r), minus), 'row', [(q, q - 1) for q in ra...  3.96 us
  transfers between devices with their start and end apart: 23, of which 5 were waited for; matrix products, arithmetic and copies ran while one was open for 18% of the time, Pallas kernels for 0%

profile of v17, /device:TPU:0, one launch (start us, length us, event | category | flops | bytes accessed | tf_op | source)
XLA Modules:
  0.0 105.9 jit_solution(5891045578926123708)
XLA Ops:
  0.5 1.9 %collective-permute-start.2 = (bf16[32,2560]{1,0:T(8,128)(2,1)}, bf16[32,2560]{1,0:T(8,128)(2,1)S(1)}, u32[]{:S(2)}, u32[]{:S(2)}) collective-permute-start(bf16[32,2560]{1,0:T(8,128)(2,1)} %param.2), channel_id=1, source_target_pairs={{0,3},{1,0},{2,1},{3,2},{4,7},{5,4},{6,5},{7,6},{8,11},{9,8},{10,9... | collective-permute-start | bytes 491528 | tf_op jit(solution)/shard_map/ppermute | solution.py:15
  2.4 2.3 %collective-permute-start.1 = (bf16[32,2560]{1,0:T(8,128)(2,1)}, bf16[32,2560]{1,0:T(8,128)(2,1)S(1)}, u32[]{:S(2)}, u32[]{:S(2)}) collective-permute-start(bf16[32,2560]{1,0:T(8,128)(2,1)} %param.2), channel_id=1, source_target_pairs={{0,2},{1,3},{2,0},{3,1},{4,6},{5,7},{6,4},{7,5},{8,10},{9,11},{10,... | collective-permute-start | bytes 491528 | tf_op jit(solution)/shard_map/ppermute | solution.py:15
  4.8 1.0 bitcast_dynamic-update-slice_fusion.3
  5.8 5.4 %collective-permute-done.1 = bf16[32,2560]{1,0:T(8,128)(2,1)S(1)} collective-permute-done((bf16[32,2560]{1,0:T(8,128)(2,1)}, bf16[32,2560]{1,0:T(8,128)(2,1)S(1)}, u32[]{:S(2)}, u32[]{:S(2)}) %collective-permute-start.1) | collective-permute-done | bytes 163872 | tf_op jit(solution)/shard_map/ppermute | solution.py:15
  11.2 13.4 %fusion.4 = bf16[128,2,3328]{2,0,1:T(8,128)(2,1)S(1)} fusion(bf16[128,2560,1]{1,0,2:T(8,128)(2,1)S(1)} %bitcast.93, bf16[2,2560,6656]{2,1,0:T(8,128)(2,1)} %param.3), kind=kOutput, calls=%fused_computation.4 | convolution fusion | flops 4362928128 | bytes 36438016 | tf_op jit(solution)/shard_map/td,gdf->tgf/dot_general | solution.py:57
  24.6 1.1 %fusion.25 = (bf16[32,2,3328]{2,0,1:T(8,128)(2,1)}, bf16[32,2,3328]{2,0,1:T(8,128)(2,1)S(1)}, bf16[32,2,3328]{2,0,1:T(8,128)(2,1)}, bf16[32,2,3328]{2,0,1:T(8,128)(2,1)}) fusion(bf16[128,2,3328]{2,0,1:T(8,128)(2,1)S(1)} %fusion.4), kind=kLoop, calls=%fused_computation.40 | loop fusion | bytes 3407872 | tf_op jit(solution)/shard_map/up/slice | solution.py:28
  26.4 1.5 %collective-permute-start.8 = (bf16[32,2,3328]{2,0,1:T(8,128)(2,1)}, bf16[32,2,3328]{2,0,1:T(8,128)(2,1)}, u32[]{:S(2)}, u32[]{:S(2)}) collective-permute-start(bf16[32,2,3328]{2,0,1:T(8,128)(2,1)} %get-tuple-element.13), channel_id=1, source_target_pairs={{12,8},{13,9},{14,10},{15,11},{28,24},{29,25},{30,26},{31,27}} | collective-permute-start | bytes 1277960 | tf_op jit(solution)/shard_map/down/ppermute | solution.py:35
  27.8 4.8 %collective-permute-start.4 = (bf16[32,2,3328]{2,0,1:T(8,128)(2,1)}, bf16[32,2,3328]{2,0,1:T(8,128)(2,1)}, u32[]{:S(2)}, u32[]{:S(2)}) collective-permute-start(bf16[32,2,3328]{2,0,1:T(8,128)(2,1)} %get-tuple-element.13), channel_id=1, source_target_pairs={{0,4},{1,5},{2,6},{3,7},{16,20},{17,21},{18,22},{19,23}} | collective-permute-start | bytes 1277960 | tf_op jit(solution)/shard_map/up/ppermute | solution.py:28
  32.6 2.0 %collective-permute-start.5 = (bf16[32,2,3328]{2,0,1:T(8,128)(2,1)}, bf16[32,2,3328]{2,0,1:T(8,128)(2,1)}, u32[]{:S(2)}, u32[]{:S(2)}) collective-permute-start(bf16[32,2,3328]{2,0,1:T(8,128)(2,1)} %get-tuple-element.11), channel_id=1, source_target_pairs={{0,4},{1,5},{2,6},{3,7},{16,20},{17,21},{18,22},{19,23}} | collective-permute-start | bytes 1277960 | tf_op jit(solution)/shard_map/up/ppermute | solution.py:28
  34.7 1.4 %collective-permute-start.9 = (bf16[32,2,3328]{2,0,1:T(8,128)(2,1)}, bf16[32,2,3328]{2,0,1:T(8,128)(2,1)}, u32[]{:S(2)}, u32[]{:S(2)}) collective-permute-start(bf16[32,2,3328]{2,0,1:T(8,128)(2,1)} %get-tuple-element.14), channel_id=1, source_target_pairs={{12,8},{13,9},{14,10},{15,11},{28,24},{29,25},{30,26},{31,27}} | collective-permute-start | bytes 1277960 | tf_op jit(solution)/shard_map/down/ppermute | solution.py:35
  36.1 0.8 copy-done.1
  36.9 13.6 %fusion.7 = bf16[128,2,3328]{2,0,1:T(8,128)(2,1)S(1)} fusion(bf16[2,2560,6656]{2,1,0:T(8,128)(2,1)} %param.3, bf16[128,2560]{1,0:T(8,128)(2,1)} %bitcast.94), kind=kOutput, calls=%fused_computation.5 | convolution fusion | flops 4362928128 | bytes 36438016 | tf_op jit(solution)/shard_map/td,gdf->tgf/dot_general | solution.py:57
  50.6 1.3 %collective-permute-start.15 = (bf16[32,2,3328]{2,0,1:T(8,128)(2,1)S(1)}, bf16[32,2,3328]{2,0,1:T(8,128)(2,1)S(1)}, u32[]{:S(2)}, u32[]{:S(2)}) collective-permute-start(bf16[32,2,3328]{2,0,1:T(8,128)(2,1)S(1)} %get-tuple-element.19), channel_id=1, source_target_pairs={{0,4},{1,5},{2,6},{3,7},{16,20},{17,21},{18,22},{19,23}} | collective-permute-start | bytes 1277960 | tf_op jit(solution)/shard_map/up/ppermute | solution.py:28
  51.9 0.7 collective-permute-start.20
  52.6 1.2 %fusion.17 = (bf16[32,2,3328]{2,0,1:T(8,128)(2,1)S(1)}, bf16[32,2,3328]{2,0,1:T(8,128)(2,1)S(1)}) fusion(bf16[32,2,3328]{2,0,1:T(8,128)(2,1)} %collective-permute-done.5, bf16[4,32,2,3328]{3,1,0,2:T(8,128)(2,1)S(1)} %bitcast.87, s32[]{:T(128)S(6)} %min.18, bf16[32,2,3328]{2,0,1:T(8,128)(2,1)S(1)} %copy-done.2, s32[]{:T(128)S(6)} %min.20), kind=kLoop, calls=%fused_computation.21 | loop fusion | flops 1703936 | bytes 2555912 | tf_op jit(solution)/shard_map/up/convert_element_type | solution.py:25
  53.8 5.7 %collective-permute-done.15 = bf16[32,2,3328]{2,0,1:T(8,128)(2,1)S(1)} collective-permute-done((bf16[32,2,3328]{2,0,1:T(8,128)(2,1)S(1)}, bf16[32,2,3328]{2,0,1:T(8,128)(2,1)S(1)}, u32[]{:S(2)}, u32[]{:S(2)}) %collective-permute-start.15) | collective-permute-done | bytes 426016 | tf_op jit(solution)/shard_map/up/ppermute | solution.py:28
  60.2 0.7 collective-permute-start.11
  61.1 6.0 %collective-permute-start.14 = (bf16[32,2,3328]{2,0,1:T(8,128)(2,1)S(1)}, bf16[32,2,3328]{2,0,1:T(8,128)(2,1)S(1)}, u32[]{:S(2)}, u32[]{:S(2)}) collective-permute-start(bf16[32,2,3328]{2,0,1:T(8,128)(2,1)S(1)} %get-tuple-element.21), channel_id=1, source_target_pairs={{0,4},{1,5},{2,6},{3,7},{16,20},{17,21},{18,22},{19,23}} | collective-permute-start | bytes 1277960 | tf_op jit(solution)/shard_map/up/ppermute | solution.py:28
  67.8 0.7 collective-permute-start.16
  68.5 0.7 collective-permute-start.21
  69.2 1.5 %fusion.18 = (bf16[32,2,3328]{2,0,1:T(8,128)(2,1)S(1)}, bf16[32,2,3328]{2,0,1:T(8,128)(2,1)S(1)}) fusion(bf16[32,2,3328]{2,0,1:T(8,128)(2,1)} %collective-permute-done.4, bf16[32,2,3328]{2,0,1:T(8,128)(2,1)S(1)} %collective-permute-done.6, bf16[4,32,2,3328]{3,1,0,2:T(8,128)(2,1)S(1)} %bitcast.88, s32[]{:T(128)S(6)} %min.17, ...), kind=kLoop, calls=%fused_computation.23 | loop fusion | flops 2129920 | bytes 3407880 | tf_op jit(solution)/shard_map/up/convert_element_type | solution.py:25
  70.7 2.8 %collective-permute-done.14 = bf16[32,2,3328]{2,0,1:T(8,128)(2,1)S(1)} collective-permute-done((bf16[32,2,3328]{2,0,1:T(8,128)(2,1)S(1)}, bf16[32,2,3328]{2,0,1:T(8,128)(2,1)S(1)}, u32[]{:S(2)}, u32[]{:S(2)}) %collective-permute-start.14) | collective-permute-done | bytes 426016 | tf_op jit(solution)/shard_map/up/ppermute | solution.py:28
  73.5 8.7 %collective-permute-start.3 = (bf16[32,2,3328]{2,0,1:T(8,128)(2,1)}, bf16[32,2,3328]{2,0,1:T(8,128)(2,1)S(1)}, u32[]{:S(2)}, u32[]{:S(2)}) collective-permute-start(bf16[32,2,3328]{2,0,1:T(8,128)(2,1)} %get-tuple-element.14), channel_id=1, source_target_pairs={{0,4},{1,5},{2,6},{3,7},{16,20},{17,21},{18,22},{19,23}} | collective-permute-start | bytes 1277960 | tf_op jit(solution)/shard_map/up/ppermute | solution.py:28
  82.2 0.7 collective-permute-start.18
  82.9 0.7 collective-permute-start.7
  83.6 1.3 %collective-permute-start.12 = (bf16[32,2,3328]{2,0,1:T(8,128)(2,1)S(1)}, bf16[32,2,3328]{2,0,1:T(8,128)(2,1)S(1)}, u32[]{:S(2)}, u32[]{:S(2)}) collective-permute-start(bf16[32,2,3328]{2,0,1:T(8,128)(2,1)S(1)} %get-tuple-element.8), channel_id=1, source_target_pairs={{4,0},{8,4},{5,1},{9,5},{6,2},{10,6},{7,3},{11,7},{20,16},{24,20},... | collective-permute-start | bytes 1277960 | tf_op jit(solution)/shard_map/down/ppermute | solution.py:38
  85.2 8.5 %collective-permute-start.13 = (bf16[32,2,3328]{2,0,1:T(8,128)(2,1)S(1)}, bf16[32,2,3328]{2,0,1:T(8,128)(2,1)S(1)}, u32[]{:S(2)}, u32[]{:S(2)}) collective-permute-start(bf16[32,2,3328]{2,0,1:T(8,128)(2,1)S(1)} %get-tuple-element.22), channel_id=1, source_target_pairs={{0,4},{1,5},{2,6},{3,7},{16,20},{17,21},{18,22},{19,23}} | collective-permute-start | bytes 1277960 | tf_op jit(solution)/shard_map/up/ppermute | solution.py:28
  94.5 1.3 %collective-permute-start.22 = (bf16[32,2,3328]{2,0,1:T(8,128)(2,1)S(1)}, bf16[32,2,3328]{2,0,1:T(8,128)(2,1)S(1)}, u32[]{:S(2)}, u32[]{:S(2)}) collective-permute-start(bf16[32,2,3328]{2,0,1:T(8,128)(2,1)S(1)} %get-tuple-element.16), channel_id=1, source_target_pairs={{4,0},{8,4},{5,1},{9,5},{6,2},{10,6},{7,3},{11,7},{20,16},{24,20},... | collective-permute-start | bytes 1277960 | tf_op jit(solution)/shard_map/down/ppermute | solution.py:38
  95.8 3.4 %collective-permute-done.12 = bf16[32,2,3328]{2,0,1:T(8,128)(2,1)S(1)} collective-permute-done((bf16[32,2,3328]{2,0,1:T(8,128)(2,1)S(1)}, bf16[32,2,3328]{2,0,1:T(8,128)(2,1)S(1)}, u32[]{:S(2)}, u32[]{:S(2)}) %collective-permute-start.12) | collective-permute-done | bytes 426016 | tf_op jit(solution)/shard_map/down/ppermute | solution.py:38
  99.2 1.3 %fusion.19 = f32[32,2,3328]{2,0,1:T(8,128)S(1)} fusion(bf16[32,2,3328]{2,0,1:T(8,128)(2,1)} %collective-permute-done.8, bf16[32,2,3328]{2,0,1:T(8,128)(2,1)S(1)} %collective-permute-done.12, bf16[32,2,3328]{2,0,1:T(8,128)(2,1)S(1)} %collective-permute-done.3, bf16[32,2,3328]{2,0,1:T(8,128)(2,1)S(1)} %collective-permute-done.7, ...), kind=kLoop, calls=%fused_computation.25 | loop fusion | flops 1490944 | bytes 2981892 | tf_op jit(solution)/shard_map/add | solution.py:63
  100.6 4.1 %collective-permute-done.22 = bf16[32,2,3328]{2,0,1:T(8,128)(2,1)S(1)} collective-permute-done((bf16[32,2,3328]{2,0,1:T(8,128)(2,1)S(1)}, bf16[32,2,3328]{2,0,1:T(8,128)(2,1)S(1)}, u32[]{:S(2)}, u32[]{:S(2)}) %collective-permute-start.22) | collective-permute-done | bytes 426016 | tf_op jit(solution)/shard_map/down/ppermute | solution.py:38
  105.2 0.8 pad_maximum_fusion
  (38 shorter events, 4.5 us)
Async XLA Ops:
  0.0 5.8 %collective-permute-start = (bf16[32,2560]{1,0:T(8,128)(2,1)}, bf16[32,2560]{1,0:T(8,128)(2,1)S(1)}, u32[]{:S(2)}, u32[]{:S(2)}) collective-permute-start(bf16[32,2560]{1,0:T(8,128)(2,1)} %param.2), channel_id=1, source_target_pairs={{0,1},{1,2},{2,3},{3,0},{4,5},{5,6},{6,7},{7,4},{8,9},{9,10},{10,1... | collective-permute-start | bytes 491528 | tf_op jit(solution)/shard_map/ppermute | solution.py:15
  0.5 10.7 %collective-permute-start.2 = (bf16[32,2560]{1,0:T(8,128)(2,1)}, bf16[32,2560]{1,0:T(8,128)(2,1)S(1)}, u32[]{:S(2)}, u32[]{:S(2)}) collective-permute-start(bf16[32,2560]{1,0:T(8,128)(2,1)} %param.2), channel_id=1, source_target_pairs={{0,3},{1,0},{2,1},{3,2},{4,7},{5,4},{6,5},{7,6},{8,11},{9,8},{10,9... | collective-permute-start | bytes 491528 | tf_op jit(solution)/shard_map/ppermute | solution.py:15
  2.4 8.7 %collective-permute-start.1 = (bf16[32,2560]{1,0:T(8,128)(2,1)}, bf16[32,2560]{1,0:T(8,128)(2,1)S(1)}, u32[]{:S(2)}, u32[]{:S(2)}) collective-permute-start(bf16[32,2560]{1,0:T(8,128)(2,1)} %param.2), channel_id=1, source_target_pairs={{0,2},{1,3},{2,0},{3,1},{4,6},{5,7},{6,4},{7,5},{8,10},{9,11},{10,... | collective-permute-start | bytes 491528 | tf_op jit(solution)/shard_map/ppermute | solution.py:15
  11.2 13.4 %copy-start = (bf16[4,32,2560]{2,1,0:T(8,128)(2,1)}, bf16[4,32,2560]{2,1,0:T(8,128)(2,1)S(1)}, u32[]{:S(2)}) copy-start(bf16[4,32,2560]{2,1,0:T(8,128)(2,1)S(1)} %bitcast_dynamic-update-slice_fusion) | copy-start | bytes 1966084
  25.7 10.4 %collective-permute-start.10 = (bf16[32,2,3328]{2,0,1:T(8,128)(2,1)S(1)}, bf16[32,2,3328]{2,0,1:T(8,128)(2,1)S(1)}, u32[]{:S(2)}, u32[]{:S(2)}) collective-permute-start(bf16[32,2,3328]{2,0,1:T(8,128)(2,1)S(1)} %get-tuple-element.12), channel_id=1, source_target_pairs={{12,8},{13,9},{14,10},{15,11},{28,24},{29,25},{30,26},{31,27}} | collective-permute-start | bytes 1277960 | tf_op jit(solution)/shard_map/down/ppermute | solution.py:35
  26.4 58.9 %collective-permute-start.8 = (bf16[32,2,3328]{2,0,1:T(8,128)(2,1)}, bf16[32,2,3328]{2,0,1:T(8,128)(2,1)}, u32[]{:S(2)}, u32[]{:S(2)}) collective-permute-start(bf16[32,2,3328]{2,0,1:T(8,128)(2,1)} %get-tuple-element.13), channel_id=1, source_target_pairs={{12,8},{13,9},{14,10},{15,11},{28,24},{29,25},{30,26},{31,27}} | collective-permute-start | bytes 1277960 | tf_op jit(solution)/shard_map/down/ppermute | solution.py:35
  27.8 33.3 %collective-permute-start.4 = (bf16[32,2,3328]{2,0,1:T(8,128)(2,1)}, bf16[32,2,3328]{2,0,1:T(8,128)(2,1)}, u32[]{:S(2)}, u32[]{:S(2)}) collective-permute-start(bf16[32,2,3328]{2,0,1:T(8,128)(2,1)} %get-tuple-element.13), channel_id=1, source_target_pairs={{0,4},{1,5},{2,6},{3,7},{16,20},{17,21},{18,22},{19,23}} | collective-permute-start | bytes 1277960 | tf_op jit(solution)/shard_map/up/ppermute | solution.py:28
  32.6 19.3 %collective-permute-start.5 = (bf16[32,2,3328]{2,0,1:T(8,128)(2,1)}, bf16[32,2,3328]{2,0,1:T(8,128)(2,1)}, u32[]{:S(2)}, u32[]{:S(2)}) collective-permute-start(bf16[32,2,3328]{2,0,1:T(8,128)(2,1)} %get-tuple-element.11), channel_id=1, source_target_pairs={{0,4},{1,5},{2,6},{3,7},{16,20},{17,21},{18,22},{19,23}} | collective-permute-start | bytes 1277960 | tf_op jit(solution)/shard_map/up/ppermute | solution.py:28
  34.7 32.4 %collective-permute-start.9 = (bf16[32,2,3328]{2,0,1:T(8,128)(2,1)}, bf16[32,2,3328]{2,0,1:T(8,128)(2,1)}, u32[]{:S(2)}, u32[]{:S(2)}) collective-permute-start(bf16[32,2,3328]{2,0,1:T(8,128)(2,1)} %get-tuple-element.14), channel_id=1, source_target_pairs={{12,8},{13,9},{14,10},{15,11},{28,24},{29,25},{30,26},{31,27}} | collective-permute-start | bytes 1277960 | tf_op jit(solution)/shard_map/down/ppermute | solution.py:35
  36.1 0.8 copy-start.1
  50.5 2.2 %copy-start.2 = (bf16[32,2,3328]{2,0,1:T(8,128)(2,1)S(1)}, bf16[32,2,3328]{2,0,1:T(8,128)(2,1)}, u32[]{:S(2)}) copy-start(bf16[32,2,3328]{2,0,1:T(8,128)(2,1)} %copy-done.1) | copy-start | bytes 1277956
  50.6 8.9 %collective-permute-start.15 = (bf16[32,2,3328]{2,0,1:T(8,128)(2,1)S(1)}, bf16[32,2,3328]{2,0,1:T(8,128)(2,1)S(1)}, u32[]{:S(2)}, u32[]{:S(2)}) collective-permute-start(bf16[32,2,3328]{2,0,1:T(8,128)(2,1)S(1)} %get-tuple-element.19), channel_id=1, source_target_pairs={{0,4},{1,5},{2,6},{3,7},{16,20},{17,21},{18,22},{19,23}} | collective-permute-start | bytes 1277960 | tf_op jit(solution)/shard_map/up/ppermute | solution.py:28
  51.9 8.3 %collective-permute-start.20 = (bf16[32,2,3328]{2,0,1:T(8,128)(2,1)S(1)}, bf16[32,2,3328]{2,0,1:T(8,128)(2,1)S(1)}, u32[]{:S(2)}, u32[]{:S(2)}) collective-permute-start(bf16[32,2,3328]{2,0,1:T(8,128)(2,1)S(1)} %get-tuple-element.20), channel_id=1, source_target_pairs={{12,8},{13,9},{14,10},{15,11},{28,24},{29,25},{30,26},{31,27}} | collective-permute-start | bytes 1277960 | tf_op jit(solution)/shard_map/down/ppermute | solution.py:35
  59.5 8.3 %collective-permute-start.6 = (bf16[32,2,3328]{2,0,1:T(8,128)(2,1)S(1)}, bf16[32,2,3328]{2,0,1:T(8,128)(2,1)S(1)}, u32[]{:S(2)}, u32[]{:S(2)}) collective-permute-start(bf16[32,2,3328]{2,0,1:T(8,128)(2,1)S(1)} %get-tuple-element.9), channel_id=1, source_target_pairs={{4,8},{5,9},{6,10},{7,11},{20,24},{21,25},{22,26},{23,27}} | collective-permute-start | bytes 1277960 | tf_op jit(solution)/shard_map/up/ppermute | solution.py:32
  60.2 8.3 %collective-permute-start.11 = (bf16[32,2,3328]{2,0,1:T(8,128)(2,1)S(1)}, bf16[32,2,3328]{2,0,1:T(8,128)(2,1)S(1)}, u32[]{:S(2)}, u32[]{:S(2)}) collective-permute-start(bf16[32,2,3328]{2,0,1:T(8,128)(2,1)S(1)} %get-tuple-element.10), channel_id=1, source_target_pairs={{8,4},{9,5},{10,6},{11,7},{24,20},{25,21},{26,22},{27,23}} | collective-permute-start | bytes 1277960 | tf_op jit(solution)/shard_map/down/ppermute | solution.py:38
  61.1 12.4 %collective-permute-start.14 = (bf16[32,2,3328]{2,0,1:T(8,128)(2,1)S(1)}, bf16[32,2,3328]{2,0,1:T(8,128)(2,1)S(1)}, u32[]{:S(2)}, u32[]{:S(2)}) collective-permute-start(bf16[32,2,3328]{2,0,1:T(8,128)(2,1)S(1)} %get-tuple-element.21), channel_id=1, source_target_pairs={{0,4},{1,5},{2,6},{3,7},{16,20},{17,21},{18,22},{19,23}} | collective-permute-start | bytes 1277960 | tf_op jit(solution)/shard_map/up/ppermute | solution.py:28
  67.1 15.1 %collective-permute-start.19 = (bf16[32,2,3328]{2,0,1:T(8,128)(2,1)S(1)}, bf16[32,2,3328]{2,0,1:T(8,128)(2,1)S(1)}, u32[]{:S(2)}, u32[]{:S(2)}) collective-permute-start(bf16[32,2,3328]{2,0,1:T(8,128)(2,1)S(1)} %get-tuple-element.22), channel_id=1, source_target_pairs={{12,8},{13,9},{14,10},{15,11},{28,24},{29,25},{30,26},{31,27}} | collective-permute-start | bytes 1277960 | tf_op jit(solution)/shard_map/down/ppermute | solution.py:35
  67.8 15.1 %collective-permute-start.16 = (bf16[32,2,3328]{2,0,1:T(8,128)(2,1)S(1)}, bf16[32,2,3328]{2,0,1:T(8,128)(2,1)S(1)}, u32[]{:S(2)}, u32[]{:S(2)}) collective-permute-start(bf16[32,2,3328]{2,0,1:T(8,128)(2,1)S(1)} %get-tuple-element.17), channel_id=1, source_target_pairs={{4,8},{5,9},{6,10},{7,11},{20,24},{21,25},{22,26},{23,27}} | collective-permute-start | bytes 1277960 | tf_op jit(solution)/shard_map/up/ppermute | solution.py:32
  68.5 15.1 %collective-permute-start.21 = (bf16[32,2,3328]{2,0,1:T(8,128)(2,1)S(1)}, bf16[32,2,3328]{2,0,1:T(8,128)(2,1)S(1)}, u32[]{:S(2)}, u32[]{:S(2)}) collective-permute-start(bf16[32,2,3328]{2,0,1:T(8,128)(2,1)S(1)} %get-tuple-element.18), channel_id=1, source_target_pairs={{8,4},{9,5},{10,6},{11,7},{24,20},{25,21},{26,22},{27,23}} | collective-permute-start | bytes 1277960 | tf_op jit(solution)/shard_map/down/ppermute | solution.py:38
  73.5 20.3 %collective-permute-start.3 = (bf16[32,2,3328]{2,0,1:T(8,128)(2,1)}, bf16[32,2,3328]{2,0,1:T(8,128)(2,1)S(1)}, u32[]{:S(2)}, u32[]{:S(2)}) collective-permute-start(bf16[32,2,3328]{2,0,1:T(8,128)(2,1)} %get-tuple-element.14), channel_id=1, source_target_pairs={{0,4},{1,5},{2,6},{3,7},{16,20},{17,21},{18,22},{19,23}} | collective-permute-start | bytes 1277960 | tf_op jit(solution)/shard_map/up/ppermute | solution.py:28
  82.2 18.4 %collective-permute-start.18 = (bf16[32,2,3328]{2,0,1:T(8,128)(2,1)S(1)}, bf16[32,2,3328]{2,0,1:T(8,128)(2,1)S(1)}, u32[]{:S(2)}, u32[]{:S(2)}) collective-permute-start(bf16[32,2,3328]{2,0,1:T(8,128)(2,1)S(1)} %get-tuple-element.21), channel_id=1, source_target_pairs={{12,8},{13,9},{14,10},{15,11},{28,24},{29,25},{30,26},{31,27}} | collective-permute-start | bytes 1277960 | tf_op jit(solution)/shard_map/down/ppermute | solution.py:35
  82.9 11.6 %collective-permute-start.7 = (bf16[32,2,3328]{2,0,1:T(8,128)(2,1)S(1)}, bf16[32,2,3328]{2,0,1:T(8,128)(2,1)S(1)}, u32[]{:S(2)}, u32[]{:S(2)}) collective-permute-start(bf16[32,2,3328]{2,0,1:T(8,128)(2,1)S(1)} %get-tuple-element.7), channel_id=1, source_target_pairs={{4,8},{8,12},{5,9},{9,13},{6,10},{10,14},{7,11},{11,15},{20,24},{2... | collective-permute-start | bytes 1277960 | tf_op jit(solution)/shard_map/up/ppermute | solution.py:32
  83.6 15.6 %collective-permute-start.12 = (bf16[32,2,3328]{2,0,1:T(8,128)(2,1)S(1)}, bf16[32,2,3328]{2,0,1:T(8,128)(2,1)S(1)}, u32[]{:S(2)}, u32[]{:S(2)}) collective-permute-start(bf16[32,2,3328]{2,0,1:T(8,128)(2,1)S(1)} %get-tuple-element.8), channel_id=1, source_target_pairs={{4,0},{8,4},{5,1},{9,5},{6,2},{10,6},{7,3},{11,7},{20,16},{24,20},... | collective-permute-start | bytes 1277960 | tf_op jit(solution)/shard_map/down/ppermute | solution.py:38
  85.2 15.4 %collective-permute-start.13 = (bf16[32,2,3328]{2,0,1:T(8,128)(2,1)S(1)}, bf16[32,2,3328]{2,0,1:T(8,128)(2,1)S(1)}, u32[]{:S(2)}, u32[]{:S(2)}) collective-permute-start(bf16[32,2,3328]{2,0,1:T(8,128)(2,1)S(1)} %get-tuple-element.22), channel_id=1, source_target_pairs={{0,4},{1,5},{2,6},{3,7},{16,20},{17,21},{18,22},{19,23}} | collective-permute-start | bytes 1277960 | tf_op jit(solution)/shard_map/up/ppermute | solution.py:28
  93.8 6.8 %collective-permute-start.17 = (bf16[32,2,3328]{2,0,1:T(8,128)(2,1)S(1)}, bf16[32,2,3328]{2,0,1:T(8,128)(2,1)S(1)}, u32[]{:S(2)}, u32[]{:S(2)}) collective-permute-start(bf16[32,2,3328]{2,0,1:T(8,128)(2,1)S(1)} %get-tuple-element.15), channel_id=1, source_target_pairs={{4,8},{8,12},{5,9},{9,13},{6,10},{10,14},{7,11},{11,15},{20,24},{2... | collective-permute-start | bytes 1277960 | tf_op jit(solution)/shard_map/up/ppermute | solution.py:32
  94.5 10.3 %collective-permute-start.22 = (bf16[32,2,3328]{2,0,1:T(8,128)(2,1)S(1)}, bf16[32,2,3328]{2,0,1:T(8,128)(2,1)S(1)}, u32[]{:S(2)}, u32[]{:S(2)}) collective-permute-start(bf16[32,2,3328]{2,0,1:T(8,128)(2,1)S(1)} %get-tuple-element.16), channel_id=1, source_target_pairs={{4,0},{8,4},{5,1},{9,5},{6,2},{10,6},{7,3},{11,7},{20,16},{24,20},... | collective-permute-start | bytes 1277960 | tf_op jit(solution)/shard_map/down/ppermute | solution.py:38
